TPU v7x, 32 devices: a whole 2x2x4 slice. The times are simulated.
32 devices in a mesh: seq: 8 (over z, y), mp: 4 (over x, core).
Axes of the slice: x: 2, y: 2, z: 4, core: 2. Of those that a mesh axis runs over, the one named last changes fastest.
Arguments:
- queries: bfloat16 [64, 64, 4096], P('seq', None, 'mp'), may hold values from -5 to 5
- out_grad: bfloat16 [64, 64, 4096], P('seq', None, 'mp'), may hold values from -6 to 6
- row_keys: bfloat16 [64, 128, 4096], P('seq', None, 'mp'), may hold values from -5 to 5
- row_values: bfloat16 [64, 128, 4096], P('seq', None, 'mp'), may hold values from -6 to 6
- neighbours: int32 [64, 2], P(('seq', 'mp')), may hold values from 0 to 63, as said below
Outputs:
- query_grad: bfloat16 [64, 64, 4096], P('seq', None, 'mp')
- key_grad: bfloat16 [64, 128, 4096], P('seq', None, 'mp')
- value_grad: bfloat16 [64, 128, 4096], P('seq', None, 'mp')
Inputs may be any that keep to these rules, and one draw needn't show every extreme that they name: Row r lies with seq index r // 8. The 2 neighbours of a span are different rows. The spans of one seq index retrieve at most 2 rows lying with any one seq index, and some seq indices are retrieved from that often by every seq index.
All inputs are finite; a program needn't handle non-finite values.
Results may differ from a plain program's by a relative error of at most 0.008.
Values may be sent and summed in bfloat16 or wider, within the bound.
No kernel may reach another device: no remote copies, remote signals or barrier semaphores. Data moves between devices by JAX's collectives and lax.ppermute only.
A program may use at most 320 MiB of HBM per device.

v0:
```python
import jax
import jax.numpy as jnp
from jax import lax
from jax.sharding import PartitionSpec as P

HEAD = 128
SPAN = 64
NLEN = 128
NBR = 2


slot_group = 8


def split_heads(tensor):
    return tensor.reshape(tensor.shape[:-1] + (tensor.shape[-1] // HEAD, HEAD))


def per_device(queries, out_grad, row_keys, row_values, neighbours):
    seq_count = lax.axis_size("seq")
    own_lists = lax.all_gather(neighbours, "mp", axis=0, tiled=True)
    span_count = queries.shape[0]
    rows_here = row_keys.shape[0]
    width_here = queries.shape[2]
    heads_here = width_here // HEAD
    flat_rows = own_lists.reshape(-1)
    item_count = flat_rows.shape[0]
    owner_dev = flat_rows // rows_here
    local_row = flat_rows % rows_here
    slot_depth = (item_count + seq_count - 1) // seq_count
    slot_total = seq_count * slot_depth
    position = jnp.arange(item_count)
    same_before = (owner_dev[:, None] == owner_dev[None, :]) & (
        position[None, :] < position[:, None]
    )
    earlier = jnp.sum(same_before.astype(jnp.int32), axis=1)
    target = owner_dev * slot_depth + earlier
    item_span = position // NBR
    score_scale = HEAD ** (-0.5)
    row_send = jnp.zeros((slot_total,), jnp.int32).at[target].set(local_row)
    query_send = (
        jnp.zeros((slot_total,) + queries.shape[1:], queries.dtype)
        .at[target]
        .set(queries[item_span])
    )
    grad_send = (
        jnp.zeros((slot_total,) + out_grad.shape[1:], out_grad.dtype)
        .at[target]
        .set(out_grad[item_span])
    )
    query_recv, grad_recv, row_recv = (
        lax.all_to_all(query_send, "seq", split_axis=0, concat_axis=0, tiled=True),
        lax.all_to_all(grad_send, "seq", split_axis=0, concat_axis=0, tiled=True),
        lax.all_to_all(row_send, "seq", split_axis=0, concat_axis=0, tiled=True),
    )
    group_count = slot_total // slot_group

    def grouped(tensor):
        return tensor.reshape((group_count, slot_group) + tensor.shape[1:])

    def first_pass(block):
        query_block, grad_block, row_block = block
        query_heads = split_heads(query_block)
        grad_heads = split_heads(grad_block)
        key_heads = split_heads(row_keys[row_block])
        value_heads = split_heads(row_values[row_block])
        scores = (
            jnp.einsum(
                "bihd,bjhd->bhij", query_heads, key_heads, preferred_element_type=jnp.float32
            )
            * score_scale
        )
        highest = jnp.max(scores, axis=3)
        expons = jnp.exp(scores - highest[..., None])
        grad_p = jnp.einsum(
            "bihd,bjhd->bhij", grad_heads, value_heads, preferred_element_type=jnp.float32
        )
        return (highest, jnp.sum(expons, axis=3), jnp.sum(expons * grad_p, axis=3))

    part_max, part_sum, part_cross = lax.map(
        first_pass, (grouped(query_recv), grouped(grad_recv), grouped(row_recv))
    )
    stat_shape = (slot_total, heads_here * SPAN)
    part_max = part_max.reshape(stat_shape)
    part_sum = part_sum.reshape(stat_shape)
    part_cross = part_cross.reshape(stat_shape)
    back_max, back_sum, back_cross = (
        lax.all_to_all(part_max, "seq", split_axis=0, concat_axis=0, tiled=True),
        lax.all_to_all(part_sum, "seq", split_axis=0, concat_axis=0, tiled=True),
        lax.all_to_all(part_cross, "seq", split_axis=0, concat_axis=0, tiled=True),
    )

    def per_item(tensor):
        return tensor[target].reshape(span_count, NBR, heads_here * SPAN)

    item_max = per_item(back_max)
    item_sum = per_item(back_sum)
    item_cross = per_item(back_cross)
    span_max = jnp.max(item_max, axis=1, keepdims=True)
    factor = jnp.exp(item_max - span_max)
    span_sum = jnp.sum(item_sum * factor, axis=1)
    log_total = span_max[:, 0] + jnp.log(span_sum)
    row_delta = jnp.sum(item_cross * factor, axis=1) / span_sum
    norm_send = jnp.zeros(stat_shape, jnp.float32).at[target].set(log_total[item_span])
    delta_send = jnp.zeros(stat_shape, jnp.float32).at[target].set(row_delta[item_span])
    norm_recv, delta_recv = (
        lax.all_to_all(norm_send, "seq", split_axis=0, concat_axis=0, tiled=True),
        lax.all_to_all(delta_send, "seq", split_axis=0, concat_axis=0, tiled=True),
    )

    def second_pass(carry, block):
        key_acc, value_acc = carry
        query_block, grad_block, row_block, norm_block, delta_block = block
        query_heads = split_heads(query_block)
        grad_heads = split_heads(grad_block)
        key_heads = split_heads(row_keys[row_block])
        value_heads = split_heads(row_values[row_block])
        scores = (
            jnp.einsum(
                "bihd,bjhd->bhij", query_heads, key_heads, preferred_element_type=jnp.float32
            )
            * score_scale
        )
        norm_here = norm_block.reshape(slot_group, heads_here, SPAN)
        delta_here = delta_block.reshape(slot_group, heads_here, SPAN)
        softmax_p = jnp.exp(scores - norm_here[..., None])
        grad_p = jnp.einsum(
            "bihd,bjhd->bhij", grad_heads, value_heads, preferred_element_type=jnp.float32
        )
        grad_s = (softmax_p * (grad_p - delta_here[..., None]) * score_scale).astype(jnp.bfloat16)
        probs_low = softmax_p.astype(jnp.bfloat16)
        value_part = jnp.einsum(
            "bhij,bihd->bjhd", probs_low, grad_heads, preferred_element_type=jnp.float32
        )
        key_part = jnp.einsum(
            "bhij,bihd->bjhd", grad_s, query_heads, preferred_element_type=jnp.float32
        )
        query_part = jnp.einsum(
            "bhij,bjhd->bihd", grad_s, key_heads, preferred_element_type=jnp.float32
        )
        value_part = value_part.reshape(slot_group, NLEN, width_here)
        key_part = key_part.reshape(slot_group, NLEN, width_here)
        query_part = query_part.astype(jnp.bfloat16).reshape(slot_group, SPAN, width_here)
        return (
            (key_acc.at[row_block].add(key_part), value_acc.at[row_block].add(value_part)),
            query_part,
        )

    start = (
        jnp.zeros((rows_here, NLEN, width_here), jnp.float32),
        jnp.zeros((rows_here, NLEN, width_here), jnp.float32),
    )
    blocks = (
        grouped(query_recv),
        grouped(grad_recv),
        grouped(row_recv),
        grouped(norm_recv),
        grouped(delta_recv),
    )
    (key_acc, value_acc), query_parts = lax.scan(second_pass, start, blocks)
    query_parts = query_parts.reshape(slot_total, SPAN, width_here)
    query_back = lax.all_to_all(query_parts, "seq", split_axis=0, concat_axis=0, tiled=True)
    returned = query_back[target].reshape(span_count, NBR, SPAN, width_here).astype(jnp.float32)
    query_grad = jnp.sum(returned, axis=1).astype(jnp.bfloat16)
    return (query_grad, key_acc.astype(jnp.bfloat16), value_acc.astype(jnp.bfloat16))


def solution(mesh):
    in_specs = (
        P("seq", None, "mp"),
        P("seq", None, "mp"),
        P("seq", None, "mp"),
        P("seq", None, "mp"),
        P(("seq", "mp"), None),
    )
    out_specs = (P("seq", None, "mp"), P("seq", None, "mp"), P("seq", None, "mp"))
    return jax.shard_map(
        per_device, mesh=mesh, in_specs=in_specs, out_specs=out_specs, check_vma=False
    )
```

profile of v0, /device:TPU:0, one launch (start us, length us, event | category | flops | bytes accessed | tf_op | source)
XLA Modules:
  0.0 379.6 jit_solution(11986066804225251472)
XLA Ops:
  0.6 6.4 %all-gather = s32[4,2,2]{2,1,0:T(2,128)S(1)} all-gather(s32[1,2,2]{2,1,0:T(2,128)} %bitcast.197), channel_id=1, replica_groups=mesh['seq'=8,'mp'=4] {'mp'}, dimensions={0}, use_global_device_ids=true | all-gather | bytes 80 | tf_op jit(solution)/shard_map/all_gather | solution.py:21
  8.7 6.3 %all-to-all-start = ((s32[8,2,1]{1,2,0:T(1,128)}), s32[8,2,1]{1,2,0:T(1,128)S(1)}, u32[]{:S(2)}, u32[]{:S(2)}) async-start(s32[8,2,1]{1,2,0:T(1,128)} %bitcast.15), calls=%async_computation | async-start | bytes 8192 | tf_op jit(solution)/shard_map/all_to_all | solution.py:54
  17.3 5.1 %scatter_fusion.2 = bf16[16,64,1024]{2,1,0:T(8,128)(2,1)} fusion(bf16[16,64,1024]{2,1,0:T(8,128)(2,1)} %broadcast.258.clone, s32[16]{0:T(128)S(1)} %fusion.51, bf16[16,64,1024]{2,1,0:T(8,128)(2,1)S(1)} %gather_fusion.4), kind=kCustom, calls=%fused_computation.15 | custom fusion | bytes 6291520 | tf_op jit(solution)/shard_map/scatter | solution.py:44
  22.5 6.1 %all-to-all-start.1 = ((bf16[16,64,1024]{2,1,0:T(8,128)(2,1)}), bf16[16,64,1024]{2,1,0:T(8,128)(2,1)}, u32[]{:S(2)}, u32[]{:S(2)}) async-start(bf16[16,64,1024]{2,1,0:T(8,128)(2,1)} %scatter_fusion.2), calls=%async_computation.1 | async-start | bytes 4194304 | tf_op jit(solution)/shard_map/all_to_all | solution.py:52
  30.9 5.1 %scatter_fusion.3 = bf16[16,64,1024]{2,1,0:T(8,128)(2,1)} fusion(bf16[16,64,1024]{2,1,0:T(8,128)(2,1)} %broadcast.258.clone.1, s32[16]{0:T(128)S(1)} %fusion.51, bf16[16,64,1024]{2,1,0:T(8,128)(2,1)S(1)} %gather_fusion.5), kind=kCustom, calls=%fused_computation.16 | custom fusion | bytes 6291520 | tf_op jit(solution)/shard_map/scatter | solution.py:49
  36.1 40.8 %all-to-all-done.1 = bf16[16,64,1024]{2,1,0:T(8,128)(2,1)} async-done(((bf16[16,64,1024]{2,1,0:T(8,128)(2,1)}), bf16[16,64,1024]{2,1,0:T(8,128)(2,1)}, u32[]{:S(2)}, u32[]{:S(2)}) %all-to-all-start.1) | async-done | bytes 2097184 | tf_op jit(solution)/shard_map/all_to_all | solution.py:52
  76.9 4.4 %all-to-all-start.2 = ((bf16[16,64,1024]{2,1,0:T(8,128)(2,1)}), bf16[16,64,1024]{2,1,0:T(8,128)(2,1)}, u32[]{:S(2)}, u32[]{:S(2)}) async-start(bf16[16,64,1024]{2,1,0:T(8,128)(2,1)} %scatter_fusion.3), calls=%async_computation.2 | async-start | bytes 4194304 | tf_op jit(solution)/shard_map/all_to_all | solution.py:53
  82.6 46.5 %all-to-all-done.2 = bf16[16,64,1024]{2,1,0:T(8,128)(2,1)} async-done(((bf16[16,64,1024]{2,1,0:T(8,128)(2,1)}), bf16[16,64,1024]{2,1,0:T(8,128)(2,1)}, u32[]{:S(2)}, u32[]{:S(2)}) %all-to-all-start.2) | async-done | bytes 2097184 | tf_op jit(solution)/shard_map/all_to_all | solution.py:53
  129.1 30.4 %while.28 = (s32[]{:T(128)}, f32[2,8,8,64]{3,2,1,0:T(8,128)S(1)}, f32[2,8,8,64]{3,2,1,0:T(8,128)S(1)}, f32[2,8,8,64]{3,2,1,0:T(8,128)S(1)}, bf16[2,8,64,1024]{3,...) while((s32[]{:T(128)}, f32[2,8,8,64]{3,2,1,0:T(8,128)S(1)}, ...), condition=%wide.region_8.9_spmd, body=%wide.region_4.8_spmd.sunk | while | flops 273142816 | bytes 42226008 | solution.py:80
  133.3 3.6 gather_fusion.1
  136.8 2.3 gather_fusion
  148.4 3.6 gather_fusion.1
  152.0 2.3 gather_fusion
  160.1 3.6 all-to-all-start.6
  164.5 6.0 %all-to-all-done.6 = f32[8,2,512]{2,1,0:T(2,128)S(1)} async-done(((f32[8,2,512]{2,1,0:T(2,128)}), f32[8,2,512]{2,1,0:T(2,128)S(1)}, u32[]{:S(2)}, u32[]{:S(2)}) %all-to-all-start.6) | async-done | bytes 32800 | tf_op jit(solution)/shard_map/all_to_all | solution.py:90
  170.4 3.3 all-to-all-start.3
  174.5 5.9 %all-to-all-done.3 = f32[8,2,512]{2,1,0:T(2,128)S(1)} async-done(((f32[8,2,512]{2,1,0:T(2,128)}), f32[8,2,512]{2,1,0:T(2,128)S(1)}, u32[]{:S(2)}, u32[]{:S(2)}) %all-to-all-start.3) | async-done | bytes 32800 | tf_op jit(solution)/shard_map/all_to_all | solution.py:88
  180.4 3.3 all-to-all-start.4
  185.1 5.3 %all-to-all-done.4 = f32[8,2,512]{2,1,0:T(2,128)S(1)} async-done(((f32[8,2,512]{2,1,0:T(2,128)}), f32[8,2,512]{2,1,0:T(2,128)S(1)}, u32[]{:S(2)}, u32[]{:S(2)}) %all-to-all-start.4) | async-done | bytes 32800 | tf_op jit(solution)/shard_map/all_to_all | solution.py:89
  192.6 3.3 all-to-all-start.7
  197.3 5.3 %all-to-all-done.7 = f32[8,2,512]{2,1,0:T(2,128)S(1)} async-done(((f32[8,2,512]{2,1,0:T(2,128)}), f32[8,2,512]{2,1,0:T(2,128)S(1)}, u32[]{:S(2)}, u32[]{:S(2)}) %all-to-all-start.7) | async-done | bytes 32800 | tf_op jit(solution)/shard_map/all_to_all | solution.py:108
  202.5 3.5 all-to-all-start.5
  206.1 6.4 %all-to-all-done.5 = f32[8,2,512]{2,1,0:T(2,128)S(1)} async-done(((f32[8,2,512]{2,1,0:T(2,128)}), f32[8,2,512]{2,1,0:T(2,128)S(1)}, u32[]{:S(2)}, u32[]{:S(2)}) %all-to-all-start.5) | async-done | bytes 32800 | tf_op jit(solution)/shard_map/all_to_all | solution.py:107
  212.5 2.5 broadcast.253.clone
  215.0 2.5 broadcast.253
  217.5 110.4 %while.29 = (s32[]{:T(128)}, f32[8,128,1024]{2,1,0:T(8,128)}, f32[8,128,1024]{2,1,0:T(8,128)}, bf16[2,8,64,1024]{3,2,1,0:T(8,128)(2,1)}, s32[2,8]{1,0:T(2,128)S(...) while((s32[]{:T(128)}, f32[8,128,1024]{2,1,0:T(8,128)}, ...), condition=%wide.region_17.18_spmd, body=%wide.region_14.17_spmd.sunk | while | flops 678429696 | bytes 136499760 | solution.py:160
  217.7 2.3 gather_fusion.2
  219.9 3.6 gather_fusion.3
  232.6 2.3 broadcast_in_dim.20
  234.9 4.5 %fusion.108 = f32[8,8,128,128]{3,2,1,0:T(8,128)} fusion(f32[8,8,64,128]{3,2,1,0:T(8,128)S(1)} %copy-done.3, f32[8,8,64]{2,1,0:T(8,128)S(1)} %sub.115, bf16[8,64,8,128]{3,2,1,0:T(8,128)(2,1)} %bitcast.187), kind=kOutput, calls=%fused_computation.55.clone.1 | convolution fusion | flops 135790592 | bytes 7356416 | tf_op jit(solution)/shard_map/while/body/eval_jaxpr/bhij,bihd->bjhd/dot_general | solution.py:132
  239.4 5.3 %copy.145 = f32[8,128,1024]{2,1,0:T(8,128)} copy(f32[8,128,1024]{1,2,0:T(8,128)} %bitcast.182) | data formatting | bytes 8388608 | tf_op jit(solution)/shard_map/while/body/eval_jaxpr/reshape | solution.py:141
  244.8 9.5 %scatter_fusion.1 = f32[8,128,1024]{2,1,0:T(8,128)} fusion(f32[8,128,1024]{2,1,0:T(8,128)} %get-tuple-element.353, s32[8]{0:T(128)S(1)} %fusion.105, f32[8,128,1024]{2,1,0:T(8,128)} %copy.145), kind=kCustom, calls=%fused_computation.13.clone.1 | custom fusion | flops 1048576 | bytes 12582944 | tf_op jit(solution)/shard_map/while/body/eval_jaxpr/scatter-add | solution.py:145
  255.8 2.7 fusion.107
  258.6 5.3 %copy.144 = f32[8,128,1024]{2,1,0:T(8,128)} copy(f32[8,128,1024]{1,2,0:T(8,128)} %bitcast.183) | data formatting | bytes 8388608 | tf_op jit(solution)/shard_map/while/body/eval_jaxpr/reshape | solution.py:142
  263.9 9.4 %scatter_fusion = f32[8,128,1024]{2,1,0:T(8,128)} fusion(f32[8,128,1024]{2,1,0:T(8,128)} %get-tuple-element.352, s32[8]{0:T(128)S(1)} %fusion.105, f32[8,128,1024]{2,1,0:T(8,128)} %copy.144), kind=kCustom, calls=%fused_computation.12.clone.1 | custom fusion | flops 1048576 | bytes 12582944 | tf_op jit(solution)/shard_map/while/body/eval_jaxpr/scatter-add | solution.py:145
  273.5 2.3 gather_fusion.2
  275.8 3.6 gather_fusion.3
  288.4 2.3 broadcast_in_dim.20
  290.7 4.5 %fusion.108 = f32[8,8,128,128]{3,2,1,0:T(8,128)} fusion(f32[8,8,64,128]{3,2,1,0:T(8,128)S(1)} %copy-done.3, f32[8,8,64]{2,1,0:T(8,128)S(1)} %sub.115, bf16[8,64,8,128]{3,2,1,0:T(8,128)(2,1)} %bitcast.187), kind=kOutput, calls=%fused_computation.55.clone.1 | convolution fusion | flops 135790592 | bytes 7356416 | tf_op jit(solution)/shard_map/while/body/eval_jaxpr/bhij,bihd->bjhd/dot_general | solution.py:132
  295.3 5.3 %copy.145 = f32[8,128,1024]{2,1,0:T(8,128)} copy(f32[8,128,1024]{1,2,0:T(8,128)} %bitcast.182) | data formatting | bytes 8388608 | tf_op jit(solution)/shard_map/while/body/eval_jaxpr/reshape | solution.py:141
  300.6 8.8 %scatter_fusion.1 = f32[8,128,1024]{2,1,0:T(8,128)} fusion(f32[8,128,1024]{2,1,0:T(8,128)} %get-tuple-element.353, s32[8]{0:T(128)S(1)} %fusion.105, f32[8,128,1024]{2,1,0:T(8,128)} %copy.145), kind=kCustom, calls=%fused_computation.13.clone.1 | custom fusion | flops 1048576 | bytes 12582944 | tf_op jit(solution)/shard_map/while/body/eval_jaxpr/scatter-add | solution.py:145
  311.0 2.7 fusion.107
  313.7 5.3 %copy.144 = f32[8,128,1024]{2,1,0:T(8,128)} copy(f32[8,128,1024]{1,2,0:T(8,128)} %bitcast.183) | data formatting | bytes 8388608 | tf_op jit(solution)/shard_map/while/body/eval_jaxpr/reshape | solution.py:142
  319.1 8.8 %scatter_fusion = f32[8,128,1024]{2,1,0:T(8,128)} fusion(f32[8,128,1024]{2,1,0:T(8,128)} %get-tuple-element.352, s32[8]{0:T(128)S(1)} %fusion.105, f32[8,128,1024]{2,1,0:T(8,128)} %copy.144), kind=kCustom, calls=%fused_computation.12.clone.1 | custom fusion | flops 1048576 | bytes 12582944 | tf_op jit(solution)/shard_map/while/body/eval_jaxpr/scatter-add | solution.py:145
  327.8 3.6 all-to-all-start.8
  331.5 4.0 %convert_element_type.24 = bf16[8,128,1024]{2,1,0:T(8,128)(2,1)} convert(f32[8,128,1024]{2,1,0:T(8,128)} %get-tuple-element.115) | non-fusion elementwise | flops 1048576 | bytes 6291456 | tf_op jit(solution)/shard_map/convert_element_type | solution.py:165
  337.1 37.1 %all-to-all-done.8 = bf16[16,64,1024]{2,1,0:T(8,128)(2,1)S(1)} async-done(((bf16[16,64,1024]{2,1,0:T(8,128)(2,1)}), bf16[16,64,1024]{2,1,0:T(8,128)(2,1)S(1)}, u32[]{:S(2)}, u32[]{:S(2)}) %all-to-all-start.8) | async-done | bytes 2097184 | tf_op jit(solution)/shard_map/all_to_all | solution.py:162
  376.3 3.3 bitcast_reduce_fusion
  (137 shorter events, 57.9 us)
Async XLA Ops:
  0.6 14.4 %copy-start = (bf16[8,64,1024]{2,1,0:T(8,128)(2,1)S(1)}, bf16[8,64,1024]{2,1,0:T(8,128)(2,1)}, u32[]{:S(2)}) copy-start(bf16[8,64,1024]{2,1,0:T(8,128)(2,1)} %param.9) | copy-start | bytes 3145732
  8.7 13.8 %all-to-all-start = ((s32[8,2,1]{1,2,0:T(1,128)}), s32[8,2,1]{1,2,0:T(1,128)S(1)}, u32[]{:S(2)}, u32[]{:S(2)}) async-start(s32[8,2,1]{1,2,0:T(1,128)} %bitcast.15), calls=%async_computation | async-start | bytes 8192 | tf_op jit(solution)/shard_map/all_to_all | solution.py:54
  22.5 6.1 %copy-start.12 = (bf16[8,64,1024]{2,1,0:T(8,128)(2,1)S(1)}, bf16[8,64,1024]{2,1,0:T(8,128)(2,1)}, u32[]{:S(2)}) copy-start(bf16[8,64,1024]{2,1,0:T(8,128)(2,1)} %param.10) | copy-start | bytes 3145732
  22.5 54.4 %all-to-all-start.1 = ((bf16[16,64,1024]{2,1,0:T(8,128)(2,1)}), bf16[16,64,1024]{2,1,0:T(8,128)(2,1)}, u32[]{:S(2)}, u32[]{:S(2)}) async-start(bf16[16,64,1024]{2,1,0:T(8,128)(2,1)} %scatter_fusion.2), calls=%async_computation.1 | async-start | bytes 4194304 | tf_op jit(solution)/shard_map/all_to_all | solution.py:52
  76.9 52.2 %all-to-all-start.2 = ((bf16[16,64,1024]{2,1,0:T(8,128)(2,1)}), bf16[16,64,1024]{2,1,0:T(8,128)(2,1)}, u32[]{:S(2)}, u32[]{:S(2)}) async-start(bf16[16,64,1024]{2,1,0:T(8,128)(2,1)} %scatter_fusion.3), calls=%async_computation.2 | async-start | bytes 4194304 | tf_op jit(solution)/shard_map/all_to_all | solution.py:53
  139.1 1.7 copy-start.10
  139.1 1.8 copy-start.11
  154.3 1.7 copy-start.10
  154.3 1.8 copy-start.11
  160.1 10.3 %all-to-all-start.6 = ((f32[8,2,512]{2,1,0:T(2,128)}), f32[8,2,512]{2,1,0:T(2,128)S(1)}, u32[]{:S(2)}, u32[]{:S(2)}) async-start(f32[8,2,512]{2,1,0:T(2,128)} %all_to_all.63), calls=%async_computation.6 | async-start | bytes 65536 | tf_op jit(solution)/shard_map/all_to_all | solution.py:90
  170.4 10.0 %all-to-all-start.3 = ((f32[8,2,512]{2,1,0:T(2,128)}), f32[8,2,512]{2,1,0:T(2,128)S(1)}, u32[]{:S(2)}, u32[]{:S(2)}) async-start(f32[8,2,512]{2,1,0:T(2,128)} %all_to_all.55), calls=%async_computation.3 | async-start | bytes 65536 | tf_op jit(solution)/shard_map/all_to_all | solution.py:88
  180.4 10.0 %all-to-all-start.4 = ((f32[8,2,512]{2,1,0:T(2,128)}), f32[8,2,512]{2,1,0:T(2,128)S(1)}, u32[]{:S(2)}, u32[]{:S(2)}) async-start(f32[8,2,512]{2,1,0:T(2,128)} %all_to_all.58), calls=%async_computation.4 | async-start | bytes 65536 | tf_op jit(solution)/shard_map/all_to_all | solution.py:89
  192.6 10.0 %all-to-all-start.7 = ((f32[8,2,512]{2,1,0:T(2,128)}), f32[8,2,512]{2,1,0:T(2,128)S(1)}, u32[]{:S(2)}, u32[]{:S(2)}) async-start(f32[8,2,512]{2,1,0:T(2,128)} %all_to_all.66), calls=%async_computation.7 | async-start | bytes 65536 | tf_op jit(solution)/shard_map/all_to_all | solution.py:108
  202.5 10.0 %all-to-all-start.5 = ((f32[8,2,512]{2,1,0:T(2,128)}), f32[8,2,512]{2,1,0:T(2,128)S(1)}, u32[]{:S(2)}, u32[]{:S(2)}) async-start(f32[8,2,512]{2,1,0:T(2,128)} %all_to_all.61), calls=%async_computation.5 | async-start | bytes 65536 | tf_op jit(solution)/shard_map/all_to_all | solution.py:107
  225.8 1.6 copy-start.5
  225.8 2.0 copy-start.9
  227.8 2.0 copy-start.2
  229.8 1.0 copy-start.7
  230.8 4.1 %copy-start.3 = (f32[8,8,64,128]{3,2,1,0:T(8,128)S(1)}, f32[8,8,64,128]{3,2,1,0:T(8,128)}, u32[]{:S(2)}) copy-start(f32[8,8,64,128]{3,2,1,0:T(8,128)} %copy-done.2) | copy-start | bytes 6291460 | tf_op jit(solution)/shard_map/while
  244.8 9.5 %copy-start.6 = (bf16[1,8,64,1024]{3,2,1,0:T(8,128)(2,1)S(1)}, bf16[1,8,64,1024]{3,2,1,0:T(8,128)(2,1)}, u32[]{:S(2)}) copy-start(bf16[1,8,64,1024]{3,2,1,0:T(8,128)(2,1)} %broadcast_in_dim.20) | copy-start | bytes 3145732 | tf_op jit(solution)/shard_map/while
  254.2 1.6 copy-start.8
  281.7 1.6 copy-start.5
  281.7 2.0 copy-start.9
  283.6 2.0 copy-start.2
  285.6 1.0 copy-start.7
  286.6 4.1 %copy-start.3 = (f32[8,8,64,128]{3,2,1,0:T(8,128)S(1)}, f32[8,8,64,128]{3,2,1,0:T(8,128)}, u32[]{:S(2)}) copy-start(f32[8,8,64,128]{3,2,1,0:T(8,128)} %copy-done.2) | copy-start | bytes 6291460 | tf_op jit(solution)/shard_map/while
  300.6 8.8 %copy-start.6 = (bf16[1,8,64,1024]{3,2,1,0:T(8,128)(2,1)S(1)}, bf16[1,8,64,1024]{3,2,1,0:T(8,128)(2,1)}, u32[]{:S(2)}) copy-start(bf16[1,8,64,1024]{3,2,1,0:T(8,128)(2,1)} %broadcast_in_dim.20) | copy-start | bytes 3145732 | tf_op jit(solution)/shard_map/while
  309.4 1.6 copy-start.8
  327.8 46.4 %all-to-all-start.8 = ((bf16[16,64,1024]{2,1,0:T(8,128)(2,1)}), bf16[16,64,1024]{2,1,0:T(8,128)(2,1)S(1)}, u32[]{:S(2)}, u32[]{:S(2)}) async-start(bf16[16,64,1024]{2,1,0:T(8,128)(2,1)} %bitcast.196), calls=%async_computation.8 | async-start | bytes 4194304 | tf_op jit(solution)/shard_map/all_to_all | solution.py:162
  331.5 4.0 %copy-start.4 = (f32[8,128,1024]{2,1,0:T(8,128)S(1)}, f32[8,128,1024]{2,1,0:T(8,128)}, u32[]{:S(2)}) copy-start(f32[8,128,1024]{2,1,0:T(8,128)} %get-tuple-element.116) | copy-start | bytes 12582916
  374.2 5.4 %copy-start.1 = (bf16[8,64,1024]{2,1,0:T(8,128)(2,1)S(1)}, bf16[8,64,1024]{2,1,0:T(8,128)(2,1)}, u32[]{:S(2)}) copy-start(bf16[8,64,1024]{2,1,0:T(8,128)(2,1)} %param.9) | copy-start | bytes 3145732
where the time goes:
time: 382 us; the launch traced here: 380 us
  waiting for transfers between devices  153 us (40%)
  local copies, waits for them, and re-layouts  102 us (27%)
  other arithmetic  49.2 us (13%)
  starting transfers between devices  37.6 us (10%)
  matrix products  29.9 us (8%)
  blocking collectives  6.39 us (2%)
    all_to_all x1, waiting for transfers between devices, per_device(): lax.all_to_all(grad_send, 'seq', split_axis=0, concat_axis=0, tiled=True)  46.5 us
    all_to_all x1, waiting for transfers between devices, per_device(): lax.all_to_all(query_send, 'seq', split_axis=0, concat_axis=0, tiled=True)  40.8 us
    all_to_all x1, waiting for transfers between devices, per_device(): lax.all_to_all(query_parts, 'seq', split_axis=0, concat_axis=0, tiled=True)  37.1 us
    scatter-add x2, other arithmetic, second_pass(): value_acc.at[row_block].add(value_part)  18.3 us
    scatter-add x2, other arithmetic, second_pass(): key_acc.at[row_block].add(key_part)  18.2 us
    reshape x2, local copies, waits for them, and re-layouts, second_pass(): key_part = key_part.reshape(slot_group, NLEN, width_here)  10.7 us
    reshape x2, local copies, waits for them, and re-layouts, second_pass(): value_part = value_part.reshape(slot_group, NLEN, width_here)  10.7 us
    dot_general x2, matrix products, second_pass(): jnp.einsum('bhij,bihd->bjhd', probs_low, grad_heads, preferred_element_ty...  9.09 us
  transfers between devices with their start and end apart: 9, of which 8 were waited for; matrix products, arithmetic and copies ran while one was open for 6% of the time, Pallas kernels for 0%

commit v1 on v0

v1 whole, which is shorter than its diff:
```python
import jax
import jax.numpy as jnp
from jax import lax
from jax.sharding import PartitionSpec as P

HEAD = 128
SPAN = 64
NLEN = 128
NBR = 2


def split_heads(tensor):
    return tensor.reshape(tensor.shape[:-1] + (tensor.shape[-1] // HEAD, HEAD))


def per_device(queries, out_grad, row_keys, row_values, neighbours):
    seq_count = lax.axis_size("seq")
    own_lists = lax.all_gather(neighbours, "mp", axis=0, tiled=True)
    span_count = queries.shape[0]
    rows_here = row_keys.shape[0]
    width_here = queries.shape[2]
    heads_here = width_here // HEAD
    flat_rows = own_lists.reshape(-1)
    item_count = flat_rows.shape[0]
    owner_dev = flat_rows // rows_here
    local_row = flat_rows % rows_here
    slot_depth = (item_count + seq_count - 1) // seq_count
    slot_total = seq_count * slot_depth
    position = jnp.arange(item_count)
    same_before = (owner_dev[:, None] == owner_dev[None, :]) & (
        position[None, :] < position[:, None]
    )
    earlier = jnp.sum(same_before.astype(jnp.int32), axis=1)
    target = owner_dev * slot_depth + earlier
    item_span = position // NBR
    score_scale = HEAD ** (-0.5)

    match = target[None, :] == jnp.arange(slot_total)[:, None]
    slot_valid = jnp.any(match, axis=1)
    slot_item = jnp.sum(jnp.where(match, position[None, :], 0), axis=1)
    slot_span = item_span[slot_item]

    both = jnp.stack([queries, out_grad], axis=1)
    pair_send = jnp.where(
        slot_valid[:, None, None, None], both[slot_span], jnp.zeros((), both.dtype)
    )
    row_send = jnp.where(slot_valid, local_row[slot_item], -1)
    pair_recv = lax.all_to_all(pair_send, "seq", split_axis=0, concat_axis=0, tiled=True)
    row_recv = lax.all_to_all(row_send, "seq", split_axis=0, concat_axis=0, tiled=True)

    recv_valid = row_recv >= 0
    row_index = jnp.clip(row_recv, 0, rows_here - 1)
    query_heads = split_heads(pair_recv[:, 0])
    grad_heads = split_heads(pair_recv[:, 1])
    key_heads = split_heads(row_keys[row_index])
    value_heads = split_heads(row_values[row_index])

    scores = (
        jnp.einsum("bihd,bjhd->bhij", query_heads, key_heads, preferred_element_type=jnp.float32)
        * score_scale
    )
    grad_p = jnp.einsum(
        "bihd,bjhd->bhij", grad_heads, value_heads, preferred_element_type=jnp.float32
    )
    highest = jnp.max(scores, axis=3)
    expons = jnp.exp(scores - highest[..., None])
    part = jnp.stack(
        [highest, jnp.sum(expons, axis=3), jnp.sum(expons * grad_p, axis=3)], axis=1
    ).reshape(slot_total, 3, heads_here * SPAN)
    back = lax.all_to_all(part, "seq", split_axis=0, concat_axis=0, tiled=True)

    item_part = back[target].reshape(span_count, NBR, 3, heads_here * SPAN)
    item_max = item_part[:, :, 0]
    item_sum = item_part[:, :, 1]
    item_cross = item_part[:, :, 2]
    span_max = jnp.max(item_max, axis=1, keepdims=True)
    factor = jnp.exp(item_max - span_max)
    span_sum = jnp.sum(item_sum * factor, axis=1)
    log_total = span_max[:, 0] + jnp.log(span_sum)
    row_delta = jnp.sum(item_cross * factor, axis=1) / span_sum
    span_stats = jnp.stack([log_total, row_delta], axis=1)
    stats_send = jnp.where(slot_valid[:, None, None], span_stats[slot_span], 0.0)
    stats_recv = lax.all_to_all(stats_send, "seq", split_axis=0, concat_axis=0, tiled=True)

    norm_here = stats_recv[:, 0].reshape(slot_total, heads_here, SPAN)
    delta_here = stats_recv[:, 1].reshape(slot_total, heads_here, SPAN)
    softmax_p = jnp.exp(scores - norm_here[..., None])
    grad_s = (softmax_p * (grad_p - delta_here[..., None]) * score_scale).astype(jnp.bfloat16)
    probs_low = softmax_p.astype(jnp.bfloat16)
    value_part = jnp.einsum(
        "bhij,bihd->bjhd", probs_low, grad_heads, preferred_element_type=jnp.float32
    ).reshape(slot_total, NLEN * width_here)
    key_part = jnp.einsum(
        "bhij,bihd->bjhd", grad_s, query_heads, preferred_element_type=jnp.float32
    ).reshape(slot_total, NLEN * width_here)
    query_part = jnp.einsum(
        "bhij,bjhd->bihd", grad_s, key_heads, preferred_element_type=jnp.float32
    ).astype(jnp.bfloat16).reshape(slot_total, SPAN, width_here)

    pick = (
        (row_recv[None, :] == jnp.arange(rows_here)[:, None]) & recv_valid[None, :]
    ).astype(jnp.float32)
    key_acc = jnp.dot(pick, key_part, precision=lax.Precision.HIGHEST)
    value_acc = jnp.dot(pick, value_part, precision=lax.Precision.HIGHEST)
    key_grad = key_acc.astype(jnp.bfloat16).reshape(rows_here, NLEN, width_here)
    value_grad = value_acc.astype(jnp.bfloat16).reshape(rows_here, NLEN, width_here)

    query_back = lax.all_to_all(query_part, "seq", split_axis=0, concat_axis=0, tiled=True)
    returned = query_back[target].reshape(span_count, NBR, SPAN, width_here).astype(jnp.float32)
    query_grad = jnp.sum(returned, axis=1).astype(jnp.bfloat16)
    return (query_grad, key_grad, value_grad)


def solution(mesh):
    in_specs = (
        P("seq", None, "mp"),
        P("seq", None, "mp"),
        P("seq", None, "mp"),
        P("seq", None, "mp"),
        P(("seq", "mp"), None),
    )
    out_specs = (P("seq", None, "mp"), P("seq", None, "mp"), P("seq", None, "mp"))
    return jax.shard_map(
        per_device, mesh=mesh, in_specs=in_specs, out_specs=out_specs, check_vma=False
    )
```

time: 382 us -> 246 us (0.64)
  waiting for transfers between devices: 153 us -> 92 us
  local copies, waits for them, and re-layouts: 102 us -> 51 us
  other arithmetic: 49.2 us -> 18.6 us
  starting transfers between devices: 37.6 us -> 20.5 us
  matrix products: 29.9 us -> 46.2 us
  blocking collectives: 6.39 us -> 15.7 us
    all_to_all x8 -> x3, waiting for transfers between devices: 153 us -> 92 us  [the longest x1 84.7 us: per_device(): lax.all_to_all(pair_send, 'seq', split_axis=0, concat_axis=0, tiled=True)]
    scatter-add x4 -> x0, other arithmetic: 36.5 us -> none  [the longest x2 18.3 us: second_pass(): value_acc.at[row_block].add(value_part)]
    reshape x10 -> x1, local copies, waits for them, and re-layouts: 21.5 us -> 1.91 us  [per_device(): query_part = jnp.einsum('bhij,bjhd->bihd', grad_s, key_heads, preferred_e...]
    transpose x0 -> x2, local copies, waits for them, and re-layouts: none -> 18.5 us  [the longest x1 9.26 us: per_device(): jnp.einsum('bhij,bihd->bjhd', grad_s, query_heads, preferred_element_type...]
    all_to_all x8 -> x3, starting transfers between devices: 31.3 us -> 14.2 us  [the longest x1 5.99 us: per_device(): lax.all_to_all(pair_send, 'seq', split_axis=0, concat_axis=0, tiled=True)]
    dot_general x14 -> x7, matrix products: 29.9 us -> 46.2 us  [the longest x1 11 us: per_device(): key_acc = jnp.dot(pick, key_part, precision=lax.Precision.HIGHEST)]
    gather x13 -> x7, local copies, waits for them, and re-layouts: 26.5 us -> 14 us  [the longest x1 4.37 us: per_device(): value_heads = split_heads(row_values[row_index])]
    scatter x5 -> x0, local copies, waits for them, and re-layouts: 12.3 us -> none  [the longest x1 5.15 us: per_device(): query_send = jnp.zeros((slot_total,) + queries.shape[1:], queries.dtype)....]
  transfers between devices with their start and end apart: 9 -> 4, of which waited for: 8 -> 2; matrix products, arithmetic and copies ran while one was open for 6% -> 32% of each run, Pallas kernels for 0% -> 0%
where the time goes in v1:
time: 246 us; the launch traced here: 245 us
  waiting for transfers between devices  92 us (37%)
  local copies, waits for them, and re-layouts  51 us (21%)
  matrix products  46.2 us (19%)
  starting transfers between devices  20.5 us (8%)
  other arithmetic  18.6 us (8%)
  blocking collectives  15.7 us (6%)
    all_to_all x1, waiting for transfers between devices, per_device(): lax.all_to_all(pair_send, 'seq', split_axis=0, concat_axis=0, tiled=True)  84.7 us
    dot_general x1, matrix products, per_device(): key_acc = jnp.dot(pick, key_part, precision=lax.Precision.HIGHEST)  11 us
    dot_general x1, matrix products, per_device(): value_acc = jnp.dot(pick, value_part, precision=lax.Precision.HIGHEST)  11 us
    all_to_all x1, blocking collectives, per_device(): lax.all_to_all(stats_send, 'seq', split_axis=0, concat_axis=0, tiled=True)  9.29 us
    transpose x1, local copies, waits for them, and re-layouts, per_device(): jnp.einsum('bhij,bihd->bjhd', grad_s, query_heads, preferred_element_type...  9.26 us
    transpose x1, local copies, waits for them, and re-layouts, per_device(): jnp.einsum('bhij,bihd->bjhd', probs_low, grad_heads, preferred_element_ty...  9.26 us
    unnamed x20, local copies, waits for them, and re-layouts  7.97 us
    all_to_all x1, waiting for transfers between devices, per_device(): back = lax.all_to_all(part, 'seq', split_axis=0, concat_axis=0, tiled=True)  7.32 us
  transfers between devices with their start and end apart: 4, of which 2 were waited for; matrix products, arithmetic and copies ran while one was open for 32% of the time, Pallas kernels for 0%

profile of v1, /device:TPU:0, one launch (start us, length us, event | category | flops | bytes accessed | tf_op | source)
XLA Modules:
  0.0 244.9 jit_solution(11363516858974016374)
XLA Ops:
  0.6 6.4 %all-gather = s32[4,2,2]{2,1,0:T(2,128)S(1)} all-gather(s32[1,2,2]{2,1,0:T(2,128)} %bitcast.119), channel_id=1, replica_groups=mesh['seq'=8,'mp'=4] {'mp'}, dimensions={0}, use_global_device_ids=true | all-gather | bytes 80 | tf_op jit(solution)/shard_map/all_gather | solution.py:18
  7.1 0.2 convert_reduce_fusion
  7.3 0.1 fusion.29
  7.4 0.1 select_reduce_fusion
  7.6 0.7 gather_fusion
  8.3 0.7 select_n.109
  8.9 6.3 %all-to-all-start = ((s32[8,2,1]{1,2,0:T(1,128)}), s32[8,2,1]{1,2,0:T(1,128)S(1)}, u32[]{:S(2)}, u32[]{:S(2)}) async-start(s32[8,2,1]{1,2,0:T(1,128)} %bitcast.3), calls=%async_computation | async-start | bytes 8192 | tf_op jit(solution)/shard_map/all_to_all | solution.py:49
  15.3 0.7 gather_fusion.2
  15.9 3.1 %pad_maximum_fusion = bf16[8,2,64,1024]{3,2,0,1:T(8,128)(2,1)} fusion(bf16[8,1,64,1024]{3,2,0,1:T(8,128)(2,1)} %bitcast.116, bf16[8,1,64,1024]{3,2,0,1:T(8,128)(2,1)} %bitcast.117), kind=kLoop, calls=%fused_computation.34 | loop fusion | flops 1048576 | bytes 4194304 | tf_op jit(solution)/shard_map/stack | solution.py:43
  19.0 4.4 %gather_fusion.3 = bf16[16,2,64,1024]{3,2,1,0:T(8,128)(2,1)} fusion(bf16[8,2,64,1024]{3,2,0,1:T(8,128)(2,1)} %pad_maximum_fusion, s32[1024]{0:T(1024)S(1)} %pad_clamp_fusion.2), kind=kCustom, calls=%fused_computation.3 | custom fusion | bytes 8388672 | tf_op jit(solution)/shard_map/gather | solution.py:45
  23.4 4.5 %broadcast_select_fusion = bf16[16,2,64,1024]{3,2,1,0:T(8,128)(2,1)} fusion(bf16[16,2,64,1024]{3,2,1,0:T(8,128)(2,1)} %gather_fusion.3, pred[16]{0:T(512)(128)(4,1)S(1)} %fusion.29), kind=kLoop, calls=%fused_computation.25 | loop fusion | flops 2097152 | bytes 8388624 | tf_op jit(solution)/shard_map/jit(_where)/select_n | solution.py:44
  27.8 6.0 %all-to-all-start.1 = ((bf16[16,2,64,1024]{3,2,1,0:T(8,128)(2,1)}), bf16[16,2,64,1024]{3,2,1,0:T(8,128)(2,1)}, u32[]{:S(2)}, u32[]{:S(2)}) async-start(bf16[16,2,64,1024]{3,2,1,0:T(8,128)(2,1)} %broadcast_select_fusion), calls=%async_computation.1 | async-start | bytes 8388608 | tf_op jit(solution)/shard_map/all_to_all | solution.py:48
  33.9 0.5 broadcast.308
  34.4 0.7 fusion.43
  35.2 2.7 %gather_fusion.1 = bf16[16,128,1024]{2,1,0:T(8,128)(2,1)} fusion(bf16[8,128,1024]{2,1,0:T(8,128)(2,1)S(1)} %copy-done, s32[1024]{0:T(1024)S(1)} %pad_clamp_fusion.1), kind=kCustom, calls=%fused_computation.1 | custom fusion | bytes 8388672 | tf_op jit(solution)/shard_map/gather | solution.py:55
  38.0 4.4 %gather_fusion.4 = bf16[16,128,1024]{2,1,0:T(8,128)(2,1)} fusion(bf16[8,128,1024]{2,1,0:T(8,128)(2,1)} %param.8, s32[1024]{0:T(1024)S(1)} %pad_clamp_fusion.1), kind=kCustom, calls=%fused_computation.4 | custom fusion | bytes 8388672 | tf_op jit(solution)/shard_map/gather | solution.py:56
  42.3 84.7 %all-to-all-done.1 = bf16[16,2,64,1024]{3,2,1,0:T(8,128)(2,1)} async-done(((bf16[16,2,64,1024]{3,2,1,0:T(8,128)(2,1)}), bf16[16,2,64,1024]{3,2,1,0:T(8,128)(2,1)}, u32[]{:S(2)}, u32[]{:S(2)}) %all-to-all-start.1) | async-done | bytes 4194336 | tf_op jit(solution)/shard_map/all_to_all | solution.py:48
  127.0 2.8 %fusion.44 = (bf16[16,1,64,1024]{3,2,1,0:T(8,128)(2,1)S(1)}, bf16[16,1,64,1024]{3,2,1,0:T(8,128)(2,1)S(1)}) fusion(bf16[16,2,64,1024]{3,2,1,0:T(8,128)(2,1)} %all-to-all-done.1), kind=kLoop, calls=%fused_computation.102 | loop fusion | bytes 8388608 | tf_op jit(solution)/shard_map/slice | solution.py:53
  129.9 0.6 copy.67
  130.5 0.6 copy.68
  131.1 1.7 copy-done.2
  132.8 5.0 %multiply_reduce_fusion.1 = (f32[16,8,64]{2,1,0:T(8,128)S(1)}, f32[16,8,64,128]{3,2,1,0:T(8,128)}) fusion(bf16[16,64,8,128]{3,2,1,0:T(8,128)(2,1)S(1)} %bitcast.109, bf16[16,128,1024]{2,1,0:T(8,128)(2,1)S(1)} %copy-done.2), kind=kOutput, calls=%fused_computation.32 | convolution fusion | flops 270524416 | bytes 10518528 | tf_op jit(solution)/shard_map/bihd,bjhd->bhij/dot_general | solution.py:59
  137.9 7.2 %fusion.11 = (f32[16,8,64]{2,1,0:T(8,128)S(1)}, f32[16,8,64]{2,1,0:T(8,128)S(1)}, f32[16,8,64,128]{3,2,1,0:T(8,128)}) fusion(f32[16,8,64,128]{3,2,1,0:T(8,128)} %get-tuple-element.34, f32[16,8,64]{2,1,0:T(8,128)S(1)} %get-tuple-element.33, bf16[16,64,8,128]{3,2,1,0:T(8,128)(2,1)S(1)} %bitcast.107, bf16[16,128,1024]{2,1,0:T(8,128)(2,1)} %gather_fusion.4), kind=kOutput, calls=%fused_computation.26 | convolution fusion | flops 273661952 | bytes 14778368 | tf_op jit(solution)/shard_map/bihd,bjhd->bhij/dot_general | solution.py:62
  145.1 0.1 stack.30
  145.2 0.1 stack.31
  145.3 0.7 pad_maximum_fusion.1
  146.1 3.6 %all-to-all-start.2 = ((f32[16,3,512]{2,1,0:T(4,128)}), f32[16,3,512]{2,1,0:T(4,128)S(1)}, u32[]{:S(2)}, u32[]{:S(2)}) async-start(f32[16,3,512]{2,1,0:T(4,128)} %pad_maximum_fusion.1), calls=%async_computation.2 | async-start | bytes 262144 | tf_op jit(solution)/shard_map/all_to_all | solution.py:70
  149.7 7.3 %all-to-all-done.2 = f32[16,3,512]{2,1,0:T(4,128)S(1)} async-done(((f32[16,3,512]{2,1,0:T(4,128)}), f32[16,3,512]{2,1,0:T(4,128)S(1)}, u32[]{:S(2)}, u32[]{:S(2)}) %all-to-all-start.2) | async-done | bytes 98336 | tf_op jit(solution)/shard_map/all_to_all | solution.py:70
  157.1 0.6 gather_fusion.5
  157.7 0.1 fusion.45
  157.8 0.1 fusion.25
  158.0 0.6 gather_fusion.6
  158.8 9.3 %all_to_all.26 = f32[16,2,512]{2,1,0:T(2,128)S(1)} all-to-all(f32[16,2,512]{2,1,0:T(2,128)S(1)} %broadcast_select_fusion.1), channel_id=1, replica_groups=mesh['seq'=8,'mp'=4] {'seq'}, dimensions={0} | all-to-all | bytes 131072 | tf_op jit(solution)/shard_map/all_to_all | solution.py:83
  168.0 0.2 slice_reduce_fusion.1
  168.4 5.4 %multiply_convert_fusion = bf16[16,8,64,128]{3,2,1,0:T(8,128)(2,1)S(1)} fusion(f32[16,8,64,128]{3,2,1,0:T(8,128)} %get-tuple-element.35, f32[16,8,64,128]{3,2,1,0:T(8,128)} %get-tuple-element.34, f32[16,8,64]{2,1,0:T(8,128)S(1)} %sub.55, f32[16,8,64]{2,1,0:T(8,128)S(1)} %sub.52), kind=kLoop, calls=%fused_computation.21 | loop fusion | flops 6291456 | bytes 10551296 | tf_op jit(solution)/shard_map/convert_element_type | solution.py:88
  173.8 1.2 convert_bitcast_fusion
  175.1 1.9 copy.125
  177.0 4.5 %all-to-all-start.4 = ((bf16[16,64,1024]{2,1,0:T(8,128)(2,1)}), bf16[16,64,1024]{2,1,0:T(8,128)(2,1)}, u32[]{:S(2)}, u32[]{:S(2)}) async-start(bf16[16,64,1024]{2,1,0:T(8,128)(2,1)} %bitcast.111), calls=%async_computation.4 | async-start | bytes 4194304 | tf_op jit(solution)/shard_map/all_to_all | solution.py:108
  181.7 6.3 %convolution_bitcast_fusion = f32[16,128,8,128]{1,3,2,0:T(8,128)} fusion(f32[16,8,64,128]{3,2,1,0:T(8,128)} %get-tuple-element.34, f32[16,8,64]{2,1,0:T(8,128)S(1)} %sub.52, bf16[16,64,8,128]{3,2,1,0:T(8,128)(2,1)S(1)} %bitcast.108), kind=kOutput, calls=%fused_computation.30 | convolution fusion | flops 271581184 | bytes 14712832 | tf_op jit(solution)/shard_map/bhij,bihd->bjhd/dot_general | solution.py:90
  188.0 9.3 %copy.57 = f32[16,128,8,128]{3,2,1,0:T(8,128)} copy(f32[16,128,8,128]{1,3,2,0:T(8,128)} %convolution_bitcast_fusion) | data formatting | bytes 16777216 | tf_op jit(solution)/shard_map/bhij,bihd->bjhd/transpose | solution.py:90
  197.2 11.0 %convolution_convert_fusion = bf16[8,131072]{1,0:T(8,128)(2,1)S(1)} fusion(f32[2,8,1024,128]{3,2,1,0:T(8,128)} %bitcast.106, s32[16]{0:T(128)S(1)} %eq.46, pred[16]{0:T(512)(128)(4,1)S(1)} %broadcast_compare_fusion), kind=kOutput, calls=%fused_computation.8 | convolution fusion | flops 202375424 | bytes 10485840 | tf_op jit(solution)/shard_map/dot_general | solution.py:104
  208.2 2.5 %copy.59 = bf16[8,128,1024]{2,1,0:T(8,128)(2,1)} copy(bf16[8,128,1024]{2,0,1:T(8,128)(2,1)S(1)} %bitcast.115) | data formatting | bytes 4194304
  210.7 4.5 %convolution_bitcast_fusion.1 = f32[16,128,8,128]{1,3,2,0:T(8,128)} fusion(bf16[16,8,64,128]{3,2,1,0:T(8,128)(2,1)S(1)} %copy-done.7, bf16[16,64,8,128]{3,2,1,0:T(8,128)(2,1)S(1)} %bitcast.110), kind=kOutput, calls=%fused_computation.31 | convolution fusion | flops 268435456 | bytes 12582912 | tf_op jit(solution)/shard_map/bhij,bihd->bjhd/dot_general | solution.py:93
  215.3 9.3 %copy.55 = f32[16,128,8,128]{3,2,1,0:T(8,128)} copy(f32[16,128,8,128]{1,3,2,0:T(8,128)} %convolution_bitcast_fusion.1) | data formatting | bytes 16777216 | tf_op jit(solution)/shard_map/bhij,bihd->bjhd/transpose | solution.py:93
  224.5 11.0 %convolution_convert_fusion.1 = bf16[8,131072]{1,0:T(8,128)(2,1)S(1)} fusion(f32[2,8,1024,128]{3,2,1,0:T(8,128)} %bitcast.105, s32[16]{0:T(128)S(1)} %eq.46, pred[16]{0:T(512)(128)(4,1)S(1)} %broadcast_compare_fusion), kind=kOutput, calls=%fused_computation.9 | convolution fusion | flops 202375424 | bytes 10485840 | tf_op jit(solution)/shard_map/dot_general | solution.py:103
  235.5 2.5 %copy.58 = bf16[8,128,1024]{2,1,0:T(8,128)(2,1)} copy(bf16[8,128,1024]{2,0,1:T(8,128)(2,1)S(1)} %bitcast.114) | data formatting | bytes 4194304
  238.0 3.6 %gather_fusion.7 = bf16[16,64,1024]{2,1,0:T(8,128)(2,1)} fusion(bf16[16,64,1024]{2,1,0:T(8,128)(2,1)} %all-to-all-done.4, s32[1024]{0:T(1024)S(1)} %pad_clamp_fusion), kind=kCustom, calls=%fused_computation.7 | custom fusion | bytes 4194368 | tf_op jit(solution)/shard_map/gather | solution.py:109
  241.6 3.3 %bitcast_reduce_fusion = bf16[8,64,1024]{2,1,0:T(8,128)(2,1)} fusion(bf16[16,64,1024]{2,1,0:T(8,128)(2,1)} %gather_fusion.7), kind=kLoop, calls=%fused_computation.35 | loop fusion | flops 524288 | bytes 3145728 | tf_op jit(solution)/shard_map/reduce_sum | solution.py:110
  (42 shorter events, 1.0 us)
Async XLA Ops:
  0.6 34.6 %copy-start = (bf16[8,128,1024]{2,1,0:T(8,128)(2,1)S(1)}, bf16[8,128,1024]{2,1,0:T(8,128)(2,1)}, u32[]{:S(2)}) copy-start(bf16[8,128,1024]{2,1,0:T(8,128)(2,1)} %param.7) | copy-start | bytes 6291460
  8.9 18.9 %all-to-all-start = ((s32[8,2,1]{1,2,0:T(1,128)}), s32[8,2,1]{1,2,0:T(1,128)S(1)}, u32[]{:S(2)}, u32[]{:S(2)}) async-start(s32[8,2,1]{1,2,0:T(1,128)} %bitcast.3), calls=%async_computation | async-start | bytes 8192 | tf_op jit(solution)/shard_map/all_to_all | solution.py:49
  27.8 99.2 %all-to-all-start.1 = ((bf16[16,2,64,1024]{3,2,1,0:T(8,128)(2,1)}), bf16[16,2,64,1024]{3,2,1,0:T(8,128)(2,1)}, u32[]{:S(2)}, u32[]{:S(2)}) async-start(bf16[16,2,64,1024]{3,2,1,0:T(8,128)(2,1)} %broadcast_select_fusion), calls=%async_computation.1 | async-start | bytes 8388608 | tf_op jit(solution)/shard_map/all_to_all | solution.py:48
  129.9 2.9 %copy-start.2 = (bf16[16,128,1024]{2,1,0:T(8,128)(2,1)S(1)}, bf16[16,128,1024]{2,1,0:T(8,128)(2,1)}, u32[]{:S(2)}) copy-start(bf16[16,128,1024]{2,1,0:T(8,128)(2,1)} %gather_fusion.1) | copy-start | bytes 12582916
  130.5 7.3 %copy-start.4 = (bf16[128,8,8,128]{3,2,1,0:T(8,128)(2,1)}, bf16[128,8,8,128]{3,2,1,0:T(8,128)(2,1)S(1)}, u32[]{:S(2)}) copy-start(bf16[128,8,8,128]{3,2,1,0:T(8,128)(2,1)S(1)} %copy.67) | copy-start | bytes 6291460
  146.1 11.0 %all-to-all-start.2 = ((f32[16,3,512]{2,1,0:T(4,128)}), f32[16,3,512]{2,1,0:T(4,128)S(1)}, u32[]{:S(2)}, u32[]{:S(2)}) async-start(f32[16,3,512]{2,1,0:T(4,128)} %pad_maximum_fusion.1), calls=%async_computation.2 | async-start | bytes 262144 | tf_op jit(solution)/shard_map/all_to_all | solution.py:70
  168.4 5.4 %copy-start.3 = (bf16[16,128,1024]{2,1,0:T(8,128)(2,1)S(1)}, bf16[16,128,1024]{2,1,0:T(8,128)(2,1)}, u32[]{:S(2)}) copy-start(bf16[16,128,1024]{2,1,0:T(8,128)(2,1)} %gather_fusion.1) | copy-start | bytes 12582916
  173.8 1.3 copy-start.6
  177.0 60.9 %all-to-all-start.4 = ((bf16[16,64,1024]{2,1,0:T(8,128)(2,1)}), bf16[16,64,1024]{2,1,0:T(8,128)(2,1)}, u32[]{:S(2)}, u32[]{:S(2)}) async-start(bf16[16,64,1024]{2,1,0:T(8,128)(2,1)} %bitcast.111), calls=%async_computation.4 | async-start | bytes 4194304 | tf_op jit(solution)/shard_map/all_to_all | solution.py:108
  208.2 2.5 %copy-start.5 = (bf16[128,8,8,128]{3,2,1,0:T(8,128)(2,1)S(1)}, bf16[128,8,8,128]{3,2,1,0:T(8,128)(2,1)}, u32[]{:S(2)}) copy-start(bf16[128,8,8,128]{3,2,1,0:T(8,128)(2,1)} %copy-done.4) | copy-start | bytes 6291460
  208.2 2.5 %copy-start.7 = (bf16[16,8,64,128]{3,2,1,0:T(8,128)(2,1)S(1)}, bf16[16,8,64,128]{3,2,1,0:T(8,128)(2,1)}, u32[]{:S(2)}) copy-start(bf16[16,8,64,128]{3,2,1,0:T(8,128)(2,1)} %copy-done.6) | copy-start | bytes 6291460
  235.5 9.4 %copy-start.1 = (bf16[8,128,1024]{2,1,0:T(8,128)(2,1)S(1)}, bf16[8,128,1024]{2,1,0:T(8,128)(2,1)}, u32[]{:S(2)}) copy-start(bf16[8,128,1024]{2,1,0:T(8,128)(2,1)} %param.7) | copy-start | bytes 6291460

commit v2 on v1

v2 whole, which is shorter than its diff:
```python
import jax
import jax.numpy as jnp
from jax import lax
from jax.sharding import PartitionSpec as P

HEAD = 128
SPAN = 64
NLEN = 128
NBR = 2


def split_heads(tensor):
    return tensor.reshape(tensor.shape[:-1] + (tensor.shape[-1] // HEAD, HEAD))


def send_stage(queries, out_grad, slot_valid, slot_span):
    both = jnp.stack([queries, out_grad], axis=1)
    pair_send = jnp.where(
        slot_valid[:, None, None, None], both[slot_span], jnp.zeros((), both.dtype)
    )
    return lax.all_to_all(pair_send, "seq", split_axis=0, concat_axis=0, tiled=True)


def first_stage(pair_recv, row_keys, row_values, row_index):
    slot_total = pair_recv.shape[0]
    heads_chunk = pair_recv.shape[-1] // HEAD
    score_scale = HEAD ** (-0.5)
    query_heads = split_heads(pair_recv[:, 0])
    grad_heads = split_heads(pair_recv[:, 1])
    key_heads = split_heads(row_keys[row_index])
    value_heads = split_heads(row_values[row_index])
    scores = (
        jnp.einsum("bihd,bjhd->bhij", query_heads, key_heads, preferred_element_type=jnp.float32)
        * score_scale
    )
    grad_p = jnp.einsum(
        "bihd,bjhd->bhij", grad_heads, value_heads, preferred_element_type=jnp.float32
    )
    highest = jnp.max(scores, axis=3)
    expons = jnp.exp(scores - highest[..., None])
    part = jnp.stack(
        [highest, jnp.sum(expons, axis=3), jnp.sum(expons * grad_p, axis=3)], axis=1
    ).reshape(slot_total, 3, heads_chunk * SPAN)
    return part, (query_heads, grad_heads, key_heads, scores, grad_p)


def stats_stage(part, target, slot_valid, slot_span, span_count):
    back = lax.all_to_all(part, "seq", split_axis=0, concat_axis=0, tiled=True)
    item_part = back[target].reshape((span_count, NBR) + part.shape[1:])
    item_max = item_part[:, :, 0]
    item_sum = item_part[:, :, 1]
    item_cross = item_part[:, :, 2]
    span_max = jnp.max(item_max, axis=1, keepdims=True)
    factor = jnp.exp(item_max - span_max)
    span_sum = jnp.sum(item_sum * factor, axis=1)
    log_total = span_max[:, 0] + jnp.log(span_sum)
    row_delta = jnp.sum(item_cross * factor, axis=1) / span_sum
    span_stats = jnp.stack([log_total, row_delta], axis=1)
    stats_send = jnp.where(slot_valid[:, None, None], span_stats[slot_span], 0.0)
    return lax.all_to_all(stats_send, "seq", split_axis=0, concat_axis=0, tiled=True)


def second_stage(kept, stats_recv, pick):
    query_heads, grad_heads, key_heads, scores, grad_p = kept
    slot_total, heads_chunk, span_len = scores.shape[:3]
    width_chunk = heads_chunk * HEAD
    score_scale = HEAD ** (-0.5)
    norm_here = stats_recv[:, 0].reshape(slot_total, heads_chunk, span_len)
    delta_here = stats_recv[:, 1].reshape(slot_total, heads_chunk, span_len)
    softmax_p = jnp.exp(scores - norm_here[..., None])
    grad_s = (softmax_p * (grad_p - delta_here[..., None]) * score_scale).astype(jnp.bfloat16)
    probs_low = softmax_p.astype(jnp.bfloat16)
    value_part = jnp.einsum(
        "bhij,bihd->bjhd", probs_low, grad_heads, preferred_element_type=jnp.float32
    ).reshape(slot_total, NLEN * width_chunk)
    key_part = jnp.einsum(
        "bhij,bihd->bjhd", grad_s, query_heads, preferred_element_type=jnp.float32
    ).reshape(slot_total, NLEN * width_chunk)
    query_part = jnp.einsum(
        "bhij,bjhd->bihd", grad_s, key_heads, preferred_element_type=jnp.float32
    ).astype(jnp.bfloat16).reshape(slot_total, span_len, width_chunk)
    query_back = lax.all_to_all(query_part, "seq", split_axis=0, concat_axis=0, tiled=True)
    key_acc = jnp.dot(pick, key_part, precision=lax.Precision.HIGHEST)
    value_acc = jnp.dot(pick, value_part, precision=lax.Precision.HIGHEST)
    rows_here = pick.shape[0]
    key_grad = key_acc.astype(jnp.bfloat16).reshape(rows_here, NLEN, width_chunk)
    value_grad = value_acc.astype(jnp.bfloat16).reshape(rows_here, NLEN, width_chunk)
    return query_back, key_grad, value_grad


def per_device(queries, out_grad, row_keys, row_values, neighbours):
    seq_count = lax.axis_size("seq")
    own_lists = lax.all_gather(neighbours, "mp", axis=0, tiled=True)
    span_count = queries.shape[0]
    rows_here = row_keys.shape[0]
    width_here = queries.shape[2]
    heads_here = width_here // HEAD
    flat_rows = own_lists.reshape(-1)
    item_count = flat_rows.shape[0]
    owner_dev = flat_rows // rows_here
    local_row = flat_rows % rows_here
    slot_depth = (item_count + seq_count - 1) // seq_count
    slot_total = seq_count * slot_depth
    position = jnp.arange(item_count)
    same_before = (owner_dev[:, None] == owner_dev[None, :]) & (
        position[None, :] < position[:, None]
    )
    earlier = jnp.sum(same_before.astype(jnp.int32), axis=1)
    target = owner_dev * slot_depth + earlier
    item_span = position // NBR

    match = target[None, :] == jnp.arange(slot_total)[:, None]
    slot_valid = jnp.any(match, axis=1)
    slot_item = jnp.sum(jnp.where(match, position[None, :], 0), axis=1)
    slot_span = item_span[slot_item]

    row_send = jnp.where(slot_valid, local_row[slot_item], -1)
    row_recv = lax.all_to_all(row_send, "seq", split_axis=0, concat_axis=0, tiled=True)
    recv_valid = row_recv >= 0
    row_index = jnp.clip(row_recv, 0, rows_here - 1)
    pick = (
        (row_recv[None, :] == jnp.arange(rows_here)[:, None]) & recv_valid[None, :]
    ).astype(jnp.float32)

    chunk_count = 2 if heads_here % 2 == 0 else 1
    chunk_width = width_here // chunk_count
    col_sets = [slice(k * chunk_width, (k + 1) * chunk_width) for k in range(chunk_count)]
    received = [
        send_stage(queries[..., cols], out_grad[..., cols], slot_valid, slot_span)
        for cols in col_sets
    ]
    parts, kept = [], []
    for k, cols in enumerate(col_sets):
        part, held = first_stage(
            received[k], row_keys[..., cols], row_values[..., cols], row_index
        )
        if k + 1 < chunk_count:
            part, received[k + 1] = lax.optimization_barrier((part, received[k + 1]))
        parts.append(part)
        kept.append(held)
    stats = [stats_stage(p, target, slot_valid, slot_span, span_count) for p in parts]
    outs = [second_stage(kept[k], stats[k], pick) for k in range(chunk_count)]
    query_grads = []
    for query_back, _, _ in outs:
        returned = query_back[target].reshape((span_count, NBR) + query_back.shape[1:])
        query_grads.append(jnp.sum(returned.astype(jnp.float32), axis=1).astype(jnp.bfloat16))
    query_grad = jnp.concatenate(query_grads, axis=-1)
    key_grad = jnp.concatenate([o[1] for o in outs], axis=-1)
    value_grad = jnp.concatenate([o[2] for o in outs], axis=-1)
    return (query_grad, key_grad, value_grad)


def solution(mesh):
    in_specs = (
        P("seq", None, "mp"),
        P("seq", None, "mp"),
        P("seq", None, "mp"),
        P("seq", None, "mp"),
        P(("seq", "mp"), None),
    )
    out_specs = (P("seq", None, "mp"), P("seq", None, "mp"), P("seq", None, "mp"))
    return jax.shard_map(
        per_device, mesh=mesh, in_specs=in_specs, out_specs=out_specs, check_vma=False
    )
```

time: 246 us -> 291 us (1.18)
  waiting for transfers between devices: 92 us -> 34.9 us
  blocking collectives: 15.7 us -> 60.3 us
  local copies, waits for them, and re-layouts: 51 us -> 89.3 us
  starting transfers between devices: 20.5 us -> 37.8 us
    all_to_all x3 -> x7, waiting for transfers between devices: 92 us -> 34.9 us  [the longest x1 21 us: send_stage(): lax.all_to_all(pair_send, 'seq', split_axis=0, concat_axis=0, tiled=True)]
    all_to_all x1, blocking collectives: 9.29 us -> 54.1 us  [send_stage(): lax.all_to_all(pair_send, 'seq', split_axis=0, concat_axis=0, tiled=True)]
    reshape x1 -> x10, local copies, waits for them, and re-layouts: 1.91 us -> 26.2 us  [the longest x2 9.82 us: second_stage(): key_part = jnp.einsum('bhij,bihd->bjhd', grad_s, query_heads, preferred_e...]
    all_to_all x3 -> x7, starting transfers between devices: 14.2 us -> 31.5 us  [the longest x2 10.7 us: second_stage(): lax.all_to_all(query_part, 'seq', split_axis=0, concat_axis=0, tiled=True)]
    another operation x3 -> x12, local copies, waits for them, and re-layouts: 0.29 us -> 7.71 us  [the longest x4 5.66 us: split_heads(): return tensor.reshape(tensor.shape[:-1] + (tensor.shape[-1] // HEAD, HEAD))]
    slice x2 -> x6, local copies, waits for them, and re-layouts: 2.96 us -> 8.09 us  [the longest x1 3.08 us: first_stage(): query_heads = split_heads(pair_recv[:, 0])]
    concatenate x0 -> x3, other arithmetic: none -> 4.29 us  [the longest x1 1.6 us: per_device(): key_grad = jnp.concatenate([o[1] for o in outs], axis=-1)]
    unnamed x20 -> x26, local copies, waits for them, and re-layouts: 7.97 us -> 3.72 us
  transfers between devices with their start and end apart: 4 -> 8, of which waited for: 2 -> 4; matrix products, arithmetic and copies ran while one was open for 32% -> 47% of each run, Pallas kernels for 0% -> 0%
where the time goes in v2:
time: 291 us; the launch traced here: 290 us
  local copies, waits for them, and re-layouts  89.3 us (31%)
  blocking collectives  60.3 us (21%)
  matrix products  48.4 us (17%)
  starting transfers between devices  37.8 us (13%)
  waiting for transfers between devices  34.9 us (12%)
  other arithmetic  17.8 us (6%)
    all_to_all x1, blocking collectives, send_stage(): lax.all_to_all(pair_send, 'seq', split_axis=0, concat_axis=0, tiled=True)  54.1 us
    all_to_all x1, waiting for transfers between devices, send_stage(): lax.all_to_all(pair_send, 'seq', split_axis=0, concat_axis=0, tiled=True)  21 us
    all_to_all x2, starting transfers between devices, second_stage(): lax.all_to_all(query_part, 'seq', split_axis=0, concat_axis=0, tiled=True)  10.7 us
    transpose x2, local copies, waits for them, and re-layouts, second_stage(): jnp.einsum('bhij,bihd->bjhd', grad_s, query_heads, preferred_element_type...  10.5 us
    transpose x2, local copies, waits for them, and re-layouts, second_stage(): jnp.einsum('bhij,bihd->bjhd', probs_low, grad_heads, preferred_element_ty...  10.5 us
    dot_general x2, matrix products, first_stage(): jnp.einsum('bihd,bjhd->bhij', grad_heads, value_heads, preferred_element_...  9.94 us
    reshape x2, local copies, waits for them, and re-layouts, second_stage(): key_part = jnp.einsum('bhij,bihd->bjhd', grad_s, query_heads, preferred_e...  9.82 us
    reshape x2, local copies, waits for them, and re-layouts, second_stage(): value_part = jnp.einsum('bhij,bihd->bjhd', probs_low, grad_heads, preferr...  9.82 us
  transfers between devices with their start and end apart: 8, of which 4 were waited for; matrix products, arithmetic and copies ran while one was open for 47% of the time, Pallas kernels for 0%

profile of v2, /device:TPU:0, one launch (start us, length us, event | category | flops | bytes accessed | tf_op | source)
XLA Modules:
  0.0 289.6 jit_solution(2918728603181363252)
XLA Ops:
  0.6 6.3 %all-gather = s32[4,2,2]{2,1,0:T(2,128)S(1)} all-gather(s32[1,2,2]{2,1,0:T(2,128)} %bitcast.183), channel_id=1, replica_groups=mesh['seq'=8,'mp'=4] {'mp'}, dimensions={0}, use_global_device_ids=true | all-gather | bytes 80 | tf_op jit(solution)/shard_map/all_gather | solution.py:93
  8.8 6.3 %all-to-all-start = ((s32[8,2,1]{1,2,0:T(1,128)}), s32[8,2,1]{1,2,0:T(1,128)S(1)}, u32[]{:S(2)}, u32[]{:S(2)}) async-start(s32[8,2,1]{1,2,0:T(1,128)} %bitcast.3), calls=%async_computation | async-start | bytes 8192 | tf_op jit(solution)/shard_map/all_to_all | solution.py:118
  17.5 2.0 gather_fusion.5
  19.6 2.0 gather_fusion.3
  21.6 3.9 %broadcast_select_fusion = (bf16[16,2,64,512]{3,2,1,0:T(8,128)(2,1)}, bf16[16,2,64,512]{3,2,1,0:T(8,128)(2,1)S(1)}) fusion(bf16[16,2,64,512]{3,2,1,0:T(8,128)(2,1)} %gather_fusion.5, pred[16]{0:T(512)(128)(4,1)S(1)} %fusion.62, bf16[16,2,64,512]{3,2,1,0:T(8,128)(2,1)} %gather_fusion.3), kind=kLoop, calls=%fused_computation.46 | loop fusion | flops 2097152 | bytes 8388624 | tf_op jit(solution)/shard_map/jit(_where)/select_n | solution.py:18
  25.5 54.1 %all_to_all.46 = bf16[16,2,64,512]{3,2,1,0:T(8,128)(2,1)} all-to-all(bf16[16,2,64,512]{3,2,1,0:T(8,128)(2,1)S(1)} %get-tuple-element.48), channel_id=1, replica_groups=mesh['seq'=8,'mp'=4] {'seq'}, dimensions={0} | all-to-all | bytes 4194304 | tf_op jit(solution)/shard_map/all_to_all | solution.py:21
  79.6 4.3 %all-to-all-start.2 = ((bf16[16,2,64,512]{3,2,1,0:T(8,128)(2,1)}), bf16[16,2,64,512]{3,2,1,0:T(8,128)(2,1)}, u32[]{:S(2)}, u32[]{:S(2)}) async-start(bf16[16,2,64,512]{3,2,1,0:T(8,128)(2,1)} %get-tuple-element.47), calls=%async_computation.2 | async-start | bytes 4194304 | tf_op jit(solution)/shard_map/all_to_all | solution.py:21
  84.0 1.9 fusion.83
  88.8 2.0 gather_fusion.1
  90.8 3.3 %gather_fusion.4 = bf16[16,128,512]{2,1,0:T(8,128)(2,1)} fusion(bf16[8,128,512]{2,1,0:T(8,128)(2,1)} %get-tuple-element.27, s32[1024]{0:T(1024)S(1)} %pad_clamp_fusion.1), kind=kCustom, calls=%fused_computation.4 | custom fusion | bytes 4194368 | tf_op jit(solution)/shard_map/gather | solution.py:31
  94.1 2.0 gather_fusion.9
  96.1 2.0 gather_fusion.10
  101.3 3.6 %fusion.88 = (f32[16,4,64]{2,1,0:T(4,128)S(1)}, f32[16,4,64,128]{3,2,1,0:T(8,128)S(1)}) fusion(bf16[16,64,4,128]{3,2,1,0:T(4,128)(2,1)} %reshape_squeeze.12, bf16[16,128,512]{2,1,0:T(8,128)(2,1)} %gather_fusion.1), kind=kOutput, calls=%fused_computation.166 | convolution fusion | flops 135262208 | bytes 5259264 | tf_op jit(solution)/shard_map/bihd,bjhd->bhij/dot_general | solution.py:33
  104.9 4.5 %fusion.14 = (f32[16,4,64]{2,1,0:T(4,128)S(1)}, f32[16,4,64]{2,1,0:T(4,128)S(1)}, f32[16,4,64,128]{3,2,1,0:T(8,128)}) fusion(f32[16,4,64,128]{3,2,1,0:T(8,128)S(1)} %get-tuple-element.52, f32[16,4,64]{2,1,0:T(4,128)S(1)} %get-tuple-element.51, bf16[16,64,4,128]{3,2,1,0:T(4,128)(2,1)S(1)} %reshape_squeeze.13, bf16[16,128,512]{2,1,0:T(8,128)(2,1)} %gather_fusion.4), kind=kOutput, calls=%fused_computation.48 | convolution fusion | flops 136306688 | bytes 7389184 | tf_op jit(solution)/shard_map/bihd,bjhd->bhij/dot_general | solution.py:36
  110.3 21.0 %all-to-all-done.2 = bf16[16,2,64,512]{3,2,1,0:T(8,128)(2,1)} async-done(((bf16[16,2,64,512]{3,2,1,0:T(8,128)(2,1)}), bf16[16,2,64,512]{3,2,1,0:T(8,128)(2,1)}, u32[]{:S(2)}, u32[]{:S(2)}) %all-to-all-start.2) | async-done | bytes 2097184 | tf_op jit(solution)/shard_map/all_to_all | solution.py:21
  131.3 3.1 %fusion.82 = (bf16[16,1,64,512]{3,2,1,0:T(8,128)(2,1)}, bf16[16,1,64,512]{3,2,1,0:T(8,128)(2,1)}) fusion(bf16[16,2,64,512]{3,2,1,0:T(8,128)(2,1)} %all-to-all-done.2), kind=kLoop, calls=%fused_computation.160 | loop fusion | bytes 4194304 | tf_op jit(solution)/shard_map/slice | solution.py:28
  134.4 2.1 reshape_squeeze.14
  136.5 2.1 reshape_squeeze.15
  138.6 3.6 %all-to-all-start.3 = ((f32[16,3,256]{2,1,0:T(4,128)}), f32[16,3,256]{2,1,0:T(4,128)S(1)}, u32[]{:S(2)}, u32[]{:S(2)}) async-start(f32[16,3,256]{2,1,0:T(4,128)} %pad_maximum_fusion.5), calls=%async_computation.3 | async-start | bytes 131072 | tf_op jit(solution)/shard_map/all_to_all | solution.py:48
  142.3 4.8 %fusion.89 = (f32[16,4,64]{2,1,0:T(4,128)S(1)}, f32[16,4,64,128]{3,2,1,0:T(8,128)}) fusion(bf16[16,64,4,128]{3,2,1,0:T(4,128)(2,1)} %reshape_squeeze.14, bf16[16,128,512]{2,1,0:T(8,128)(2,1)} %gather_fusion.9), kind=kOutput, calls=%fused_computation.167 | convolution fusion | flops 135262208 | bytes 5259264 | tf_op jit(solution)/shard_map/bihd,bjhd->bhij/dot_general | solution.py:33
  147.2 5.5 %fusion.16 = (f32[16,4,64]{2,1,0:T(4,128)S(1)}, f32[16,4,64]{2,1,0:T(4,128)S(1)}, f32[16,4,64,128]{3,2,1,0:T(8,128)}) fusion(f32[16,4,64,128]{3,2,1,0:T(8,128)} %get-tuple-element.55, f32[16,4,64]{2,1,0:T(4,128)S(1)} %get-tuple-element.54, bf16[16,64,4,128]{3,2,1,0:T(4,128)(2,1)} %reshape_squeeze.15, bf16[16,128,512]{2,1,0:T(8,128)(2,1)} %gather_fusion.10), kind=kOutput, calls=%fused_computation.50 | convolution fusion | flops 136306688 | bytes 7389184 | tf_op jit(solution)/shard_map/bihd,bjhd->bhij/dot_general | solution.py:36
  153.5 6.0 %all-to-all-start.6 = ((f32[16,3,256]{2,1,0:T(4,128)}), f32[16,3,256]{2,1,0:T(4,128)S(1)}, u32[]{:S(2)}, u32[]{:S(2)}) async-start(f32[16,3,256]{2,1,0:T(4,128)} %pad_maximum_fusion.6), calls=%async_computation.6 | async-start | bytes 131072 | tf_op jit(solution)/shard_map/all_to_all | solution.py:48
  160.2 6.2 %all-to-all-done.6 = f32[16,3,256]{2,1,0:T(4,128)S(1)} async-done(((f32[16,3,256]{2,1,0:T(4,128)}), f32[16,3,256]{2,1,0:T(4,128)S(1)}, u32[]{:S(2)}, u32[]{:S(2)}) %all-to-all-start.6) | async-done | bytes 49184 | tf_op jit(solution)/shard_map/all_to_all | solution.py:48
  169.3 3.3 %all-to-all-start.7 = ((f32[16,2,256]{2,1,0:T(2,128)}), f32[16,2,256]{2,1,0:T(2,128)S(1)}, u32[]{:S(2)}, u32[]{:S(2)}) async-start(f32[16,2,256]{2,1,0:T(2,128)} %get-tuple-element.46), calls=%async_computation.7 | async-start | bytes 65536 | tf_op jit(solution)/shard_map/all_to_all | solution.py:60
  172.6 6.6 %all-to-all-done.7 = f32[16,2,256]{2,1,0:T(2,128)S(1)} async-done(((f32[16,2,256]{2,1,0:T(2,128)}), f32[16,2,256]{2,1,0:T(2,128)S(1)}, u32[]{:S(2)}, u32[]{:S(2)}) %all-to-all-start.7) | async-done | bytes 32800 | tf_op jit(solution)/shard_map/all_to_all | solution.py:60
  179.3 3.5 %all-to-all-start.4 = ((f32[16,2,256]{2,1,0:T(2,128)}), f32[16,2,256]{2,1,0:T(2,128)S(1)}, u32[]{:S(2)}, u32[]{:S(2)}) async-start(f32[16,2,256]{2,1,0:T(2,128)} %get-tuple-element.45), calls=%async_computation.4 | async-start | bytes 65536 | tf_op jit(solution)/shard_map/all_to_all | solution.py:60
  183.1 3.0 %multiply_convert_fusion = bf16[16,4,64,128]{3,2,1,0:T(8,128)(2,1)S(1)} fusion(f32[16,4,64,128]{3,2,1,0:T(8,128)} %get-tuple-element.56, f32[16,4,64,128]{3,2,1,0:T(8,128)} %get-tuple-element.55, f32[16,4,64]{2,1,0:T(4,128)S(1)} %sub.101, f32[16,4,64]{2,1,0:T(4,128)S(1)} %sub.98), kind=kLoop, calls=%fused_computation.38 | loop fusion | flops 2621440 | bytes 5275648 | tf_op jit(solution)/shard_map/convert_element_type | solution.py:71
  189.2 4.7 %all-to-all-start.8 = ((bf16[16,64,512]{2,1,0:T(8,128)(2,1)}), bf16[16,64,512]{2,1,0:T(8,128)(2,1)}, u32[]{:S(2)}, u32[]{:S(2)}) async-start(bf16[16,64,512]{2,1,0:T(8,128)(2,1)} %bitcast.176), calls=%async_computation.8 | async-start | bytes 2097152 | tf_op jit(solution)/shard_map/all_to_all | solution.py:82
  194.2 2.6 multiply_convert_fusion.1
  199.8 2.7 convolution_bitcast_fusion.2
  202.5 5.2 %copy.101 = f32[16,128,4,128]{3,2,1,0:T(4,128)} copy(f32[16,128,4,128]{1,3,2,0:T(8,128)} %convolution_bitcast_fusion.2) | data formatting | bytes 8388608 | tf_op jit(solution)/shard_map/bhij,bihd->bjhd/transpose | solution.py:76
  207.8 4.9 %reshape.374 = f32[16,65536]{1,0:T(8,128)} reshape(f32[16,128,4,128]{3,2,1,0:T(4,128)} %copy.101) | data formatting | bytes 8388608 | tf_op jit(solution)/shard_map/reshape | solution.py:78
  212.7 3.8 %convolution_convert_fusion.2 = bf16[8,65536]{1,0:T(8,128)(2,1)S(1)} fusion(f32[16,65536]{1,0:T(8,128)} %reshape.374, s32[16]{0:T(128)S(1)} %eq.46, pred[16]{0:T(512)(128)(4,1)S(1)} %broadcast_compare_fusion), kind=kOutput, calls=%fused_computation.16 | convolution fusion | flops 101187840 | bytes 5242960 | tf_op jit(solution)/shard_map/dot_general | solution.py:83
  218.4 2.7 convolution_bitcast_fusion.3
  221.1 5.2 %copy.99 = f32[16,128,4,128]{3,2,1,0:T(4,128)} copy(f32[16,128,4,128]{1,3,2,0:T(8,128)} %convolution_bitcast_fusion.3) | data formatting | bytes 8388608 | tf_op jit(solution)/shard_map/bhij,bihd->bjhd/transpose | solution.py:76
  226.3 4.9 %reshape.372 = f32[16,65536]{1,0:T(8,128)} reshape(f32[16,128,4,128]{3,2,1,0:T(4,128)} %copy.99) | data formatting | bytes 8388608 | tf_op jit(solution)/shard_map/reshape | solution.py:78
  231.2 3.8 %convolution_convert_fusion.3 = bf16[8,65536]{1,0:T(8,128)(2,1)S(1)} fusion(f32[16,65536]{1,0:T(8,128)} %reshape.372, s32[16]{0:T(128)S(1)} %eq.46, pred[16]{0:T(512)(128)(4,1)S(1)} %broadcast_compare_fusion), kind=kOutput, calls=%fused_computation.17 | convolution fusion | flops 101187840 | bytes 5242960 | tf_op jit(solution)/shard_map/dot_general | solution.py:83
  236.4 6.0 %all-to-all-start.5 = ((bf16[16,64,512]{2,1,0:T(8,128)(2,1)}), bf16[16,64,512]{2,1,0:T(8,128)(2,1)}, u32[]{:S(2)}, u32[]{:S(2)}) async-start(bf16[16,64,512]{2,1,0:T(8,128)(2,1)} %bitcast.175), calls=%async_computation.5 | async-start | bytes 2097152 | tf_op jit(solution)/shard_map/all_to_all | solution.py:82
  242.4 5.3 %convolution_bitcast_fusion = f32[16,128,4,128]{1,3,2,0:T(8,128)} fusion(f32[16,4,64,128]{3,2,1,0:T(8,128)} %get-tuple-element.55, f32[16,4,64]{2,1,0:T(4,128)S(1)} %sub.98, bf16[16,64,4,128]{3,2,1,0:T(4,128)(2,1)} %reshape_squeeze.15), kind=kOutput, calls=%fused_computation.18 | convolution fusion | flops 135266304 | bytes 7356416 | tf_op jit(solution)/shard_map/bhij,bihd->bjhd/dot_general | solution.py:73
  247.6 5.2 %copy.107 = f32[16,128,4,128]{3,2,1,0:T(4,128)} copy(f32[16,128,4,128]{1,3,2,0:T(8,128)} %convolution_bitcast_fusion) | data formatting | bytes 8388608 | tf_op jit(solution)/shard_map/bhij,bihd->bjhd/transpose | solution.py:73
  252.9 4.9 %reshape.378 = f32[16,65536]{1,0:T(8,128)} reshape(f32[16,128,4,128]{3,2,1,0:T(4,128)} %copy.107) | data formatting | bytes 8388608 | tf_op jit(solution)/shard_map/reshape | solution.py:75
  257.8 3.8 %convolution_convert_fusion = bf16[8,65536]{1,0:T(8,128)(2,1)S(1)} fusion(f32[16,65536]{1,0:T(8,128)} %reshape.378, s32[16]{0:T(128)S(1)} %eq.46, pred[16]{0:T(512)(128)(4,1)S(1)} %broadcast_compare_fusion), kind=kOutput, calls=%fused_computation.14 | convolution fusion | flops 101187840 | bytes 5242960 | tf_op jit(solution)/shard_map/dot_general | solution.py:84
  262.8 3.0 %convolution_bitcast_fusion.1 = f32[16,128,4,128]{1,3,2,0:T(8,128)} fusion(f32[16,4,64,128]{3,2,1,0:T(8,128)S(1)} %get-tuple-element.52, f32[16,4,64]{2,1,0:T(4,128)S(1)} %sub.88, bf16[16,64,4,128]{3,2,1,0:T(4,128)(2,1)S(1)} %reshape_squeeze.13), kind=kOutput, calls=%fused_computation.19 | convolution fusion | flops 135266304 | bytes 7356416 | tf_op jit(solution)/shard_map/bhij,bihd->bjhd/dot_general | solution.py:73
  265.8 5.2 %copy.105 = f32[16,128,4,128]{3,2,1,0:T(4,128)} copy(f32[16,128,4,128]{1,3,2,0:T(8,128)} %convolution_bitcast_fusion.1) | data formatting | bytes 8388608 | tf_op jit(solution)/shard_map/bhij,bihd->bjhd/transpose | solution.py:73
  271.0 4.9 %reshape.376 = f32[16,65536]{1,0:T(8,128)} reshape(f32[16,128,4,128]{3,2,1,0:T(4,128)} %copy.105) | data formatting | bytes 8388608 | tf_op jit(solution)/shard_map/reshape | solution.py:75
  275.9 3.8 %convolution_convert_fusion.1 = bf16[8,65536]{1,0:T(8,128)(2,1)S(1)} fusion(f32[16,65536]{1,0:T(8,128)} %reshape.376, s32[16]{0:T(128)S(1)} %eq.46, pred[16]{0:T(512)(128)(4,1)S(1)} %broadcast_compare_fusion), kind=kOutput, calls=%fused_computation.15 | convolution fusion | flops 101187840 | bytes 5242960 | tf_op jit(solution)/shard_map/dot_general | solution.py:84
  284.4 1.8 gather_fusion.13
  286.5 1.8 gather_fusion.8
  (107 shorter events, 33.2 us)
Async XLA Ops:
  8.8 16.7 %all-to-all-start = ((s32[8,2,1]{1,2,0:T(1,128)}), s32[8,2,1]{1,2,0:T(1,128)S(1)}, u32[]{:S(2)}, u32[]{:S(2)}) async-start(s32[8,2,1]{1,2,0:T(1,128)} %bitcast.3), calls=%async_computation | async-start | bytes 8192 | tf_op jit(solution)/shard_map/all_to_all | solution.py:118
  15.1 1.5 copy-start.12
  79.6 51.7 %all-to-all-start.2 = ((bf16[16,2,64,512]{3,2,1,0:T(8,128)(2,1)}), bf16[16,2,64,512]{3,2,1,0:T(8,128)(2,1)}, u32[]{:S(2)}, u32[]{:S(2)}) async-start(bf16[16,2,64,512]{3,2,1,0:T(8,128)(2,1)} %get-tuple-element.47), calls=%async_computation.2 | async-start | bytes 4194304 | tf_op jit(solution)/shard_map/all_to_all | solution.py:21
  84.0 2.2 copy-start.11
  138.6 14.8 %all-to-all-start.3 = ((f32[16,3,256]{2,1,0:T(4,128)}), f32[16,3,256]{2,1,0:T(4,128)S(1)}, u32[]{:S(2)}, u32[]{:S(2)}) async-start(f32[16,3,256]{2,1,0:T(4,128)} %pad_maximum_fusion.5), calls=%async_computation.3 | async-start | bytes 131072 | tf_op jit(solution)/shard_map/all_to_all | solution.py:48
  153.5 12.9 %all-to-all-start.6 = ((f32[16,3,256]{2,1,0:T(4,128)}), f32[16,3,256]{2,1,0:T(4,128)S(1)}, u32[]{:S(2)}, u32[]{:S(2)}) async-start(f32[16,3,256]{2,1,0:T(4,128)} %pad_maximum_fusion.6), calls=%async_computation.6 | async-start | bytes 131072 | tf_op jit(solution)/shard_map/all_to_all | solution.py:48
  169.3 10.0 %all-to-all-start.7 = ((f32[16,2,256]{2,1,0:T(2,128)}), f32[16,2,256]{2,1,0:T(2,128)S(1)}, u32[]{:S(2)}, u32[]{:S(2)}) async-start(f32[16,2,256]{2,1,0:T(2,128)} %get-tuple-element.46), calls=%async_computation.7 | async-start | bytes 65536 | tf_op jit(solution)/shard_map/all_to_all | solution.py:60
  179.3 10.0 %all-to-all-start.4 = ((f32[16,2,256]{2,1,0:T(2,128)}), f32[16,2,256]{2,1,0:T(2,128)S(1)}, u32[]{:S(2)}, u32[]{:S(2)}) async-start(f32[16,2,256]{2,1,0:T(2,128)} %get-tuple-element.45), calls=%async_computation.4 | async-start | bytes 65536 | tf_op jit(solution)/shard_map/all_to_all | solution.py:60
  183.0 3.0 %copy-start.1 = (bf16[16,128,512]{2,1,0:T(8,128)(2,1)S(1)}, bf16[16,128,512]{2,1,0:T(8,128)(2,1)}, u32[]{:S(2)}) copy-start(bf16[16,128,512]{2,1,0:T(8,128)(2,1)} %gather_fusion.9) | copy-start | bytes 6291460
  186.0 1.0 copy-start.4
  189.2 47.1 %all-to-all-start.8 = ((bf16[16,64,512]{2,1,0:T(8,128)(2,1)}), bf16[16,64,512]{2,1,0:T(8,128)(2,1)}, u32[]{:S(2)}, u32[]{:S(2)}) async-start(bf16[16,64,512]{2,1,0:T(8,128)(2,1)} %bitcast.176), calls=%async_computation.8 | async-start | bytes 2097152 | tf_op jit(solution)/shard_map/all_to_all | solution.py:82
  194.2 2.6 copy-start
  196.8 1.1 copy-start.6
  197.9 1.5 copy-start.3
  197.9 1.9 copy-start.5
  216.4 1.3 copy-start.2
  216.5 1.9 copy-start.7
  236.4 50.1 %all-to-all-start.5 = ((bf16[16,64,512]{2,1,0:T(8,128)(2,1)}), bf16[16,64,512]{2,1,0:T(8,128)(2,1)}, u32[]{:S(2)}, u32[]{:S(2)}) async-start(bf16[16,64,512]{2,1,0:T(8,128)(2,1)} %bitcast.175), calls=%async_computation.5 | async-start | bytes 2097152 | tf_op jit(solution)/shard_map/all_to_all | solution.py:82
  279.7 1.2 copy-start.8
  279.7 1.5 copy-start.9
  281.2 1.6 copy-start.10

commit v3 on v1

--- a/solution.py
+++ b/solution.py
@@ -1,6 +1,8 @@
 import jax
 import jax.numpy as jnp
 from jax import lax
+from jax.experimental import pallas as pl
+from jax.experimental.pallas import tpu as pltpu
 from jax.sharding import PartitionSpec as P
 
 HEAD = 128
@@ -8,9 +10,75 @@
 NLEN = 128
 NBR = 2
 
+TRANS_A = (((0,), (0,)), ((), ()))
+
 
 def split_heads(tensor):
     return tensor.reshape(tensor.shape[:-1] + (tensor.shape[-1] // HEAD, HEAD))
+
+
+def kv_kernel(rows_ref, probs_ref, grads_ref, pair_ref, key_out, value_out, key_acc, value_acc):
+    slot = pl.program_id(0)
+    heads = probs_ref.shape[1]
+
+    @pl.when(slot == 0)
+    def _():
+        key_acc[...] = jnp.zeros_like(key_acc)
+        value_acc[...] = jnp.zeros_like(value_acc)
+
+    row = rows_ref[slot]
+
+    @pl.when(row >= 0)
+    def _():
+        here = jnp.maximum(row, 0)
+        for h in range(heads):
+            cols = pl.ds(h * HEAD, HEAD)
+            value_part = lax.dot_general(
+                probs_ref[0, h], pair_ref[0, 1, :, cols], TRANS_A,
+                preferred_element_type=jnp.float32,
+            )
+            key_part = lax.dot_general(
+                grads_ref[0, h], pair_ref[0, 0, :, cols], TRANS_A,
+                preferred_element_type=jnp.float32,
+            )
+            value_acc[here, :, cols] += value_part
+            key_acc[here, :, cols] += key_part
+
+    @pl.when(slot == pl.num_programs(0) - 1)
+    def _():
+        key_out[...] = key_acc[...].astype(key_out.dtype)
+        value_out[...] = value_acc[...].astype(value_out.dtype)
+
+
+def kv_grads(row_recv, probs_low, grad_s, pair_recv, rows_here):
+    slot_total, heads, span_len, nlen = probs_low.shape
+    width = pair_recv.shape[-1]
+    out_shape = jax.ShapeDtypeStruct((rows_here, nlen, width), jnp.bfloat16)
+    grid_spec = pltpu.PrefetchScalarGridSpec(
+        num_scalar_prefetch=1,
+        grid=(slot_total,),
+        in_specs=[
+            pl.BlockSpec((1, heads, span_len, nlen), lambda t, rows: (t, 0, 0, 0)),
+            pl.BlockSpec((1, heads, span_len, nlen), lambda t, rows: (t, 0, 0, 0)),
+            pl.BlockSpec((1, 2, span_len, width), lambda t, rows: (t, 0, 0, 0)),
+        ],
+        out_specs=[
+            pl.BlockSpec((rows_here, nlen, width), lambda t, rows: (0, 0, 0)),
+            pl.BlockSpec((rows_here, nlen, width), lambda t, rows: (0, 0, 0)),
+        ],
+        scratch_shapes=[
+            pltpu.VMEM((rows_here, nlen, width), jnp.float32),
+            pltpu.VMEM((rows_here, nlen, width), jnp.float32),
+        ],
+    )
+    return pl.pallas_call(
+        kv_kernel,
+        grid_spec=grid_spec,
+        out_shape=[out_shape, out_shape],
+        compiler_params=pltpu.CompilerParams(
+            dimension_semantics=("arbitrary",), vmem_limit_bytes=48 * 1024 * 1024
+        ),
+    )(row_recv, probs_low, grad_s, pair_recv)
 
 
 def per_device(queries, out_grad, row_keys, row_values, neighbours):
@@ -40,15 +108,11 @@
     slot_item = jnp.sum(jnp.where(match, position[None, :], 0), axis=1)
     slot_span = item_span[slot_item]
 
-    both = jnp.stack([queries, out_grad], axis=1)
-    pair_send = jnp.where(
-        slot_valid[:, None, None, None], both[slot_span], jnp.zeros((), both.dtype)
-    )
+    pair_send = jnp.stack([queries[slot_span], out_grad[slot_span]], axis=1)
     row_send = jnp.where(slot_valid, local_row[slot_item], -1)
     pair_recv = lax.all_to_all(pair_send, "seq", split_axis=0, concat_axis=0, tiled=True)
     row_recv = lax.all_to_all(row_send, "seq", split_axis=0, concat_axis=0, tiled=True)
 
-    recv_valid = row_recv >= 0
     row_index = jnp.clip(row_recv, 0, rows_here - 1)
     query_heads = split_heads(pair_recv[:, 0])
     grad_heads = split_heads(pair_recv[:, 1])
@@ -79,33 +143,22 @@
     log_total = span_max[:, 0] + jnp.log(span_sum)
     row_delta = jnp.sum(item_cross * factor, axis=1) / span_sum
     span_stats = jnp.stack([log_total, row_delta], axis=1)
-    stats_send = jnp.where(slot_valid[:, None, None], span_stats[slot_span], 0.0)
-    stats_recv = lax.all_to_all(stats_send, "seq", split_axis=0, concat_axis=0, tiled=True)
+    stats_recv = lax.all_to_all(
+        span_stats[slot_span], "seq", split_axis=0, concat_axis=0, tiled=True
+    )
 
     norm_here = stats_recv[:, 0].reshape(slot_total, heads_here, SPAN)
     delta_here = stats_recv[:, 1].reshape(slot_total, heads_here, SPAN)
     softmax_p = jnp.exp(scores - norm_here[..., None])
     grad_s = (softmax_p * (grad_p - delta_here[..., None]) * score_scale).astype(jnp.bfloat16)
     probs_low = softmax_p.astype(jnp.bfloat16)
-    value_part = jnp.einsum(
-        "bhij,bihd->bjhd", probs_low, grad_heads, preferred_element_type=jnp.float32
-    ).reshape(slot_total, NLEN * width_here)
-    key_part = jnp.einsum(
-        "bhij,bihd->bjhd", grad_s, query_heads, preferred_element_type=jnp.float32
-    ).reshape(slot_total, NLEN * width_here)
     query_part = jnp.einsum(
         "bhij,bjhd->bihd", grad_s, key_heads, preferred_element_type=jnp.float32
     ).astype(jnp.bfloat16).reshape(slot_total, SPAN, width_here)
+    query_back = lax.all_to_all(query_part, "seq", split_axis=0, concat_axis=0, tiled=True)
 
-    pick = (
-        (row_recv[None, :] == jnp.arange(rows_here)[:, None]) & recv_valid[None, :]
-    ).astype(jnp.float32)
-    key_acc = jnp.dot(pick, key_part, precision=lax.Precision.HIGHEST)
-    value_acc = jnp.dot(pick, value_part, precision=lax.Precision.HIGHEST)
-    key_grad = key_acc.astype(jnp.bfloat16).reshape(rows_here, NLEN, width_here)
-    value_grad = value_acc.astype(jnp.bfloat16).reshape(rows_here, NLEN, width_here)
+    key_grad, value_grad = kv_grads(row_recv, probs_low, grad_s, pair_recv, rows_here)
 
-    query_back = lax.all_to_all(query_part, "seq", split_axis=0, concat_axis=0, tiled=True)
     returned = query_back[target].reshape(span_count, NBR, SPAN, width_here).astype(jnp.float32)
     query_grad = jnp.sum(returned, axis=1).astype(jnp.bfloat16)
     return (query_grad, key_grad, value_grad)

time: 246 us -> 236 us (0.959)
  matrix products: 46.2 us -> 15.2 us
  waiting for transfers between devices: 92 us -> 121 us
  local copies, waits for them, and re-layouts: 51 us -> 31.2 us
  Pallas kernels: 0 us -> 14.7 us
    dot_general x4 -> x0, matrix products: 32.8 us -> none  [the longest x1 11 us: per_device(): key_acc = jnp.dot(pick, key_part, precision=lax.Precision.HIGHEST)]
    all_to_all x1, waiting for transfers between devices: 0.01 us -> 28.7 us  [per_device(): lax.all_to_all(query_part, 'seq', split_axis=0, concat_axis=0, tiled=True)]
    transpose x2 -> x0, local copies, waits for them, and re-layouts: 18.5 us -> none  [the longest x1 9.26 us: per_device(): jnp.einsum('bhij,bihd->bjhd', grad_s, query_heads, preferred_element_type...]
    pallas_call x0 -> x1, Pallas kernels: none -> 14.7 us  [kv_grads(): pl.pallas_call(kv_kernel, grid_spec=grid_spec, out_shape=[out_shape, out_...]
    select_n x3 -> x1, other arithmetic: 4.58 us -> 0.01 us  [per_device(): pair_send = jnp.stack([queries[slot_span], out_grad[slot_span]], axis=1)]
    unnamed x20 -> x16, local copies, waits for them, and re-layouts: 7.97 us -> 5.88 us
    gather x1 -> x2, local copies, waits for them, and re-layouts: 4.36 us -> 5.22 us  [per_device(): pair_send = jnp.stack([queries[slot_span], out_grad[slot_span]], axis=1)]
  transfers between devices with their start and end apart: 4 -> 4, of which waited for: 2 -> 3; matrix products, arithmetic and copies ran while one was open for 32% -> 8% of each run, Pallas kernels for 0% -> 6%
where the time goes in v3:
time: 236 us; the launch traced here: 235 us
  waiting for transfers between devices  121 us (51%)
  local copies, waits for them, and re-layouts  31.2 us (13%)
  starting transfers between devices  20.3 us (9%)
  other arithmetic  16.6 us (7%)
  blocking collectives  15.6 us (7%)
  matrix products  15.2 us (6%)
  Pallas kernels  14.7 us (6%)
    all_to_all x1, waiting for transfers between devices, per_device(): lax.all_to_all(pair_send, 'seq', split_axis=0, concat_axis=0, tiled=True)  84.7 us
    all_to_all x1, waiting for transfers between devices, per_device(): lax.all_to_all(query_part, 'seq', split_axis=0, concat_axis=0, tiled=True)  28.7 us
    pallas_call x1, Pallas kernels, kv_grads(): pl.pallas_call(kv_kernel, grid_spec=grid_spec, out_shape=[out_shape, out_...  14.7 us
    all_to_all x1, blocking collectives, per_device(): lax.all_to_all(span_stats[slot_span], 'seq', split_axis=0, concat_axis=0,...  9.29 us
    dot_general x1, matrix products, per_device(): jnp.einsum('bihd,bjhd->bhij', grad_heads, value_heads, preferred_element_...  9.01 us
    all_to_all x1, waiting for transfers between devices, per_device(): back = lax.all_to_all(part, 'seq', split_axis=0, concat_axis=0, tiled=True)  7.32 us
    convert_element_type x1, other arithmetic, per_device(): probs_low = softmax_p.astype(jnp.bfloat16)  6.5 us
    all_to_all x1, starting transfers between devices, per_device(): lax.all_to_all(row_send, 'seq', split_axis=0, concat_axis=0, tiled=True)  6.35 us
  transfers between devices with their start and end apart: 4, of which 3 were waited for; matrix products, arithmetic and copies ran while one was open for 8% of the time, Pallas kernels for 6%

profile of v3, /device:TPU:0, one launch (start us, length us, event | category | flops | bytes accessed | tf_op | source)
XLA Modules:
  0.0 235.3 jit_solution(16681962693520673534)
XLA Ops:
  0.7 6.3 %all-gather = s32[4,2,2]{2,1,0:T(2,128)S(1)} all-gather(s32[1,2,2]{2,1,0:T(2,128)} %bitcast.96), channel_id=1, replica_groups=mesh['seq'=8,'mp'=4] {'mp'}, dimensions={0}, use_global_device_ids=true | all-gather | bytes 80 | tf_op jit(solution)/shard_map/all_gather | solution.py:86
  7.0 0.1 reshape.273
  7.1 0.2 convert_reduce_fusion
  7.3 0.1 select_reduce_fusion
  7.4 0.1 fusion.20
  7.6 0.7 gather_fusion
  8.2 0.7 select_n.102
  8.9 6.3 %all-to-all-start = ((s32[8,2,1]{1,2,0:T(1,128)}), s32[8,2,1]{1,2,0:T(1,128)S(1)}, u32[]{:S(2)}, u32[]{:S(2)}) async-start(s32[8,2,1]{1,2,0:T(1,128)} %bitcast.3), calls=%async_computation | async-start | bytes 8192 | tf_op jit(solution)/shard_map/all_to_all | solution.py:114
  15.3 0.7 gather_fusion.2
  15.9 3.2 %gather_fusion.4 = bf16[16,64,1024]{2,1,0:T(8,128)(2,1)} fusion(bf16[8,64,1024]{2,1,0:T(8,128)(2,1)} %param.6, s32[1024]{0:T(1024)S(1)} %pad_clamp_fusion.2), kind=kCustom, calls=%fused_computation.4 | custom fusion | bytes 4194368 | tf_op jit(solution)/shard_map/gather | solution.py:111
  19.2 2.0 gather_fusion.3
  21.2 4.6 %pad_maximum_fusion = bf16[16,2,64,1024]{3,2,1,0:T(8,128)(2,1)} fusion(bf16[16,1,64,1024]{3,2,1,0:T(8,128)(2,1)} %bitcast.93, bf16[16,1,64,1024]{3,2,1,0:T(8,128)(2,1)} %bitcast.94), kind=kLoop, calls=%fused_computation.16 | loop fusion | flops 2097152 | bytes 8388608 | tf_op jit(solution)/shard_map/stack | solution.py:111
  25.8 6.0 %all-to-all-start.1 = ((bf16[16,2,64,1024]{3,2,1,0:T(8,128)(2,1)}), bf16[16,2,64,1024]{3,2,1,0:T(8,128)(2,1)}, u32[]{:S(2)}, u32[]{:S(2)}) async-start(bf16[16,2,64,1024]{3,2,1,0:T(8,128)(2,1)} %pad_maximum_fusion), calls=%async_computation.1 | async-start | bytes 8388608 | tf_op jit(solution)/shard_map/all_to_all | solution.py:113
  31.8 0.1 reshape.276
  31.8 0.5 broadcast.300
  32.4 0.7 fusion.26
  33.1 2.8 %gather_fusion.1 = bf16[16,128,1024]{2,1,0:T(8,128)(2,1)} fusion(bf16[8,128,1024]{2,1,0:T(8,128)(2,1)S(1)} %copy-done, s32[1024]{0:T(1024)S(1)} %pad_clamp_fusion.1), kind=kCustom, calls=%fused_computation.1 | custom fusion | bytes 8388672 | tf_op jit(solution)/shard_map/gather | solution.py:119
  35.9 4.4 %gather_fusion.5 = bf16[16,128,1024]{2,1,0:T(8,128)(2,1)} fusion(bf16[8,128,1024]{2,1,0:T(8,128)(2,1)} %param.8, s32[1024]{0:T(1024)S(1)} %pad_clamp_fusion.1), kind=kCustom, calls=%fused_computation.5 | custom fusion | bytes 8388672 | tf_op jit(solution)/shard_map/gather | solution.py:120
  40.3 84.7 %all-to-all-done.1.pair_ref = bf16[16,2,64,1024]{3,2,1,0:T(8,128)(2,1)} async-done(((bf16[16,2,64,1024]{3,2,1,0:T(8,128)(2,1)}), bf16[16,2,64,1024]{3,2,1,0:T(8,128)(2,1)}, u32[]{:S(2)}, u32[]{:S(2)}) %all-to-all-start.1) | async-done | bytes 4194336 | tf_op jit(solution)/shard_map/all_to_all | solution.py:113
  125.0 2.7 %fusion.27 = (bf16[16,1,64,1024]{3,2,1,0:T(8,128)(2,1)S(1)}, bf16[16,1,64,1024]{3,2,1,0:T(8,128)(2,1)S(1)}) fusion(bf16[16,2,64,1024]{3,2,1,0:T(8,128)(2,1)} %all-to-all-done.1.pair_ref), kind=kLoop, calls=%fused_computation.81 | loop fusion | bytes 8388608 | tf_op jit(solution)/shard_map/slice | solution.py:117
  127.7 0.6 copy.49
  128.3 2.0 copy.50
  130.3 5.0 %multiply_reduce_fusion.1 = (f32[16,8,64]{2,1,0:T(8,128)S(1)}, f32[16,8,64,128]{3,2,1,0:T(8,128)}) fusion(bf16[16,64,8,128]{3,2,1,0:T(8,128)(2,1)S(1)} %bitcast.89, bf16[16,128,1024]{2,1,0:T(8,128)(2,1)S(1)} %copy-done.4), kind=kOutput, calls=%fused_computation.25 | convolution fusion | flops 270524416 | bytes 10518528 | tf_op jit(solution)/shard_map/bihd,bjhd->bhij/dot_general | solution.py:123
  135.3 0.1 stack.29
  135.4 9.0 %fusion.7 = (f32[16,8,64]{2,1,0:T(8,128)S(1)}, f32[16,8,64]{2,1,0:T(8,128)S(1)}, f32[16,8,64,128]{3,2,1,0:T(8,128)}) fusion(f32[16,8,64,128]{3,2,1,0:T(8,128)} %get-tuple-element.28, f32[16,8,64]{2,1,0:T(8,128)S(1)} %get-tuple-element.27, bf16[16,64,8,128]{3,2,1,0:T(8,128)(2,1)} %bitcast.88, bf16[16,128,1024]{2,1,0:T(8,128)(2,1)} %gather_fusion.5), kind=kOutput, calls=%fused_computation.21 | convolution fusion | flops 273661952 | bytes 14778368 | tf_op jit(solution)/shard_map/bihd,bjhd->bhij/dot_general | solution.py:126
  144.4 0.1 stack.30
  144.5 0.1 stack.31
  144.6 0.7 pad_maximum_fusion.1
  145.3 3.6 %all-to-all-start.2 = ((f32[16,3,512]{2,1,0:T(4,128)}), f32[16,3,512]{2,1,0:T(4,128)S(1)}, u32[]{:S(2)}, u32[]{:S(2)}) async-start(f32[16,3,512]{2,1,0:T(4,128)} %pad_maximum_fusion.1), calls=%async_computation.2 | async-start | bytes 262144 | tf_op jit(solution)/shard_map/all_to_all | solution.py:134
  149.0 7.3 %all-to-all-done.2 = f32[16,3,512]{2,1,0:T(4,128)S(1)} async-done(((f32[16,3,512]{2,1,0:T(4,128)}), f32[16,3,512]{2,1,0:T(4,128)S(1)}, u32[]{:S(2)}, u32[]{:S(2)}) %all-to-all-start.2) | async-done | bytes 98336 | tf_op jit(solution)/shard_map/all_to_all | solution.py:134
  156.3 0.6 gather_fusion.6
  156.9 0.1 fusion.28
  157.1 0.1 fusion.16
  157.3 0.6 gather_fusion.7
  157.9 9.3 %all_to_all.28 = f32[16,2,512]{2,1,0:T(2,128)S(1)} all-to-all(f32[16,2,512]{2,1,0:T(2,128)S(1)} %gather_fusion.7), channel_id=1, replica_groups=mesh['seq'=8,'mp'=4] {'seq'}, dimensions={0} | all-to-all | bytes 131072 | tf_op jit(solution)/shard_map/all_to_all | solution.py:146
  167.2 0.2 slice_reduce_fusion.1
  167.5 6.5 %fusion.8 = (bf16[16,8,64,128]{3,2,1,0:T(8,128)(2,1)}, bf16[16,8,64,128]{3,2,1,0:T(8,128)(2,1)S(1)}) fusion(f32[16,8,64,128]{3,2,1,0:T(8,128)} %get-tuple-element.28, f32[16,8,64]{2,1,0:T(8,128)S(1)} %sub.52, f32[16,8,64,128]{3,2,1,0:T(8,128)} %get-tuple-element.29, f32[16,8,64]{2,1,0:T(8,128)S(1)} %sub.55), kind=kLoop, calls=%fused_computation.22 | loop fusion | flops 7340032 | bytes 12648448 | tf_op jit(solution)/shard_map/convert_element_type | solution.py:154
  174.0 1.2 convert_bitcast_fusion
  175.3 0.1 copy-done.1
  175.3 1.9 copy.93
  177.3 4.3 %all-to-all-start.4 = ((bf16[16,64,1024]{2,1,0:T(8,128)(2,1)}), bf16[16,64,1024]{2,1,0:T(8,128)(2,1)}, u32[]{:S(2)}, u32[]{:S(2)}) async-start(bf16[16,64,1024]{2,1,0:T(8,128)(2,1)} %bitcast.90), calls=%async_computation.4 | async-start | bytes 4194304 | tf_op jit(solution)/shard_map/all_to_all | solution.py:158
  181.6 0.1 all_to_all.22.rows_ref
  181.7 1.6 copy-done.2
  183.3 1.6 copy-done.3
  184.9 14.7 %shard_map.76 = (bf16[8,128,1024]{2,1,0:T(8,128)(2,1)}, bf16[8,128,1024]{2,1,0:T(8,128)(2,1)}) custom-call(s32[16]{0:T(128)S(1)} %all_to_all.22.rows_ref, bf16[16,8,64,128]{3,2,1,0:T(8,128)(2,1)S(1)} %copy-done.3, bf16[16,8,64,128]{3,2,1,0:T(8,128)(2,1)S(1)} %copy-done.2, bf16[16,2,64,1024]{3,2,1,0:T(8,128)(2,1)} %all-to-all-done.1.pair_ref), custom_call_target="tpu_custom_call" | custom-call | tf_op jit(solution)/shard_map/pallas_call | solution.py:74
  199.6 28.7 %all-to-all-done.4 = bf16[16,64,1024]{2,1,0:T(8,128)(2,1)} async-done(((bf16[16,64,1024]{2,1,0:T(8,128)(2,1)}), bf16[16,64,1024]{2,1,0:T(8,128)(2,1)}, u32[]{:S(2)}, u32[]{:S(2)}) %all-to-all-start.4) | async-done | bytes 2097184 | tf_op jit(solution)/shard_map/all_to_all | solution.py:158
  228.3 3.6 %gather_fusion.8 = bf16[16,64,1024]{2,1,0:T(8,128)(2,1)} fusion(bf16[16,64,1024]{2,1,0:T(8,128)(2,1)} %all-to-all-done.4, s32[1024]{0:T(1024)S(1)} %pad_clamp_fusion), kind=kCustom, calls=%fused_computation.8 | custom fusion | bytes 4194368 | tf_op jit(solution)/shard_map/gather | solution.py:162
  231.9 3.3 %bitcast_reduce_fusion = bf16[8,64,1024]{2,1,0:T(8,128)(2,1)} fusion(bf16[16,64,1024]{2,1,0:T(8,128)(2,1)} %gather_fusion.8), kind=kLoop, calls=%fused_computation.27 | loop fusion | flops 524288 | bytes 3145728 | tf_op jit(solution)/shard_map/reduce_sum | solution.py:163
  (31 shorter events, 0.4 us)
Async XLA Ops:
  0.6 32.5 %copy-start = (bf16[8,128,1024]{2,1,0:T(8,128)(2,1)S(1)}, bf16[8,128,1024]{2,1,0:T(8,128)(2,1)}, u32[]{:S(2)}) copy-start(bf16[8,128,1024]{2,1,0:T(8,128)(2,1)} %param.7) | copy-start | bytes 6291460
  0.6 18.5 %copy-start.6 = (bf16[8,64,1024]{2,1,0:T(8,128)(2,1)S(1)}, bf16[8,64,1024]{2,1,0:T(8,128)(2,1)}, u32[]{:S(2)}) copy-start(bf16[8,64,1024]{2,1,0:T(8,128)(2,1)} %param.5) | copy-start | bytes 3145732
  8.9 16.8 %all-to-all-start = ((s32[8,2,1]{1,2,0:T(1,128)}), s32[8,2,1]{1,2,0:T(1,128)S(1)}, u32[]{:S(2)}, u32[]{:S(2)}) async-start(s32[8,2,1]{1,2,0:T(1,128)} %bitcast.3), calls=%async_computation | async-start | bytes 8192 | tf_op jit(solution)/shard_map/all_to_all | solution.py:114
  25.8 99.2 %all-to-all-start.1 = ((bf16[16,2,64,1024]{3,2,1,0:T(8,128)(2,1)}), bf16[16,2,64,1024]{3,2,1,0:T(8,128)(2,1)}, u32[]{:S(2)}, u32[]{:S(2)}) async-start(bf16[16,2,64,1024]{3,2,1,0:T(8,128)(2,1)} %pad_maximum_fusion), calls=%async_computation.1 | async-start | bytes 8388608 | tf_op jit(solution)/shard_map/all_to_all | solution.py:113
  127.7 2.6 %copy-start.4 = (bf16[16,128,1024]{2,1,0:T(8,128)(2,1)S(1)}, bf16[16,128,1024]{2,1,0:T(8,128)(2,1)}, u32[]{:S(2)}) copy-start(bf16[16,128,1024]{2,1,0:T(8,128)(2,1)} %gather_fusion.1) | copy-start | bytes 12582916
  145.3 11.0 %all-to-all-start.2 = ((f32[16,3,512]{2,1,0:T(4,128)}), f32[16,3,512]{2,1,0:T(4,128)S(1)}, u32[]{:S(2)}, u32[]{:S(2)}) async-start(f32[16,3,512]{2,1,0:T(4,128)} %pad_maximum_fusion.1), calls=%async_computation.2 | async-start | bytes 262144 | tf_op jit(solution)/shard_map/all_to_all | solution.py:134
  167.5 6.5 %copy-start.5 = (bf16[16,128,1024]{2,1,0:T(8,128)(2,1)S(1)}, bf16[16,128,1024]{2,1,0:T(8,128)(2,1)}, u32[]{:S(2)}) copy-start(bf16[16,128,1024]{2,1,0:T(8,128)(2,1)} %gather_fusion.1) | copy-start | bytes 12582916
  174.0 1.3 copy-start.1
  177.3 51.0 %all-to-all-start.4 = ((bf16[16,64,1024]{2,1,0:T(8,128)(2,1)}), bf16[16,64,1024]{2,1,0:T(8,128)(2,1)}, u32[]{:S(2)}, u32[]{:S(2)}) async-start(bf16[16,64,1024]{2,1,0:T(8,128)(2,1)} %bitcast.90), calls=%async_computation.4 | async-start | bytes 4194304 | tf_op jit(solution)/shard_map/all_to_all | solution.py:158
  181.7 1.6 copy-start.2
  183.3 1.6 copy-start.3

commit v4 on v3

--- a/solution.py
+++ b/solution.py
@@ -83,35 +83,41 @@
 
 def per_device(queries, out_grad, row_keys, row_values, neighbours):
     seq_count = lax.axis_size("seq")
-    own_lists = lax.all_gather(neighbours, "mp", axis=0, tiled=True)
+    my_seq = lax.axis_index("seq")
     span_count = queries.shape[0]
     rows_here = row_keys.shape[0]
     width_here = queries.shape[2]
     heads_here = width_here // HEAD
-    flat_rows = own_lists.reshape(-1)
-    item_count = flat_rows.shape[0]
-    owner_dev = flat_rows // rows_here
-    local_row = flat_rows % rows_here
+    all_lists = lax.all_gather(neighbours, ("seq", "mp"), axis=0, tiled=True)
+    lists = all_lists.reshape(seq_count, span_count * NBR)
+    item_count = lists.shape[1]
+    owner_all = lists // rows_here
+    local_all = lists % rows_here
     slot_depth = (item_count + seq_count - 1) // seq_count
     slot_total = seq_count * slot_depth
     position = jnp.arange(item_count)
-    same_before = (owner_dev[:, None] == owner_dev[None, :]) & (
-        position[None, :] < position[:, None]
+    same_before = (owner_all[:, :, None] == owner_all[:, None, :]) & (
+        position[None, None, :] < position[None, :, None]
     )
-    earlier = jnp.sum(same_before.astype(jnp.int32), axis=1)
-    target = owner_dev * slot_depth + earlier
+    earlier_all = jnp.sum(same_before.astype(jnp.int32), axis=2)
+    target_all = owner_all * slot_depth + earlier_all
+    target = lax.dynamic_index_in_dim(target_all, my_seq, axis=0, keepdims=False)
     item_span = position // NBR
     score_scale = HEAD ** (-0.5)
 
     match = target[None, :] == jnp.arange(slot_total)[:, None]
-    slot_valid = jnp.any(match, axis=1)
     slot_item = jnp.sum(jnp.where(match, position[None, :], 0), axis=1)
     slot_span = item_span[slot_item]
 
-    pair_send = jnp.stack([queries[slot_span], out_grad[slot_span]], axis=1)
-    row_send = jnp.where(slot_valid, local_row[slot_item], -1)
+    wanted = my_seq * slot_depth + jnp.arange(slot_depth)
+    hit = target_all[:, None, :] == wanted[None, :, None]
+    row_recv = jnp.where(
+        jnp.any(hit, axis=2), jnp.sum(jnp.where(hit, local_all[:, None, :], 0), axis=2), -1
+    ).reshape(slot_total)
+
+    joined = jnp.concatenate([queries, out_grad], axis=1)
+    pair_send = joined[slot_span].reshape(slot_total, 2, SPAN, width_here)
     pair_recv = lax.all_to_all(pair_send, "seq", split_axis=0, concat_axis=0, tiled=True)
-    row_recv = lax.all_to_all(row_send, "seq", split_axis=0, concat_axis=0, tiled=True)
 
     row_index = jnp.clip(row_recv, 0, rows_here - 1)
     query_heads = split_heads(pair_recv[:, 0])

time: 236 us -> 263 us (1.11)
  blocking collectives: 15.6 us -> 52.9 us
  starting transfers between devices: 20.3 us -> 12.5 us
    all_gather x1, blocking collectives: 6.35 us -> 43.6 us  [per_device(): all_lists = lax.all_gather(neighbours, ('seq', 'mp'), axis=0, tiled=True)]
    all_to_all x1 -> x0, starting transfers between devices: 6.35 us -> none  [per_device(): lax.all_to_all(row_send, 'seq', split_axis=0, concat_axis=0, tiled=True)]
    another operation x1 -> x0, other arithmetic: 4.58 us -> none  [per_device(): pair_send = jnp.stack([queries[slot_span], out_grad[slot_span]], axis=1)]
    concatenate x0 -> x1, other arithmetic: none -> 3.04 us  [per_device(): joined = jnp.concatenate([queries, out_grad], axis=1)]
    gather x3 -> x1, local copies, waits for them, and re-layouts: 5.88 us -> 4.38 us  [per_device(): pair_send = joined[slot_span].reshape(slot_total, 2, SPAN, width_here)]
    unnamed x16 -> x14, local copies, waits for them, and re-layouts: 5.88 us -> 5.87 us
  transfers between devices with their start and end apart: 4 -> 3, of which waited for: 3 -> 3; matrix products, arithmetic and copies ran while one was open for 8% -> 3% of each run, Pallas kernels for 6% -> 6%
where the time goes in v4:
time: 263 us; the launch traced here: 262 us
  waiting for transfers between devices  122 us (46%)
  blocking collectives  52.9 us (20%)
  local copies, waits for them, and re-layouts  28.6 us (11%)
  matrix products  15.2 us (6%)
  other arithmetic  14.8 us (6%)
  Pallas kernels  14.8 us (6%)
  starting transfers between devices  12.5 us (5%)
    all_to_all x1, waiting for transfers between devices, per_device(): lax.all_to_all(pair_send, 'seq', split_axis=0, concat_axis=0, tiled=True)  86.1 us
    all_gather x1, blocking collectives, per_device(): all_lists = lax.all_gather(neighbours, ('seq', 'mp'), axis=0, tiled=True)  43.6 us
    all_to_all x1, waiting for transfers between devices, per_device(): lax.all_to_all(query_part, 'seq', split_axis=0, concat_axis=0, tiled=True)  28.7 us
    pallas_call x1, Pallas kernels, kv_grads(): pl.pallas_call(kv_kernel, grid_spec=grid_spec, out_shape=[out_shape, out_...  14.8 us
    all_to_all x1, blocking collectives, per_device(): lax.all_to_all(span_stats[slot_span], 'seq', split_axis=0, concat_axis=0,...  9.29 us
    dot_general x1, matrix products, per_device(): jnp.einsum('bihd,bjhd->bhij', grad_heads, value_heads, preferred_element_...  9.01 us
    all_to_all x1, waiting for transfers between devices, per_device(): back = lax.all_to_all(part, 'seq', split_axis=0, concat_axis=0, tiled=True)  7.32 us
    convert_element_type x1, other arithmetic, per_device(): probs_low = softmax_p.astype(jnp.bfloat16)  6.5 us
  transfers between devices with their start and end apart: 3, of which 3 were waited for; matrix products, arithmetic and copies ran while one was open for 3% of the time, Pallas kernels for 6%

profile of v4, /device:TPU:0, one launch (start us, length us, event | category | flops | bytes accessed | tf_op | source)
XLA Modules:
  0.0 261.9 jit_solution(11158862112657386770)
XLA Ops:
  0.6 0.0 copy-start
  0.7 43.6 %all-gather = s32[32,2,2]{2,1,0:T(2,128)S(1)} all-gather(s32[1,2,2]{2,1,0:T(2,128)} %bitcast.92), channel_id=1, replica_groups=mesh['seq'=8,'mp'=4] {'seq','mp'}, dimensions={0}, use_global_device_ids=true | all-gather | bytes 528 | tf_op jit(solution)/shard_map/all_gather | solution.py:91
  44.3 0.1 reshape.268
  44.4 0.3 convert_reduce_fusion
  44.8 0.1 select_reduce_fusion
  44.9 0.7 gather_fusion.1
  45.6 3.0 %pad_maximum_fusion = bf16[8,128,1024]{2,1,0:T(8,128)(2,1)} fusion(bf16[8,64,1024]{2,1,0:T(8,128)(2,1)} %param.6, bf16[8,64,1024]{2,1,0:T(8,128)(2,1)} %param.5), kind=kLoop, calls=%fused_computation.24 | loop fusion | flops 4194304 | bytes 4194304 | tf_op jit(solution)/shard_map/concatenate | solution.py:118
  48.6 4.4 %gather_fusion.2 = bf16[16,128,1024]{2,1,0:T(8,128)(2,1)} fusion(bf16[8,128,1024]{2,1,0:T(8,128)(2,1)} %pad_maximum_fusion, s32[1024]{0:T(1024)S(1)} %pad_clamp_fusion.2), kind=kCustom, calls=%fused_computation.2 | custom fusion | bytes 8388672 | tf_op jit(solution)/shard_map/gather | solution.py:119
  53.0 4.5 %all-to-all-start = ((bf16[16,2,64,1024]{3,2,1,0:T(8,128)(2,1)}), bf16[16,2,64,1024]{3,2,1,0:T(8,128)(2,1)}, u32[]{:S(2)}, u32[]{:S(2)}) async-start(bf16[16,2,64,1024]{3,2,1,0:T(8,128)(2,1)} %bitcast.85), calls=%async_computation | async-start | bytes 8388608 | tf_op jit(solution)/shard_map/all_to_all | solution.py:120
  57.6 0.2 compare_reduce_fusion
  57.8 0.2 fusion.20
  58.0 0.1 copy.31
  58.1 0.1 min.12
  58.2 2.8 %gather_fusion = bf16[16,128,1024]{2,1,0:T(8,128)(2,1)} fusion(bf16[8,128,1024]{2,1,0:T(8,128)(2,1)S(1)} %copy-done, s32[1024]{0:T(1024)S(1)} %pad_clamp_fusion.1), kind=kCustom, calls=%fused_computation | custom fusion | bytes 8388672 | tf_op jit(solution)/shard_map/gather | solution.py:125
  61.0 4.4 %gather_fusion.3 = bf16[16,128,1024]{2,1,0:T(8,128)(2,1)} fusion(bf16[8,128,1024]{2,1,0:T(8,128)(2,1)} %param.8, s32[1024]{0:T(1024)S(1)} %pad_clamp_fusion.1), kind=kCustom, calls=%fused_computation.3 | custom fusion | bytes 8388672 | tf_op jit(solution)/shard_map/gather | solution.py:126
  65.4 86.1 %all-to-all-done.pair_ref = bf16[16,2,64,1024]{3,2,1,0:T(8,128)(2,1)} async-done(((bf16[16,2,64,1024]{3,2,1,0:T(8,128)(2,1)}), bf16[16,2,64,1024]{3,2,1,0:T(8,128)(2,1)}, u32[]{:S(2)}, u32[]{:S(2)}) %all-to-all-start) | async-done | bytes 4194336 | tf_op jit(solution)/shard_map/all_to_all | solution.py:120
  151.5 2.7 %fusion.28 = (bf16[16,1,64,1024]{3,2,1,0:T(8,128)(2,1)S(1)}, bf16[16,1,64,1024]{3,2,1,0:T(8,128)(2,1)S(1)}) fusion(bf16[16,2,64,1024]{3,2,1,0:T(8,128)(2,1)} %all-to-all-done.pair_ref), kind=kLoop, calls=%fused_computation.80 | loop fusion | bytes 8388608 | tf_op jit(solution)/shard_map/slice | solution.py:123
  154.2 0.6 copy.49
  154.9 2.0 copy.50
  156.8 5.0 %multiply_reduce_fusion.1 = (f32[16,8,64]{2,1,0:T(8,128)S(1)}, f32[16,8,64,128]{3,2,1,0:T(8,128)}) fusion(bf16[16,64,8,128]{3,2,1,0:T(8,128)(2,1)S(1)} %bitcast.87, bf16[16,128,1024]{2,1,0:T(8,128)(2,1)S(1)} %copy-done.4), kind=kOutput, calls=%fused_computation.22 | convolution fusion | flops 270524416 | bytes 10518528 | tf_op jit(solution)/shard_map/bihd,bjhd->bhij/dot_general | solution.py:129
  161.8 0.1 stack.17
  161.9 9.0 %fusion.7 = (f32[16,8,64]{2,1,0:T(8,128)S(1)}, f32[16,8,64]{2,1,0:T(8,128)S(1)}, f32[16,8,64,128]{3,2,1,0:T(8,128)}) fusion(f32[16,8,64,128]{3,2,1,0:T(8,128)} %get-tuple-element.28, f32[16,8,64]{2,1,0:T(8,128)S(1)} %get-tuple-element.27, bf16[16,64,8,128]{3,2,1,0:T(8,128)(2,1)} %bitcast.86, bf16[16,128,1024]{2,1,0:T(8,128)(2,1)} %gather_fusion.3), kind=kOutput, calls=%fused_computation.18 | convolution fusion | flops 273661952 | bytes 14778368 | tf_op jit(solution)/shard_map/bihd,bjhd->bhij/dot_general | solution.py:132
  170.9 0.1 stack.18
  171.0 0.1 stack.19
  171.1 0.7 pad_maximum_fusion.1
  171.9 3.6 %all-to-all-start.1 = ((f32[16,3,512]{2,1,0:T(4,128)}), f32[16,3,512]{2,1,0:T(4,128)S(1)}, u32[]{:S(2)}, u32[]{:S(2)}) async-start(f32[16,3,512]{2,1,0:T(4,128)} %pad_maximum_fusion.1), calls=%async_computation.1 | async-start | bytes 262144 | tf_op jit(solution)/shard_map/all_to_all | solution.py:140
  175.5 7.3 %all-to-all-done.1 = f32[16,3,512]{2,1,0:T(4,128)S(1)} async-done(((f32[16,3,512]{2,1,0:T(4,128)}), f32[16,3,512]{2,1,0:T(4,128)S(1)}, u32[]{:S(2)}, u32[]{:S(2)}) %all-to-all-start.1) | async-done | bytes 98336 | tf_op jit(solution)/shard_map/all_to_all | solution.py:140
  182.8 0.6 gather_fusion.4
  183.5 0.1 fusion.29
  183.6 0.1 fusion.16
  183.8 0.6 gather_fusion.5
  184.4 9.3 %all_to_all.20 = f32[16,2,512]{2,1,0:T(2,128)S(1)} all-to-all(f32[16,2,512]{2,1,0:T(2,128)S(1)} %gather_fusion.5), channel_id=1, replica_groups=mesh['seq'=8,'mp'=4] {'seq'}, dimensions={0} | all-to-all | bytes 131072 | tf_op jit(solution)/shard_map/all_to_all | solution.py:152
  193.7 0.2 slice_reduce_fusion.1
  193.9 0.1 sub.52
  194.0 0.1 sub.55
  194.0 6.5 %fusion.8 = (bf16[16,8,64,128]{3,2,1,0:T(8,128)(2,1)}, bf16[16,8,64,128]{3,2,1,0:T(8,128)(2,1)S(1)}) fusion(f32[16,8,64,128]{3,2,1,0:T(8,128)} %get-tuple-element.28, f32[16,8,64]{2,1,0:T(8,128)S(1)} %sub.52, f32[16,8,64,128]{3,2,1,0:T(8,128)} %get-tuple-element.29, f32[16,8,64]{2,1,0:T(8,128)S(1)} %sub.55), kind=kLoop, calls=%fused_computation.19 | loop fusion | flops 7340032 | bytes 12648448 | tf_op jit(solution)/shard_map/convert_element_type | solution.py:160
  200.5 1.2 convert_bitcast_fusion
  201.8 0.1 copy-done.1
  201.9 1.9 copy.93
  203.8 4.3 %all-to-all-start.3 = ((bf16[16,64,1024]{2,1,0:T(8,128)(2,1)}), bf16[16,64,1024]{2,1,0:T(8,128)(2,1)}, u32[]{:S(2)}, u32[]{:S(2)}) async-start(bf16[16,64,1024]{2,1,0:T(8,128)(2,1)} %bitcast.88), calls=%async_computation.3 | async-start | bytes 4194304 | tf_op jit(solution)/shard_map/all_to_all | solution.py:164
  208.1 0.1 copy.41
  208.2 0.1 select_n.114.rows_ref
  208.3 1.6 copy-done.2
  209.9 1.6 copy-done.3
  211.5 14.8 %shard_map.76 = (bf16[8,128,1024]{2,1,0:T(8,128)(2,1)}, bf16[8,128,1024]{2,1,0:T(8,128)(2,1)}) custom-call(s32[16]{0:T(128)S(1)} %select_n.114.rows_ref, bf16[16,8,64,128]{3,2,1,0:T(8,128)(2,1)S(1)} %copy-done.3, bf16[16,8,64,128]{3,2,1,0:T(8,128)(2,1)S(1)} %copy-done.2, bf16[16,2,64,1024]{3,2,1,0:T(8,128)(2,1)} %all-to-all-done.pair_ref), custom_call_target="tpu_custom_call" | custom-call | tf_op jit(solution)/shard_map/pallas_call | solution.py:74
  226.2 28.7 %all-to-all-done.3 = bf16[16,64,1024]{2,1,0:T(8,128)(2,1)} async-done(((bf16[16,64,1024]{2,1,0:T(8,128)(2,1)}), bf16[16,64,1024]{2,1,0:T(8,128)(2,1)}, u32[]{:S(2)}, u32[]{:S(2)}) %all-to-all-start.3) | async-done | bytes 2097184 | tf_op jit(solution)/shard_map/all_to_all | solution.py:164
  254.9 3.6 %gather_fusion.6 = bf16[16,64,1024]{2,1,0:T(8,128)(2,1)} fusion(bf16[16,64,1024]{2,1,0:T(8,128)(2,1)} %all-to-all-done.3, s32[1024]{0:T(1024)S(1)} %pad_clamp_fusion), kind=kCustom, calls=%fused_computation.6 | custom fusion | bytes 4194368 | tf_op jit(solution)/shard_map/gather | solution.py:168
  258.6 3.3 %bitcast_reduce_fusion = bf16[8,64,1024]{2,1,0:T(8,128)(2,1)} fusion(bf16[16,64,1024]{2,1,0:T(8,128)(2,1)} %gather_fusion.6), kind=kLoop, calls=%fused_computation.25 | loop fusion | flops 524288 | bytes 3145728 | tf_op jit(solution)/shard_map/reduce_sum | solution.py:169
  (27 shorter events, 0.2 us)
Async XLA Ops:
  0.6 57.6 %copy-start = (bf16[8,128,1024]{2,1,0:T(8,128)(2,1)S(1)}, bf16[8,128,1024]{2,1,0:T(8,128)(2,1)}, u32[]{:S(2)}) copy-start(bf16[8,128,1024]{2,1,0:T(8,128)(2,1)} %param.7) | copy-start | bytes 6291460
  53.0 98.5 %all-to-all-start = ((bf16[16,2,64,1024]{3,2,1,0:T(8,128)(2,1)}), bf16[16,2,64,1024]{3,2,1,0:T(8,128)(2,1)}, u32[]{:S(2)}, u32[]{:S(2)}) async-start(bf16[16,2,64,1024]{3,2,1,0:T(8,128)(2,1)} %bitcast.85), calls=%async_computation | async-start | bytes 8388608 | tf_op jit(solution)/shard_map/all_to_all | solution.py:120
  154.2 2.6 copy-start.4
  171.9 11.0 %all-to-all-start.1 = ((f32[16,3,512]{2,1,0:T(4,128)}), f32[16,3,512]{2,1,0:T(4,128)S(1)}, u32[]{:S(2)}, u32[]{:S(2)}) async-start(f32[16,3,512]{2,1,0:T(4,128)} %pad_maximum_fusion.1), calls=%async_computation.1 | async-start | bytes 262144 | tf_op jit(solution)/shard_map/all_to_all | solution.py:140
  194.0 6.5 %copy-start.5 = (bf16[16,128,1024]{2,1,0:T(8,128)(2,1)S(1)}, bf16[16,128,1024]{2,1,0:T(8,128)(2,1)}, u32[]{:S(2)}) copy-start(bf16[16,128,1024]{2,1,0:T(8,128)(2,1)} %gather_fusion) | copy-start | bytes 12582916
  200.5 1.3 copy-start.1
  203.8 51.2 %all-to-all-start.3 = ((bf16[16,64,1024]{2,1,0:T(8,128)(2,1)}), bf16[16,64,1024]{2,1,0:T(8,128)(2,1)}, u32[]{:S(2)}, u32[]{:S(2)}) async-start(bf16[16,64,1024]{2,1,0:T(8,128)(2,1)} %bitcast.88), calls=%async_computation.3 | async-start | bytes 4194304 | tf_op jit(solution)/shard_map/all_to_all | solution.py:164
  208.3 1.6 copy-start.2
  209.9 1.6 copy-start.3

commit v5 on v3

--- a/solution.py
+++ b/solution.py
@@ -104,14 +104,26 @@
     score_scale = HEAD ** (-0.5)
 
     match = target[None, :] == jnp.arange(slot_total)[:, None]
-    slot_valid = jnp.any(match, axis=1)
     slot_item = jnp.sum(jnp.where(match, position[None, :], 0), axis=1)
     slot_span = item_span[slot_item]
 
-    pair_send = jnp.stack([queries[slot_span], out_grad[slot_span]], axis=1)
-    row_send = jnp.where(slot_valid, local_row[slot_item], -1)
+    joined = jnp.concatenate([queries, out_grad], axis=1)
+    pair_send = joined[slot_span].reshape(slot_total, 2, SPAN, width_here)
     pair_recv = lax.all_to_all(pair_send, "seq", split_axis=0, concat_axis=0, tiled=True)
-    row_recv = lax.all_to_all(row_send, "seq", split_axis=0, concat_axis=0, tiled=True)
+
+    my_seq = lax.axis_index("seq")
+    lists = lax.all_gather(flat_rows, "seq", axis=0, tiled=False)
+    owner_all = lists // rows_here
+    local_all = lists % rows_here
+    before_all = (owner_all[:, :, None] == owner_all[:, None, :]) & (
+        position[None, None, :] < position[None, :, None]
+    )
+    target_all = owner_all * slot_depth + jnp.sum(before_all.astype(jnp.int32), axis=2)
+    wanted = my_seq * slot_depth + jnp.arange(slot_depth)
+    hit = target_all[:, None, :] == wanted[None, :, None]
+    row_recv = jnp.where(
+        jnp.any(hit, axis=2), jnp.sum(jnp.where(hit, local_all[:, None, :], 0), axis=2), -1
+    ).reshape(slot_total)
 
     row_index = jnp.clip(row_recv, 0, rows_here - 1)
     query_heads = split_heads(pair_recv[:, 0])

time: 236 us -> 240 us (1.017)
  waiting for transfers between devices: 121 us -> 34.4 us
  blocking collectives: 15.6 us -> 99.4 us
  starting transfers between devices: 20.3 us -> 30.3 us
    all_gather x0 -> x1, blocking collectives: none -> 83.7 us  [per_device(): lists = lax.all_gather(flat_rows, 'seq', axis=0, tiled=False)]
    all_to_all x1, waiting for transfers between devices: 84.7 us -> 1.79 us  [per_device(): lax.all_to_all(pair_send, 'seq', split_axis=0, concat_axis=0, tiled=True)]
    all_to_all x1, starting transfers between devices: 3.63 us -> 19.7 us  [per_device(): back = lax.all_to_all(part, 'seq', split_axis=0, concat_axis=0, tiled=True)]
    all_to_all x1 -> x0, starting transfers between devices: 6.35 us -> none  [per_device(): lax.all_to_all(row_send, 'seq', split_axis=0, concat_axis=0, tiled=True)]
    another operation x1 -> x0, other arithmetic: 4.58 us -> none  [per_device(): pair_send = jnp.stack([queries[slot_span], out_grad[slot_span]], axis=1)]
    all_to_all x1, waiting for transfers between devices: 28.7 us -> 25.3 us  [per_device(): lax.all_to_all(query_part, 'seq', split_axis=0, concat_axis=0, tiled=True)]
    concatenate x0 -> x1, other arithmetic: none -> 3.04 us  [per_device(): joined = jnp.concatenate([queries, out_grad], axis=1)]
    gather x3 -> x1, local copies, waits for them, and re-layouts: 5.88 us -> 4.38 us  [per_device(): pair_send = joined[slot_span].reshape(slot_total, 2, SPAN, width_here)]
  transfers between devices with their start and end apart: 4 -> 3, of which waited for: 3 -> 3; matrix products, arithmetic and copies ran while one was open for 8% -> 4% of each run, Pallas kernels for 6% -> 6%
where the time goes in v5:
time: 240 us; the launch traced here: 239 us
  blocking collectives  99.4 us (41%)
  waiting for transfers between devices  34.4 us (14%)
  starting transfers between devices  30.3 us (13%)
  local copies, waits for them, and re-layouts  28.8 us (12%)
  matrix products  15.2 us (6%)
  other arithmetic  15 us (6%)
  Pallas kernels  14.8 us (6%)
    all_gather x1, blocking collectives, per_device(): lists = lax.all_gather(flat_rows, 'seq', axis=0, tiled=False)  83.7 us
    all_to_all x1, waiting for transfers between devices, per_device(): lax.all_to_all(query_part, 'seq', split_axis=0, concat_axis=0, tiled=True)  25.3 us
    all_to_all x1, starting transfers between devices, per_device(): back = lax.all_to_all(part, 'seq', split_axis=0, concat_axis=0, tiled=True)  19.7 us
    pallas_call x1, Pallas kernels, kv_grads(): pl.pallas_call(kv_kernel, grid_spec=grid_spec, out_shape=[out_shape, out_...  14.8 us
    all_to_all x1, blocking collectives, per_device(): lax.all_to_all(span_stats[slot_span], 'seq', split_axis=0, concat_axis=0,...  9.29 us
    dot_general x1, matrix products, per_device(): jnp.einsum('bihd,bjhd->bhij', grad_heads, value_heads, preferred_element_...  9.01 us
    all_to_all x1, waiting for transfers between devices, per_device(): back = lax.all_to_all(part, 'seq', split_axis=0, concat_axis=0, tiled=True)  7.32 us
    convert_element_type x1, other arithmetic, per_device(): probs_low = softmax_p.astype(jnp.bfloat16)  6.5 us
  transfers between devices with their start and end apart: 3, of which 3 were waited for; matrix products, arithmetic and copies ran while one was open for 4% of the time, Pallas kernels for 6%

profile of v5, /device:TPU:0, one launch (start us, length us, event | category | flops | bytes accessed | tf_op | source)
XLA Modules:
  0.0 238.7 jit_solution(15758859784962385982)
XLA Ops:
  0.7 6.4 %all-gather = s32[4,2,2]{2,1,0:T(2,128)S(1)} all-gather(s32[1,2,2]{2,1,0:T(2,128)} %bitcast.95), channel_id=1, replica_groups=mesh['seq'=8,'mp'=4] {'mp'}, dimensions={0}, use_global_device_ids=true | all-gather | bytes 80 | tf_op jit(solution)/shard_map/all_gather | solution.py:86
  7.0 0.1 all_gather_reshape.6
  7.1 0.2 convert_reduce_fusion.1
  7.3 0.1 select_reduce_fusion
  7.5 0.7 gather_fusion.1
  8.2 3.0 %pad_maximum_fusion = bf16[8,128,1024]{2,1,0:T(8,128)(2,1)} fusion(bf16[8,64,1024]{2,1,0:T(8,128)(2,1)} %param.6, bf16[8,64,1024]{2,1,0:T(8,128)(2,1)} %param.5), kind=kLoop, calls=%fused_computation.24 | loop fusion | flops 4194304 | bytes 4194304 | tf_op jit(solution)/shard_map/concatenate | solution.py:110
  11.2 4.4 %gather_fusion.2 = bf16[16,128,1024]{2,1,0:T(8,128)(2,1)} fusion(bf16[8,128,1024]{2,1,0:T(8,128)(2,1)} %pad_maximum_fusion, s32[1024]{0:T(1024)S(1)} %pad_clamp_fusion.2), kind=kCustom, calls=%fused_computation.2 | custom fusion | bytes 8388672 | tf_op jit(solution)/shard_map/gather | solution.py:111
  15.6 6.3 %all-to-all-start = ((bf16[16,2,64,1024]{3,2,1,0:T(8,128)(2,1)}), bf16[16,2,64,1024]{3,2,1,0:T(8,128)(2,1)}, u32[]{:S(2)}, u32[]{:S(2)}) async-start(bf16[16,2,64,1024]{3,2,1,0:T(8,128)(2,1)} %bitcast.86), calls=%async_computation | async-start | bytes 8388608 | tf_op jit(solution)/shard_map/all_to_all | solution.py:112
  21.9 0.1 reshape.358
  22.0 0.1 reshape.296
  22.1 83.7 %all-gather.1 = s32[8,1,16]{2,1,0:T(1,128)S(1)} all-gather(s32[1,1,16]{2,1,0:T(1,128)S(1)} %reshape.358), channel_id=1, replica_groups=mesh['seq'=8,'mp'=4] {'seq'}, dimensions={0}, use_global_device_ids=true | all-gather | bytes 576 | tf_op jit(solution)/shard_map/all_gather | solution.py:115
  105.8 0.3 convert_reduce_fusion
  106.1 0.2 compare_reduce_fusion
  106.3 0.2 fusion.20
  106.6 0.1 min.14
  106.7 2.8 %gather_fusion = bf16[16,128,1024]{2,1,0:T(8,128)(2,1)} fusion(bf16[8,128,1024]{2,1,0:T(8,128)(2,1)S(1)} %copy-done, s32[1024]{0:T(1024)S(1)} %pad_clamp_fusion.1), kind=kCustom, calls=%fused_computation | custom fusion | bytes 8388672 | tf_op jit(solution)/shard_map/gather | solution.py:131
  109.5 4.4 %gather_fusion.3 = bf16[16,128,1024]{2,1,0:T(8,128)(2,1)} fusion(bf16[8,128,1024]{2,1,0:T(8,128)(2,1)} %param.8, s32[1024]{0:T(1024)S(1)} %pad_clamp_fusion.1), kind=kCustom, calls=%fused_computation.3 | custom fusion | bytes 8388672 | tf_op jit(solution)/shard_map/gather | solution.py:132
  113.9 1.8 all-to-all-done.pair_ref
  115.7 2.7 %fusion.27 = (bf16[16,1,64,1024]{3,2,1,0:T(8,128)(2,1)S(1)}, bf16[16,1,64,1024]{3,2,1,0:T(8,128)(2,1)S(1)}) fusion(bf16[16,2,64,1024]{3,2,1,0:T(8,128)(2,1)} %all-to-all-done.pair_ref), kind=kLoop, calls=%fused_computation.89 | loop fusion | bytes 8388608 | tf_op jit(solution)/shard_map/slice | solution.py:129
  118.4 0.6 copy.49
  119.0 2.0 copy.50
  121.0 5.0 %multiply_reduce_fusion.1 = (f32[16,8,64]{2,1,0:T(8,128)S(1)}, f32[16,8,64,128]{3,2,1,0:T(8,128)}) fusion(bf16[16,64,8,128]{3,2,1,0:T(8,128)(2,1)S(1)} %bitcast.88, bf16[16,128,1024]{2,1,0:T(8,128)(2,1)S(1)} %copy-done.4), kind=kOutput, calls=%fused_computation.22 | convolution fusion | flops 270524416 | bytes 10518528 | tf_op jit(solution)/shard_map/bihd,bjhd->bhij/dot_general | solution.py:135
  126.0 0.1 stack.17
  126.1 9.0 %fusion.7 = (f32[16,8,64]{2,1,0:T(8,128)S(1)}, f32[16,8,64]{2,1,0:T(8,128)S(1)}, f32[16,8,64,128]{3,2,1,0:T(8,128)}) fusion(f32[16,8,64,128]{3,2,1,0:T(8,128)} %get-tuple-element.28, f32[16,8,64]{2,1,0:T(8,128)S(1)} %get-tuple-element.27, bf16[16,64,8,128]{3,2,1,0:T(8,128)(2,1)} %bitcast.87, bf16[16,128,1024]{2,1,0:T(8,128)(2,1)} %gather_fusion.3), kind=kOutput, calls=%fused_computation.18 | convolution fusion | flops 273661952 | bytes 14778368 | tf_op jit(solution)/shard_map/bihd,bjhd->bhij/dot_general | solution.py:138
  135.1 0.1 stack.18
  135.2 0.1 stack.19
  135.3 0.7 pad_maximum_fusion.1
  136.0 19.7 %all-to-all-start.1 = ((f32[16,3,512]{2,1,0:T(4,128)}), f32[16,3,512]{2,1,0:T(4,128)S(1)}, u32[]{:S(2)}, u32[]{:S(2)}) async-start(f32[16,3,512]{2,1,0:T(4,128)} %pad_maximum_fusion.1), calls=%async_computation.1 | async-start | bytes 262144 | tf_op jit(solution)/shard_map/all_to_all | solution.py:146
  155.7 7.3 %all-to-all-done.1 = f32[16,3,512]{2,1,0:T(4,128)S(1)} async-done(((f32[16,3,512]{2,1,0:T(4,128)}), f32[16,3,512]{2,1,0:T(4,128)S(1)}, u32[]{:S(2)}, u32[]{:S(2)}) %all-to-all-start.1) | async-done | bytes 98336 | tf_op jit(solution)/shard_map/all_to_all | solution.py:146
  163.1 0.6 gather_fusion.4
  163.7 0.1 fusion.28
  163.8 0.1 fusion.16
  164.0 0.6 gather_fusion.5
  164.7 9.3 %all_to_all.20 = f32[16,2,512]{2,1,0:T(2,128)S(1)} all-to-all(f32[16,2,512]{2,1,0:T(2,128)S(1)} %gather_fusion.5), channel_id=1, replica_groups=mesh['seq'=8,'mp'=4] {'seq'}, dimensions={0} | all-to-all | bytes 131072 | tf_op jit(solution)/shard_map/all_to_all | solution.py:158
  173.9 0.2 slice_reduce_fusion.1
  174.3 6.5 %fusion.8 = (bf16[16,8,64,128]{3,2,1,0:T(8,128)(2,1)}, bf16[16,8,64,128]{3,2,1,0:T(8,128)(2,1)S(1)}) fusion(f32[16,8,64,128]{3,2,1,0:T(8,128)} %get-tuple-element.28, f32[16,8,64]{2,1,0:T(8,128)S(1)} %sub.59, f32[16,8,64,128]{3,2,1,0:T(8,128)} %get-tuple-element.29, f32[16,8,64]{2,1,0:T(8,128)S(1)} %sub.62), kind=kLoop, calls=%fused_computation.19 | loop fusion | flops 7340032 | bytes 12648448 | tf_op jit(solution)/shard_map/convert_element_type | solution.py:166
  180.8 1.2 convert_bitcast_fusion
  182.0 0.1 copy-done.1
  182.1 1.9 copy.93
  184.0 4.3 %all-to-all-start.3 = ((bf16[16,64,1024]{2,1,0:T(8,128)(2,1)}), bf16[16,64,1024]{2,1,0:T(8,128)(2,1)}, u32[]{:S(2)}, u32[]{:S(2)}) async-start(bf16[16,64,1024]{2,1,0:T(8,128)(2,1)} %bitcast.89), calls=%async_computation.3 | async-start | bytes 4194304 | tf_op jit(solution)/shard_map/all_to_all | solution.py:170
  188.3 0.1 copy.41
  188.4 0.1 select_n.118.rows_ref
  188.5 1.6 copy-done.2
  190.1 1.6 copy-done.3
  191.7 14.8 %shard_map.76 = (bf16[8,128,1024]{2,1,0:T(8,128)(2,1)}, bf16[8,128,1024]{2,1,0:T(8,128)(2,1)}) custom-call(s32[16]{0:T(128)S(1)} %select_n.118.rows_ref, bf16[16,8,64,128]{3,2,1,0:T(8,128)(2,1)S(1)} %copy-done.3, bf16[16,8,64,128]{3,2,1,0:T(8,128)(2,1)S(1)} %copy-done.2, bf16[16,2,64,1024]{3,2,1,0:T(8,128)(2,1)} %all-to-all-done.pair_ref), custom_call_target="tpu_custom_call" | custom-call | tf_op jit(solution)/shard_map/pallas_call | solution.py:74
  206.4 25.3 %all-to-all-done.3 = bf16[16,64,1024]{2,1,0:T(8,128)(2,1)} async-done(((bf16[16,64,1024]{2,1,0:T(8,128)(2,1)}), bf16[16,64,1024]{2,1,0:T(8,128)(2,1)}, u32[]{:S(2)}, u32[]{:S(2)}) %all-to-all-start.3) | async-done | bytes 2097184 | tf_op jit(solution)/shard_map/all_to_all | solution.py:170
  231.8 3.6 %gather_fusion.6 = bf16[16,64,1024]{2,1,0:T(8,128)(2,1)} fusion(bf16[16,64,1024]{2,1,0:T(8,128)(2,1)} %all-to-all-done.3, s32[1024]{0:T(1024)S(1)} %pad_clamp_fusion), kind=kCustom, calls=%fused_computation.6 | custom fusion | bytes 4194368 | tf_op jit(solution)/shard_map/gather | solution.py:174
  235.4 3.3 %bitcast_reduce_fusion = bf16[8,64,1024]{2,1,0:T(8,128)(2,1)} fusion(bf16[16,64,1024]{2,1,0:T(8,128)(2,1)} %gather_fusion.6), kind=kLoop, calls=%fused_computation.25 | loop fusion | flops 524288 | bytes 3145728 | tf_op jit(solution)/shard_map/reduce_sum | solution.py:175
  (32 shorter events, 0.5 us)
Async XLA Ops:
  0.6 106.1 %copy-start = (bf16[8,128,1024]{2,1,0:T(8,128)(2,1)S(1)}, bf16[8,128,1024]{2,1,0:T(8,128)(2,1)}, u32[]{:S(2)}) copy-start(bf16[8,128,1024]{2,1,0:T(8,128)(2,1)} %param.7) | copy-start | bytes 6291460
  15.6 100.1 %all-to-all-start = ((bf16[16,2,64,1024]{3,2,1,0:T(8,128)(2,1)}), bf16[16,2,64,1024]{3,2,1,0:T(8,128)(2,1)}, u32[]{:S(2)}, u32[]{:S(2)}) async-start(bf16[16,2,64,1024]{3,2,1,0:T(8,128)(2,1)} %bitcast.86), calls=%async_computation | async-start | bytes 8388608 | tf_op jit(solution)/shard_map/all_to_all | solution.py:112
  118.4 2.6 %copy-start.4 = (bf16[16,128,1024]{2,1,0:T(8,128)(2,1)S(1)}, bf16[16,128,1024]{2,1,0:T(8,128)(2,1)}, u32[]{:S(2)}) copy-start(bf16[16,128,1024]{2,1,0:T(8,128)(2,1)} %gather_fusion) | copy-start | bytes 12582916
  136.0 27.0 %all-to-all-start.1 = ((f32[16,3,512]{2,1,0:T(4,128)}), f32[16,3,512]{2,1,0:T(4,128)S(1)}, u32[]{:S(2)}, u32[]{:S(2)}) async-start(f32[16,3,512]{2,1,0:T(4,128)} %pad_maximum_fusion.1), calls=%async_computation.1 | async-start | bytes 262144 | tf_op jit(solution)/shard_map/all_to_all | solution.py:146
  174.3 6.5 %copy-start.5 = (bf16[16,128,1024]{2,1,0:T(8,128)(2,1)S(1)}, bf16[16,128,1024]{2,1,0:T(8,128)(2,1)}, u32[]{:S(2)}) copy-start(bf16[16,128,1024]{2,1,0:T(8,128)(2,1)} %gather_fusion) | copy-start | bytes 12582916
  180.8 1.3 copy-start.1
  184.0 47.8 %all-to-all-start.3 = ((bf16[16,64,1024]{2,1,0:T(8,128)(2,1)}), bf16[16,64,1024]{2,1,0:T(8,128)(2,1)}, u32[]{:S(2)}, u32[]{:S(2)}) async-start(bf16[16,64,1024]{2,1,0:T(8,128)(2,1)} %bitcast.89), calls=%async_computation.3 | async-start | bytes 4194304 | tf_op jit(solution)/shard_map/all_to_all | solution.py:170
  188.5 1.6 copy-start.2
  190.1 1.6 copy-start.3

commit v6 on v5

--- a/solution.py
+++ b/solution.py
@@ -17,6 +17,106 @@
     return tensor.reshape(tensor.shape[:-1] + (tensor.shape[-1] // HEAD, HEAD))
 
 
+TRANS_B = (((1,), (1,)), ((), ()))
+
+
+def stats_kernel(rows_ref, pair_ref, key_ref, value_ref, part_ref):
+    heads = part_ref.shape[2]
+    score_scale = HEAD ** (-0.5)
+    for h in range(heads):
+        cols = pl.ds(h * HEAD, HEAD)
+        scores = lax.dot_general(
+            key_ref[0, :, cols], pair_ref[0, 0, :, cols], TRANS_B,
+            preferred_element_type=jnp.float32,
+        ) * score_scale
+        grad_p = lax.dot_general(
+            value_ref[0, :, cols], pair_ref[0, 1, :, cols], TRANS_B,
+            preferred_element_type=jnp.float32,
+        )
+        highest = jnp.max(scores, axis=0, keepdims=True)
+        expons = jnp.exp(scores - highest)
+        part_ref[0, 0, pl.ds(h, 1), :] = highest
+        part_ref[0, 1, pl.ds(h, 1), :] = jnp.sum(expons, axis=0, keepdims=True)
+        part_ref[0, 2, pl.ds(h, 1), :] = jnp.sum(expons * grad_p, axis=0, keepdims=True)
+
+
+def grad_kernel(rows_ref, pair_ref, key_ref, value_ref, stats_ref, query_out, probs_out, grads_out):
+    heads = stats_ref.shape[2]
+    score_scale = HEAD ** (-0.5)
+    for h in range(heads):
+        cols = pl.ds(h * HEAD, HEAD)
+        keys = key_ref[0, :, cols]
+        scores = lax.dot_general(
+            keys, pair_ref[0, 0, :, cols], TRANS_B, preferred_element_type=jnp.float32
+        ) * score_scale
+        grad_p = lax.dot_general(
+            value_ref[0, :, cols], pair_ref[0, 1, :, cols], TRANS_B,
+            preferred_element_type=jnp.float32,
+        )
+        softmax_p = jnp.exp(scores - stats_ref[0, 0, pl.ds(h, 1), :])
+        grad_s = (softmax_p * (grad_p - stats_ref[0, 1, pl.ds(h, 1), :]) * score_scale).astype(
+            jnp.bfloat16
+        )
+        probs_out[0, h] = softmax_p.astype(jnp.bfloat16)
+        grads_out[0, h] = grad_s
+        query_out[0, :, cols] = lax.dot_general(
+            grad_s, keys, TRANS_A, preferred_element_type=jnp.float32
+        ).astype(query_out.dtype)
+
+
+def slot_specs(span_len, nlen, width):
+    return [
+        pl.BlockSpec((1, 2, span_len, width), lambda t, rows: (t, 0, 0, 0)),
+        pl.BlockSpec((1, nlen, width), lambda t, rows: (rows[t], 0, 0)),
+        pl.BlockSpec((1, nlen, width), lambda t, rows: (rows[t], 0, 0)),
+    ]
+
+
+def slot_stats(row_index, pair_recv, row_keys, row_values):
+    slot_total, _, span_len, width = pair_recv.shape
+    nlen = row_keys.shape[1]
+    heads = width // HEAD
+    grid_spec = pltpu.PrefetchScalarGridSpec(
+        num_scalar_prefetch=1,
+        grid=(slot_total,),
+        in_specs=slot_specs(span_len, nlen, width),
+        out_specs=pl.BlockSpec((1, 3, heads, span_len), lambda t, rows: (t, 0, 0, 0)),
+    )
+    return pl.pallas_call(
+        stats_kernel,
+        grid_spec=grid_spec,
+        out_shape=jax.ShapeDtypeStruct((slot_total, 3, heads, span_len), jnp.float32),
+        compiler_params=pltpu.CompilerParams(dimension_semantics=("arbitrary",)),
+    )(row_index, pair_recv, row_keys, row_values)
+
+
+def slot_grads(row_index, pair_recv, row_keys, row_values, stats_recv):
+    slot_total, _, span_len, width = pair_recv.shape
+    nlen = row_keys.shape[1]
+    heads = width // HEAD
+    grid_spec = pltpu.PrefetchScalarGridSpec(
+        num_scalar_prefetch=1,
+        grid=(slot_total,),
+        in_specs=slot_specs(span_len, nlen, width)
+        + [pl.BlockSpec((1, 2, heads, span_len), lambda t, rows: (t, 0, 0, 0))],
+        out_specs=[
+            pl.BlockSpec((1, span_len, width), lambda t, rows: (t, 0, 0)),
+            pl.BlockSpec((1, heads, nlen, span_len), lambda t, rows: (t, 0, 0, 0)),
+            pl.BlockSpec((1, heads, nlen, span_len), lambda t, rows: (t, 0, 0, 0)),
+        ],
+    )
+    return pl.pallas_call(
+        grad_kernel,
+        grid_spec=grid_spec,
+        out_shape=[
+            jax.ShapeDtypeStruct((slot_total, span_len, width), jnp.bfloat16),
+            jax.ShapeDtypeStruct((slot_total, heads, nlen, span_len), jnp.bfloat16),
+            jax.ShapeDtypeStruct((slot_total, heads, nlen, span_len), jnp.bfloat16),
+        ],
+        compiler_params=pltpu.CompilerParams(dimension_semantics=("arbitrary",)),
+    )(row_index, pair_recv, row_keys, row_values, stats_recv)
+
+
 def kv_kernel(rows_ref, probs_ref, grads_ref, pair_ref, key_out, value_out, key_acc, value_acc):
     slot = pl.program_id(0)
     heads = probs_ref.shape[1]
@@ -33,13 +133,11 @@
         here = jnp.maximum(row, 0)
         for h in range(heads):
             cols = pl.ds(h * HEAD, HEAD)
-            value_part = lax.dot_general(
-                probs_ref[0, h], pair_ref[0, 1, :, cols], TRANS_A,
-                preferred_element_type=jnp.float32,
+            value_part = jnp.dot(
+                probs_ref[0, h], pair_ref[0, 1, :, cols], preferred_element_type=jnp.float32
             )
-            key_part = lax.dot_general(
-                grads_ref[0, h], pair_ref[0, 0, :, cols], TRANS_A,
-                preferred_element_type=jnp.float32,
+            key_part = jnp.dot(
+                grads_ref[0, h], pair_ref[0, 0, :, cols], preferred_element_type=jnp.float32
             )
             value_acc[here, :, cols] += value_part
             key_acc[here, :, cols] += key_part
@@ -51,15 +149,15 @@
 
 
 def kv_grads(row_recv, probs_low, grad_s, pair_recv, rows_here):
-    slot_total, heads, span_len, nlen = probs_low.shape
+    slot_total, heads, nlen, span_len = probs_low.shape
     width = pair_recv.shape[-1]
     out_shape = jax.ShapeDtypeStruct((rows_here, nlen, width), jnp.bfloat16)
     grid_spec = pltpu.PrefetchScalarGridSpec(
         num_scalar_prefetch=1,
         grid=(slot_total,),
         in_specs=[
-            pl.BlockSpec((1, heads, span_len, nlen), lambda t, rows: (t, 0, 0, 0)),
-            pl.BlockSpec((1, heads, span_len, nlen), lambda t, rows: (t, 0, 0, 0)),
+            pl.BlockSpec((1, heads, nlen, span_len), lambda t, rows: (t, 0, 0, 0)),
+            pl.BlockSpec((1, heads, nlen, span_len), lambda t, rows: (t, 0, 0, 0)),
             pl.BlockSpec((1, 2, span_len, width), lambda t, rows: (t, 0, 0, 0)),
         ],
         out_specs=[
@@ -126,23 +224,9 @@
     ).reshape(slot_total)
 
     row_index = jnp.clip(row_recv, 0, rows_here - 1)
-    query_heads = split_heads(pair_recv[:, 0])
-    grad_heads = split_heads(pair_recv[:, 1])
-    key_heads = split_heads(row_keys[row_index])
-    value_heads = split_heads(row_values[row_index])
-
-    scores = (
-        jnp.einsum("bihd,bjhd->bhij", query_heads, key_heads, preferred_element_type=jnp.float32)
-        * score_scale
-    )
-    grad_p = jnp.einsum(
-        "bihd,bjhd->bhij", grad_heads, value_heads, preferred_element_type=jnp.float32
-    )
-    highest = jnp.max(scores, axis=3)
-    expons = jnp.exp(scores - highest[..., None])
-    part = jnp.stack(
-        [highest, jnp.sum(expons, axis=3), jnp.sum(expons * grad_p, axis=3)], axis=1
-    ).reshape(slot_total, 3, heads_here * SPAN)
+    part = slot_stats(row_index, pair_recv, row_keys, row_values).reshape(
+        slot_total, 3, heads_here * SPAN
+    )
     back = lax.all_to_all(part, "seq", split_axis=0, concat_axis=0, tiled=True)
 
     item_part = back[target].reshape(span_count, NBR, 3, heads_here * SPAN)
@@ -159,14 +243,10 @@
         span_stats[slot_span], "seq", split_axis=0, concat_axis=0, tiled=True
     )
 
-    norm_here = stats_recv[:, 0].reshape(slot_total, heads_here, SPAN)
-    delta_here = stats_recv[:, 1].reshape(slot_total, heads_here, SPAN)
-    softmax_p = jnp.exp(scores - norm_here[..., None])
-    grad_s = (softmax_p * (grad_p - delta_here[..., None]) * score_scale).astype(jnp.bfloat16)
-    probs_low = softmax_p.astype(jnp.bfloat16)
-    query_part = jnp.einsum(
-        "bhij,bjhd->bihd", grad_s, key_heads, preferred_element_type=jnp.float32
-    ).astype(jnp.bfloat16).reshape(slot_total, SPAN, width_here)
+    query_part, probs_low, grad_s = slot_grads(
+        row_index, pair_recv, row_keys, row_values,
+        stats_recv.reshape(slot_total, 2, heads_here, SPAN),
+    )
     query_back = lax.all_to_all(query_part, "seq", split_axis=0, concat_axis=0, tiled=True)
 
     key_grad, value_grad = kv_grads(row_recv, probs_low, grad_s, pair_recv, rows_here)

time: 240 us -> 244 us (1.017)
  Pallas kernels: 14.8 us -> 59.4 us
  local copies, waits for them, and re-layouts: 28.8 us -> 11.8 us
  matrix products: 15.2 us -> 0 us
  other arithmetic: 15 us -> 7.08 us
  waiting for transfers between devices: 34.4 us -> 42 us
  starting transfers between devices: 30.3 us -> 23 us
    pallas_call x0 -> x2, Pallas kernels: none -> 44.5 us  [the longest x1 30.1 us: slot_grads(): pl.pallas_call(grad_kernel, grid_spec=grid_spec, out_shape=[jax.ShapeDtyp...]
    dot_general x3 -> x0, matrix products: 15.2 us -> none  [the longest x1 9.01 us: per_device(): jnp.einsum('bihd,bjhd->bhij', grad_heads, value_heads, preferred_element_...]
    gather x2 -> x0, local copies, waits for them, and re-layouts: 7.15 us -> none  [the longest x1 4.36 us: per_device(): value_heads = split_heads(row_values[row_index])]
    all_to_all x1, waiting for transfers between devices: 1.79 us -> 8.45 us  [per_device(): lax.all_to_all(pair_send, 'seq', split_axis=0, concat_axis=0, tiled=True)]
    all_to_all x1, starting transfers between devices: 19.7 us -> 13 us  [per_device(): back = lax.all_to_all(part, 'seq', split_axis=0, concat_axis=0, tiled=True)]
    convert_element_type x1 -> x0, other arithmetic: 6.5 us -> none  [per_device(): probs_low = softmax_p.astype(jnp.bfloat16)]
    unnamed x15 -> x3, local copies, waits for them, and re-layouts: 5.95 us -> 2.26 us
    slice x2 -> x0, local copies, waits for them, and re-layouts: 2.88 us -> none  [the longest x1 2.72 us: per_device(): query_heads = split_heads(pair_recv[:, 0])]
  transfers between devices with their start and end apart: 3 -> 3, of which waited for: 3 -> 3; matrix products, arithmetic and copies ran while one was open for 4% -> 1% of each run, Pallas kernels for 6% -> 6%
where the time goes in v6:
time: 244 us; the launch traced here: 243 us
  blocking collectives  99.2 us (41%)
  Pallas kernels  59.4 us (24%)
  waiting for transfers between devices  42 us (17%)
  starting transfers between devices  23 us (9%)
  local copies, waits for them, and re-layouts  11.8 us (5%)
  other arithmetic  7.08 us (3%)
    all_gather x1, blocking collectives, per_device(): lists = lax.all_gather(flat_rows, 'seq', axis=0, tiled=False)  83.7 us
    pallas_call x1, Pallas kernels, slot_grads(): pl.pallas_call(grad_kernel, grid_spec=grid_spec, out_shape=[jax.ShapeDtyp...  30.1 us
    all_to_all x1, waiting for transfers between devices, per_device(): lax.all_to_all(query_part, 'seq', split_axis=0, concat_axis=0, tiled=True)  26.2 us
    pallas_call x1, Pallas kernels, kv_grads(): pl.pallas_call(kv_kernel, grid_spec=grid_spec, out_shape=[out_shape, out_...  14.9 us
    pallas_call x1, Pallas kernels, slot_stats(): pl.pallas_call(stats_kernel, grid_spec=grid_spec, out_shape=jax.ShapeDtyp...  14.4 us
    all_to_all x1, starting transfers between devices, per_device(): back = lax.all_to_all(part, 'seq', split_axis=0, concat_axis=0, tiled=True)  13 us
    all_to_all x1, blocking collectives, per_device(): lax.all_to_all(span_stats[slot_span], 'seq', split_axis=0, concat_axis=0,...  9.29 us
    all_to_all x1, waiting for transfers between devices, per_device(): lax.all_to_all(pair_send, 'seq', split_axis=0, concat_axis=0, tiled=True)  8.45 us
  transfers between devices with their start and end apart: 3, of which 3 were waited for; matrix products, arithmetic and copies ran while one was open for 1% of the time, Pallas kernels for 6%

profile of v6, /device:TPU:0, one launch (start us, length us, event | category | flops | bytes accessed | tf_op | source)
XLA Modules:
  0.0 243.3 jit_solution(16581604810811336383)
XLA Ops:
  0.6 6.3 %all-gather = s32[4,2,2]{2,1,0:T(2,128)S(1)} all-gather(s32[1,2,2]{2,1,0:T(2,128)} %bitcast.48), channel_id=1, replica_groups=mesh['seq'=8,'mp'=4] {'mp'}, dimensions={0}, use_global_device_ids=true | all-gather | bytes 80 | tf_op jit(solution)/shard_map/all_gather | solution.py:184
  6.9 0.1 all_gather_reshape.6
  7.0 0.2 convert_reduce_fusion.1
  7.2 0.1 select_reduce_fusion
  7.3 0.7 gather_fusion
  8.0 1.8 pad_maximum_fusion
  9.8 2.8 %gather_fusion.1 = bf16[16,128,1024]{2,1,0:T(8,128)(2,1)} fusion(bf16[8,128,1024]{2,1,0:T(8,128)(2,1)S(1)} %pad_maximum_fusion, s32[1024]{0:T(1024)S(1)} %pad_clamp_fusion.1), kind=kCustom, calls=%fused_computation.1 | custom fusion | bytes 8388672 | tf_op jit(solution)/shard_map/gather | solution.py:209
  12.6 6.3 %all-to-all-start = ((bf16[16,2,64,1024]{3,2,1,0:T(8,128)(2,1)}), bf16[16,2,64,1024]{3,2,1,0:T(8,128)(2,1)}, u32[]{:S(2)}, u32[]{:S(2)}) async-start(bf16[16,2,64,1024]{3,2,1,0:T(8,128)(2,1)} %bitcast.44), calls=%async_computation | async-start | bytes 8388608 | tf_op jit(solution)/shard_map/all_to_all | solution.py:210
  18.9 0.1 reshape.294
  19.0 0.1 reshape.248
  19.1 83.7 %all-gather.1 = s32[8,1,16]{2,1,0:T(1,128)S(1)} all-gather(s32[1,1,16]{2,1,0:T(1,128)S(1)} %reshape.294), channel_id=1, replica_groups=mesh['seq'=8,'mp'=4] {'seq'}, dimensions={0}, use_global_device_ids=true | all-gather | bytes 576 | tf_op jit(solution)/shard_map/all_gather | solution.py:213
  102.8 0.3 convert_reduce_fusion
  103.1 0.2 compare_reduce_fusion
  103.4 0.2 fusion.5
  103.6 0.1 copy.22
  103.7 0.1 select_n.91.rows_ref
  103.7 0.5 broadcast_clamp_fusion.rows_ref
  104.3 8.4 %all-to-all-done.pair_ref = bf16[16,2,64,1024]{3,2,1,0:T(8,128)(2,1)} async-done(((bf16[16,2,64,1024]{3,2,1,0:T(8,128)(2,1)}), bf16[16,2,64,1024]{3,2,1,0:T(8,128)(2,1)}, u32[]{:S(2)}, u32[]{:S(2)}) %all-to-all-start) | async-done | bytes 4194336 | tf_op jit(solution)/shard_map/all_to_all | solution.py:210
  112.7 14.4 %shard_map.76 = f32[16,3,8,64]{3,2,1,0:T(8,128)} custom-call(s32[16]{0:T(128)} %broadcast_clamp_fusion.rows_ref, bf16[16,2,64,1024]{3,2,1,0:T(8,128)(2,1)} %all-to-all-done.pair_ref, bf16[8,128,1024]{2,1,0:T(8,128)(2,1)} %key_ref.3, bf16[8,128,1024]{2,1,0:T(8,128)(2,1)} %value_ref.3), custom_call_target="tpu_custom_call" | custom-call | tf_op jit(solution)/shard_map/pallas_call | solution.py:85
  127.1 1.7 reshape.300
  128.8 13.0 %all-to-all-start.1 = ((f32[16,3,512]{2,1,0:T(4,128)}), f32[16,3,512]{2,1,0:T(4,128)S(1)}, u32[]{:S(2)}, u32[]{:S(2)}) async-start(f32[16,3,512]{2,1,0:T(4,128)} %reshape.300), calls=%async_computation.1 | async-start | bytes 262144 | tf_op jit(solution)/shard_map/all_to_all | solution.py:230
  141.9 7.3 %all-to-all-done.1 = f32[16,3,512]{2,1,0:T(4,128)S(1)} async-done(((f32[16,3,512]{2,1,0:T(4,128)}), f32[16,3,512]{2,1,0:T(4,128)S(1)}, u32[]{:S(2)}, u32[]{:S(2)}) %all-to-all-start.1) | async-done | bytes 98336 | tf_op jit(solution)/shard_map/all_to_all | solution.py:230
  149.2 0.6 gather_fusion.2
  149.8 0.1 fusion.11
  150.0 0.1 fusion.1
  150.2 0.6 gather_fusion.3
  150.8 9.3 %all_to_all.20 = f32[16,2,512]{2,1,0:T(2,128)S(1)} all-to-all(f32[16,2,512]{2,1,0:T(2,128)S(1)} %gather_fusion.3), channel_id=1, replica_groups=mesh['seq'=8,'mp'=4] {'seq'}, dimensions={0} | all-to-all | bytes 131072 | tf_op jit(solution)/shard_map/all_to_all | solution.py:242
  160.1 0.8 reshape.250.stats_ref
  160.9 30.1 %shard_map.77 = (bf16[16,64,1024]{2,1,0:T(8,128)(2,1)}, bf16[16,8,128,64]{3,2,1,0:T(8,128)(2,1)}, bf16[16,8,128,64]{3,2,1,0:T(8,128)(2,1)}) custom-call(s32[16]{0:T(128)} %broadcast_clamp_fusion.rows_ref, bf16[16,2,64,1024]{3,2,1,0:T(8,128)(2,1)} %all-to-all-done.pair_ref, bf16[8,128,1024]{2,1,0:T(8,128)(2,1)} %key_ref.3, bf16[8,128,1024]{2,1,0:T(8,128)(2,1)} %value_ref.3, ...), custom_call_target="tpu_custom_call" | custom-call | tf_op jit(solution)/shard_map/pallas_call | solution.py:108
  191.0 3.6 %all-to-all-start.3 = ((bf16[16,64,1024]{2,1,0:T(8,128)(2,1)}), bf16[16,64,1024]{2,1,0:T(8,128)(2,1)S(1)}, u32[]{:S(2)}, u32[]{:S(2)}) async-start(bf16[16,64,1024]{2,1,0:T(8,128)(2,1)} %get-tuple-element.8), calls=%async_computation.3 | async-start | bytes 4194304 | tf_op jit(solution)/shard_map/all_to_all | solution.py:250
  194.6 0.0 copy-start
  194.6 2.2 copy-done
  196.8 14.9 %shard_map.78 = (bf16[8,128,1024]{2,1,0:T(8,128)(2,1)}, bf16[8,128,1024]{2,1,0:T(8,128)(2,1)}) custom-call(s32[16]{0:T(128)S(1)} %select_n.91.rows_ref, bf16[16,8,128,64]{3,2,1,0:T(8,128)(2,1)S(1)} %copy-done, bf16[16,8,128,64]{3,2,1,0:T(8,128)(2,1)} %get-tuple-element.10.grads_ref, bf16[16,2,64,1024]{3,2,1,0:T(8,128)(2,1)} %all-to-all-done.pair_ref), custom_call_target="tpu_custom_call" | custom-call | tf_op jit(solution)/shard_map/pallas_call | solution.py:172
  211.7 26.2 %all-to-all-done.3 = bf16[16,64,1024]{2,1,0:T(8,128)(2,1)S(1)} async-done(((bf16[16,64,1024]{2,1,0:T(8,128)(2,1)}), bf16[16,64,1024]{2,1,0:T(8,128)(2,1)S(1)}, u32[]{:S(2)}, u32[]{:S(2)}) %all-to-all-start.3) | async-done | bytes 2097184 | tf_op jit(solution)/shard_map/all_to_all | solution.py:250
  237.9 2.0 gather_fusion.4
  239.9 3.3 %bitcast_reduce_fusion = bf16[8,64,1024]{2,1,0:T(8,128)(2,1)} fusion(bf16[16,64,1024]{2,1,0:T(8,128)(2,1)} %gather_fusion.4), kind=kLoop, calls=%fused_computation.6 | loop fusion | flops 524288 | bytes 3145728 | tf_op jit(solution)/shard_map/reduce_sum | solution.py:255
  (18 shorter events, 0.2 us)
Async XLA Ops:
  12.6 100.1 %all-to-all-start = ((bf16[16,2,64,1024]{3,2,1,0:T(8,128)(2,1)}), bf16[16,2,64,1024]{3,2,1,0:T(8,128)(2,1)}, u32[]{:S(2)}, u32[]{:S(2)}) async-start(bf16[16,2,64,1024]{3,2,1,0:T(8,128)(2,1)} %bitcast.44), calls=%async_computation | async-start | bytes 8388608 | tf_op jit(solution)/shard_map/all_to_all | solution.py:210
  128.8 20.4 %all-to-all-start.1 = ((f32[16,3,512]{2,1,0:T(4,128)}), f32[16,3,512]{2,1,0:T(4,128)S(1)}, u32[]{:S(2)}, u32[]{:S(2)}) async-start(f32[16,3,512]{2,1,0:T(4,128)} %reshape.300), calls=%async_computation.1 | async-start | bytes 262144 | tf_op jit(solution)/shard_map/all_to_all | solution.py:230
  191.0 46.9 %all-to-all-start.3 = ((bf16[16,64,1024]{2,1,0:T(8,128)(2,1)}), bf16[16,64,1024]{2,1,0:T(8,128)(2,1)S(1)}, u32[]{:S(2)}, u32[]{:S(2)}) async-start(bf16[16,64,1024]{2,1,0:T(8,128)(2,1)} %get-tuple-element.8), calls=%async_computation.3 | async-start | bytes 4194304 | tf_op jit(solution)/shard_map/all_to_all | solution.py:250
  194.6 2.2 copy-start

commit v7 on v6

--- a/solution.py
+++ b/solution.py
@@ -35,9 +35,9 @@
         )
         highest = jnp.max(scores, axis=0, keepdims=True)
         expons = jnp.exp(scores - highest)
-        part_ref[0, 0, pl.ds(h, 1), :] = highest
-        part_ref[0, 1, pl.ds(h, 1), :] = jnp.sum(expons, axis=0, keepdims=True)
-        part_ref[0, 2, pl.ds(h, 1), :] = jnp.sum(expons * grad_p, axis=0, keepdims=True)
+        total = jnp.sum(expons, axis=0, keepdims=True)
+        part_ref[0, 0, pl.ds(h, 1), :] = highest + jnp.log(total)
+        part_ref[0, 1, pl.ds(h, 1), :] = jnp.sum(expons * grad_p, axis=0, keepdims=True) / total
 
 
 def grad_kernel(rows_ref, pair_ref, key_ref, value_ref, stats_ref, query_out, probs_out, grads_out):
@@ -80,12 +80,12 @@
         num_scalar_prefetch=1,
         grid=(slot_total,),
         in_specs=slot_specs(span_len, nlen, width),
-        out_specs=pl.BlockSpec((1, 3, heads, span_len), lambda t, rows: (t, 0, 0, 0)),
+        out_specs=pl.BlockSpec((1, 2, heads, span_len), lambda t, rows: (t, 0, 0, 0)),
     )
     return pl.pallas_call(
         stats_kernel,
         grid_spec=grid_spec,
-        out_shape=jax.ShapeDtypeStruct((slot_total, 3, heads, span_len), jnp.float32),
+        out_shape=jax.ShapeDtypeStruct((slot_total, 2, heads, span_len), jnp.float32),
         compiler_params=pltpu.CompilerParams(dimension_semantics=("arbitrary",)),
     )(row_index, pair_recv, row_keys, row_values)
 
@@ -224,28 +224,26 @@
     ).reshape(slot_total)
 
     row_index = jnp.clip(row_recv, 0, rows_here - 1)
-    part = slot_stats(row_index, pair_recv, row_keys, row_values).reshape(
-        slot_total, 3, heads_here * SPAN
-    )
-    back = lax.all_to_all(part, "seq", split_axis=0, concat_axis=0, tiled=True)
-
-    item_part = back[target].reshape(span_count, NBR, 3, heads_here * SPAN)
-    item_max = item_part[:, :, 0]
-    item_sum = item_part[:, :, 1]
-    item_cross = item_part[:, :, 2]
-    span_max = jnp.max(item_max, axis=1, keepdims=True)
-    factor = jnp.exp(item_max - span_max)
-    span_sum = jnp.sum(item_sum * factor, axis=1)
-    log_total = span_max[:, 0] + jnp.log(span_sum)
-    row_delta = jnp.sum(item_cross * factor, axis=1) / span_sum
-    span_stats = jnp.stack([log_total, row_delta], axis=1)
-    stats_recv = lax.all_to_all(
-        span_stats[slot_span], "seq", split_axis=0, concat_axis=0, tiled=True
-    )
+    part = slot_stats(row_index, pair_recv, row_keys, row_values)
+    every_part = lax.all_gather(part, "seq", axis=0, tiled=True)
+
+    sender = jnp.arange(slot_total) // slot_depth
+    item_here = jnp.sum(jnp.where(hit, position[None, None, :], 0), axis=2).reshape(slot_total)
+    partner = item_here + 1 - 2 * (item_here % NBR)
+    partner_owner = owner_all[sender, partner]
+    partner_slot = sender * slot_depth + target_all[sender, partner] - partner_owner * slot_depth
+    other = every_part[partner_owner * slot_total + partner_slot]
+    own_total, other_total = part[:, 0], other[:, 0]
+    top = jnp.maximum(own_total, other_total)
+    log_total = top + jnp.log(jnp.exp(own_total - top) + jnp.exp(other_total - top))
+    row_delta = (
+        jnp.exp(own_total - log_total) * part[:, 1] + jnp.exp(other_total - log_total) * other[:, 1]
+    )
+    stats_recv = jnp.stack([log_total, row_delta], axis=1)
 
     query_part, probs_low, grad_s = slot_grads(
         row_index, pair_recv, row_keys, row_values,
-        stats_recv.reshape(slot_total, 2, heads_here, SPAN),
+        stats_recv,
     )
     query_back = lax.all_to_all(query_part, "seq", split_axis=0, concat_axis=0, tiled=True)
 

time: 244 us -> 254 us (1.041)
  blocking collectives: 99.2 us -> 134 us
  starting transfers between devices: 23 us -> 9.91 us
  waiting for transfers between devices: 42 us -> 30.4 us
    all_gather x0 -> x1, blocking collectives: none -> 44 us  [per_device(): every_part = lax.all_gather(part, 'seq', axis=0, tiled=True)]
    all_to_all x1 -> x0, starting transfers between devices: 13 us -> none  [per_device(): back = lax.all_to_all(part, 'seq', split_axis=0, concat_axis=0, tiled=True)]
    all_to_all x1 -> x0, blocking collectives: 9.29 us -> none  [per_device(): lax.all_to_all(span_stats[slot_span], 'seq', split_axis=0, concat_axis=0,...]
    all_to_all x1 -> x0, waiting for transfers between devices: 7.32 us -> none  [per_device(): back = lax.all_to_all(part, 'seq', split_axis=0, concat_axis=0, tiled=True)]
    all_to_all x1, waiting for transfers between devices: 26.2 us -> 23.4 us  [per_device(): lax.all_to_all(query_part, 'seq', split_axis=0, concat_axis=0, tiled=True)]
  transfers between devices with their start and end apart: 3 -> 2, of which waited for: 3 -> 2; matrix products, arithmetic and copies ran while one was open for 1% -> 1% of each run, Pallas kernels for 6% -> 6%
where the time goes in v7:
time: 254 us; the launch traced here: 253 us
  blocking collectives  134 us (53%)
  Pallas kernels  59.5 us (23%)
  waiting for transfers between devices  30.4 us (12%)
  local copies, waits for them, and re-layouts  10.1 us (4%)
  starting transfers between devices  9.91 us (4%)
  other arithmetic  8.46 us (3%)
    all_gather x1, blocking collectives, per_device(): lists = lax.all_gather(flat_rows, 'seq', axis=0, tiled=False)  83.8 us
    all_gather x1, blocking collectives, per_device(): every_part = lax.all_gather(part, 'seq', axis=0, tiled=True)  44 us
    pallas_call x1, Pallas kernels, slot_grads(): pl.pallas_call(grad_kernel, grid_spec=grid_spec, out_shape=[jax.ShapeDtyp...  30.1 us
    all_to_all x1, waiting for transfers between devices, per_device(): lax.all_to_all(query_part, 'seq', split_axis=0, concat_axis=0, tiled=True)  23.4 us
    pallas_call x1, Pallas kernels, kv_grads(): pl.pallas_call(kv_kernel, grid_spec=grid_spec, out_shape=[out_shape, out_...  14.9 us
    pallas_call x1, Pallas kernels, slot_stats(): pl.pallas_call(stats_kernel, grid_spec=grid_spec, out_shape=jax.ShapeDtyp...  14.4 us
    all_to_all x1, waiting for transfers between devices, per_device(): lax.all_to_all(pair_send, 'seq', split_axis=0, concat_axis=0, tiled=True)  6.93 us
    all_to_all x1, starting transfers between devices, per_device(): lax.all_to_all(pair_send, 'seq', split_axis=0, concat_axis=0, tiled=True)  6.31 us
  transfers between devices with their start and end apart: 2, of which 2 were waited for; matrix products, arithmetic and copies ran while one was open for 1% of the time, Pallas kernels for 6%

profile of v7, /device:TPU:0, one launch (start us, length us, event | category | flops | bytes accessed | tf_op | source)
XLA Modules:
  0.0 253.1 jit_solution(290783346115610130)
XLA Ops:
  0.6 6.3 %all-gather = s32[4,2,2]{2,1,0:T(2,128)S(1)} all-gather(s32[1,2,2]{2,1,0:T(2,128)} %bitcast.38), channel_id=1, replica_groups=mesh['seq'=8,'mp'=4] {'mp'}, dimensions={0}, use_global_device_ids=true | all-gather | bytes 80 | tf_op jit(solution)/shard_map/all_gather | solution.py:184
  6.9 0.1 all_gather_reshape.6
  7.0 0.2 convert_reduce_fusion.1
  7.2 0.1 select_reduce_fusion
  7.3 0.7 gather_fusion
  8.0 1.8 pad_maximum_fusion
  9.8 2.8 %gather_fusion.1 = bf16[16,128,1024]{2,1,0:T(8,128)(2,1)} fusion(bf16[8,128,1024]{2,1,0:T(8,128)(2,1)S(1)} %pad_maximum_fusion, s32[1024]{0:T(1024)S(1)} %pad_clamp_fusion.2), kind=kCustom, calls=%fused_computation.1 | custom fusion | bytes 8388672 | tf_op jit(solution)/shard_map/gather | solution.py:209
  12.6 6.3 %all-to-all-start = ((bf16[16,2,64,1024]{3,2,1,0:T(8,128)(2,1)}), bf16[16,2,64,1024]{3,2,1,0:T(8,128)(2,1)}, u32[]{:S(2)}, u32[]{:S(2)}) async-start(bf16[16,2,64,1024]{3,2,1,0:T(8,128)(2,1)} %bitcast.35), calls=%async_computation | async-start | bytes 8388608 | tf_op jit(solution)/shard_map/all_to_all | solution.py:210
  18.9 0.1 reshape.420
  19.0 83.8 %all-gather.1 = s32[8,1,16]{2,1,0:T(1,128)S(1)} all-gather(s32[1,1,16]{2,1,0:T(1,128)S(1)} %reshape.420), channel_id=1, replica_groups=mesh['seq'=8,'mp'=4] {'seq'}, dimensions={0}, use_global_device_ids=true | all-gather | bytes 576 | tf_op jit(solution)/shard_map/all_gather | solution.py:213
  102.8 0.3 convert_reduce_fusion
  103.1 0.2 fusion.3
  103.4 0.1 copy.9
  103.4 0.1 reshape.371
  103.6 0.6 gather_fusion.3
  104.2 0.6 gather_fusion.2
  104.8 0.2 compare_reduce_fusion
  105.1 0.1 copy.8
  105.2 0.1 select_n.154.rows_ref
  105.3 0.5 broadcast_clamp_fusion.rows_ref
  105.8 6.9 %all-to-all-done.pair_ref = bf16[16,2,64,1024]{3,2,1,0:T(8,128)(2,1)} async-done(((bf16[16,2,64,1024]{3,2,1,0:T(8,128)(2,1)}), bf16[16,2,64,1024]{3,2,1,0:T(8,128)(2,1)}, u32[]{:S(2)}, u32[]{:S(2)}) %all-to-all-start) | async-done | bytes 4194336 | tf_op jit(solution)/shard_map/all_to_all | solution.py:210
  112.7 14.4 %shard_map.76 = f32[16,2,8,64]{3,2,1,0:T(8,128)} custom-call(s32[16]{0:T(128)} %broadcast_clamp_fusion.rows_ref, bf16[16,2,64,1024]{3,2,1,0:T(8,128)(2,1)} %all-to-all-done.pair_ref, bf16[8,128,1024]{2,1,0:T(8,128)(2,1)} %key_ref.3, bf16[8,128,1024]{2,1,0:T(8,128)(2,1)} %value_ref.3), custom_call_target="tpu_custom_call" | custom-call | tf_op jit(solution)/shard_map/pallas_call | solution.py:85
  127.2 44.0 %all_gather.11 = f32[128,2,8,64]{3,2,1,0:T(8,128)S(1)} all-gather(f32[16,2,8,64]{3,2,1,0:T(8,128)} %shard_map.76), channel_id=1, replica_groups=mesh['seq'=8,'mp'=4] {'seq'}, dimensions={0}, use_global_device_ids=true | all-gather | bytes 589824 | tf_op jit(solution)/shard_map/all_gather | solution.py:228
  171.2 0.6 gather_fusion.4
  171.8 0.9 fusion
  172.7 0.7 pad_maximum_fusion.1.stats_ref
  173.4 30.1 %shard_map.77 = (bf16[16,64,1024]{2,1,0:T(8,128)(2,1)}, bf16[16,8,128,64]{3,2,1,0:T(8,128)(2,1)}, bf16[16,8,128,64]{3,2,1,0:T(8,128)(2,1)}) custom-call(s32[16]{0:T(128)} %broadcast_clamp_fusion.rows_ref, bf16[16,2,64,1024]{3,2,1,0:T(8,128)(2,1)} %all-to-all-done.pair_ref, bf16[8,128,1024]{2,1,0:T(8,128)(2,1)} %key_ref.3, bf16[8,128,1024]{2,1,0:T(8,128)(2,1)} %value_ref.3, ...), custom_call_target="tpu_custom_call" | custom-call | tf_op jit(solution)/shard_map/pallas_call | solution.py:108
  203.5 3.6 %all-to-all-start.1 = ((bf16[16,64,1024]{2,1,0:T(8,128)(2,1)}), bf16[16,64,1024]{2,1,0:T(8,128)(2,1)S(1)}, u32[]{:S(2)}, u32[]{:S(2)}) async-start(bf16[16,64,1024]{2,1,0:T(8,128)(2,1)} %get-tuple-element.8), calls=%async_computation.1 | async-start | bytes 4194304 | tf_op jit(solution)/shard_map/all_to_all | solution.py:248
  207.1 0.1 reshape.372
  207.3 0.0 copy-start
  207.3 2.2 copy-done
  209.4 14.9 %shard_map.78 = (bf16[8,128,1024]{2,1,0:T(8,128)(2,1)}, bf16[8,128,1024]{2,1,0:T(8,128)(2,1)}) custom-call(s32[16]{0:T(128)S(1)} %select_n.154.rows_ref, bf16[16,8,128,64]{3,2,1,0:T(8,128)(2,1)S(1)} %copy-done, bf16[16,8,128,64]{3,2,1,0:T(8,128)(2,1)} %get-tuple-element.10.grads_ref, bf16[16,2,64,1024]{3,2,1,0:T(8,128)(2,1)} %all-to-all-done.pair_ref), custom_call_target="tpu_custom_call" | custom-call | tf_op jit(solution)/shard_map/pallas_call | solution.py:172
  224.3 23.4 %all-to-all-done.1 = bf16[16,64,1024]{2,1,0:T(8,128)(2,1)S(1)} async-done(((bf16[16,64,1024]{2,1,0:T(8,128)(2,1)}), bf16[16,64,1024]{2,1,0:T(8,128)(2,1)S(1)}, u32[]{:S(2)}, u32[]{:S(2)}) %all-to-all-start.1) | async-done | bytes 2097184 | tf_op jit(solution)/shard_map/all_to_all | solution.py:248
  247.8 2.0 gather_fusion.5
  249.8 3.3 %bitcast_reduce_fusion = bf16[8,64,1024]{2,1,0:T(8,128)(2,1)} fusion(bf16[16,64,1024]{2,1,0:T(8,128)(2,1)} %gather_fusion.5), kind=kLoop, calls=%fused_computation.7 | loop fusion | flops 524288 | bytes 3145728 | tf_op jit(solution)/shard_map/reduce_sum | solution.py:253
  (17 shorter events, 0.2 us)
Async XLA Ops:
  12.6 100.1 %all-to-all-start = ((bf16[16,2,64,1024]{3,2,1,0:T(8,128)(2,1)}), bf16[16,2,64,1024]{3,2,1,0:T(8,128)(2,1)}, u32[]{:S(2)}, u32[]{:S(2)}) async-start(bf16[16,2,64,1024]{3,2,1,0:T(8,128)(2,1)} %bitcast.35), calls=%async_computation | async-start | bytes 8388608 | tf_op jit(solution)/shard_map/all_to_all | solution.py:210
  203.5 44.2 %all-to-all-start.1 = ((bf16[16,64,1024]{2,1,0:T(8,128)(2,1)}), bf16[16,64,1024]{2,1,0:T(8,128)(2,1)S(1)}, u32[]{:S(2)}, u32[]{:S(2)}) async-start(bf16[16,64,1024]{2,1,0:T(8,128)(2,1)} %get-tuple-element.8), calls=%async_computation.1 | async-start | bytes 4194304 | tf_op jit(solution)/shard_map/all_to_all | solution.py:248
  207.3 2.2 copy-start

commit v8 on v6

--- a/solution.py
+++ b/solution.py
@@ -40,7 +40,7 @@
         part_ref[0, 2, pl.ds(h, 1), :] = jnp.sum(expons * grad_p, axis=0, keepdims=True)
 
 
-def grad_kernel(rows_ref, pair_ref, key_ref, value_ref, stats_ref, query_out, probs_out, grads_out):
+def grad_kernel(rows_ref, pair_ref, key_ref, value_ref, stats_ref, query_out):
     heads = stats_ref.shape[2]
     score_scale = HEAD ** (-0.5)
     for h in range(heads):
@@ -57,8 +57,6 @@
         grad_s = (softmax_p * (grad_p - stats_ref[0, 1, pl.ds(h, 1), :]) * score_scale).astype(
             jnp.bfloat16
         )
-        probs_out[0, h] = softmax_p.astype(jnp.bfloat16)
-        grads_out[0, h] = grad_s
         query_out[0, :, cols] = lax.dot_general(
             grad_s, keys, TRANS_A, preferred_element_type=jnp.float32
         ).astype(query_out.dtype)
@@ -99,27 +97,20 @@
         grid=(slot_total,),
         in_specs=slot_specs(span_len, nlen, width)
         + [pl.BlockSpec((1, 2, heads, span_len), lambda t, rows: (t, 0, 0, 0))],
-        out_specs=[
-            pl.BlockSpec((1, span_len, width), lambda t, rows: (t, 0, 0)),
-            pl.BlockSpec((1, heads, nlen, span_len), lambda t, rows: (t, 0, 0, 0)),
-            pl.BlockSpec((1, heads, nlen, span_len), lambda t, rows: (t, 0, 0, 0)),
-        ],
+        out_specs=pl.BlockSpec((1, span_len, width), lambda t, rows: (t, 0, 0)),
     )
     return pl.pallas_call(
         grad_kernel,
         grid_spec=grid_spec,
-        out_shape=[
-            jax.ShapeDtypeStruct((slot_total, span_len, width), jnp.bfloat16),
-            jax.ShapeDtypeStruct((slot_total, heads, nlen, span_len), jnp.bfloat16),
-            jax.ShapeDtypeStruct((slot_total, heads, nlen, span_len), jnp.bfloat16),
-        ],
+        out_shape=jax.ShapeDtypeStruct((slot_total, span_len, width), jnp.bfloat16),
         compiler_params=pltpu.CompilerParams(dimension_semantics=("arbitrary",)),
     )(row_index, pair_recv, row_keys, row_values, stats_recv)
 
 
-def kv_kernel(rows_ref, probs_ref, grads_ref, pair_ref, key_out, value_out, key_acc, value_acc):
+def kv_kernel(rows_ref, pair_ref, key_ref, value_ref, stats_ref, key_out, value_out, key_acc, value_acc):
     slot = pl.program_id(0)
-    heads = probs_ref.shape[1]
+    heads = stats_ref.shape[2]
+    score_scale = HEAD ** (-0.5)
 
     @pl.when(slot == 0)
     def _():
@@ -133,14 +124,24 @@
         here = jnp.maximum(row, 0)
         for h in range(heads):
             cols = pl.ds(h * HEAD, HEAD)
-            value_part = jnp.dot(
-                probs_ref[0, h], pair_ref[0, 1, :, cols], preferred_element_type=jnp.float32
+            query_rows = pair_ref[0, 0, :, cols]
+            grad_rows = pair_ref[0, 1, :, cols]
+            scores = lax.dot_general(
+                key_ref[0, :, cols], query_rows, TRANS_B, preferred_element_type=jnp.float32
+            ) * score_scale
+            grad_p = lax.dot_general(
+                value_ref[0, :, cols], grad_rows, TRANS_B, preferred_element_type=jnp.float32
             )
-            key_part = jnp.dot(
-                grads_ref[0, h], pair_ref[0, 0, :, cols], preferred_element_type=jnp.float32
+            softmax_p = jnp.exp(scores - stats_ref[0, 0, pl.ds(h, 1), :])
+            grad_s = (
+                softmax_p * (grad_p - stats_ref[0, 1, pl.ds(h, 1), :]) * score_scale
+            ).astype(jnp.bfloat16)
+            value_acc[here, :, cols] += jnp.dot(
+                softmax_p.astype(jnp.bfloat16), grad_rows, preferred_element_type=jnp.float32
             )
-            value_acc[here, :, cols] += value_part
-            key_acc[here, :, cols] += key_part
+            key_acc[here, :, cols] += jnp.dot(
+                grad_s, query_rows, preferred_element_type=jnp.float32
+            )
 
     @pl.when(slot == pl.num_programs(0) - 1)
     def _():
@@ -148,17 +149,19 @@
         value_out[...] = value_acc[...].astype(value_out.dtype)
 
 
-def kv_grads(row_recv, probs_low, grad_s, pair_recv, rows_here):
-    slot_total, heads, nlen, span_len = probs_low.shape
-    width = pair_recv.shape[-1]
+def kv_grads(rows, pair_recv, row_keys, row_values, stats_recv):
+    slot_total, _, span_len, width = pair_recv.shape
+    rows_here, nlen = row_keys.shape[:2]
+    heads = width // HEAD
     out_shape = jax.ShapeDtypeStruct((rows_here, nlen, width), jnp.bfloat16)
     grid_spec = pltpu.PrefetchScalarGridSpec(
         num_scalar_prefetch=1,
         grid=(slot_total,),
         in_specs=[
-            pl.BlockSpec((1, heads, nlen, span_len), lambda t, rows: (t, 0, 0, 0)),
-            pl.BlockSpec((1, heads, nlen, span_len), lambda t, rows: (t, 0, 0, 0)),
             pl.BlockSpec((1, 2, span_len, width), lambda t, rows: (t, 0, 0, 0)),
+            pl.BlockSpec((1, nlen, width), lambda t, rows: (jnp.maximum(rows[t], 0), 0, 0)),
+            pl.BlockSpec((1, nlen, width), lambda t, rows: (jnp.maximum(rows[t], 0), 0, 0)),
+            pl.BlockSpec((1, 2, heads, span_len), lambda t, rows: (t, 0, 0, 0)),
         ],
         out_specs=[
             pl.BlockSpec((rows_here, nlen, width), lambda t, rows: (0, 0, 0)),
@@ -176,7 +179,7 @@
         compiler_params=pltpu.CompilerParams(
             dimension_semantics=("arbitrary",), vmem_limit_bytes=48 * 1024 * 1024
         ),
-    )(row_recv, probs_low, grad_s, pair_recv)
+    )(rows, pair_recv, row_keys, row_values, stats_recv)
 
 
 def per_device(queries, out_grad, row_keys, row_values, neighbours):
@@ -243,13 +246,11 @@
         span_stats[slot_span], "seq", split_axis=0, concat_axis=0, tiled=True
     )
 
-    query_part, probs_low, grad_s = slot_grads(
-        row_index, pair_recv, row_keys, row_values,
-        stats_recv.reshape(slot_total, 2, heads_here, SPAN),
-    )
+    stats_here = stats_recv.reshape(slot_total, 2, heads_here, SPAN)
+    query_part = slot_grads(row_index, pair_recv, row_keys, row_values, stats_here)
     query_back = lax.all_to_all(query_part, "seq", split_axis=0, concat_axis=0, tiled=True)
 
-    key_grad, value_grad = kv_grads(row_recv, probs_low, grad_s, pair_recv, rows_here)
+    key_grad, value_grad = kv_grads(row_recv, pair_recv, row_keys, row_values, stats_here)
 
     returned = query_back[target].reshape(span_count, NBR, SPAN, width_here).astype(jnp.float32)
     query_grad = jnp.sum(returned, axis=1).astype(jnp.bfloat16)

time: 244 us -> 243 us (level)
  Pallas kernels: 59.4 us -> 70.8 us
  waiting for transfers between devices: 42 us -> 30.6 us
    pallas_call x1, Pallas kernels: 14.9 us -> 27 us  [kv_grads(): pl.pallas_call(kv_kernel, grid_spec=grid_spec, out_shape=[out_shape, out_...]
    all_to_all x1, waiting for transfers between devices: 26.2 us -> 14.8 us  [per_device(): lax.all_to_all(query_part, 'seq', split_axis=0, concat_axis=0, tiled=True)]
  transfers between devices with their start and end apart: 3 -> 3, of which waited for: 3 -> 3; matrix products, arithmetic and copies ran while one was open for 1% -> 1% of each run, Pallas kernels for 6% -> 11%
where the time goes in v8:
time: 243 us; the launch traced here: 242 us
  blocking collectives  99.2 us (41%)
  Pallas kernels  70.8 us (29%)
  waiting for transfers between devices  30.6 us (13%)
  starting transfers between devices  23.9 us (10%)
  local copies, waits for them, and re-layouts  11.5 us (5%)
  other arithmetic  5.28 us (2%)
    all_gather x1, blocking collectives, per_device(): lists = lax.all_gather(flat_rows, 'seq', axis=0, tiled=False)  83.7 us
    pallas_call x1, Pallas kernels, slot_grads(): pl.pallas_call(grad_kernel, grid_spec=grid_spec, out_shape=jax.ShapeDtype...  29.4 us
    pallas_call x1, Pallas kernels, kv_grads(): pl.pallas_call(kv_kernel, grid_spec=grid_spec, out_shape=[out_shape, out_...  27 us
    all_to_all x1, waiting for transfers between devices, per_device(): lax.all_to_all(query_part, 'seq', split_axis=0, concat_axis=0, tiled=True)  14.8 us
    pallas_call x1, Pallas kernels, slot_stats(): pl.pallas_call(stats_kernel, grid_spec=grid_spec, out_shape=jax.ShapeDtyp...  14.3 us
    all_to_all x1, starting transfers between devices, per_device(): back = lax.all_to_all(part, 'seq', split_axis=0, concat_axis=0, tiled=True)  13.1 us
    all_to_all x1, blocking collectives, per_device(): lax.all_to_all(span_stats[slot_span], 'seq', split_axis=0, concat_axis=0,...  9.29 us
    all_to_all x1, waiting for transfers between devices, per_device(): lax.all_to_all(pair_send, 'seq', split_axis=0, concat_axis=0, tiled=True)  8.45 us
  transfers between devices with their start and end apart: 3, of which 3 were waited for; matrix products, arithmetic and copies ran while one was open for 1% of the time, Pallas kernels for 11%

profile of v8, /device:TPU:0, one launch (start us, length us, event | category | flops | bytes accessed | tf_op | source)
XLA Modules:
  0.0 242.0 jit_solution(6017934766387420723)
XLA Ops:
  0.6 6.3 %all-gather = s32[4,2,2]{2,1,0:T(2,128)S(1)} all-gather(s32[1,2,2]{2,1,0:T(2,128)} %bitcast.48), channel_id=1, replica_groups=mesh['seq'=8,'mp'=4] {'mp'}, dimensions={0}, use_global_device_ids=true | all-gather | bytes 80 | tf_op jit(solution)/shard_map/all_gather | solution.py:187
  6.9 0.1 all_gather_reshape.6
  7.0 0.2 convert_reduce_fusion.1
  7.2 0.1 select_reduce_fusion
  7.3 0.7 gather_fusion
  8.0 1.8 pad_maximum_fusion
  9.8 2.8 %gather_fusion.1 = bf16[16,128,1024]{2,1,0:T(8,128)(2,1)} fusion(bf16[8,128,1024]{2,1,0:T(8,128)(2,1)S(1)} %pad_maximum_fusion, s32[1024]{0:T(1024)S(1)} %pad_clamp_fusion.1), kind=kCustom, calls=%fused_computation.1 | custom fusion | bytes 8388672 | tf_op jit(solution)/shard_map/gather | solution.py:212
  12.6 6.3 %all-to-all-start = ((bf16[16,2,64,1024]{3,2,1,0:T(8,128)(2,1)}), bf16[16,2,64,1024]{3,2,1,0:T(8,128)(2,1)}, u32[]{:S(2)}, u32[]{:S(2)}) async-start(bf16[16,2,64,1024]{3,2,1,0:T(8,128)(2,1)} %bitcast.44), calls=%async_computation | async-start | bytes 8388608 | tf_op jit(solution)/shard_map/all_to_all | solution.py:213
  18.9 0.1 reshape.294
  19.0 0.1 reshape.248
  19.1 83.7 %all-gather.1 = s32[8,1,16]{2,1,0:T(1,128)S(1)} all-gather(s32[1,1,16]{2,1,0:T(1,128)S(1)} %reshape.294), channel_id=1, replica_groups=mesh['seq'=8,'mp'=4] {'seq'}, dimensions={0}, use_global_device_ids=true | all-gather | bytes 576 | tf_op jit(solution)/shard_map/all_gather | solution.py:216
  102.8 0.3 convert_reduce_fusion
  103.1 0.2 compare_reduce_fusion
  103.4 0.2 fusion.5
  103.6 0.1 copy.22
  103.7 0.1 select_n.91.rows_ref
  103.7 0.5 broadcast_clamp_fusion.rows_ref
  104.3 8.4 %all-to-all-done.pair_ref = bf16[16,2,64,1024]{3,2,1,0:T(8,128)(2,1)} async-done(((bf16[16,2,64,1024]{3,2,1,0:T(8,128)(2,1)}), bf16[16,2,64,1024]{3,2,1,0:T(8,128)(2,1)}, u32[]{:S(2)}, u32[]{:S(2)}) %all-to-all-start) | async-done | bytes 4194336 | tf_op jit(solution)/shard_map/all_to_all | solution.py:213
  112.7 14.3 %shard_map.76 = f32[16,3,8,64]{3,2,1,0:T(8,128)} custom-call(s32[16]{0:T(128)} %broadcast_clamp_fusion.rows_ref, bf16[16,2,64,1024]{3,2,1,0:T(8,128)(2,1)} %all-to-all-done.pair_ref, bf16[8,128,1024]{2,1,0:T(8,128)(2,1)} %key_ref.5, bf16[8,128,1024]{2,1,0:T(8,128)(2,1)} %value_ref.5), custom_call_target="tpu_custom_call" | custom-call | tf_op jit(solution)/shard_map/pallas_call | solution.py:83
  127.1 1.7 reshape.300
  128.8 13.1 %all-to-all-start.1 = ((f32[16,3,512]{2,1,0:T(4,128)}), f32[16,3,512]{2,1,0:T(4,128)S(1)}, u32[]{:S(2)}, u32[]{:S(2)}) async-start(f32[16,3,512]{2,1,0:T(4,128)} %reshape.300), calls=%async_computation.1 | async-start | bytes 262144 | tf_op jit(solution)/shard_map/all_to_all | solution.py:233
  141.9 7.3 %all-to-all-done.1 = f32[16,3,512]{2,1,0:T(4,128)S(1)} async-done(((f32[16,3,512]{2,1,0:T(4,128)}), f32[16,3,512]{2,1,0:T(4,128)S(1)}, u32[]{:S(2)}, u32[]{:S(2)}) %all-to-all-start.1) | async-done | bytes 98336 | tf_op jit(solution)/shard_map/all_to_all | solution.py:233
  149.2 0.6 gather_fusion.2
  149.8 0.1 fusion.11
  150.0 0.1 fusion.1
  150.2 0.6 gather_fusion.3
  150.8 9.3 %all_to_all.20 = f32[16,2,512]{2,1,0:T(2,128)S(1)} all-to-all(f32[16,2,512]{2,1,0:T(2,128)S(1)} %gather_fusion.3), channel_id=1, replica_groups=mesh['seq'=8,'mp'=4] {'seq'}, dimensions={0} | all-to-all | bytes 131072 | tf_op jit(solution)/shard_map/all_to_all | solution.py:245
  160.1 0.8 reshape.250.stats_ref
  160.9 29.4 %shard_map.77 = bf16[16,64,1024]{2,1,0:T(8,128)(2,1)} custom-call(s32[16]{0:T(128)} %broadcast_clamp_fusion.rows_ref, bf16[16,2,64,1024]{3,2,1,0:T(8,128)(2,1)} %all-to-all-done.pair_ref, bf16[8,128,1024]{2,1,0:T(8,128)(2,1)} %key_ref.5, bf16[8,128,1024]{2,1,0:T(8,128)(2,1)} %value_ref.5, f32[16,2,8,64]{3,2,1,0:T(8,128)} %reshape.250.stats_ref), custom_call_target="tpu_custom_call" | custom-call | tf_op jit(solution)/shard_map/pallas_call | solution.py:102
  190.3 0.0 copy-start
  190.3 0.0 copy-start.2
  190.3 4.5 %all-to-all-start.3 = ((bf16[16,64,1024]{2,1,0:T(8,128)(2,1)}), bf16[16,64,1024]{2,1,0:T(8,128)(2,1)}, u32[]{:S(2)}, u32[]{:S(2)}) async-start(bf16[16,64,1024]{2,1,0:T(8,128)(2,1)} %shard_map.77), calls=%async_computation.3 | async-start | bytes 4194304 | tf_op jit(solution)/shard_map/all_to_all | solution.py:251
  194.8 0.0 copy-done
  194.8 0.0 copy-done.2
  194.8 0.0 copy-start.1
  194.8 1.6 copy-done.1
  196.4 27.0 %shard_map.78 = (bf16[8,128,1024]{2,1,0:T(8,128)(2,1)}, bf16[8,128,1024]{2,1,0:T(8,128)(2,1)}) custom-call(s32[16]{0:T(128)S(1)} %select_n.91.rows_ref, bf16[16,2,64,1024]{3,2,1,0:T(8,128)(2,1)} %all-to-all-done.pair_ref, bf16[8,128,1024]{2,1,0:T(8,128)(2,1)S(1)} %copy-done, bf16[8,128,1024]{2,1,0:T(8,128)(2,1)S(1)} %copy-done.1, f32[16,2,8,64]{3,2,1,0:T(8,128)S(1)} %copy-done.2), custom_call_target="tpu_custom_call" | custom-call | tf_op jit(solution)/shard_map/pallas_call | solution.py:175
  223.4 14.8 %all-to-all-done.3 = bf16[16,64,1024]{2,1,0:T(8,128)(2,1)} async-done(((bf16[16,64,1024]{2,1,0:T(8,128)(2,1)}), bf16[16,64,1024]{2,1,0:T(8,128)(2,1)}, u32[]{:S(2)}, u32[]{:S(2)}) %all-to-all-start.3) | async-done | bytes 2097184 | tf_op jit(solution)/shard_map/all_to_all | solution.py:251
  238.2 2.3 gather_fusion.4
  240.5 1.5 bitcast_reduce_fusion
  (18 shorter events, 0.2 us)
Async XLA Ops:
  12.6 100.1 %all-to-all-start = ((bf16[16,2,64,1024]{3,2,1,0:T(8,128)(2,1)}), bf16[16,2,64,1024]{3,2,1,0:T(8,128)(2,1)}, u32[]{:S(2)}, u32[]{:S(2)}) async-start(bf16[16,2,64,1024]{3,2,1,0:T(8,128)(2,1)} %bitcast.44), calls=%async_computation | async-start | bytes 8388608 | tf_op jit(solution)/shard_map/all_to_all | solution.py:213
  128.8 20.4 %all-to-all-start.1 = ((f32[16,3,512]{2,1,0:T(4,128)}), f32[16,3,512]{2,1,0:T(4,128)S(1)}, u32[]{:S(2)}, u32[]{:S(2)}) async-start(f32[16,3,512]{2,1,0:T(4,128)} %reshape.300), calls=%async_computation.1 | async-start | bytes 262144 | tf_op jit(solution)/shard_map/all_to_all | solution.py:233
  190.3 4.5 %copy-start = (bf16[8,128,1024]{2,1,0:T(8,128)(2,1)S(1)}, bf16[8,128,1024]{2,1,0:T(8,128)(2,1)}, u32[]{:S(2)}) copy-start(bf16[8,128,1024]{2,1,0:T(8,128)(2,1)} %key_ref.5) | copy-start | bytes 6291460
  190.3 4.5 %copy-start.2 = (f32[16,2,8,64]{3,2,1,0:T(8,128)S(1)}, f32[16,2,8,64]{3,2,1,0:T(8,128)}, u32[]{:S(2)}) copy-start(f32[16,2,8,64]{3,2,1,0:T(8,128)} %reshape.250.stats_ref) | copy-start | bytes 196612
  190.3 47.9 %all-to-all-start.3 = ((bf16[16,64,1024]{2,1,0:T(8,128)(2,1)}), bf16[16,64,1024]{2,1,0:T(8,128)(2,1)}, u32[]{:S(2)}, u32[]{:S(2)}) async-start(bf16[16,64,1024]{2,1,0:T(8,128)(2,1)} %shard_map.77), calls=%async_computation.3 | async-start | bytes 4194304 | tf_op jit(solution)/shard_map/all_to_all | solution.py:251
  194.8 1.6 copy-start.1

commit v9 on v3

--- a/solution.py
+++ b/solution.py
@@ -108,7 +108,8 @@
     slot_item = jnp.sum(jnp.where(match, position[None, :], 0), axis=1)
     slot_span = item_span[slot_item]
 
-    pair_send = jnp.stack([queries[slot_span], out_grad[slot_span]], axis=1)
+    joined = jnp.concatenate([queries, out_grad], axis=1)
+    pair_send = joined[slot_span].reshape(slot_total, 2, SPAN, width_here)
     row_send = jnp.where(slot_valid, local_row[slot_item], -1)
     pair_recv = lax.all_to_all(pair_send, "seq", split_axis=0, concat_axis=0, tiled=True)
     row_recv = lax.all_to_all(row_send, "seq", split_axis=0, concat_axis=0, tiled=True)
@@ -159,8 +160,11 @@
 
     key_grad, value_grad = kv_grads(row_recv, probs_low, grad_s, pair_recv, rows_here)
 
-    returned = query_back[target].reshape(span_count, NBR, SPAN, width_here).astype(jnp.float32)
-    query_grad = jnp.sum(returned, axis=1).astype(jnp.bfloat16)
+    pair_target = target.reshape(span_count, NBR)
+    query_grad = (
+        query_back[pair_target[:, 0]].astype(jnp.float32)
+        + query_back[pair_target[:, 1]].astype(jnp.float32)
+    ).astype(jnp.bfloat16)
     return (query_grad, key_grad, value_grad)
 
 

time: 236 us -> 235 us (level)
    another operation x1 -> x0, other arithmetic: 4.58 us -> none  [per_device(): pair_send = jnp.stack([queries[slot_span], out_grad[slot_span]], axis=1)]
    reduce_sum x1 -> x0, other arithmetic: 3.34 us -> none  [per_device(): query_grad = jnp.sum(returned, axis=1).astype(jnp.bfloat16)]
    concatenate x0 -> x1, other arithmetic: none -> 3.04 us  [per_device(): joined = jnp.concatenate([queries, out_grad], axis=1)]
    convert_element_type x0 -> x1, other arithmetic: none -> 2.6 us  [per_device(): query_grad = (query_back[pair_target[:, 0]].astype(jnp.float32) + query_b...]
    unnamed x16 -> x15, local copies, waits for them, and re-layouts: 5.88 us -> 5.95 us
  transfers between devices with their start and end apart: 4 -> 4, of which waited for: 3 -> 3; matrix products, arithmetic and copies ran while one was open for 8% -> 7% of each run, Pallas kernels for 6% -> 6%
where the time goes in v9:
time: 235 us; the launch traced here: 234 us
  waiting for transfers between devices  120 us (51%)
  local copies, waits for them, and re-layouts  32.4 us (14%)
  starting transfers between devices  20.3 us (9%)
  blocking collectives  15.7 us (7%)
  matrix products  15.2 us (6%)
  Pallas kernels  14.7 us (6%)
  other arithmetic  14.3 us (6%)
    all_to_all x1, waiting for transfers between devices, per_device(): lax.all_to_all(pair_send, 'seq', split_axis=0, concat_axis=0, tiled=True)  84.7 us
    all_to_all x1, waiting for transfers between devices, per_device(): lax.all_to_all(query_part, 'seq', split_axis=0, concat_axis=0, tiled=True)  28.4 us
    pallas_call x1, Pallas kernels, kv_grads(): pl.pallas_call(kv_kernel, grid_spec=grid_spec, out_shape=[out_shape, out_...  14.7 us
    all_to_all x1, blocking collectives, per_device(): lax.all_to_all(span_stats[slot_span], 'seq', split_axis=0, concat_axis=0,...  9.29 us
    dot_general x1, matrix products, per_device(): jnp.einsum('bihd,bjhd->bhij', grad_heads, value_heads, preferred_element_...  9.01 us
    all_to_all x1, waiting for transfers between devices, per_device(): back = lax.all_to_all(part, 'seq', split_axis=0, concat_axis=0, tiled=True)  7.32 us
    convert_element_type x1, other arithmetic, per_device(): probs_low = softmax_p.astype(jnp.bfloat16)  6.5 us
    all_gather x1, blocking collectives, per_device(): own_lists = lax.all_gather(neighbours, 'mp', axis=0, tiled=True)  6.39 us
  transfers between devices with their start and end apart: 4, of which 3 were waited for; matrix products, arithmetic and copies ran while one was open for 7% of the time, Pallas kernels for 6%

profile of v9, /device:TPU:0, one launch (start us, length us, event | category | flops | bytes accessed | tf_op | source)
XLA Modules:
  0.0 233.9 jit_solution(11611583177088597588)
XLA Ops:
  0.6 6.4 %all-gather = s32[4,2,2]{2,1,0:T(2,128)S(1)} all-gather(s32[1,2,2]{2,1,0:T(2,128)} %bitcast.98), channel_id=1, replica_groups=mesh['seq'=8,'mp'=4] {'mp'}, dimensions={0}, use_global_device_ids=true | all-gather | bytes 80 | tf_op jit(solution)/shard_map/all_gather | solution.py:86
  7.0 0.1 reshape.275
  7.1 0.2 convert_reduce_fusion
  7.3 0.1 select_reduce_fusion
  7.4 0.1 fusion.20
  7.6 0.7 gather_fusion
  8.3 0.7 select_n.111
  8.9 6.3 %all-to-all-start = ((s32[8,2,1]{1,2,0:T(1,128)}), s32[8,2,1]{1,2,0:T(1,128)S(1)}, u32[]{:S(2)}, u32[]{:S(2)}) async-start(s32[8,2,1]{1,2,0:T(1,128)} %bitcast.3), calls=%async_computation | async-start | bytes 8192 | tf_op jit(solution)/shard_map/all_to_all | solution.py:115
  15.3 0.7 gather_fusion.2
  15.9 3.0 %pad_maximum_fusion = bf16[8,128,1024]{2,1,0:T(8,128)(2,1)} fusion(bf16[8,64,1024]{2,1,0:T(8,128)(2,1)} %param.6, bf16[8,64,1024]{2,1,0:T(8,128)(2,1)} %param.5), kind=kLoop, calls=%fused_computation.26 | loop fusion | flops 4194304 | bytes 4194304 | tf_op jit(solution)/shard_map/concatenate | solution.py:111
  19.0 4.4 %gather_fusion.3 = bf16[16,128,1024]{2,1,0:T(8,128)(2,1)} fusion(bf16[8,128,1024]{2,1,0:T(8,128)(2,1)} %pad_maximum_fusion, s32[1024]{0:T(1024)S(1)} %pad_clamp_fusion.4), kind=kCustom, calls=%fused_computation.3 | custom fusion | bytes 8388672 | tf_op jit(solution)/shard_map/gather | solution.py:112
  23.3 6.0 %all-to-all-start.1 = ((bf16[16,2,64,1024]{3,2,1,0:T(8,128)(2,1)}), bf16[16,2,64,1024]{3,2,1,0:T(8,128)(2,1)}, u32[]{:S(2)}, u32[]{:S(2)}) async-start(bf16[16,2,64,1024]{3,2,1,0:T(8,128)(2,1)} %bitcast.90), calls=%async_computation.1 | async-start | bytes 8388608 | tf_op jit(solution)/shard_map/all_to_all | solution.py:114
  29.3 0.1 reshape.279
  29.4 0.5 broadcast.336
  29.9 0.7 fusion.28
  30.7 2.8 %gather_fusion.1 = bf16[16,128,1024]{2,1,0:T(8,128)(2,1)} fusion(bf16[8,128,1024]{2,1,0:T(8,128)(2,1)S(1)} %copy-done, s32[1024]{0:T(1024)S(1)} %pad_clamp_fusion.3), kind=kCustom, calls=%fused_computation.1 | custom fusion | bytes 8388672 | tf_op jit(solution)/shard_map/gather | solution.py:120
  33.5 4.4 %gather_fusion.4 = bf16[16,128,1024]{2,1,0:T(8,128)(2,1)} fusion(bf16[8,128,1024]{2,1,0:T(8,128)(2,1)} %param.8, s32[1024]{0:T(1024)S(1)} %pad_clamp_fusion.3), kind=kCustom, calls=%fused_computation.4 | custom fusion | bytes 8388672 | tf_op jit(solution)/shard_map/gather | solution.py:121
  37.9 84.7 %all-to-all-done.1.pair_ref = bf16[16,2,64,1024]{3,2,1,0:T(8,128)(2,1)} async-done(((bf16[16,2,64,1024]{3,2,1,0:T(8,128)(2,1)}), bf16[16,2,64,1024]{3,2,1,0:T(8,128)(2,1)}, u32[]{:S(2)}, u32[]{:S(2)}) %all-to-all-start.1) | async-done | bytes 4194336 | tf_op jit(solution)/shard_map/all_to_all | solution.py:114
  122.5 2.7 %fusion.29 = (bf16[16,1,64,1024]{3,2,1,0:T(8,128)(2,1)S(1)}, bf16[16,1,64,1024]{3,2,1,0:T(8,128)(2,1)S(1)}) fusion(bf16[16,2,64,1024]{3,2,1,0:T(8,128)(2,1)} %all-to-all-done.1.pair_ref), kind=kLoop, calls=%fused_computation.92 | loop fusion | bytes 8388608 | tf_op jit(solution)/shard_map/slice | solution.py:118
  125.3 0.6 copy.58
  125.9 2.0 copy.59
  127.9 5.0 %multiply_reduce_fusion.1 = (f32[16,8,64]{2,1,0:T(8,128)S(1)}, f32[16,8,64,128]{3,2,1,0:T(8,128)}) fusion(bf16[16,64,8,128]{3,2,1,0:T(8,128)(2,1)S(1)} %bitcast.92, bf16[16,128,1024]{2,1,0:T(8,128)(2,1)S(1)} %copy-done.4), kind=kOutput, calls=%fused_computation.24 | convolution fusion | flops 270524416 | bytes 10518528 | tf_op jit(solution)/shard_map/bihd,bjhd->bhij/dot_general | solution.py:124
  132.9 0.1 stack.17
  133.0 9.0 %fusion.7 = (f32[16,8,64]{2,1,0:T(8,128)S(1)}, f32[16,8,64]{2,1,0:T(8,128)S(1)}, f32[16,8,64,128]{3,2,1,0:T(8,128)}) fusion(f32[16,8,64,128]{3,2,1,0:T(8,128)} %get-tuple-element.30, f32[16,8,64]{2,1,0:T(8,128)S(1)} %get-tuple-element.29, bf16[16,64,8,128]{3,2,1,0:T(8,128)(2,1)} %bitcast.91, bf16[16,128,1024]{2,1,0:T(8,128)(2,1)} %gather_fusion.4), kind=kOutput, calls=%fused_computation.20 | convolution fusion | flops 273661952 | bytes 14778368 | tf_op jit(solution)/shard_map/bihd,bjhd->bhij/dot_general | solution.py:127
  142.0 0.1 stack.18
  142.1 0.1 stack.19
  142.2 0.7 pad_maximum_fusion.1
  142.9 3.6 %all-to-all-start.2 = ((f32[16,3,512]{2,1,0:T(4,128)}), f32[16,3,512]{2,1,0:T(4,128)S(1)}, u32[]{:S(2)}, u32[]{:S(2)}) async-start(f32[16,3,512]{2,1,0:T(4,128)} %pad_maximum_fusion.1), calls=%async_computation.2 | async-start | bytes 262144 | tf_op jit(solution)/shard_map/all_to_all | solution.py:135
  146.6 7.3 %all-to-all-done.2 = f32[16,3,512]{2,1,0:T(4,128)S(1)} async-done(((f32[16,3,512]{2,1,0:T(4,128)}), f32[16,3,512]{2,1,0:T(4,128)S(1)}, u32[]{:S(2)}, u32[]{:S(2)}) %all-to-all-start.2) | async-done | bytes 98336 | tf_op jit(solution)/shard_map/all_to_all | solution.py:135
  153.9 0.6 gather_fusion.5
  154.5 0.1 fusion.30
  154.7 0.1 fusion.16
  154.9 0.6 gather_fusion.6
  155.5 9.3 %all_to_all.28 = f32[16,2,512]{2,1,0:T(2,128)S(1)} all-to-all(f32[16,2,512]{2,1,0:T(2,128)S(1)} %gather_fusion.6), channel_id=1, replica_groups=mesh['seq'=8,'mp'=4] {'seq'}, dimensions={0} | all-to-all | bytes 131072 | tf_op jit(solution)/shard_map/all_to_all | solution.py:147
  164.8 0.2 slice_reduce_fusion.1
  165.1 6.5 %fusion.8 = (bf16[16,8,64,128]{3,2,1,0:T(8,128)(2,1)}, bf16[16,8,64,128]{3,2,1,0:T(8,128)(2,1)S(1)}) fusion(f32[16,8,64,128]{3,2,1,0:T(8,128)} %get-tuple-element.30, f32[16,8,64]{2,1,0:T(8,128)S(1)} %sub.54, f32[16,8,64,128]{3,2,1,0:T(8,128)} %get-tuple-element.31, f32[16,8,64]{2,1,0:T(8,128)S(1)} %sub.57), kind=kLoop, calls=%fused_computation.21 | loop fusion | flops 7340032 | bytes 12648448 | tf_op jit(solution)/shard_map/convert_element_type | solution.py:155
  171.6 1.2 convert_bitcast_fusion
  172.8 0.1 copy-done.1
  172.9 1.9 copy.102
  174.9 4.3 %all-to-all-start.4 = ((bf16[16,64,1024]{2,1,0:T(8,128)(2,1)}), bf16[16,64,1024]{2,1,0:T(8,128)(2,1)}, u32[]{:S(2)}, u32[]{:S(2)}) async-start(bf16[16,64,1024]{2,1,0:T(8,128)(2,1)} %bitcast.93), calls=%async_computation.4 | async-start | bytes 4194304 | tf_op jit(solution)/shard_map/all_to_all | solution.py:159
  179.3 0.1 copy.49
  179.6 1.6 copy-done.2
  181.2 1.6 copy-done.3
  182.8 14.7 %shard_map.76 = (bf16[8,128,1024]{2,1,0:T(8,128)(2,1)}, bf16[8,128,1024]{2,1,0:T(8,128)(2,1)}) custom-call(s32[16]{0:T(128)S(1)} %all_to_all.22.rows_ref, bf16[16,8,64,128]{3,2,1,0:T(8,128)(2,1)S(1)} %copy-done.3, bf16[16,8,64,128]{3,2,1,0:T(8,128)(2,1)S(1)} %copy-done.2, bf16[16,2,64,1024]{3,2,1,0:T(8,128)(2,1)} %all-to-all-done.1.pair_ref), custom_call_target="tpu_custom_call" | custom-call | tf_op jit(solution)/shard_map/pallas_call | solution.py:74
  197.5 28.4 %all-to-all-done.4 = bf16[16,64,1024]{2,1,0:T(8,128)(2,1)} async-done(((bf16[16,64,1024]{2,1,0:T(8,128)(2,1)}), bf16[16,64,1024]{2,1,0:T(8,128)(2,1)}, u32[]{:S(2)}, u32[]{:S(2)}) %all-to-all-start.4) | async-done | bytes 2097184 | tf_op jit(solution)/shard_map/all_to_all | solution.py:159
  225.9 2.2 gather_fusion.7
  228.1 3.2 %gather_fusion.8 = bf16[8,64,1024]{2,1,0:T(8,128)(2,1)} fusion(bf16[16,64,1024]{2,1,0:T(8,128)(2,1)} %all-to-all-done.4, s32[1024]{0:T(1024)S(1)} %get-tuple-element.32), kind=kCustom, calls=%fused_computation.8 | custom fusion | bytes 2097184 | tf_op jit(solution)/shard_map/gather | solution.py:166
  231.3 2.6 %add_convert_fusion = bf16[8,64,1024]{2,1,0:T(8,128)(2,1)} fusion(bf16[8,64,1024]{2,1,0:T(8,128)(2,1)} %gather_fusion.8, bf16[8,64,1024]{2,1,0:T(8,128)(2,1)S(1)} %gather_fusion.7), kind=kLoop, calls=%fused_computation.29 | loop fusion | flops 2097152 | bytes 3145728 | tf_op jit(solution)/shard_map/convert_element_type | solution.py:167
  (35 shorter events, 0.7 us)
Async XLA Ops:
  0.6 30.1 %copy-start = (bf16[8,128,1024]{2,1,0:T(8,128)(2,1)S(1)}, bf16[8,128,1024]{2,1,0:T(8,128)(2,1)}, u32[]{:S(2)}) copy-start(bf16[8,128,1024]{2,1,0:T(8,128)(2,1)} %param.7) | copy-start | bytes 6291460
  8.9 14.4 %all-to-all-start = ((s32[8,2,1]{1,2,0:T(1,128)}), s32[8,2,1]{1,2,0:T(1,128)S(1)}, u32[]{:S(2)}, u32[]{:S(2)}) async-start(s32[8,2,1]{1,2,0:T(1,128)} %bitcast.3), calls=%async_computation | async-start | bytes 8192 | tf_op jit(solution)/shard_map/all_to_all | solution.py:115
  23.3 99.2 %all-to-all-start.1 = ((bf16[16,2,64,1024]{3,2,1,0:T(8,128)(2,1)}), bf16[16,2,64,1024]{3,2,1,0:T(8,128)(2,1)}, u32[]{:S(2)}, u32[]{:S(2)}) async-start(bf16[16,2,64,1024]{3,2,1,0:T(8,128)(2,1)} %bitcast.90), calls=%async_computation.1 | async-start | bytes 8388608 | tf_op jit(solution)/shard_map/all_to_all | solution.py:114
  125.3 2.6 %copy-start.4 = (bf16[16,128,1024]{2,1,0:T(8,128)(2,1)S(1)}, bf16[16,128,1024]{2,1,0:T(8,128)(2,1)}, u32[]{:S(2)}) copy-start(bf16[16,128,1024]{2,1,0:T(8,128)(2,1)} %gather_fusion.1) | copy-start | bytes 12582916
  142.9 11.0 %all-to-all-start.2 = ((f32[16,3,512]{2,1,0:T(4,128)}), f32[16,3,512]{2,1,0:T(4,128)S(1)}, u32[]{:S(2)}, u32[]{:S(2)}) async-start(f32[16,3,512]{2,1,0:T(4,128)} %pad_maximum_fusion.1), calls=%async_computation.2 | async-start | bytes 262144 | tf_op jit(solution)/shard_map/all_to_all | solution.py:135
  165.1 6.5 %copy-start.5 = (bf16[16,128,1024]{2,1,0:T(8,128)(2,1)S(1)}, bf16[16,128,1024]{2,1,0:T(8,128)(2,1)}, u32[]{:S(2)}) copy-start(bf16[16,128,1024]{2,1,0:T(8,128)(2,1)} %gather_fusion.1) | copy-start | bytes 12582916
  171.6 1.3 copy-start.1
  174.9 51.0 %all-to-all-start.4 = ((bf16[16,64,1024]{2,1,0:T(8,128)(2,1)}), bf16[16,64,1024]{2,1,0:T(8,128)(2,1)}, u32[]{:S(2)}, u32[]{:S(2)}) async-start(bf16[16,64,1024]{2,1,0:T(8,128)(2,1)} %bitcast.93), calls=%async_computation.4 | async-start | bytes 4194304 | tf_op jit(solution)/shard_map/all_to_all | solution.py:159
  179.6 1.6 copy-start.2
  181.2 1.6 copy-start.3

commit v10 on v3

--- a/solution.py
+++ b/solution.py
@@ -79,6 +79,65 @@
             dimension_semantics=("arbitrary",), vmem_limit_bytes=48 * 1024 * 1024
         ),
     )(row_recv, probs_low, grad_s, pair_recv)
+
+
+def pair_kernel(span_ref, query_ref, grad_ref, pair_out):
+    pair_out[0, 0] = query_ref[0]
+    pair_out[0, 1] = grad_ref[0]
+
+
+def gather_pairs(slot_span, queries, out_grad):
+    span_count, span_len, width = queries.shape
+    slot_total = slot_span.shape[0]
+
+    def source(t, spans):
+        return (jnp.clip(spans[t], 0, span_count - 1), 0, 0)
+
+    grid_spec = pltpu.PrefetchScalarGridSpec(
+        num_scalar_prefetch=1,
+        grid=(slot_total,),
+        in_specs=[
+            pl.BlockSpec((1, span_len, width), source),
+            pl.BlockSpec((1, span_len, width), source),
+        ],
+        out_specs=pl.BlockSpec((1, 2, span_len, width), lambda t, spans: (t, 0, 0, 0)),
+    )
+    return pl.pallas_call(
+        pair_kernel,
+        grid_spec=grid_spec,
+        out_shape=jax.ShapeDtypeStruct((slot_total, 2, span_len, width), queries.dtype),
+        compiler_params=pltpu.CompilerParams(dimension_semantics=("arbitrary",)),
+    )(slot_span, queries, out_grad)
+
+
+def sum_kernel(target_ref, first_ref, second_ref, query_out):
+    query_out[0] = (
+        first_ref[0].astype(jnp.float32) + second_ref[0].astype(jnp.float32)
+    ).astype(query_out.dtype)
+
+
+def sum_parts(target, query_back):
+    slot_total, span_len, width = query_back.shape
+    span_count = target.shape[0] // NBR
+
+    def part(n):
+        return lambda c, tgt: (jnp.clip(tgt[c * NBR + n], 0, slot_total - 1), 0, 0)
+
+    grid_spec = pltpu.PrefetchScalarGridSpec(
+        num_scalar_prefetch=1,
+        grid=(span_count,),
+        in_specs=[
+            pl.BlockSpec((1, span_len, width), part(0)),
+            pl.BlockSpec((1, span_len, width), part(1)),
+        ],
+        out_specs=pl.BlockSpec((1, span_len, width), lambda c, tgt: (c, 0, 0)),
+    )
+    return pl.pallas_call(
+        sum_kernel,
+        grid_spec=grid_spec,
+        out_shape=jax.ShapeDtypeStruct((span_count, span_len, width), query_back.dtype),
+        compiler_params=pltpu.CompilerParams(dimension_semantics=("arbitrary",)),
+    )(target, query_back, query_back)
 
 
 def per_device(queries, out_grad, row_keys, row_values, neighbours):
@@ -108,7 +167,7 @@
     slot_item = jnp.sum(jnp.where(match, position[None, :], 0), axis=1)
     slot_span = item_span[slot_item]
 
-    pair_send = jnp.stack([queries[slot_span], out_grad[slot_span]], axis=1)
+    pair_send = gather_pairs(slot_span, queries, out_grad)
     row_send = jnp.where(slot_valid, local_row[slot_item], -1)
     pair_recv = lax.all_to_all(pair_send, "seq", split_axis=0, concat_axis=0, tiled=True)
     row_recv = lax.all_to_all(row_send, "seq", split_axis=0, concat_axis=0, tiled=True)
@@ -159,8 +218,7 @@
 
     key_grad, value_grad = kv_grads(row_recv, probs_low, grad_s, pair_recv, rows_here)
 
-    returned = query_back[target].reshape(span_count, NBR, SPAN, width_here).astype(jnp.float32)
-    query_grad = jnp.sum(returned, axis=1).astype(jnp.bfloat16)
+    query_grad = sum_parts(target, query_back)
     return (query_grad, key_grad, value_grad)
 
 

time: 236 us -> 237 us (level)
  Pallas kernels: 14.7 us -> 32 us
  local copies, waits for them, and re-layouts: 31.2 us -> 22.9 us
  other arithmetic: 16.6 us -> 8.67 us
    pallas_call x0 -> x2, Pallas kernels: none -> 17.3 us  [the longest x1 11 us: gather_pairs(): pl.pallas_call(pair_kernel, grid_spec=grid_spec, out_shape=jax.ShapeDtype...]
    gather x3 -> x0, local copies, waits for them, and re-layouts: 8.84 us -> none  [the longest x2 5.22 us: per_device(): pair_send = jnp.stack([queries[slot_span], out_grad[slot_span]], axis=1)]
    another operation x1 -> x0, other arithmetic: 4.58 us -> none  [per_device(): pair_send = jnp.stack([queries[slot_span], out_grad[slot_span]], axis=1)]
    reduce_sum x1 -> x0, other arithmetic: 3.34 us -> none  [per_device(): query_grad = jnp.sum(returned, axis=1).astype(jnp.bfloat16)]
    unnamed x16 -> x18, local copies, waits for them, and re-layouts: 5.88 us -> 5.88 us
  transfers between devices with their start and end apart: 4 -> 4, of which waited for: 3 -> 3; matrix products, arithmetic and copies ran while one was open for 8% -> 4% of each run, Pallas kernels for 6% -> 11%
where the time goes in v10:
time: 237 us; the launch traced here: 236 us
  waiting for transfers between devices  121 us (51%)
  Pallas kernels  32 us (14%)
  local copies, waits for them, and re-layouts  22.9 us (10%)
  starting transfers between devices  20.4 us (9%)
  blocking collectives  15.7 us (7%)
  matrix products  15.2 us (6%)
  other arithmetic  8.67 us (4%)
    all_to_all x1, waiting for transfers between devices, per_device(): lax.all_to_all(pair_send, 'seq', split_axis=0, concat_axis=0, tiled=True)  84.7 us
    all_to_all x1, waiting for transfers between devices, per_device(): lax.all_to_all(query_part, 'seq', split_axis=0, concat_axis=0, tiled=True)  28.7 us
    pallas_call x1, Pallas kernels, kv_grads(): pl.pallas_call(kv_kernel, grid_spec=grid_spec, out_shape=[out_shape, out_...  14.7 us
    pallas_call x1, Pallas kernels, gather_pairs(): pl.pallas_call(pair_kernel, grid_spec=grid_spec, out_shape=jax.ShapeDtype...  11 us
    all_to_all x1, blocking collectives, per_device(): lax.all_to_all(span_stats[slot_span], 'seq', split_axis=0, concat_axis=0,...  9.29 us
    dot_general x1, matrix products, per_device(): jnp.einsum('bihd,bjhd->bhij', grad_heads, value_heads, preferred_element_...  9.01 us
    all_to_all x1, waiting for transfers between devices, per_device(): back = lax.all_to_all(part, 'seq', split_axis=0, concat_axis=0, tiled=True)  7.32 us
    convert_element_type x1, other arithmetic, per_device(): probs_low = softmax_p.astype(jnp.bfloat16)  6.5 us
  transfers between devices with their start and end apart: 4, of which 3 were waited for; matrix products, arithmetic and copies ran while one was open for 4% of the time, Pallas kernels for 11%

profile of v10, /device:TPU:0, one launch (start us, length us, event | category | flops | bytes accessed | tf_op | source)
XLA Modules:
  0.0 236.3 jit_solution(14909118424657601627)
XLA Ops:
  0.6 6.4 %all-gather = s32[4,2,2]{2,1,0:T(2,128)S(1)} all-gather(s32[1,2,2]{2,1,0:T(2,128)} %bitcast.90), channel_id=1, replica_groups=mesh['seq'=8,'mp'=4] {'mp'}, dimensions={0}, use_global_device_ids=true | all-gather | bytes 80 | tf_op jit(solution)/shard_map/all_gather | solution.py:145
  7.0 0.1 reshape.270
  7.1 0.2 convert_reduce_fusion
  7.3 0.1 select_reduce_fusion
  7.4 0.1 fusion.20
  7.6 0.7 gather_fusion
  8.3 0.7 select_n.99
  8.9 6.3 %all-to-all-start = ((s32[8,2,1]{1,2,0:T(1,128)}), s32[8,2,1]{1,2,0:T(1,128)S(1)}, u32[]{:S(2)}, u32[]{:S(2)}) async-start(s32[8,2,1]{1,2,0:T(1,128)} %bitcast.3), calls=%async_computation | async-start | bytes 8192 | tf_op jit(solution)/shard_map/all_to_all | solution.py:173
  15.3 1.2 gather_fusion.2
  16.4 11.0 %shard_map.76 = bf16[16,2,64,1024]{3,2,1,0:T(8,128)(2,1)} custom-call(s32[16]{0:T(128)} %gather_fusion.2, bf16[8,64,1024]{2,1,0:T(8,128)(2,1)} %query_ref.1, bf16[8,64,1024]{2,1,0:T(8,128)(2,1)} %grad_ref.1), custom_call_target="tpu_custom_call" | custom-call | tf_op jit(solution)/shard_map/pallas_call | solution.py:105
  27.5 6.1 %all-to-all-start.1 = ((bf16[16,2,64,1024]{3,2,1,0:T(8,128)(2,1)}), bf16[16,2,64,1024]{3,2,1,0:T(8,128)(2,1)}, u32[]{:S(2)}, u32[]{:S(2)}) async-start(bf16[16,2,64,1024]{3,2,1,0:T(8,128)(2,1)} %shard_map.76), calls=%async_computation.1 | async-start | bytes 8388608 | tf_op jit(solution)/shard_map/all_to_all | solution.py:172
  33.6 0.1 reshape.273
  33.7 0.5 broadcast.305
  34.2 0.7 fusion.26
  34.9 0.1 min.9
  35.0 2.8 %gather_fusion.1 = bf16[16,128,1024]{2,1,0:T(8,128)(2,1)} fusion(bf16[8,128,1024]{2,1,0:T(8,128)(2,1)S(1)} %copy-done, s32[1024]{0:T(1024)S(1)} %pad_clamp_fusion.2), kind=kCustom, calls=%fused_computation.1 | custom fusion | bytes 8388672 | tf_op jit(solution)/shard_map/gather | solution.py:178
  37.8 4.4 %gather_fusion.3 = bf16[16,128,1024]{2,1,0:T(8,128)(2,1)} fusion(bf16[8,128,1024]{2,1,0:T(8,128)(2,1)} %param.8, s32[1024]{0:T(1024)S(1)} %pad_clamp_fusion.2), kind=kCustom, calls=%fused_computation.3 | custom fusion | bytes 8388672 | tf_op jit(solution)/shard_map/gather | solution.py:179
  42.1 84.7 %all-to-all-done.1.pair_ref = bf16[16,2,64,1024]{3,2,1,0:T(8,128)(2,1)} async-done(((bf16[16,2,64,1024]{3,2,1,0:T(8,128)(2,1)}), bf16[16,2,64,1024]{3,2,1,0:T(8,128)(2,1)}, u32[]{:S(2)}, u32[]{:S(2)}) %all-to-all-start.1) | async-done | bytes 4194336 | tf_op jit(solution)/shard_map/all_to_all | solution.py:172
  126.8 2.7 %fusion.27 = (bf16[16,1,64,1024]{3,2,1,0:T(8,128)(2,1)S(1)}, bf16[16,1,64,1024]{3,2,1,0:T(8,128)(2,1)S(1)}) fusion(bf16[16,2,64,1024]{3,2,1,0:T(8,128)(2,1)} %all-to-all-done.1.pair_ref), kind=kLoop, calls=%fused_computation.76 | loop fusion | bytes 8388608 | tf_op jit(solution)/shard_map/slice | solution.py:176
  129.5 0.6 copy.50
  130.1 2.0 copy.51
  132.1 5.0 %multiply_reduce_fusion.1 = (f32[16,8,64]{2,1,0:T(8,128)S(1)}, f32[16,8,64,128]{3,2,1,0:T(8,128)}) fusion(bf16[16,64,8,128]{3,2,1,0:T(8,128)(2,1)S(1)} %bitcast.85, bf16[16,128,1024]{2,1,0:T(8,128)(2,1)S(1)} %copy-done.4), kind=kOutput, calls=%fused_computation.21 | convolution fusion | flops 270524416 | bytes 10518528 | tf_op jit(solution)/shard_map/bihd,bjhd->bhij/dot_general | solution.py:182
  137.1 0.1 stack.17
  137.2 9.0 %fusion.7 = (f32[16,8,64]{2,1,0:T(8,128)S(1)}, f32[16,8,64]{2,1,0:T(8,128)S(1)}, f32[16,8,64,128]{3,2,1,0:T(8,128)}) fusion(f32[16,8,64,128]{3,2,1,0:T(8,128)} %get-tuple-element.28, f32[16,8,64]{2,1,0:T(8,128)S(1)} %get-tuple-element.27, bf16[16,64,8,128]{3,2,1,0:T(8,128)(2,1)} %bitcast.84, bf16[16,128,1024]{2,1,0:T(8,128)(2,1)} %gather_fusion.3), kind=kOutput, calls=%fused_computation.17 | convolution fusion | flops 273661952 | bytes 14778368 | tf_op jit(solution)/shard_map/bihd,bjhd->bhij/dot_general | solution.py:185
  146.2 0.1 stack.18
  146.3 0.1 stack.19
  146.4 0.7 pad_maximum_fusion
  147.1 3.6 %all-to-all-start.2 = ((f32[16,3,512]{2,1,0:T(4,128)}), f32[16,3,512]{2,1,0:T(4,128)S(1)}, u32[]{:S(2)}, u32[]{:S(2)}) async-start(f32[16,3,512]{2,1,0:T(4,128)} %pad_maximum_fusion), calls=%async_computation.2 | async-start | bytes 262144 | tf_op jit(solution)/shard_map/all_to_all | solution.py:193
  150.8 7.3 %all-to-all-done.2 = f32[16,3,512]{2,1,0:T(4,128)S(1)} async-done(((f32[16,3,512]{2,1,0:T(4,128)}), f32[16,3,512]{2,1,0:T(4,128)S(1)}, u32[]{:S(2)}, u32[]{:S(2)}) %all-to-all-start.2) | async-done | bytes 98336 | tf_op jit(solution)/shard_map/all_to_all | solution.py:193
  158.1 0.6 gather_fusion.4
  158.8 0.1 fusion.28
  158.9 0.1 fusion.16
  159.1 0.6 gather_fusion.5
  159.7 9.3 %all_to_all.28 = f32[16,2,512]{2,1,0:T(2,128)S(1)} all-to-all(f32[16,2,512]{2,1,0:T(2,128)S(1)} %gather_fusion.5), channel_id=1, replica_groups=mesh['seq'=8,'mp'=4] {'seq'}, dimensions={0} | all-to-all | bytes 131072 | tf_op jit(solution)/shard_map/all_to_all | solution.py:205
  169.0 0.2 slice_reduce_fusion.1
  169.2 0.1 sub.52
  169.3 0.1 sub.55
  169.3 6.5 %fusion.8 = (bf16[16,8,64,128]{3,2,1,0:T(8,128)(2,1)}, bf16[16,8,64,128]{3,2,1,0:T(8,128)(2,1)S(1)}) fusion(f32[16,8,64,128]{3,2,1,0:T(8,128)} %get-tuple-element.28, f32[16,8,64]{2,1,0:T(8,128)S(1)} %sub.52, f32[16,8,64,128]{3,2,1,0:T(8,128)} %get-tuple-element.29, f32[16,8,64]{2,1,0:T(8,128)S(1)} %sub.55), kind=kLoop, calls=%fused_computation.18 | loop fusion | flops 7340032 | bytes 12648448 | tf_op jit(solution)/shard_map/convert_element_type | solution.py:213
  175.8 1.2 convert_bitcast_fusion
  177.1 0.1 copy-done.1
  177.2 1.9 copy.94
  179.1 4.3 %all-to-all-start.4 = ((bf16[16,64,1024]{2,1,0:T(8,128)(2,1)}), bf16[16,64,1024]{2,1,0:T(8,128)(2,1)}, u32[]{:S(2)}, u32[]{:S(2)}) async-start(bf16[16,64,1024]{2,1,0:T(8,128)(2,1)} %bitcast.86), calls=%async_computation.4 | async-start | bytes 4194304 | tf_op jit(solution)/shard_map/all_to_all | solution.py:217
  183.4 0.1 all_to_all.22.rows_ref
  183.5 1.6 copy-done.2
  185.1 1.6 copy-done.3
  186.7 14.7 %shard_map.78 = (bf16[8,128,1024]{2,1,0:T(8,128)(2,1)}, bf16[8,128,1024]{2,1,0:T(8,128)(2,1)}) custom-call(s32[16]{0:T(128)S(1)} %all_to_all.22.rows_ref, bf16[16,8,64,128]{3,2,1,0:T(8,128)(2,1)S(1)} %copy-done.3, bf16[16,8,64,128]{3,2,1,0:T(8,128)(2,1)S(1)} %copy-done.2, bf16[16,2,64,1024]{3,2,1,0:T(8,128)(2,1)} %all-to-all-done.1.pair_ref), custom_call_target="tpu_custom_call" | custom-call | tf_op jit(solution)/shard_map/pallas_call | solution.py:74
  201.4 28.7 %all-to-all-done.4.first_ref.second_ref = bf16[16,64,1024]{2,1,0:T(8,128)(2,1)} async-done(((bf16[16,64,1024]{2,1,0:T(8,128)(2,1)}), bf16[16,64,1024]{2,1,0:T(8,128)(2,1)}, u32[]{:S(2)}, u32[]{:S(2)}) %all-to-all-start.4) | async-done | bytes 2097184 | tf_op jit(solution)/shard_map/all_to_all | solution.py:217
  230.1 6.2 %shard_map.77 = bf16[8,64,1024]{2,1,0:T(8,128)(2,1)} custom-call(s32[16]{0:T(128)} %copy-done.7, bf16[16,64,1024]{2,1,0:T(8,128)(2,1)} %all-to-all-done.4.first_ref.second_ref, bf16[16,64,1024]{2,1,0:T(8,128)(2,1)} %all-to-all-done.4.first_ref.second_ref), custom_call_target="tpu_custom_call" | custom-call | tf_op jit(solution)/shard_map/pallas_call | solution.py:135
  (30 shorter events, 0.2 us)
Async XLA Ops:
  0.6 34.3 %copy-start = (bf16[8,128,1024]{2,1,0:T(8,128)(2,1)S(1)}, bf16[8,128,1024]{2,1,0:T(8,128)(2,1)}, u32[]{:S(2)}) copy-start(bf16[8,128,1024]{2,1,0:T(8,128)(2,1)} %param.7) | copy-start | bytes 6291460
  7.3 20.2 %copy-start.7 = (s32[16]{0:T(128)}, s32[16]{0:T(128)S(1)}, u32[]{:S(2)}) copy-start(s32[16]{0:T(128)S(1)} %multiply_add_fusion.target_ref) | copy-start | bytes 196
  8.9 18.5 %all-to-all-start = ((s32[8,2,1]{1,2,0:T(1,128)}), s32[8,2,1]{1,2,0:T(1,128)S(1)}, u32[]{:S(2)}, u32[]{:S(2)}) async-start(s32[8,2,1]{1,2,0:T(1,128)} %bitcast.3), calls=%async_computation | async-start | bytes 8192 | tf_op jit(solution)/shard_map/all_to_all | solution.py:173
  27.5 6.2 %copy-start.6 = (s32[16]{0:T(128)S(1)}, s32[16]{0:T(128)}, u32[]{:S(2)}) copy-start(s32[16]{0:T(128)} %gather_fusion.2) | copy-start | bytes 196
  27.5 99.3 %all-to-all-start.1 = ((bf16[16,2,64,1024]{3,2,1,0:T(8,128)(2,1)}), bf16[16,2,64,1024]{3,2,1,0:T(8,128)(2,1)}, u32[]{:S(2)}, u32[]{:S(2)}) async-start(bf16[16,2,64,1024]{3,2,1,0:T(8,128)(2,1)} %shard_map.76), calls=%async_computation.1 | async-start | bytes 8388608 | tf_op jit(solution)/shard_map/all_to_all | solution.py:172
  129.5 2.6 %copy-start.4 = (bf16[16,128,1024]{2,1,0:T(8,128)(2,1)S(1)}, bf16[16,128,1024]{2,1,0:T(8,128)(2,1)}, u32[]{:S(2)}) copy-start(bf16[16,128,1024]{2,1,0:T(8,128)(2,1)} %gather_fusion.1) | copy-start | bytes 12582916
  147.1 11.0 %all-to-all-start.2 = ((f32[16,3,512]{2,1,0:T(4,128)}), f32[16,3,512]{2,1,0:T(4,128)S(1)}, u32[]{:S(2)}, u32[]{:S(2)}) async-start(f32[16,3,512]{2,1,0:T(4,128)} %pad_maximum_fusion), calls=%async_computation.2 | async-start | bytes 262144 | tf_op jit(solution)/shard_map/all_to_all | solution.py:193
  169.3 6.5 %copy-start.5 = (bf16[16,128,1024]{2,1,0:T(8,128)(2,1)S(1)}, bf16[16,128,1024]{2,1,0:T(8,128)(2,1)}, u32[]{:S(2)}) copy-start(bf16[16,128,1024]{2,1,0:T(8,128)(2,1)} %gather_fusion.1) | copy-start | bytes 12582916
  175.8 1.3 copy-start.1
  179.1 51.0 %all-to-all-start.4 = ((bf16[16,64,1024]{2,1,0:T(8,128)(2,1)}), bf16[16,64,1024]{2,1,0:T(8,128)(2,1)}, u32[]{:S(2)}, u32[]{:S(2)}) async-start(bf16[16,64,1024]{2,1,0:T(8,128)(2,1)} %bitcast.86), calls=%async_computation.4 | async-start | bytes 4194304 | tf_op jit(solution)/shard_map/all_to_all | solution.py:217
  183.5 1.6 copy-start.2
  185.1 1.6 copy-start.3

commit v11 on v10

--- a/solution.py
+++ b/solution.py
@@ -82,62 +82,60 @@
 
 
 def pair_kernel(span_ref, query_ref, grad_ref, pair_out):
-    pair_out[0, 0] = query_ref[0]
-    pair_out[0, 1] = grad_ref[0]
+    def body(t, carry):
+        source = span_ref[t]
+        pair_out[t, 0] = query_ref[source]
+        pair_out[t, 1] = grad_ref[source]
+        return carry
+
+    lax.fori_loop(0, pair_out.shape[0], body, 0)
 
 
 def gather_pairs(slot_span, queries, out_grad):
     span_count, span_len, width = queries.shape
     slot_total = slot_span.shape[0]
-
-    def source(t, spans):
-        return (jnp.clip(spans[t], 0, span_count - 1), 0, 0)
-
     grid_spec = pltpu.PrefetchScalarGridSpec(
         num_scalar_prefetch=1,
-        grid=(slot_total,),
+        grid=(1,),
         in_specs=[
-            pl.BlockSpec((1, span_len, width), source),
-            pl.BlockSpec((1, span_len, width), source),
-        ],
-        out_specs=pl.BlockSpec((1, 2, span_len, width), lambda t, spans: (t, 0, 0, 0)),
+            pl.BlockSpec((span_count, span_len, width), lambda i, spans: (0, 0, 0)),
+            pl.BlockSpec((span_count, span_len, width), lambda i, spans: (0, 0, 0)),
+        ],
+        out_specs=pl.BlockSpec((slot_total, 2, span_len, width), lambda i, spans: (0, 0, 0, 0)),
     )
     return pl.pallas_call(
         pair_kernel,
         grid_spec=grid_spec,
         out_shape=jax.ShapeDtypeStruct((slot_total, 2, span_len, width), queries.dtype),
-        compiler_params=pltpu.CompilerParams(dimension_semantics=("arbitrary",)),
-    )(slot_span, queries, out_grad)
-
-
-def sum_kernel(target_ref, first_ref, second_ref, query_out):
-    query_out[0] = (
-        first_ref[0].astype(jnp.float32) + second_ref[0].astype(jnp.float32)
-    ).astype(query_out.dtype)
+        compiler_params=pltpu.CompilerParams(vmem_limit_bytes=48 * 1024 * 1024),
+    )(jnp.clip(slot_span, 0, span_count - 1), queries, out_grad)
+
+
+def sum_kernel(target_ref, back_ref, query_out):
+    def body(c, carry):
+        first = back_ref[target_ref[c * NBR]].astype(jnp.float32)
+        second = back_ref[target_ref[c * NBR + 1]].astype(jnp.float32)
+        query_out[c] = (first + second).astype(query_out.dtype)
+        return carry
+
+    lax.fori_loop(0, query_out.shape[0], body, 0)
 
 
 def sum_parts(target, query_back):
     slot_total, span_len, width = query_back.shape
     span_count = target.shape[0] // NBR
-
-    def part(n):
-        return lambda c, tgt: (jnp.clip(tgt[c * NBR + n], 0, slot_total - 1), 0, 0)
-
     grid_spec = pltpu.PrefetchScalarGridSpec(
         num_scalar_prefetch=1,
-        grid=(span_count,),
-        in_specs=[
-            pl.BlockSpec((1, span_len, width), part(0)),
-            pl.BlockSpec((1, span_len, width), part(1)),
-        ],
-        out_specs=pl.BlockSpec((1, span_len, width), lambda c, tgt: (c, 0, 0)),
+        grid=(1,),
+        in_specs=[pl.BlockSpec((slot_total, span_len, width), lambda i, tgt: (0, 0, 0))],
+        out_specs=pl.BlockSpec((span_count, span_len, width), lambda i, tgt: (0, 0, 0)),
     )
     return pl.pallas_call(
         sum_kernel,
         grid_spec=grid_spec,
         out_shape=jax.ShapeDtypeStruct((span_count, span_len, width), query_back.dtype),
-        compiler_params=pltpu.CompilerParams(dimension_semantics=("arbitrary",)),
-    )(target, query_back, query_back)
+        compiler_params=pltpu.CompilerParams(vmem_limit_bytes=48 * 1024 * 1024),
+    )(jnp.clip(target, 0, slot_total - 1), query_back)
 
 
 def per_device(queries, out_grad, row_keys, row_values, neighbours):

time: 237 us -> 228 us (0.962)
  Pallas kernels: 32 us -> 21 us
    pallas_call x1, Pallas kernels: 11 us -> 2.86 us  [gather_pairs(): pl.pallas_call(pair_kernel, grid_spec=grid_spec, out_shape=jax.ShapeDtype...]
    pallas_call x1, Pallas kernels: 6.25 us -> 3.39 us  [sum_parts(): pl.pallas_call(sum_kernel, grid_spec=grid_spec, out_shape=jax.ShapeDtypeS...]
    unnamed x18, local copies, waits for them, and re-layouts: 5.88 us -> 8.32 us
  transfers between devices with their start and end apart: 4 -> 4, of which waited for: 3 -> 4; matrix products, arithmetic and copies ran while one was open for 4% -> 4% of each run, Pallas kernels for 11% -> 8%
where the time goes in v11:
time: 228 us; the launch traced here: 227 us
  waiting for transfers between devices  121 us (53%)
  local copies, waits for them, and re-layouts  24.8 us (11%)
  Pallas kernels  21 us (9%)
  starting transfers between devices  19.9 us (9%)
  blocking collectives  15.7 us (7%)
  matrix products  15.2 us (7%)
  other arithmetic  8.74 us (4%)
    all_to_all x1, waiting for transfers between devices, per_device(): lax.all_to_all(pair_send, 'seq', split_axis=0, concat_axis=0, tiled=True)  84.7 us
    all_to_all x1, waiting for transfers between devices, per_device(): lax.all_to_all(query_part, 'seq', split_axis=0, concat_axis=0, tiled=True)  28.7 us
    pallas_call x1, Pallas kernels, kv_grads(): pl.pallas_call(kv_kernel, grid_spec=grid_spec, out_shape=[out_shape, out_...  14.7 us
    all_to_all x1, blocking collectives, per_device(): lax.all_to_all(span_stats[slot_span], 'seq', split_axis=0, concat_axis=0,...  9.29 us
    dot_general x1, matrix products, per_device(): jnp.einsum('bihd,bjhd->bhij', grad_heads, value_heads, preferred_element_...  9.01 us
    unnamed x18, local copies, waits for them, and re-layouts  8.32 us
    all_to_all x1, waiting for transfers between devices, per_device(): back = lax.all_to_all(part, 'seq', split_axis=0, concat_axis=0, tiled=True)  7.32 us
    convert_element_type x1, other arithmetic, per_device(): probs_low = softmax_p.astype(jnp.bfloat16)  6.56 us
  transfers between devices with their start and end apart: 4, of which 4 were waited for; matrix products, arithmetic and copies ran while one was open for 4% of the time, Pallas kernels for 8%

profile of v11, /device:TPU:0, one launch (start us, length us, event | category | flops | bytes accessed | tf_op | source)
XLA Modules:
  0.0 227.2 jit_solution(324191440240249820)
XLA Ops:
  0.6 6.4 %all-gather = s32[4,2,2]{2,1,0:T(2,128)S(1)} all-gather(s32[1,2,2]{2,1,0:T(2,128)} %bitcast.90), channel_id=1, replica_groups=mesh['seq'=8,'mp'=4] {'mp'}, dimensions={0}, use_global_device_ids=true | all-gather | bytes 80 | tf_op jit(solution)/shard_map/all_gather | solution.py:143
  7.0 0.1 reshape.270
  7.1 0.2 convert_reduce_fusion
  7.3 0.1 fusion.20
  7.4 0.1 select_reduce_fusion
  7.6 0.7 gather_fusion
  8.3 0.7 select_n.99
  8.9 6.3 %all-to-all-start = ((s32[8,2,1]{1,2,0:T(1,128)}), s32[8,2,1]{1,2,0:T(1,128)S(1)}, u32[]{:S(2)}, u32[]{:S(2)}) async-start(s32[8,2,1]{1,2,0:T(1,128)} %bitcast.3), calls=%async_computation | async-start | bytes 8192 | tf_op jit(solution)/shard_map/all_to_all | solution.py:171
  15.3 0.7 gather_fusion.2
  15.9 1.2 copy-done.4
  17.2 1.2 copy-done.5
  18.4 2.9 %shard_map.76 = bf16[16,2,64,1024]{3,2,1,0:T(8,128)(2,1)} custom-call(s32[16]{0:T(128)S(1)} %broadcast_clamp_fusion.1.span_ref, bf16[8,64,1024]{2,1,0:T(8,128)(2,1)S(1)} %copy-done.4, bf16[8,64,1024]{2,1,0:T(8,128)(2,1)S(1)} %copy-done.5), custom_call_target="tpu_custom_call" | custom-call | tf_op jit(solution)/shard_map/pallas_call | solution.py:106
  21.2 0.4 all-to-all-done
  21.6 5.6 %all-to-all-start.1 = ((bf16[16,2,64,1024]{3,2,1,0:T(8,128)(2,1)}), bf16[16,2,64,1024]{3,2,1,0:T(8,128)(2,1)}, u32[]{:S(2)}, u32[]{:S(2)}) async-start(bf16[16,2,64,1024]{3,2,1,0:T(8,128)(2,1)} %shard_map.76), calls=%async_computation.1 | async-start | bytes 8388608 | tf_op jit(solution)/shard_map/all_to_all | solution.py:170
  27.2 0.1 reshape.273
  27.3 0.5 broadcast.289
  27.9 0.7 fusion.26
  28.5 0.1 min.21
  28.6 2.8 %gather_fusion.1 = bf16[16,128,1024]{2,1,0:T(8,128)(2,1)} fusion(bf16[8,128,1024]{2,1,0:T(8,128)(2,1)S(1)} %copy-done, s32[1024]{0:T(1024)S(1)} %pad_clamp_fusion.2), kind=kCustom, calls=%fused_computation.1 | custom fusion | bytes 8388672 | tf_op jit(solution)/shard_map/gather | solution.py:176
  31.4 4.4 %gather_fusion.3 = bf16[16,128,1024]{2,1,0:T(8,128)(2,1)} fusion(bf16[8,128,1024]{2,1,0:T(8,128)(2,1)} %param.8, s32[1024]{0:T(1024)S(1)} %pad_clamp_fusion.2), kind=kCustom, calls=%fused_computation.3 | custom fusion | bytes 8388672 | tf_op jit(solution)/shard_map/gather | solution.py:177
  35.8 84.7 %all-to-all-done.1.pair_ref = bf16[16,2,64,1024]{3,2,1,0:T(8,128)(2,1)} async-done(((bf16[16,2,64,1024]{3,2,1,0:T(8,128)(2,1)}), bf16[16,2,64,1024]{3,2,1,0:T(8,128)(2,1)}, u32[]{:S(2)}, u32[]{:S(2)}) %all-to-all-start.1) | async-done | bytes 4194336 | tf_op jit(solution)/shard_map/all_to_all | solution.py:170
  120.4 2.7 %fusion.27 = (bf16[16,1,64,1024]{3,2,1,0:T(8,128)(2,1)S(1)}, bf16[16,1,64,1024]{3,2,1,0:T(8,128)(2,1)S(1)}) fusion(bf16[16,2,64,1024]{3,2,1,0:T(8,128)(2,1)} %all-to-all-done.1.pair_ref), kind=kLoop, calls=%fused_computation.78 | loop fusion | bytes 8388608 | tf_op jit(solution)/shard_map/slice | solution.py:174
  123.2 0.6 copy.50
  123.8 2.0 copy.51
  125.8 5.0 %multiply_reduce_fusion.1 = (f32[16,8,64]{2,1,0:T(8,128)S(1)}, f32[16,8,64,128]{3,2,1,0:T(8,128)}) fusion(bf16[16,64,8,128]{3,2,1,0:T(8,128)(2,1)S(1)} %bitcast.85, bf16[16,128,1024]{2,1,0:T(8,128)(2,1)S(1)} %copy-done.6), kind=kOutput, calls=%fused_computation.21 | convolution fusion | flops 270524416 | bytes 10518528 | tf_op jit(solution)/shard_map/bihd,bjhd->bhij/dot_general | solution.py:180
  130.8 0.1 stack.17
  130.9 9.0 %fusion.7 = (f32[16,8,64]{2,1,0:T(8,128)S(1)}, f32[16,8,64]{2,1,0:T(8,128)S(1)}, f32[16,8,64,128]{3,2,1,0:T(8,128)}) fusion(f32[16,8,64,128]{3,2,1,0:T(8,128)} %get-tuple-element.30, f32[16,8,64]{2,1,0:T(8,128)S(1)} %get-tuple-element.29, bf16[16,64,8,128]{3,2,1,0:T(8,128)(2,1)} %bitcast.84, bf16[16,128,1024]{2,1,0:T(8,128)(2,1)} %gather_fusion.3), kind=kOutput, calls=%fused_computation.17 | convolution fusion | flops 273661952 | bytes 14778368 | tf_op jit(solution)/shard_map/bihd,bjhd->bhij/dot_general | solution.py:183
  139.9 0.1 stack.18
  140.0 0.1 stack.19
  140.1 0.7 pad_maximum_fusion
  140.8 3.6 %all-to-all-start.2 = ((f32[16,3,512]{2,1,0:T(4,128)}), f32[16,3,512]{2,1,0:T(4,128)S(1)}, u32[]{:S(2)}, u32[]{:S(2)}) async-start(f32[16,3,512]{2,1,0:T(4,128)} %pad_maximum_fusion), calls=%async_computation.2 | async-start | bytes 262144 | tf_op jit(solution)/shard_map/all_to_all | solution.py:191
  144.5 7.3 %all-to-all-done.2 = f32[16,3,512]{2,1,0:T(4,128)S(1)} async-done(((f32[16,3,512]{2,1,0:T(4,128)}), f32[16,3,512]{2,1,0:T(4,128)S(1)}, u32[]{:S(2)}, u32[]{:S(2)}) %all-to-all-start.2) | async-done | bytes 98336 | tf_op jit(solution)/shard_map/all_to_all | solution.py:191
  151.8 0.6 gather_fusion.4
  152.4 0.1 fusion.28
  152.6 0.1 fusion.16
  152.8 0.6 gather_fusion.5
  153.4 9.3 %all_to_all.28 = f32[16,2,512]{2,1,0:T(2,128)S(1)} all-to-all(f32[16,2,512]{2,1,0:T(2,128)S(1)} %gather_fusion.5), channel_id=1, replica_groups=mesh['seq'=8,'mp'=4] {'seq'}, dimensions={0} | all-to-all | bytes 131072 | tf_op jit(solution)/shard_map/all_to_all | solution.py:203
  162.7 0.2 slice_reduce_fusion.1
  163.0 6.6 %fusion.8 = (bf16[16,8,64,128]{3,2,1,0:T(8,128)(2,1)}, bf16[16,8,64,128]{3,2,1,0:T(8,128)(2,1)S(1)}) fusion(f32[16,8,64,128]{3,2,1,0:T(8,128)} %get-tuple-element.30, f32[16,8,64]{2,1,0:T(8,128)S(1)} %sub.52, f32[16,8,64,128]{3,2,1,0:T(8,128)} %get-tuple-element.31, f32[16,8,64]{2,1,0:T(8,128)S(1)} %sub.55), kind=kLoop, calls=%fused_computation.18 | loop fusion | flops 7340032 | bytes 12648448 | tf_op jit(solution)/shard_map/convert_element_type | solution.py:211
  169.6 1.2 convert_bitcast_fusion
  170.8 0.1 copy-done.1
  170.9 1.9 copy.94
  172.8 4.3 %all-to-all-start.4 = ((bf16[16,64,1024]{2,1,0:T(8,128)(2,1)}), bf16[16,64,1024]{2,1,0:T(8,128)(2,1)}, u32[]{:S(2)}, u32[]{:S(2)}) async-start(bf16[16,64,1024]{2,1,0:T(8,128)(2,1)} %bitcast.86), calls=%async_computation.4 | async-start | bytes 4194304 | tf_op jit(solution)/shard_map/all_to_all | solution.py:215
  177.2 1.6 copy-done.2
  178.8 1.6 copy-done.3
  180.4 14.7 %shard_map.78 = (bf16[8,128,1024]{2,1,0:T(8,128)(2,1)}, bf16[8,128,1024]{2,1,0:T(8,128)(2,1)}) custom-call(s32[16]{0:T(128)S(1)} %all_to_all.22.rows_ref, bf16[16,8,64,128]{3,2,1,0:T(8,128)(2,1)S(1)} %copy-done.3, bf16[16,8,64,128]{3,2,1,0:T(8,128)(2,1)S(1)} %copy-done.2, bf16[16,2,64,1024]{3,2,1,0:T(8,128)(2,1)} %all-to-all-done.1.pair_ref), custom_call_target="tpu_custom_call" | custom-call | tf_op jit(solution)/shard_map/pallas_call | solution.py:74
  195.1 28.7 %all-to-all-done.4.back_ref = bf16[16,64,1024]{2,1,0:T(8,128)(2,1)} async-done(((bf16[16,64,1024]{2,1,0:T(8,128)(2,1)}), bf16[16,64,1024]{2,1,0:T(8,128)(2,1)}, u32[]{:S(2)}, u32[]{:S(2)}) %all-to-all-start.4) | async-done | bytes 2097184 | tf_op jit(solution)/shard_map/all_to_all | solution.py:215
  223.8 3.4 %shard_map.77 = bf16[8,64,1024]{2,1,0:T(8,128)(2,1)} custom-call(s32[16]{0:T(128)S(1)} %get-tuple-element.15.target_ref, bf16[16,64,1024]{2,1,0:T(8,128)(2,1)} %all-to-all-done.4.back_ref), custom_call_target="tpu_custom_call" | custom-call | tf_op jit(solution)/shard_map/pallas_call | solution.py:133
  (31 shorter events, 0.4 us)
Async XLA Ops:
  0.6 28.0 %copy-start = (bf16[8,128,1024]{2,1,0:T(8,128)(2,1)S(1)}, bf16[8,128,1024]{2,1,0:T(8,128)(2,1)}, u32[]{:S(2)}) copy-start(bf16[8,128,1024]{2,1,0:T(8,128)(2,1)} %param.7) | copy-start | bytes 6291460
  8.9 12.7 %all-to-all-start = ((s32[8,2,1]{1,2,0:T(1,128)}), s32[8,2,1]{1,2,0:T(1,128)S(1)}, u32[]{:S(2)}, u32[]{:S(2)}) async-start(s32[8,2,1]{1,2,0:T(1,128)} %bitcast.3), calls=%async_computation | async-start | bytes 8192 | tf_op jit(solution)/shard_map/all_to_all | solution.py:171
  15.9 1.2 copy-start.4
  17.2 1.2 copy-start.5
  21.6 98.8 %all-to-all-start.1 = ((bf16[16,2,64,1024]{3,2,1,0:T(8,128)(2,1)}), bf16[16,2,64,1024]{3,2,1,0:T(8,128)(2,1)}, u32[]{:S(2)}, u32[]{:S(2)}) async-start(bf16[16,2,64,1024]{3,2,1,0:T(8,128)(2,1)} %shard_map.76), calls=%async_computation.1 | async-start | bytes 8388608 | tf_op jit(solution)/shard_map/all_to_all | solution.py:170
  123.2 2.6 %copy-start.6 = (bf16[16,128,1024]{2,1,0:T(8,128)(2,1)S(1)}, bf16[16,128,1024]{2,1,0:T(8,128)(2,1)}, u32[]{:S(2)}) copy-start(bf16[16,128,1024]{2,1,0:T(8,128)(2,1)} %gather_fusion.1) | copy-start | bytes 12582916
  140.8 11.0 %all-to-all-start.2 = ((f32[16,3,512]{2,1,0:T(4,128)}), f32[16,3,512]{2,1,0:T(4,128)S(1)}, u32[]{:S(2)}, u32[]{:S(2)}) async-start(f32[16,3,512]{2,1,0:T(4,128)} %pad_maximum_fusion), calls=%async_computation.2 | async-start | bytes 262144 | tf_op jit(solution)/shard_map/all_to_all | solution.py:191
  163.0 6.6 %copy-start.7 = (bf16[16,128,1024]{2,1,0:T(8,128)(2,1)S(1)}, bf16[16,128,1024]{2,1,0:T(8,128)(2,1)}, u32[]{:S(2)}) copy-start(bf16[16,128,1024]{2,1,0:T(8,128)(2,1)} %gather_fusion.1) | copy-start | bytes 12582916
  169.6 1.3 copy-start.1
  172.8 51.0 %all-to-all-start.4 = ((bf16[16,64,1024]{2,1,0:T(8,128)(2,1)}), bf16[16,64,1024]{2,1,0:T(8,128)(2,1)}, u32[]{:S(2)}, u32[]{:S(2)}) async-start(bf16[16,64,1024]{2,1,0:T(8,128)(2,1)} %bitcast.86), calls=%async_computation.4 | async-start | bytes 4194304 | tf_op jit(solution)/shard_map/all_to_all | solution.py:215
  177.2 1.6 copy-start.2
  178.8 1.6 copy-start.3

commit v12 on v11

--- a/solution.py
+++ b/solution.py
@@ -34,11 +34,11 @@
         for h in range(heads):
             cols = pl.ds(h * HEAD, HEAD)
             value_part = lax.dot_general(
-                probs_ref[0, h], pair_ref[0, 1, :, cols], TRANS_A,
+                probs_ref[0, h], pair_ref[0, 1, h], TRANS_A,
                 preferred_element_type=jnp.float32,
             )
             key_part = lax.dot_general(
-                grads_ref[0, h], pair_ref[0, 0, :, cols], TRANS_A,
+                grads_ref[0, h], pair_ref[0, 0, h], TRANS_A,
                 preferred_element_type=jnp.float32,
             )
             value_acc[here, :, cols] += value_part
@@ -52,7 +52,7 @@
 
 def kv_grads(row_recv, probs_low, grad_s, pair_recv, rows_here):
     slot_total, heads, span_len, nlen = probs_low.shape
-    width = pair_recv.shape[-1]
+    width = heads * HEAD
     out_shape = jax.ShapeDtypeStruct((rows_here, nlen, width), jnp.bfloat16)
     grid_spec = pltpu.PrefetchScalarGridSpec(
         num_scalar_prefetch=1,
@@ -60,7 +60,7 @@
         in_specs=[
             pl.BlockSpec((1, heads, span_len, nlen), lambda t, rows: (t, 0, 0, 0)),
             pl.BlockSpec((1, heads, span_len, nlen), lambda t, rows: (t, 0, 0, 0)),
-            pl.BlockSpec((1, 2, span_len, width), lambda t, rows: (t, 0, 0, 0)),
+            pl.BlockSpec((1, 2, heads, span_len, HEAD), lambda t, rows: (t, 0, 0, 0, 0)),
         ],
         out_specs=[
             pl.BlockSpec((rows_here, nlen, width), lambda t, rows: (0, 0, 0)),
@@ -82,10 +82,14 @@
 
 
 def pair_kernel(span_ref, query_ref, grad_ref, pair_out):
+    heads = pair_out.shape[2]
+
     def body(t, carry):
         source = span_ref[t]
-        pair_out[t, 0] = query_ref[source]
-        pair_out[t, 1] = grad_ref[source]
+        for h in range(heads):
+            cols = pl.ds(h * HEAD, HEAD)
+            pair_out[t, 0, h] = query_ref[source, :, cols]
+            pair_out[t, 1, h] = grad_ref[source, :, cols]
         return carry
 
     lax.fori_loop(0, pair_out.shape[0], body, 0)
@@ -94,6 +98,8 @@
 def gather_pairs(slot_span, queries, out_grad):
     span_count, span_len, width = queries.shape
     slot_total = slot_span.shape[0]
+    heads = width // HEAD
+    pair_shape = (slot_total, 2, heads, span_len, HEAD)
     grid_spec = pltpu.PrefetchScalarGridSpec(
         num_scalar_prefetch=1,
         grid=(1,),
@@ -101,33 +107,39 @@
             pl.BlockSpec((span_count, span_len, width), lambda i, spans: (0, 0, 0)),
             pl.BlockSpec((span_count, span_len, width), lambda i, spans: (0, 0, 0)),
         ],
-        out_specs=pl.BlockSpec((slot_total, 2, span_len, width), lambda i, spans: (0, 0, 0, 0)),
+        out_specs=pl.BlockSpec(pair_shape, lambda i, spans: (0, 0, 0, 0, 0)),
     )
     return pl.pallas_call(
         pair_kernel,
         grid_spec=grid_spec,
-        out_shape=jax.ShapeDtypeStruct((slot_total, 2, span_len, width), queries.dtype),
+        out_shape=jax.ShapeDtypeStruct(pair_shape, queries.dtype),
         compiler_params=pltpu.CompilerParams(vmem_limit_bytes=48 * 1024 * 1024),
     )(jnp.clip(slot_span, 0, span_count - 1), queries, out_grad)
 
 
 def sum_kernel(target_ref, back_ref, query_out):
+    heads = back_ref.shape[1]
+
     def body(c, carry):
-        first = back_ref[target_ref[c * NBR]].astype(jnp.float32)
-        second = back_ref[target_ref[c * NBR + 1]].astype(jnp.float32)
-        query_out[c] = (first + second).astype(query_out.dtype)
+        first_slot = target_ref[c * NBR]
+        second_slot = target_ref[c * NBR + 1]
+        for h in range(heads):
+            first = back_ref[first_slot, h].astype(jnp.float32)
+            second = back_ref[second_slot, h].astype(jnp.float32)
+            query_out[c, :, pl.ds(h * HEAD, HEAD)] = (first + second).astype(query_out.dtype)
         return carry
 
     lax.fori_loop(0, query_out.shape[0], body, 0)
 
 
 def sum_parts(target, query_back):
-    slot_total, span_len, width = query_back.shape
+    slot_total, heads, span_len, _ = query_back.shape
+    width = heads * HEAD
     span_count = target.shape[0] // NBR
     grid_spec = pltpu.PrefetchScalarGridSpec(
         num_scalar_prefetch=1,
         grid=(1,),
-        in_specs=[pl.BlockSpec((slot_total, span_len, width), lambda i, tgt: (0, 0, 0))],
+        in_specs=[pl.BlockSpec(query_back.shape, lambda i, tgt: (0, 0, 0, 0))],
         out_specs=pl.BlockSpec((span_count, span_len, width), lambda i, tgt: (0, 0, 0)),
     )
     return pl.pallas_call(
@@ -171,17 +183,17 @@
     row_recv = lax.all_to_all(row_send, "seq", split_axis=0, concat_axis=0, tiled=True)
 
     row_index = jnp.clip(row_recv, 0, rows_here - 1)
-    query_heads = split_heads(pair_recv[:, 0])
-    grad_heads = split_heads(pair_recv[:, 1])
-    key_heads = split_heads(row_keys[row_index])
-    value_heads = split_heads(row_values[row_index])
+    query_heads = pair_recv[:, 0]
+    grad_heads = pair_recv[:, 1]
+    key_heads = jnp.swapaxes(split_heads(row_keys), 1, 2)[row_index]
+    value_heads = jnp.swapaxes(split_heads(row_values), 1, 2)[row_index]
 
     scores = (
-        jnp.einsum("bihd,bjhd->bhij", query_heads, key_heads, preferred_element_type=jnp.float32)
+        jnp.einsum("bhid,bhjd->bhij", query_heads, key_heads, preferred_element_type=jnp.float32)
         * score_scale
     )
     grad_p = jnp.einsum(
-        "bihd,bjhd->bhij", grad_heads, value_heads, preferred_element_type=jnp.float32
+        "bhid,bhjd->bhij", grad_heads, value_heads, preferred_element_type=jnp.float32
     )
     highest = jnp.max(scores, axis=3)
     expons = jnp.exp(scores - highest[..., None])
@@ -210,8 +222,8 @@
     grad_s = (softmax_p * (grad_p - delta_here[..., None]) * score_scale).astype(jnp.bfloat16)
     probs_low = softmax_p.astype(jnp.bfloat16)
     query_part = jnp.einsum(
-        "bhij,bjhd->bihd", grad_s, key_heads, preferred_element_type=jnp.float32
-    ).astype(jnp.bfloat16).reshape(slot_total, SPAN, width_here)
+        "bhij,bhjd->bhid", grad_s, key_heads, preferred_element_type=jnp.float32
+    ).astype(jnp.bfloat16)
     query_back = lax.all_to_all(query_part, "seq", split_axis=0, concat_axis=0, tiled=True)
 
     key_grad, value_grad = kv_grads(row_recv, probs_low, grad_s, pair_recv, rows_here)

time: 228 us -> 226 us (level)
  waiting for transfers between devices: 121 us -> 108 us
  local copies, waits for them, and re-layouts: 24.8 us -> 29.7 us
  matrix products: 15.2 us -> 19.3 us
    all_to_all x1, waiting for transfers between devices: 84.7 us -> 70.9 us  [per_device(): lax.all_to_all(pair_send, 'seq', split_axis=0, concat_axis=0, tiled=True)]
    reshape x1 -> x2, local copies, waits for them, and re-layouts: 1.92 us -> 6.94 us  [split_heads(): return tensor.reshape(tensor.shape[:-1] + (tensor.shape[-1] // HEAD, HEAD))]
    dot_general x3, matrix products: 15.2 us -> 19.3 us  [the longest x1 8.99 us: per_device(): jnp.einsum('bhid,bhjd->bhij', grad_heads, value_heads, preferred_element_...]
    slice x1 -> x0, local copies, waits for them, and re-layouts: 2.72 us -> none  [per_device(): query_heads = split_heads(pair_recv[:, 0])]
    unnamed x18 -> x12, local copies, waits for them, and re-layouts: 8.32 us -> 10.3 us
  transfers between devices with their start and end apart: 4 -> 4, of which waited for: 4 -> 3; matrix products, arithmetic and copies ran while one was open for 4% -> 10% of each run, Pallas kernels for 8% -> 8%
where the time goes in v12:
time: 226 us; the launch traced here: 224 us
  waiting for transfers between devices  108 us (48%)
  local copies, waits for them, and re-layouts  29.7 us (13%)
  Pallas kernels  21.5 us (10%)
  starting transfers between devices  20.4 us (9%)
  matrix products  19.3 us (9%)
  blocking collectives  15.5 us (7%)
  other arithmetic  8.74 us (4%)
    all_to_all x1, waiting for transfers between devices, per_device(): lax.all_to_all(pair_send, 'seq', split_axis=0, concat_axis=0, tiled=True)  70.9 us
    all_to_all x1, waiting for transfers between devices, per_device(): lax.all_to_all(query_part, 'seq', split_axis=0, concat_axis=0, tiled=True)  30.3 us
    pallas_call x1, Pallas kernels, kv_grads(): pl.pallas_call(kv_kernel, grid_spec=grid_spec, out_shape=[out_shape, out_...  14.7 us
    unnamed x12, local copies, waits for them, and re-layouts  10.3 us
    all_to_all x1, blocking collectives, per_device(): lax.all_to_all(span_stats[slot_span], 'seq', split_axis=0, concat_axis=0,...  9.29 us
    dot_general x1, matrix products, per_device(): jnp.einsum('bhid,bhjd->bhij', grad_heads, value_heads, preferred_element_...  8.99 us
    dot_general x1, matrix products, per_device(): jnp.einsum('bhid,bhjd->bhij', query_heads, key_heads, preferred_element_t...  7.78 us
    all_to_all x1, waiting for transfers between devices, per_device(): back = lax.all_to_all(part, 'seq', split_axis=0, concat_axis=0, tiled=True)  7.32 us
  transfers between devices with their start and end apart: 4, of which 3 were waited for; matrix products, arithmetic and copies ran while one was open for 10% of the time, Pallas kernels for 8%

profile of v12, /device:TPU:0, one launch (start us, length us, event | category | flops | bytes accessed | tf_op | source)
XLA Modules:
  0.0 224.5 jit_solution(10135017411746246970)
XLA Ops:
  0.6 6.3 %all-gather = s32[4,2,2]{2,1,0:T(2,128)S(1)} all-gather(s32[1,2,2]{2,1,0:T(2,128)} %bitcast.65), channel_id=1, replica_groups=mesh['seq'=8,'mp'=4] {'mp'}, dimensions={0}, use_global_device_ids=true | all-gather | bytes 80 | tf_op jit(solution)/shard_map/all_gather | solution.py:155
  6.9 0.1 reshape.267
  7.0 0.2 convert_reduce_fusion
  7.2 0.1 fusion.9
  7.3 0.1 select_reduce_fusion
  7.4 0.7 gather_fusion.1
  8.1 0.7 select_n.100
  8.8 6.3 %all-to-all-start.1 = ((s32[8,2,1]{1,2,0:T(1,128)}), s32[8,2,1]{1,2,0:T(1,128)S(1)}, u32[]{:S(2)}, u32[]{:S(2)}) async-start(s32[8,2,1]{1,2,0:T(1,128)} %bitcast.6), calls=%async_computation.1 | async-start | bytes 8192 | tf_op jit(solution)/shard_map/all_to_all | solution.py:183
  15.1 0.7 gather_fusion
  15.8 1.2 copy-done.1
  17.0 1.2 copy-done.2
  18.2 3.3 %shard_map.76 = bf16[16,2,8,64,128]{4,3,2,1,0:T(8,128)(2,1)} custom-call(s32[16]{0:T(128)S(1)} %broadcast_clamp_fusion.1.span_ref, bf16[8,64,1024]{2,1,0:T(8,128)(2,1)S(1)} %copy-done.1, bf16[8,64,1024]{2,1,0:T(8,128)(2,1)S(1)} %copy-done.2), custom_call_target="tpu_custom_call" | custom-call | tf_op jit(solution)/shard_map/pallas_call | solution.py:112
  21.6 6.1 %all-to-all-start = ((bf16[16,2,8,64,128]{4,3,2,1,0:T(8,128)(2,1)}), bf16[16,2,8,64,128]{4,3,2,1,0:T(8,128)(2,1)}, u32[]{:S(2)}, u32[]{:S(2)}) async-start(bf16[16,2,8,64,128]{4,3,2,1,0:T(8,128)(2,1)} %shard_map.76), calls=%async_computation | async-start | bytes 8388608 | tf_op jit(solution)/shard_map/all_to_all | solution.py:182
  27.7 0.1 reshape.270
  27.8 2.4 %copy.26 = bf16[8,128,1024]{1,2,0:T(8,128)(2,1)} copy(bf16[8,128,1024]{2,1,0:T(8,128)(2,1)S(1)} %copy-done.4) | data formatting | bytes 4194304 | tf_op args[2]
  30.2 3.0 %copy.27 = bf16[8,128,8,128]{3,1,2,0:T(8,128)(2,1)S(1)} copy(bf16[8,128,8,128]{1,3,2,0:T(8,128)(2,1)} %bitcast.62) | data formatting | bytes 4194304 | tf_op jit(solution)/shard_map/reshape | solution.py:17
  33.2 3.9 %copy.29 = bf16[8,128,1024]{1,2,0:T(8,128)(2,1)} copy(bf16[8,128,1024]{2,1,0:T(8,128)(2,1)} %param.8) | data formatting | bytes 4194304 | tf_op args[3]
  37.1 3.9 %copy.30 = bf16[8,128,8,128]{3,1,2,0:T(8,128)(2,1)} copy(bf16[8,128,8,128]{1,3,2,0:T(8,128)(2,1)} %bitcast.63) | data formatting | bytes 4194304 | tf_op jit(solution)/shard_map/reshape | solution.py:17
  41.0 0.5 broadcast.289
  41.5 0.7 fusion.15
  42.2 0.1 min.22
  42.3 3.1 %gather_fusion.2 = bf16[16,8,128,128]{3,2,1,0:T(8,128)(2,1)} fusion(bf16[8,8,128,128]{3,2,1,0:T(8,128)(2,1)S(1)} %bitcast.60, s32[1024]{0:T(1024)S(1)} %pad_clamp_fusion.2), kind=kCustom, calls=%fused_computation.2 | custom fusion | bytes 8388672 | tf_op jit(solution)/shard_map/gather | solution.py:188
  45.4 4.6 %gather_fusion.3 = bf16[16,8,128,128]{3,2,1,0:T(8,128)(2,1)} fusion(bf16[8,8,128,128]{3,2,1,0:T(8,128)(2,1)} %bitcast.61, s32[1024]{0:T(1024)S(1)} %pad_clamp_fusion.2), kind=kCustom, calls=%fused_computation.3 | custom fusion | bytes 8388672 | tf_op jit(solution)/shard_map/gather | solution.py:189
  50.0 70.9 %all-to-all-done.pair_ref = bf16[16,2,8,64,128]{4,3,2,1,0:T(8,128)(2,1)} async-done(((bf16[16,2,8,64,128]{4,3,2,1,0:T(8,128)(2,1)}), bf16[16,2,8,64,128]{4,3,2,1,0:T(8,128)(2,1)}, u32[]{:S(2)}, u32[]{:S(2)}) %all-to-all-start) | async-done | bytes 4194336 | tf_op jit(solution)/shard_map/all_to_all | solution.py:182
  120.9 7.8 %multiply_reduce_fusion.1 = (f32[16,8,64]{2,1,0:T(8,128)S(1)}, f32[16,8,64,128]{3,2,1,0:T(8,128)}) fusion(bf16[16,8,128,128]{3,2,1,0:T(8,128)(2,1)} %gather_fusion.2, bf16[16,2,8,64,128]{4,3,2,1,0:T(8,128)(2,1)} %all-to-all-done.pair_ref), kind=kOutput, calls=%fused_computation.12 | convolution fusion | flops 270524416 | bytes 10518528 | tf_op jit(solution)/shard_map/bhid,bhjd->bhij/dot_general | solution.py:192
  128.7 0.1 stack.17
  128.8 9.0 %fusion = (f32[16,8,64]{2,1,0:T(8,128)S(1)}, f32[16,8,64]{2,1,0:T(8,128)S(1)}, f32[16,8,64,128]{3,2,1,0:T(8,128)}) fusion(f32[16,8,64,128]{3,2,1,0:T(8,128)} %get-tuple-element.28, f32[16,8,64]{2,1,0:T(8,128)S(1)} %get-tuple-element.27, bf16[16,8,128,128]{3,2,1,0:T(8,128)(2,1)} %gather_fusion.3, bf16[16,2,8,64,128]{4,3,2,1,0:T(8,128)(2,1)} %all-to-all-done.pair_ref), kind=kOutput, calls=%fused_computation.10 | convolution fusion | flops 273661952 | bytes 14778368 | tf_op jit(solution)/shard_map/bhid,bhjd->bhij/dot_general | solution.py:195
  137.8 0.1 stack.19
  137.9 0.1 stack.18
  138.0 0.7 pad_maximum_fusion
  138.7 3.6 %all-to-all-start.2 = ((f32[16,3,512]{2,1,0:T(4,128)}), f32[16,3,512]{2,1,0:T(4,128)S(1)}, u32[]{:S(2)}, u32[]{:S(2)}) async-start(f32[16,3,512]{2,1,0:T(4,128)} %pad_maximum_fusion), calls=%async_computation.2 | async-start | bytes 262144 | tf_op jit(solution)/shard_map/all_to_all | solution.py:203
  142.4 7.3 %all-to-all-done.2 = f32[16,3,512]{2,1,0:T(4,128)S(1)} async-done(((f32[16,3,512]{2,1,0:T(4,128)}), f32[16,3,512]{2,1,0:T(4,128)S(1)}, u32[]{:S(2)}, u32[]{:S(2)}) %all-to-all-start.2) | async-done | bytes 98336 | tf_op jit(solution)/shard_map/all_to_all | solution.py:203
  149.7 0.6 gather_fusion.4
  150.3 0.1 fusion.16
  150.4 0.1 fusion.5
  150.7 0.6 gather_fusion.5
  151.3 9.3 %all_to_all.28 = f32[16,2,512]{2,1,0:T(2,128)S(1)} all-to-all(f32[16,2,512]{2,1,0:T(2,128)S(1)} %gather_fusion.5), channel_id=1, replica_groups=mesh['seq'=8,'mp'=4] {'seq'}, dimensions={0} | all-to-all | bytes 131072 | tf_op jit(solution)/shard_map/all_to_all | solution.py:215
  160.6 0.2 slice_reduce_fusion.1
  160.8 0.1 sub.52
  160.8 0.1 sub.55
  160.9 6.6 %fusion.1 = (bf16[16,8,64,128]{3,2,1,0:T(8,128)(2,1)}, bf16[16,8,64,128]{3,2,1,0:T(8,128)(2,1)S(1)}) fusion(f32[16,8,64,128]{3,2,1,0:T(8,128)} %get-tuple-element.28, f32[16,8,64]{2,1,0:T(8,128)S(1)} %sub.52, f32[16,8,64,128]{3,2,1,0:T(8,128)} %get-tuple-element.29, f32[16,8,64]{2,1,0:T(8,128)S(1)} %sub.55), kind=kLoop, calls=%fused_computation.11 | loop fusion | flops 7340032 | bytes 12648448 | tf_op jit(solution)/shard_map/convert_element_type | solution.py:223
  167.5 2.6 %convolution_convert_fusion = bf16[16,8,64,128]{3,2,1,0:T(8,128)(2,1)} fusion(bf16[16,8,64,128]{3,2,1,0:T(8,128)(2,1)S(1)} %get-tuple-element.18.grads_ref, bf16[16,8,128,128]{3,2,1,0:T(8,128)(2,1)S(1)} %copy-done.3), kind=kOutput, calls=%fused_computation.17 | convolution fusion | flops 269484032 | bytes 8388608 | tf_op jit(solution)/shard_map/bhij,bhjd->bhid/dot_general | solution.py:224
  170.0 4.3 %all-to-all-start.4 = ((bf16[16,8,64,128]{3,2,1,0:T(8,128)(2,1)}), bf16[16,8,64,128]{3,2,1,0:T(8,128)(2,1)}, u32[]{:S(2)}, u32[]{:S(2)}) async-start(bf16[16,8,64,128]{3,2,1,0:T(8,128)(2,1)} %convolution_convert_fusion), calls=%async_computation.4 | async-start | bytes 4194304 | tf_op jit(solution)/shard_map/all_to_all | solution.py:227
  174.4 0.1 all_to_all.22.rows_ref
  174.5 1.6 copy-done
  176.1 14.7 %shard_map.78 = (bf16[8,128,1024]{2,1,0:T(8,128)(2,1)}, bf16[8,128,1024]{2,1,0:T(8,128)(2,1)}) custom-call(s32[16]{0:T(128)S(1)} %all_to_all.22.rows_ref, bf16[16,8,64,128]{3,2,1,0:T(8,128)(2,1)S(1)} %copy-done, bf16[16,8,64,128]{3,2,1,0:T(8,128)(2,1)S(1)} %get-tuple-element.18.grads_ref, bf16[16,2,8,64,128]{4,3,2,1,0:T(8,128)(2,1)} %all-to-all-done.pair_ref), custom_call_target="tpu_custom_call" | custom-call | tf_op jit(solution)/shard_map/pallas_call | solution.py:74
  190.8 30.3 %all-to-all-done.4.back_ref = bf16[16,8,64,128]{3,2,1,0:T(8,128)(2,1)} async-done(((bf16[16,8,64,128]{3,2,1,0:T(8,128)(2,1)}), bf16[16,8,64,128]{3,2,1,0:T(8,128)(2,1)}, u32[]{:S(2)}, u32[]{:S(2)}) %all-to-all-start.4) | async-done | bytes 2097184 | tf_op jit(solution)/shard_map/all_to_all | solution.py:227
  221.1 3.4 %shard_map.77 = bf16[8,64,1024]{2,1,0:T(8,128)(2,1)} custom-call(s32[16]{0:T(128)S(1)} %get-tuple-element.15.target_ref, bf16[16,8,64,128]{3,2,1,0:T(8,128)(2,1)} %all-to-all-done.4.back_ref), custom_call_target="tpu_custom_call" | custom-call | tf_op jit(solution)/shard_map/pallas_call | solution.py:145
  (25 shorter events, 0.2 us)
Async XLA Ops:
  8.8 12.8 %all-to-all-start.1 = ((s32[8,2,1]{1,2,0:T(1,128)}), s32[8,2,1]{1,2,0:T(1,128)S(1)}, u32[]{:S(2)}, u32[]{:S(2)}) async-start(s32[8,2,1]{1,2,0:T(1,128)} %bitcast.6), calls=%async_computation.1 | async-start | bytes 8192 | tf_op jit(solution)/shard_map/all_to_all | solution.py:183
  15.8 1.2 copy-start.1
  17.0 1.2 copy-start.2
  21.6 6.2 %copy-start.4 = (bf16[8,128,1024]{2,1,0:T(8,128)(2,1)S(1)}, bf16[8,128,1024]{2,1,0:T(8,128)(2,1)}, u32[]{:S(2)}) copy-start(bf16[8,128,1024]{2,1,0:T(8,128)(2,1)} %param.7) | copy-start | bytes 6291460
  21.6 99.3 %all-to-all-start = ((bf16[16,2,8,64,128]{4,3,2,1,0:T(8,128)(2,1)}), bf16[16,2,8,64,128]{4,3,2,1,0:T(8,128)(2,1)}, u32[]{:S(2)}, u32[]{:S(2)}) async-start(bf16[16,2,8,64,128]{4,3,2,1,0:T(8,128)(2,1)} %shard_map.76), calls=%async_computation | async-start | bytes 8388608 | tf_op jit(solution)/shard_map/all_to_all | solution.py:182
  138.7 11.0 %all-to-all-start.2 = ((f32[16,3,512]{2,1,0:T(4,128)}), f32[16,3,512]{2,1,0:T(4,128)S(1)}, u32[]{:S(2)}, u32[]{:S(2)}) async-start(f32[16,3,512]{2,1,0:T(4,128)} %pad_maximum_fusion), calls=%async_computation.2 | async-start | bytes 262144 | tf_op jit(solution)/shard_map/all_to_all | solution.py:203
  160.9 6.6 %copy-start.3 = (bf16[16,8,128,128]{3,2,1,0:T(8,128)(2,1)S(1)}, bf16[16,8,128,128]{3,2,1,0:T(8,128)(2,1)}, u32[]{:S(2)}) copy-start(bf16[16,8,128,128]{3,2,1,0:T(8,128)(2,1)} %gather_fusion.2) | copy-start | bytes 12582916
  170.0 51.0 %all-to-all-start.4 = ((bf16[16,8,64,128]{3,2,1,0:T(8,128)(2,1)}), bf16[16,8,64,128]{3,2,1,0:T(8,128)(2,1)}, u32[]{:S(2)}, u32[]{:S(2)}) async-start(bf16[16,8,64,128]{3,2,1,0:T(8,128)(2,1)} %convolution_convert_fusion), calls=%async_computation.4 | async-start | bytes 4194304 | tf_op jit(solution)/shard_map/all_to_all | solution.py:227
  174.5 1.6 copy-start

commit v13 on v12

--- a/solution.py
+++ b/solution.py
@@ -148,6 +148,24 @@
         out_shape=jax.ShapeDtypeStruct((span_count, span_len, width), query_back.dtype),
         compiler_params=pltpu.CompilerParams(vmem_limit_bytes=48 * 1024 * 1024),
     )(jnp.clip(target, 0, slot_total - 1), query_back)
+
+
+def seq_exchange(blocks, seq_count):
+    me = lax.axis_index("seq")
+    result = jnp.zeros_like(blocks)
+    result = lax.dynamic_update_index_in_dim(
+        result, lax.dynamic_index_in_dim(blocks, me, keepdims=False), me, axis=0
+    )
+    for shift in range(1, seq_count):
+        sent = lax.ppermute(
+            lax.dynamic_index_in_dim(blocks, (me + shift) % seq_count, keepdims=False),
+            "seq",
+            perm=[(i, (i + shift) % seq_count) for i in range(seq_count)],
+        )
+        result = lax.dynamic_update_index_in_dim(
+            result, sent, (me - shift) % seq_count, axis=0
+        )
+    return result
 
 
 def per_device(queries, out_grad, row_keys, row_values, neighbours):
@@ -224,7 +242,12 @@
     query_part = jnp.einsum(
         "bhij,bhjd->bhid", grad_s, key_heads, preferred_element_type=jnp.float32
     ).astype(jnp.bfloat16)
-    query_back = lax.all_to_all(query_part, "seq", split_axis=0, concat_axis=0, tiled=True)
+    if seq_count <= 8:
+        query_back = seq_exchange(
+            query_part.reshape((seq_count, slot_depth) + query_part.shape[1:]), seq_count
+        ).reshape(query_part.shape)
+    else:
+        query_back = lax.all_to_all(query_part, "seq", split_axis=0, concat_axis=0, tiled=True)
 
     key_grad, value_grad = kv_grads(row_recv, probs_low, grad_s, pair_recv, rows_here)
 

time: 226 us -> 224 us (level); the launches traced: 224 us -> 219 us
  waiting for transfers between devices: 108 us -> 94.1 us
  local copies, waits for them, and re-layouts: 29.7 us -> 40.1 us
  starting transfers between devices: 20.4 us -> 29.8 us
  blocking collectives: 15.5 us -> 6.25 us
    all_to_all x1, waiting for transfers between devices: 30.3 us -> 6.56 us  [per_device(): lax.all_to_all(span_stats[slot_span], 'seq', split_axis=0, concat_axis=0,...]
    ppermute x0 -> x7, starting transfers between devices: none -> 10.2 us  [seq_exchange(): lax.ppermute(lax.dynamic_index_in_dim(blocks, (me + shift) % seq_count, k...]
    ppermute x0 -> x7, waiting for transfers between devices: none -> 9.38 us  [seq_exchange(): lax.ppermute(lax.dynamic_index_in_dim(blocks, (me + shift) % seq_count, k...]
    all_to_all x1 -> x0, blocking collectives: 9.29 us -> none  [per_device(): lax.all_to_all(span_stats[slot_span], 'seq', split_axis=0, concat_axis=0,...]
    dynamic_update_slice x0 -> x7, local copies, waits for them, and re-layouts: none -> 7 us  [seq_exchange(): lax.dynamic_update_index_in_dim(result, sent, (me - shift) % seq_count, a...]
  transfers between devices with their start and end apart: 4 -> 11, of which waited for: 3 -> 5; matrix products, arithmetic and copies ran while one was open for 10% -> 13% of each run, Pallas kernels for 8% -> 8%
where the time goes in v13:
time: 224 us; the launch traced here: 219 us
  waiting for transfers between devices  94.1 us (42%)
  local copies, waits for them, and re-layouts  40.1 us (18%)
  starting transfers between devices  29.8 us (13%)
  Pallas kernels  21.5 us (10%)
  matrix products  18 us (8%)
  other arithmetic  8.74 us (4%)
  blocking collectives  6.25 us (3%)
    all_to_all x1, waiting for transfers between devices, per_device(): lax.all_to_all(pair_send, 'seq', split_axis=0, concat_axis=0, tiled=True)  70.9 us
    pallas_call x1, Pallas kernels, kv_grads(): pl.pallas_call(kv_kernel, grid_spec=grid_spec, out_shape=[out_shape, out_...  14.7 us
    unnamed x12, local copies, waits for them, and re-layouts  10.3 us
    ppermute x7, starting transfers between devices, seq_exchange(): lax.ppermute(lax.dynamic_index_in_dim(blocks, (me + shift) % seq_count, k...  10.2 us
    ppermute x7, waiting for transfers between devices, seq_exchange(): lax.ppermute(lax.dynamic_index_in_dim(blocks, (me + shift) % seq_count, k...  9.38 us
    dot_general x1, matrix products, per_device(): jnp.einsum('bhid,bhjd->bhij', grad_heads, value_heads, preferred_element_...  8.99 us
    dot_general x1, matrix products, per_device(): jnp.einsum('bhid,bhjd->bhij', query_heads, key_heads, preferred_element_t...  7.78 us
    all_to_all x1, waiting for transfers between devices, per_device(): back = lax.all_to_all(part, 'seq', split_axis=0, concat_axis=0, tiled=True)  7.32 us
  transfers between devices with their start and end apart: 11, of which 5 were waited for; matrix products, arithmetic and copies ran while one was open for 13% of the time, Pallas kernels for 8%

profile of v13, /device:TPU:0, one launch (start us, length us, event | category | flops | bytes accessed | tf_op | source)
XLA Modules:
  0.0 219.5 jit_solution(15128417024061758403)
XLA Ops:
  0.6 6.3 %all-gather = s32[4,2,2]{2,1,0:T(2,128)S(1)} all-gather(s32[1,2,2]{2,1,0:T(2,128)} %bitcast.96), channel_id=1, replica_groups=mesh['seq'=8,'mp'=4] {'mp'}, dimensions={0}, use_global_device_ids=true | all-gather | bytes 80 | tf_op jit(solution)/shard_map/all_gather | solution.py:173
  7.4 0.7 gather_fusion.1
  8.1 0.7 select_n.206
  8.8 6.3 %all-to-all-start.1 = ((s32[8,2,1]{1,2,0:T(1,128)}), s32[8,2,1]{1,2,0:T(1,128)S(1)}, u32[]{:S(2)}, u32[]{:S(2)}) async-start(s32[8,2,1]{1,2,0:T(1,128)} %bitcast.6), calls=%async_computation.1 | async-start | bytes 8192 | tf_op jit(solution)/shard_map/all_to_all | solution.py:201
  15.1 0.7 gather_fusion
  15.8 1.2 copy-done.1
  17.0 1.2 copy-done.2
  18.2 3.3 %shard_map.76 = bf16[16,2,8,64,128]{4,3,2,1,0:T(8,128)(2,1)} custom-call(s32[16]{0:T(128)S(1)} %broadcast_clamp_fusion.1.span_ref, bf16[8,64,1024]{2,1,0:T(8,128)(2,1)S(1)} %copy-done.1, bf16[8,64,1024]{2,1,0:T(8,128)(2,1)S(1)} %copy-done.2), custom_call_target="tpu_custom_call" | custom-call | tf_op jit(solution)/shard_map/pallas_call | solution.py:112
  21.6 6.1 %all-to-all-start = ((bf16[16,2,8,64,128]{4,3,2,1,0:T(8,128)(2,1)}), bf16[16,2,8,64,128]{4,3,2,1,0:T(8,128)(2,1)}, u32[]{:S(2)}, u32[]{:S(2)}) async-start(bf16[16,2,8,64,128]{4,3,2,1,0:T(8,128)(2,1)} %shard_map.76), calls=%async_computation | async-start | bytes 8388608 | tf_op jit(solution)/shard_map/all_to_all | solution.py:200
  27.8 2.4 %copy.26 = bf16[8,128,1024]{1,2,0:T(8,128)(2,1)} copy(bf16[8,128,1024]{2,1,0:T(8,128)(2,1)S(1)} %copy-done.4) | data formatting | bytes 4194304 | tf_op args[2]
  30.1 3.0 %copy.27 = bf16[8,128,8,128]{3,1,2,0:T(8,128)(2,1)S(1)} copy(bf16[8,128,8,128]{1,3,2,0:T(8,128)(2,1)} %bitcast.93) | data formatting | bytes 4194304 | tf_op jit(solution)/shard_map/reshape | solution.py:17
  33.2 3.9 %copy.29 = bf16[8,128,1024]{1,2,0:T(8,128)(2,1)} copy(bf16[8,128,1024]{2,1,0:T(8,128)(2,1)} %param.8) | data formatting | bytes 4194304 | tf_op args[3]
  37.1 3.9 %copy.30 = bf16[8,128,8,128]{3,1,2,0:T(8,128)(2,1)} copy(bf16[8,128,8,128]{1,3,2,0:T(8,128)(2,1)} %bitcast.94) | data formatting | bytes 4194304 | tf_op jit(solution)/shard_map/reshape | solution.py:17
  41.0 0.5 broadcast.313
  41.5 0.7 fusion.15
  42.3 3.1 %gather_fusion.2 = bf16[16,8,128,128]{3,2,1,0:T(8,128)(2,1)} fusion(bf16[8,8,128,128]{3,2,1,0:T(8,128)(2,1)S(1)} %bitcast.90, s32[1024]{0:T(1024)S(1)} %pad_clamp_fusion.2), kind=kCustom, calls=%fused_computation.2 | custom fusion | bytes 8388672 | tf_op jit(solution)/shard_map/gather | solution.py:206
  45.4 4.6 %gather_fusion.3 = bf16[16,8,128,128]{3,2,1,0:T(8,128)(2,1)} fusion(bf16[8,8,128,128]{3,2,1,0:T(8,128)(2,1)} %bitcast.91, s32[1024]{0:T(1024)S(1)} %pad_clamp_fusion.2), kind=kCustom, calls=%fused_computation.3 | custom fusion | bytes 8388672 | tf_op jit(solution)/shard_map/gather | solution.py:207
  50.0 70.9 %all-to-all-done.pair_ref = bf16[16,2,8,64,128]{4,3,2,1,0:T(8,128)(2,1)} async-done(((bf16[16,2,8,64,128]{4,3,2,1,0:T(8,128)(2,1)}), bf16[16,2,8,64,128]{4,3,2,1,0:T(8,128)(2,1)}, u32[]{:S(2)}, u32[]{:S(2)}) %all-to-all-start) | async-done | bytes 4194336 | tf_op jit(solution)/shard_map/all_to_all | solution.py:200
  120.9 7.8 %multiply_reduce_fusion.1 = (f32[16,8,64]{2,1,0:T(8,128)S(1)}, f32[16,8,64,128]{3,2,1,0:T(8,128)}) fusion(bf16[16,8,128,128]{3,2,1,0:T(8,128)(2,1)} %gather_fusion.2, bf16[16,2,8,64,128]{4,3,2,1,0:T(8,128)(2,1)} %all-to-all-done.pair_ref), kind=kOutput, calls=%fused_computation.12 | convolution fusion | flops 270524416 | bytes 10518528 | tf_op jit(solution)/shard_map/bhid,bhjd->bhij/dot_general | solution.py:210
  128.8 9.0 %fusion = (f32[16,8,64]{2,1,0:T(8,128)S(1)}, f32[16,8,64]{2,1,0:T(8,128)S(1)}, f32[16,8,64,128]{3,2,1,0:T(8,128)}) fusion(f32[16,8,64,128]{3,2,1,0:T(8,128)} %get-tuple-element.36, f32[16,8,64]{2,1,0:T(8,128)S(1)} %get-tuple-element.35, bf16[16,8,128,128]{3,2,1,0:T(8,128)(2,1)} %gather_fusion.3, bf16[16,2,8,64,128]{4,3,2,1,0:T(8,128)(2,1)} %all-to-all-done.pair_ref), kind=kOutput, calls=%fused_computation.10 | convolution fusion | flops 273661952 | bytes 14778368 | tf_op jit(solution)/shard_map/bhid,bhjd->bhij/dot_general | solution.py:213
  138.0 0.7 pad_maximum_fusion
  138.7 3.6 %all-to-all-start.2 = ((f32[16,3,512]{2,1,0:T(4,128)}), f32[16,3,512]{2,1,0:T(4,128)S(1)}, u32[]{:S(2)}, u32[]{:S(2)}) async-start(f32[16,3,512]{2,1,0:T(4,128)} %pad_maximum_fusion), calls=%async_computation.2 | async-start | bytes 262144 | tf_op jit(solution)/shard_map/all_to_all | solution.py:221
  142.4 7.3 %all-to-all-done.2 = f32[16,3,512]{2,1,0:T(4,128)S(1)} async-done(((f32[16,3,512]{2,1,0:T(4,128)}), f32[16,3,512]{2,1,0:T(4,128)S(1)}, u32[]{:S(2)}, u32[]{:S(2)}) %all-to-all-start.2) | async-done | bytes 98336 | tf_op jit(solution)/shard_map/all_to_all | solution.py:221
  149.7 0.6 gather_fusion.4
  150.7 1.2 gather_fusion.5
  151.9 3.5 %all-to-all-start.3 = ((f32[16,2,512]{2,1,0:T(2,128)}), f32[16,2,512]{2,1,0:T(2,128)S(1)}, u32[]{:S(2)}, u32[]{:S(2)}) async-start(f32[16,2,512]{2,1,0:T(2,128)} %gather_fusion.5), calls=%async_computation.3 | async-start | bytes 131072 | tf_op jit(solution)/shard_map/all_to_all | solution.py:233
  155.6 6.6 %all-to-all-done.3 = f32[16,2,512]{2,1,0:T(2,128)S(1)} async-done(((f32[16,2,512]{2,1,0:T(2,128)}), f32[16,2,512]{2,1,0:T(2,128)S(1)}, u32[]{:S(2)}, u32[]{:S(2)}) %all-to-all-start.3) | async-done | bytes 65568 | tf_op jit(solution)/shard_map/all_to_all | solution.py:233
  162.4 6.6 %fusion.1 = (bf16[16,8,64,128]{3,2,1,0:T(8,128)(2,1)}, bf16[16,8,64,128]{3,2,1,0:T(8,128)(2,1)S(1)}) fusion(f32[16,8,64,128]{3,2,1,0:T(8,128)} %get-tuple-element.36, f32[16,8,64]{2,1,0:T(8,128)S(1)} %sub.73, f32[16,8,64,128]{3,2,1,0:T(8,128)} %get-tuple-element.37, f32[16,8,64]{2,1,0:T(8,128)S(1)} %sub.76), kind=kLoop, calls=%fused_computation.11 | loop fusion | flops 7340032 | bytes 12648448 | tf_op jit(solution)/shard_map/convert_element_type | solution.py:241
  169.0 1.2 convolution_convert_fusion
  170.2 1.9 broadcast_in_dim.53
  172.1 1.0 dynamic-slice_bitcast_fusion
  173.5 0.9 collective-permute-start.1
  174.4 1.4 collective-permute-start.2
  175.8 2.9 %collective-permute-start.3 = (bf16[2,8,64,128]{3,2,1,0:T(8,128)(2,1)S(1)}, bf16[2,8,64,128]{3,2,1,0:T(8,128)(2,1)S(1)}, u32[]{:S(2)}, u32[]{:S(2)}) collective-permute-start(bf16[2,8,64,128]{3,2,1,0:T(8,128)(2,1)S(1)} %get-tuple-element.22), channel_id=1, source_target_pairs={{0,16},{4,20},{8,24},{12,28},{16,0},{20,4},{24,8},{28,12},{1,17},{... | collective-permute-start | bytes 786440 | tf_op jit(solution)/shard_map/ppermute | solution.py:160
  178.9 1.6 copy-done
  180.5 14.7 %shard_map.78 = (bf16[8,128,1024]{2,1,0:T(8,128)(2,1)}, bf16[8,128,1024]{2,1,0:T(8,128)(2,1)}) custom-call(s32[16]{0:T(128)S(1)} %all_to_all.18.rows_ref, bf16[16,8,64,128]{3,2,1,0:T(8,128)(2,1)S(1)} %copy-done, bf16[16,8,64,128]{3,2,1,0:T(8,128)(2,1)S(1)} %get-tuple-element.18.grads_ref, bf16[16,2,8,64,128]{4,3,2,1,0:T(8,128)(2,1)} %all-to-all-done.pair_ref), custom_call_target="tpu_custom_call" | custom-call | tf_op jit(solution)/shard_map/pallas_call | solution.py:74
  195.2 2.5 %collective-permute-start.5 = (bf16[2,8,64,128]{3,2,1,0:T(8,128)(2,1)S(1)}, bf16[2,8,64,128]{3,2,1,0:T(8,128)(2,1)S(1)}, u32[]{:S(2)}, u32[]{:S(2)}) collective-permute-start(bf16[2,8,64,128]{3,2,1,0:T(8,128)(2,1)S(1)} %get-tuple-element.20), channel_id=1, source_target_pairs={{0,24},{4,28},{8,0},{12,4},{16,8},{20,12},{24,16},{28,20},{1,25},{... | collective-permute-start | bytes 786440 | tf_op jit(solution)/shard_map/ppermute | solution.py:160
  197.7 1.7 bitcast_dynamic-update-slice_fusion.6
  199.4 1.9 collective-permute-start.6
  201.3 1.7 bitcast_dynamic-update-slice_fusion.5
  203.0 1.4 collective-permute-done.2
  204.4 0.7 bitcast_dynamic-update-slice_fusion.4
  205.1 0.7 bitcast_dynamic-update-slice_fusion.3
  205.8 0.7 bitcast_dynamic-update-slice_fusion.2
  206.6 8.0 %collective-permute-done.5 = bf16[2,8,64,128]{3,2,1,0:T(8,128)(2,1)S(1)} collective-permute-done((bf16[2,8,64,128]{3,2,1,0:T(8,128)(2,1)S(1)}, bf16[2,8,64,128]{3,2,1,0:T(8,128)(2,1)S(1)}, u32[]{:S(2)}, u32[]{:S(2)}) %collective-permute-start.5) | collective-permute-done | bytes 262176 | tf_op jit(solution)/shard_map/ppermute | solution.py:160
  214.6 0.7 bitcast_dynamic-update-slice_fusion.1
  215.3 0.7 bitcast_dynamic-update-slice_fusion
  216.0 3.4 %shard_map.77 = bf16[8,64,1024]{2,1,0:T(8,128)(2,1)} custom-call(s32[16]{0:T(128)S(1)} %get-tuple-element.15.target_ref, bf16[16,8,64,128]{3,2,1,0:T(8,128)(2,1)} %bitcast.34.back_ref), custom_call_target="tpu_custom_call" | custom-call | tf_op jit(solution)/shard_map/pallas_call | solution.py:145
  (46 shorter events, 2.4 us)
Async XLA Ops:
  8.8 12.8 %all-to-all-start.1 = ((s32[8,2,1]{1,2,0:T(1,128)}), s32[8,2,1]{1,2,0:T(1,128)S(1)}, u32[]{:S(2)}, u32[]{:S(2)}) async-start(s32[8,2,1]{1,2,0:T(1,128)} %bitcast.6), calls=%async_computation.1 | async-start | bytes 8192 | tf_op jit(solution)/shard_map/all_to_all | solution.py:201
  15.8 1.2 copy-start.1
  17.0 1.2 copy-start.2
  21.6 6.2 %copy-start.4 = (bf16[8,128,1024]{2,1,0:T(8,128)(2,1)S(1)}, bf16[8,128,1024]{2,1,0:T(8,128)(2,1)}, u32[]{:S(2)}) copy-start(bf16[8,128,1024]{2,1,0:T(8,128)(2,1)} %param.7) | copy-start | bytes 6291460
  21.6 99.3 %all-to-all-start = ((bf16[16,2,8,64,128]{4,3,2,1,0:T(8,128)(2,1)}), bf16[16,2,8,64,128]{4,3,2,1,0:T(8,128)(2,1)}, u32[]{:S(2)}, u32[]{:S(2)}) async-start(bf16[16,2,8,64,128]{4,3,2,1,0:T(8,128)(2,1)} %shard_map.76), calls=%async_computation | async-start | bytes 8388608 | tf_op jit(solution)/shard_map/all_to_all | solution.py:200
  138.7 11.0 %all-to-all-start.2 = ((f32[16,3,512]{2,1,0:T(4,128)}), f32[16,3,512]{2,1,0:T(4,128)S(1)}, u32[]{:S(2)}, u32[]{:S(2)}) async-start(f32[16,3,512]{2,1,0:T(4,128)} %pad_maximum_fusion), calls=%async_computation.2 | async-start | bytes 262144 | tf_op jit(solution)/shard_map/all_to_all | solution.py:221
  151.9 10.2 %all-to-all-start.3 = ((f32[16,2,512]{2,1,0:T(2,128)}), f32[16,2,512]{2,1,0:T(2,128)S(1)}, u32[]{:S(2)}, u32[]{:S(2)}) async-start(f32[16,2,512]{2,1,0:T(2,128)} %gather_fusion.5), calls=%async_computation.3 | async-start | bytes 131072 | tf_op jit(solution)/shard_map/all_to_all | solution.py:233
  162.4 6.6 %copy-start.3 = (bf16[16,8,128,128]{3,2,1,0:T(8,128)(2,1)S(1)}, bf16[16,8,128,128]{3,2,1,0:T(8,128)(2,1)}, u32[]{:S(2)}) copy-start(bf16[16,8,128,128]{3,2,1,0:T(8,128)(2,1)} %gather_fusion.2) | copy-start | bytes 12582916
  173.1 22.2 %collective-permute-start = (bf16[2,8,64,128]{3,2,1,0:T(8,128)(2,1)}, bf16[2,8,64,128]{3,2,1,0:T(8,128)(2,1)}, u32[]{:S(2)}, u32[]{:S(2)}) collective-permute-start(bf16[2,8,64,128]{3,2,1,0:T(8,128)(2,1)} %get-tuple-element.25), channel_id=1, source_target_pairs={{0,4},{4,8},{8,12},{12,16},{16,20},{20,24},{24,28},{28,0},{1,5},{5... | collective-permute-start | bytes 786440 | tf_op jit(solution)/shard_map/ppermute | solution.py:160
  173.5 25.9 %collective-permute-start.1 = (bf16[2,8,64,128]{3,2,1,0:T(8,128)(2,1)}, bf16[2,8,64,128]{3,2,1,0:T(8,128)(2,1)}, u32[]{:S(2)}, u32[]{:S(2)}) collective-permute-start(bf16[2,8,64,128]{3,2,1,0:T(8,128)(2,1)} %get-tuple-element.24), channel_id=1, source_target_pairs={{0,8},{4,12},{8,16},{12,20},{16,24},{20,28},{24,0},{28,4},{1,9},{5... | collective-permute-start | bytes 786440 | tf_op jit(solution)/shard_map/ppermute | solution.py:160
  174.4 30.0 %collective-permute-start.2 = (bf16[2,8,64,128]{3,2,1,0:T(8,128)(2,1)S(1)}, bf16[2,8,64,128]{3,2,1,0:T(8,128)(2,1)S(1)}, u32[]{:S(2)}, u32[]{:S(2)}) collective-permute-start(bf16[2,8,64,128]{3,2,1,0:T(8,128)(2,1)S(1)} %get-tuple-element.23), channel_id=1, source_target_pairs={{0,12},{4,16},{8,20},{12,24},{16,28},{20,0},{24,4},{28,8},{1,13},{... | collective-permute-start | bytes 786440 | tf_op jit(solution)/shard_map/ppermute | solution.py:160
  175.8 29.3 %collective-permute-start.3 = (bf16[2,8,64,128]{3,2,1,0:T(8,128)(2,1)S(1)}, bf16[2,8,64,128]{3,2,1,0:T(8,128)(2,1)S(1)}, u32[]{:S(2)}, u32[]{:S(2)}) collective-permute-start(bf16[2,8,64,128]{3,2,1,0:T(8,128)(2,1)S(1)} %get-tuple-element.22), channel_id=1, source_target_pairs={{0,16},{4,20},{8,24},{12,28},{16,0},{20,4},{24,8},{28,12},{1,17},{... | collective-permute-start | bytes 786440 | tf_op jit(solution)/shard_map/ppermute | solution.py:160
  178.7 27.2 %collective-permute-start.4 = (bf16[2,8,64,128]{3,2,1,0:T(8,128)(2,1)S(1)}, bf16[2,8,64,128]{3,2,1,0:T(8,128)(2,1)S(1)}, u32[]{:S(2)}, u32[]{:S(2)}) collective-permute-start(bf16[2,8,64,128]{3,2,1,0:T(8,128)(2,1)S(1)} %get-tuple-element.21), channel_id=1, source_target_pairs={{0,20},{4,24},{8,28},{12,0},{16,4},{20,8},{24,12},{28,16},{1,21},{... | collective-permute-start | bytes 786440 | tf_op jit(solution)/shard_map/ppermute | solution.py:160
  178.9 1.6 copy-start
  195.2 19.3 %collective-permute-start.5 = (bf16[2,8,64,128]{3,2,1,0:T(8,128)(2,1)S(1)}, bf16[2,8,64,128]{3,2,1,0:T(8,128)(2,1)S(1)}, u32[]{:S(2)}, u32[]{:S(2)}) collective-permute-start(bf16[2,8,64,128]{3,2,1,0:T(8,128)(2,1)S(1)} %get-tuple-element.20), channel_id=1, source_target_pairs={{0,24},{4,28},{8,0},{12,4},{16,8},{20,12},{24,16},{28,20},{1,25},{... | collective-permute-start | bytes 786440 | tf_op jit(solution)/shard_map/ppermute | solution.py:160
  199.4 15.9 %collective-permute-start.6 = (bf16[2,8,64,128]{3,2,1,0:T(8,128)(2,1)S(1)}, bf16[2,8,64,128]{3,2,1,0:T(8,128)(2,1)S(1)}, u32[]{:S(2)}, u32[]{:S(2)}) collective-permute-start(bf16[2,8,64,128]{3,2,1,0:T(8,128)(2,1)S(1)} %get-tuple-element.19), channel_id=1, source_target_pairs={{0,28},{4,0},{8,4},{12,8},{16,12},{20,16},{24,20},{28,24},{1,29},{... | collective-permute-start | bytes 786440 | tf_op jit(solution)/shard_map/ppermute | solution.py:160

commit v14 on v13

--- a/solution.py
+++ b/solution.py
@@ -197,7 +197,12 @@
 
     pair_send = gather_pairs(slot_span, queries, out_grad)
     row_send = jnp.where(slot_valid, local_row[slot_item], -1)
-    pair_recv = lax.all_to_all(pair_send, "seq", split_axis=0, concat_axis=0, tiled=True)
+    if seq_count <= 8:
+        pair_recv = seq_exchange(
+            pair_send.reshape((seq_count, slot_depth) + pair_send.shape[1:]), seq_count
+        ).reshape(pair_send.shape)
+    else:
+        pair_recv = lax.all_to_all(pair_send, "seq", split_axis=0, concat_axis=0, tiled=True)
     row_recv = lax.all_to_all(row_send, "seq", split_axis=0, concat_axis=0, tiled=True)
 
     row_index = jnp.clip(row_recv, 0, rows_here - 1)

time: 224 us -> 224 us (level)
  waiting for transfers between devices: 94.1 us -> 42.6 us
  starting transfers between devices: 29.8 us -> 59.7 us
  local copies, waits for them, and re-layouts: 40.1 us -> 54 us
  blocking collectives: 6.25 us -> 15.5 us
    all_to_all x2 -> x0, waiting for transfers between devices: 77.4 us -> none  [the longest x1 70.9 us: per_device(): lax.all_to_all(pair_send, 'seq', split_axis=0, concat_axis=0, tiled=True)]
    all_to_all x1, starting transfers between devices: 3.64 us -> 30.6 us  [per_device(): back = lax.all_to_all(part, 'seq', split_axis=0, concat_axis=0, tiled=True)]
    ppermute x7 -> x14, waiting for transfers between devices: 9.38 us -> 35.3 us  [seq_exchange(): lax.ppermute(lax.dynamic_index_in_dim(blocks, (me + shift) % seq_count, k...]
    ppermute x7 -> x14, starting transfers between devices: 10.2 us -> 22.8 us  [seq_exchange(): lax.ppermute(lax.dynamic_index_in_dim(blocks, (me + shift) % seq_count, k...]
    all_to_all x2 -> x0, starting transfers between devices: 9.66 us -> none  [the longest x1 6.13 us: per_device(): lax.all_to_all(pair_send, 'seq', split_axis=0, concat_axis=0, tiled=True)]
    all_to_all x0 -> x1, blocking collectives: none -> 9.29 us  [per_device(): lax.all_to_all(span_stats[slot_span], 'seq', split_axis=0, concat_axis=0,...]
    dynamic_update_slice x7 -> x14, local copies, waits for them, and re-layouts: 7 us -> 15.9 us  [seq_exchange(): lax.dynamic_update_index_in_dim(result, sent, (me - shift) % seq_count, a...]
    broadcast_in_dim x1 -> x2, local copies, waits for them, and re-layouts: 1.86 us -> 4.89 us  [seq_exchange(): result = jnp.zeros_like(blocks)]
  transfers between devices with their start and end apart: 11 -> 16, of which waited for: 5 -> 4; matrix products, arithmetic and copies ran while one was open for 13% -> 19% of each run, Pallas kernels for 8% -> 8%
where the time goes in v14:
time: 224 us; the launch traced here: 220 us
  starting transfers between devices  59.7 us (27%)
  local copies, waits for them, and re-layouts  54 us (24%)
  waiting for transfers between devices  42.6 us (19%)
  Pallas kernels  21.4 us (10%)
  matrix products  16.8 us (8%)
  blocking collectives  15.5 us (7%)
  other arithmetic  8.74 us (4%)
    ppermute x14, waiting for transfers between devices, seq_exchange(): lax.ppermute(lax.dynamic_index_in_dim(blocks, (me + shift) % seq_count, k...  35.3 us
    all_to_all x1, starting transfers between devices, per_device(): back = lax.all_to_all(part, 'seq', split_axis=0, concat_axis=0, tiled=True)  30.6 us
    ppermute x14, starting transfers between devices, seq_exchange(): lax.ppermute(lax.dynamic_index_in_dim(blocks, (me + shift) % seq_count, k...  22.8 us
    dynamic_update_slice x14, local copies, waits for them, and re-layouts, seq_exchange(): lax.dynamic_update_index_in_dim(result, sent, (me - shift) % seq_count, a...  15.9 us
    pallas_call x1, Pallas kernels, kv_grads(): pl.pallas_call(kv_kernel, grid_spec=grid_spec, out_shape=[out_shape, out_...  14.7 us
    unnamed x20, local copies, waits for them, and re-layouts  10.3 us
    all_to_all x1, blocking collectives, per_device(): lax.all_to_all(span_stats[slot_span], 'seq', split_axis=0, concat_axis=0,...  9.29 us
    dot_general x1, matrix products, per_device(): jnp.einsum('bhid,bhjd->bhij', grad_heads, value_heads, preferred_element_...  8.99 us
  transfers between devices with their start and end apart: 16, of which 4 were waited for; matrix products, arithmetic and copies ran while one was open for 19% of the time, Pallas kernels for 8%

profile of v14, /device:TPU:0, one launch (start us, length us, event | category | flops | bytes accessed | tf_op | source)
XLA Modules:
  0.0 219.8 jit_solution(3848569307330805840)
XLA Ops:
  0.6 6.3 %all-gather = s32[4,2,2]{2,1,0:T(2,128)S(1)} all-gather(s32[1,2,2]{2,1,0:T(2,128)} %bitcast.127), channel_id=1, replica_groups=mesh['seq'=8,'mp'=4] {'mp'}, dimensions={0}, use_global_device_ids=true | all-gather | bytes 80 | tf_op jit(solution)/shard_map/all_gather | solution.py:173
  8.8 6.3 %all-to-all-start = ((s32[8,2,1]{1,2,0:T(1,128)}), s32[8,2,1]{1,2,0:T(1,128)S(1)}, u32[]{:S(2)}, u32[]{:S(2)}) async-start(s32[8,2,1]{1,2,0:T(1,128)} %bitcast.22), calls=%async_computation | async-start | bytes 8192 | tf_op jit(solution)/shard_map/all_to_all | solution.py:206
  15.8 1.2 copy-done.1
  17.0 1.2 copy-done.2
  18.3 3.3 %shard_map.76 = bf16[16,2,8,64,128]{4,3,2,1,0:T(8,128)(2,1)} custom-call(s32[16]{0:T(128)S(1)} %broadcast_clamp_fusion.1.span_ref, bf16[8,64,1024]{2,1,0:T(8,128)(2,1)S(1)} %copy-done.1, bf16[8,64,1024]{2,1,0:T(8,128)(2,1)S(1)} %copy-done.2), custom_call_target="tpu_custom_call" | custom-call | tf_op jit(solution)/shard_map/pallas_call | solution.py:112
  21.5 3.0 %broadcast_in_dim.80 = bf16[8,2,2,8,64,128]{5,4,3,2,1,0:T(8,128)(2,1)} broadcast(bf16[]{:T(256)} %constant.228.clone.1), dimensions={} | broadcast | bytes 4194306 | tf_op jit(solution)/shard_map/broadcast_in_dim | solution.py:155
  24.6 2.4 %dynamic-slice_bitcast_fusion = (bf16[2,2,8,64,128]{4,3,2,1,0:T(8,128)(2,1)}, bf16[2,2,8,64,128]{4,3,2,1,0:T(8,128)(2,1)}, bf16[2,2,8,64,128]{4,3,2,1,0:T(8,128)...) fusion(bf16[8,2,2,8,64,128]{5,4,3,2,1,0:T(8,128)(2,1)S(1)} %bit, ...), kind=kLoop, calls=%fused_computation.26 | loop fusion | bytes 8388640 | tf_op jit(solution)/shard_map/jit(dynamic_index_in_dim)/squeeze | solution.py:161
  27.0 2.0 collective-permute-start
  29.0 1.4 collective-permute-start.1
  30.4 2.4 %collective-permute-start.2 = (bf16[2,2,8,64,128]{4,3,2,1,0:T(8,128)(2,1)}, bf16[2,2,8,64,128]{4,3,2,1,0:T(8,128)(2,1)}, u32[]{:S(2)}, u32[]{:S(2)}) collective-permute-start(bf16[2,2,8,64,128]{4,3,2,1,0:T(8,128)(2,1)} %get-tuple-element.23), channel_id=1, source_target_pairs={{0,12},{4,16},{8,20},{12,24},{16,28},{20,0},{24,4},{28,8},{1,13},{... | collective-permute-start | bytes 1572872 | tf_op jit(solution)/shard_map/ppermute | solution.py:160
  32.8 1.5 collective-permute-start.3
  34.2 2.4 %collective-permute-start.4 = (bf16[2,2,8,64,128]{4,3,2,1,0:T(8,128)(2,1)}, bf16[2,2,8,64,128]{4,3,2,1,0:T(8,128)(2,1)S(1)}, u32[]{:S(2)}, u32[]{:S(2)}) collective-permute-start(bf16[2,2,8,64,128]{4,3,2,1,0:T(8,128)(2,1)} %get-tuple-element.21), channel_id=1, source_target_pairs={{0,20},{4,24},{8,28},{12,0},{16,4},{20,8},{24,12},{28,16},{1,21},{... | collective-permute-start | bytes 1572872 | tf_op jit(solution)/shard_map/ppermute | solution.py:160
  36.9 2.4 %copy.26 = bf16[8,128,1024]{1,2,0:T(8,128)(2,1)} copy(bf16[8,128,1024]{2,1,0:T(8,128)(2,1)S(1)} %copy-done.6) | data formatting | bytes 4194304 | tf_op args[2]
  39.2 3.0 %copy.27 = bf16[8,128,8,128]{3,1,2,0:T(8,128)(2,1)S(1)} copy(bf16[8,128,8,128]{1,3,2,0:T(8,128)(2,1)} %bitcast.124) | data formatting | bytes 4194304 | tf_op jit(solution)/shard_map/reshape | solution.py:17
  42.3 3.9 %copy.29 = bf16[8,128,1024]{1,2,0:T(8,128)(2,1)} copy(bf16[8,128,1024]{2,1,0:T(8,128)(2,1)} %param.8) | data formatting | bytes 4194304 | tf_op args[3]
  46.2 3.9 %copy.30 = bf16[8,128,8,128]{3,1,2,0:T(8,128)(2,1)} copy(bf16[8,128,8,128]{1,3,2,0:T(8,128)(2,1)} %bitcast.125) | data formatting | bytes 4194304 | tf_op jit(solution)/shard_map/reshape | solution.py:17
  51.4 3.0 %gather_fusion.2 = bf16[16,8,128,128]{3,2,1,0:T(8,128)(2,1)} fusion(bf16[8,8,128,128]{3,2,1,0:T(8,128)(2,1)S(1)} %bitcast.120, s32[1024]{0:T(1024)S(1)} %pad_clamp_fusion.2), kind=kCustom, calls=%fused_computation.2 | custom fusion | bytes 8388672 | tf_op jit(solution)/shard_map/gather | solution.py:211
  54.4 4.7 %gather_fusion.3 = bf16[16,8,128,128]{3,2,1,0:T(8,128)(2,1)} fusion(bf16[8,8,128,128]{3,2,1,0:T(8,128)(2,1)} %bitcast.121, s32[1024]{0:T(1024)S(1)} %pad_clamp_fusion.2), kind=kCustom, calls=%fused_computation.3 | custom fusion | bytes 8388672 | tf_op jit(solution)/shard_map/gather | solution.py:212
  59.2 1.5 collective-permute-start.5
  60.7 1.9 bitcast_dynamic-update-slice_fusion.6
  62.5 1.5 collective-permute-start.6
  64.0 1.9 bitcast_dynamic-update-slice_fusion.5
  65.9 23.1 %collective-permute-done.2 = bf16[2,2,8,64,128]{4,3,2,1,0:T(8,128)(2,1)} collective-permute-done((bf16[2,2,8,64,128]{4,3,2,1,0:T(8,128)(2,1)}, bf16[2,2,8,64,128]{4,3,2,1,0:T(8,128)(2,1)}, u32[]{:S(2)}, u32[]{:S(2)}) %collective-permute-start.2) | collective-permute-done | bytes 524320 | tf_op jit(solution)/shard_map/ppermute | solution.py:160
  88.9 1.9 bitcast_dynamic-update-slice_fusion.4
  90.8 0.9 bitcast_dynamic-update-slice_fusion.3
  92.5 0.8 bitcast_dynamic-update-slice_fusion.1
  93.3 4.3 %collective-permute-done.6 = bf16[2,2,8,64,128]{4,3,2,1,0:T(8,128)(2,1)S(1)} collective-permute-done((bf16[2,2,8,64,128]{4,3,2,1,0:T(8,128)(2,1)S(1)}, bf16[2,2,8,64,128]{4,3,2,1,0:T(8,128)(2,1)S(1)}, u32[]{:S(2)}, u32[]{:S(2)}) %collective-permute-start.6) | collective-permute-done | bytes 524320 | tf_op jit(solution)/shard_map/ppermute | solution.py:160
  97.7 0.9 bitcast_dynamic-update-slice_fusion
  98.5 6.6 %multiply_reduce_fusion.1 = (f32[16,8,64]{2,1,0:T(8,128)S(1)}, f32[16,8,64,128]{3,2,1,0:T(8,128)}) fusion(bf16[16,8,128,128]{3,2,1,0:T(8,128)(2,1)S(1)} %copy-done.3, bf16[16,2,8,64,128]{4,3,2,1,0:T(8,128)(2,1)} %bitcast.18.pair_ref), kind=kOutput, calls=%fused_computation.12 | convolution fusion | flops 270524416 | bytes 10518528 | tf_op jit(solution)/shard_map/bhid,bhjd->bhij/dot_general | solution.py:215
  105.2 9.0 %fusion = (f32[16,8,64]{2,1,0:T(8,128)S(1)}, f32[16,8,64]{2,1,0:T(8,128)S(1)}, f32[16,8,64,128]{3,2,1,0:T(8,128)}) fusion(f32[16,8,64,128]{3,2,1,0:T(8,128)} %get-tuple-element.44, f32[16,8,64]{2,1,0:T(8,128)S(1)} %get-tuple-element.43, bf16[16,8,128,128]{3,2,1,0:T(8,128)(2,1)} %gather_fusion.3, bf16[16,2,8,64,128]{4,3,2,1,0:T(8,128)(2,1)} %bitcast.18.pair_ref), kind=kOutput, calls=%fused_computation.10 | convolution fusion | flops 273661952 | bytes 14778368 | tf_op jit(solution)/shard_map/bhid,bhjd->bhij/dot_general | solution.py:218
  115.1 30.6 %all-to-all-start.1 = ((f32[16,3,512]{2,1,0:T(4,128)}), f32[16,3,512]{2,1,0:T(4,128)S(1)}, u32[]{:S(2)}, u32[]{:S(2)}) async-start(f32[16,3,512]{2,1,0:T(4,128)} %pad_maximum_fusion), calls=%async_computation.1 | async-start | bytes 262144 | tf_op jit(solution)/shard_map/all_to_all | solution.py:226
  145.8 7.3 %all-to-all-done.1 = f32[16,3,512]{2,1,0:T(4,128)S(1)} async-done(((f32[16,3,512]{2,1,0:T(4,128)}), f32[16,3,512]{2,1,0:T(4,128)S(1)}, u32[]{:S(2)}, u32[]{:S(2)}) %all-to-all-start.1) | async-done | bytes 98336 | tf_op jit(solution)/shard_map/all_to_all | solution.py:226
  154.7 9.3 %all_to_all.18 = f32[16,2,512]{2,1,0:T(2,128)S(1)} all-to-all(f32[16,2,512]{2,1,0:T(2,128)S(1)} %gather_fusion.5), channel_id=1, replica_groups=mesh['seq'=8,'mp'=4] {'seq'}, dimensions={0} | all-to-all | bytes 131072 | tf_op jit(solution)/shard_map/all_to_all | solution.py:238
  164.3 6.6 %fusion.1 = (bf16[16,8,64,128]{3,2,1,0:T(8,128)(2,1)}, bf16[16,8,64,128]{3,2,1,0:T(8,128)(2,1)S(1)}) fusion(f32[16,8,64,128]{3,2,1,0:T(8,128)} %get-tuple-element.44, f32[16,8,64]{2,1,0:T(8,128)S(1)} %sub.87, f32[16,8,64,128]{3,2,1,0:T(8,128)} %get-tuple-element.45, f32[16,8,64]{2,1,0:T(8,128)S(1)} %sub.90), kind=kLoop, calls=%fused_computation.11 | loop fusion | flops 7340032 | bytes 12648448 | tf_op jit(solution)/shard_map/convert_element_type | solution.py:246
  170.9 1.2 convolution_convert_fusion
  172.1 1.9 broadcast_in_dim.79
  174.0 1.0 dynamic-slice_bitcast_fusion.7
  175.4 0.8 collective-permute-start.8
  176.3 1.4 collective-permute-start.9
  177.7 2.9 %collective-permute-start.10 = (bf16[2,8,64,128]{3,2,1,0:T(8,128)(2,1)S(1)}, bf16[2,8,64,128]{3,2,1,0:T(8,128)(2,1)S(1)}, u32[]{:S(2)}, u32[]{:S(2)}) collective-permute-start(bf16[2,8,64,128]{3,2,1,0:T(8,128)(2,1)S(1)} %get-tuple-element.30), channel_id=1, source_target_pairs={{0,16},{4,20},{8,24},{12,28},{16,0},{20,4},{24,8},{28,12},{1,17},{... | collective-permute-start | bytes 786440 | tf_op jit(solution)/shard_map/ppermute | solution.py:160
  180.8 1.6 copy-done
  182.4 14.7 %shard_map.78 = (bf16[8,128,1024]{2,1,0:T(8,128)(2,1)}, bf16[8,128,1024]{2,1,0:T(8,128)(2,1)}) custom-call(s32[16]{0:T(128)S(1)} %all_to_all.14.rows_ref, bf16[16,8,64,128]{3,2,1,0:T(8,128)(2,1)S(1)} %copy-done, bf16[16,8,64,128]{3,2,1,0:T(8,128)(2,1)S(1)} %get-tuple-element.18.grads_ref, bf16[16,2,8,64,128]{4,3,2,1,0:T(8,128)(2,1)} %bitcast.18.pair_ref), custom_call_target="tpu_custom_call" | custom-call | tf_op jit(solution)/shard_map/pallas_call | solution.py:74
  197.2 2.4 %collective-permute-start.12 = (bf16[2,8,64,128]{3,2,1,0:T(8,128)(2,1)S(1)}, bf16[2,8,64,128]{3,2,1,0:T(8,128)(2,1)S(1)}, u32[]{:S(2)}, u32[]{:S(2)}) collective-permute-start(bf16[2,8,64,128]{3,2,1,0:T(8,128)(2,1)S(1)} %get-tuple-element.28), channel_id=1, source_target_pairs={{0,24},{4,28},{8,0},{12,4},{16,8},{20,12},{24,16},{28,20},{1,25},{... | collective-permute-start | bytes 786440 | tf_op jit(solution)/shard_map/ppermute | solution.py:160
  199.6 1.7 bitcast_dynamic-update-slice_fusion.13
  201.3 2.0 collective-permute-start.13
  203.2 1.7 bitcast_dynamic-update-slice_fusion.12
  207.1 7.9 %collective-permute-done.12 = bf16[2,8,64,128]{3,2,1,0:T(8,128)(2,1)S(1)} collective-permute-done((bf16[2,8,64,128]{3,2,1,0:T(8,128)(2,1)S(1)}, bf16[2,8,64,128]{3,2,1,0:T(8,128)(2,1)S(1)}, u32[]{:S(2)}, u32[]{:S(2)}) %collective-permute-start.12) | collective-permute-done | bytes 262176 | tf_op jit(solution)/shard_map/ppermute | solution.py:160
  216.4 3.4 %shard_map.77 = bf16[8,64,1024]{2,1,0:T(8,128)(2,1)} custom-call(s32[16]{0:T(128)S(1)} %get-tuple-element.15.target_ref, bf16[16,8,64,128]{3,2,1,0:T(8,128)(2,1)} %bitcast.50.back_ref), custom_call_target="tpu_custom_call" | custom-call | tf_op jit(solution)/shard_map/pallas_call | solution.py:145
  (74 shorter events, 12.1 us)
Async XLA Ops:
  8.8 41.3 %all-to-all-start = ((s32[8,2,1]{1,2,0:T(1,128)}), s32[8,2,1]{1,2,0:T(1,128)S(1)}, u32[]{:S(2)}, u32[]{:S(2)}) async-start(s32[8,2,1]{1,2,0:T(1,128)} %bitcast.22), calls=%async_computation | async-start | bytes 8192 | tf_op jit(solution)/shard_map/all_to_all | solution.py:206
  15.8 1.2 copy-start.1
  17.0 1.2 copy-start.2
  21.5 3.0 %copy-start.5 = (bf16[16,2,8,64,128]{4,3,2,1,0:T(8,128)(2,1)S(1)}, bf16[16,2,8,64,128]{4,3,2,1,0:T(8,128)(2,1)}, u32[]{:S(2)}) copy-start(bf16[16,2,8,64,128]{4,3,2,1,0:T(8,128)(2,1)} %shard_map.76) | copy-start | bytes 12582916
  24.6 12.3 %copy-start.6 = (bf16[8,128,1024]{2,1,0:T(8,128)(2,1)S(1)}, bf16[8,128,1024]{2,1,0:T(8,128)(2,1)}, u32[]{:S(2)}) copy-start(bf16[8,128,1024]{2,1,0:T(8,128)(2,1)} %param.7) | copy-start | bytes 6291460
  27.0 32.2 %collective-permute-start = (bf16[2,2,8,64,128]{4,3,2,1,0:T(8,128)(2,1)}, bf16[2,2,8,64,128]{4,3,2,1,0:T(8,128)(2,1)}, u32[]{:S(2)}, u32[]{:S(2)}) collective-permute-start(bf16[2,2,8,64,128]{4,3,2,1,0:T(8,128)(2,1)} %get-tuple-element.25), channel_id=1, source_target_pairs={{0,4},{4,8},{8,12},{12,16},{16,20},{20,24},{24,28},{28,0},{1,5},{5... | collective-permute-start | bytes 1572872 | tf_op jit(solution)/shard_map/ppermute | solution.py:160
  29.0 33.5 %collective-permute-start.1 = (bf16[2,2,8,64,128]{4,3,2,1,0:T(8,128)(2,1)}, bf16[2,2,8,64,128]{4,3,2,1,0:T(8,128)(2,1)}, u32[]{:S(2)}, u32[]{:S(2)}) collective-permute-start(bf16[2,2,8,64,128]{4,3,2,1,0:T(8,128)(2,1)} %get-tuple-element.24), channel_id=1, source_target_pairs={{0,8},{4,12},{8,16},{12,20},{16,24},{20,28},{24,0},{28,4},{1,9},{5... | collective-permute-start | bytes 1572872 | tf_op jit(solution)/shard_map/ppermute | solution.py:160
  30.4 58.5 %collective-permute-start.2 = (bf16[2,2,8,64,128]{4,3,2,1,0:T(8,128)(2,1)}, bf16[2,2,8,64,128]{4,3,2,1,0:T(8,128)(2,1)}, u32[]{:S(2)}, u32[]{:S(2)}) collective-permute-start(bf16[2,2,8,64,128]{4,3,2,1,0:T(8,128)(2,1)} %get-tuple-element.23), channel_id=1, source_target_pairs={{0,12},{4,16},{8,20},{12,24},{16,28},{20,0},{24,4},{28,8},{1,13},{... | collective-permute-start | bytes 1572872 | tf_op jit(solution)/shard_map/ppermute | solution.py:160
  32.8 58.1 %collective-permute-start.3 = (bf16[2,2,8,64,128]{4,3,2,1,0:T(8,128)(2,1)}, bf16[2,2,8,64,128]{4,3,2,1,0:T(8,128)(2,1)S(1)}, u32[]{:S(2)}, u32[]{:S(2)}) collective-permute-start(bf16[2,2,8,64,128]{4,3,2,1,0:T(8,128)(2,1)} %get-tuple-element.22), channel_id=1, source_target_pairs={{0,16},{4,20},{8,24},{12,28},{16,0},{20,4},{24,8},{28,12},{1,17},{... | collective-permute-start | bytes 1572872 | tf_op jit(solution)/shard_map/ppermute | solution.py:160
  34.2 57.4 %collective-permute-start.4 = (bf16[2,2,8,64,128]{4,3,2,1,0:T(8,128)(2,1)}, bf16[2,2,8,64,128]{4,3,2,1,0:T(8,128)(2,1)S(1)}, u32[]{:S(2)}, u32[]{:S(2)}) collective-permute-start(bf16[2,2,8,64,128]{4,3,2,1,0:T(8,128)(2,1)} %get-tuple-element.21), channel_id=1, source_target_pairs={{0,20},{4,24},{8,28},{12,0},{16,4},{20,8},{24,12},{28,16},{1,21},{... | collective-permute-start | bytes 1572872 | tf_op jit(solution)/shard_map/ppermute | solution.py:160
  54.4 4.7 %copy-start.8 = (bf16[2,2,8,64,128]{4,3,2,1,0:T(8,128)(2,1)S(1)}, bf16[2,2,8,64,128]{4,3,2,1,0:T(8,128)(2,1)}, u32[]{:S(2)}) copy-start(bf16[2,2,8,64,128]{4,3,2,1,0:T(8,128)(2,1)} %get-tuple-element.20) | copy-start | bytes 1572868
  54.4 8.1 %copy-start.7 = (bf16[2,2,8,64,128]{4,3,2,1,0:T(8,128)(2,1)S(1)}, bf16[2,2,8,64,128]{4,3,2,1,0:T(8,128)(2,1)}, u32[]{:S(2)}) copy-start(bf16[2,2,8,64,128]{4,3,2,1,0:T(8,128)(2,1)} %get-tuple-element.19) | copy-start | bytes 1572868
  59.1 39.4 %copy-start.3 = (bf16[16,8,128,128]{3,2,1,0:T(8,128)(2,1)S(1)}, bf16[16,8,128,128]{3,2,1,0:T(8,128)(2,1)}, u32[]{:S(2)}) copy-start(bf16[16,8,128,128]{3,2,1,0:T(8,128)(2,1)} %gather_fusion.2) | copy-start | bytes 12582916
  59.2 33.4 %collective-permute-start.5 = (bf16[2,2,8,64,128]{4,3,2,1,0:T(8,128)(2,1)S(1)}, bf16[2,2,8,64,128]{4,3,2,1,0:T(8,128)(2,1)S(1)}, u32[]{:S(2)}, u32[]{:S(2)}) collective-permute-start(bf16[2,2,8,64,128]{4,3,2,1,0:T(8,128)(2,1)S(1)} %copy-done.8), channel_id=1, source_target_pairs={{0,24},{4,28},{8,0},{12,4},{16,8},{20,12},{24,16},{28,20},{1,25},{... | collective-permute-start | bytes 1572872 | tf_op jit(solution)/shard_map/ppermute | solution.py:160
  62.5 35.1 %collective-permute-start.6 = (bf16[2,2,8,64,128]{4,3,2,1,0:T(8,128)(2,1)S(1)}, bf16[2,2,8,64,128]{4,3,2,1,0:T(8,128)(2,1)S(1)}, u32[]{:S(2)}, u32[]{:S(2)}) collective-permute-start(bf16[2,2,8,64,128]{4,3,2,1,0:T(8,128)(2,1)S(1)} %copy-done.7), channel_id=1, source_target_pairs={{0,28},{4,0},{8,4},{12,8},{16,12},{20,16},{24,20},{28,24},{1,29},{... | collective-permute-start | bytes 1572872 | tf_op jit(solution)/shard_map/ppermute | solution.py:160
  115.1 38.0 %all-to-all-start.1 = ((f32[16,3,512]{2,1,0:T(4,128)}), f32[16,3,512]{2,1,0:T(4,128)S(1)}, u32[]{:S(2)}, u32[]{:S(2)}) async-start(f32[16,3,512]{2,1,0:T(4,128)} %pad_maximum_fusion), calls=%async_computation.1 | async-start | bytes 262144 | tf_op jit(solution)/shard_map/all_to_all | solution.py:226
  164.3 6.6 %copy-start.4 = (bf16[16,8,128,128]{3,2,1,0:T(8,128)(2,1)S(1)}, bf16[16,8,128,128]{3,2,1,0:T(8,128)(2,1)}, u32[]{:S(2)}) copy-start(bf16[16,8,128,128]{3,2,1,0:T(8,128)(2,1)} %gather_fusion.2) | copy-start | bytes 12582916
  175.0 22.2 %collective-permute-start.7 = (bf16[2,8,64,128]{3,2,1,0:T(8,128)(2,1)}, bf16[2,8,64,128]{3,2,1,0:T(8,128)(2,1)}, u32[]{:S(2)}, u32[]{:S(2)}) collective-permute-start(bf16[2,8,64,128]{3,2,1,0:T(8,128)(2,1)} %get-tuple-element.33), channel_id=1, source_target_pairs={{0,4},{4,8},{8,12},{12,16},{16,20},{20,24},{24,28},{28,0},{1,5},{5... | collective-permute-start | bytes 786440 | tf_op jit(solution)/shard_map/ppermute | solution.py:160
  175.4 25.9 %collective-permute-start.8 = (bf16[2,8,64,128]{3,2,1,0:T(8,128)(2,1)}, bf16[2,8,64,128]{3,2,1,0:T(8,128)(2,1)}, u32[]{:S(2)}, u32[]{:S(2)}) collective-permute-start(bf16[2,8,64,128]{3,2,1,0:T(8,128)(2,1)} %get-tuple-element.32), channel_id=1, source_target_pairs={{0,8},{4,12},{8,16},{12,20},{16,24},{20,28},{24,0},{28,4},{1,9},{5... | collective-permute-start | bytes 786440 | tf_op jit(solution)/shard_map/ppermute | solution.py:160
  176.3 28.6 %collective-permute-start.9 = (bf16[2,8,64,128]{3,2,1,0:T(8,128)(2,1)S(1)}, bf16[2,8,64,128]{3,2,1,0:T(8,128)(2,1)S(1)}, u32[]{:S(2)}, u32[]{:S(2)}) collective-permute-start(bf16[2,8,64,128]{3,2,1,0:T(8,128)(2,1)S(1)} %get-tuple-element.31), channel_id=1, source_target_pairs={{0,12},{4,16},{8,20},{12,24},{16,28},{20,0},{24,4},{28,8},{1,13},{... | collective-permute-start | bytes 786440 | tf_op jit(solution)/shard_map/ppermute | solution.py:160
  177.7 28.0 %collective-permute-start.10 = (bf16[2,8,64,128]{3,2,1,0:T(8,128)(2,1)S(1)}, bf16[2,8,64,128]{3,2,1,0:T(8,128)(2,1)S(1)}, u32[]{:S(2)}, u32[]{:S(2)}) collective-permute-start(bf16[2,8,64,128]{3,2,1,0:T(8,128)(2,1)S(1)} %get-tuple-element.30), channel_id=1, source_target_pairs={{0,16},{4,20},{8,24},{12,28},{16,0},{20,4},{24,8},{28,12},{1,17},{... | collective-permute-start | bytes 786440 | tf_op jit(solution)/shard_map/ppermute | solution.py:160
  180.6 25.8 %collective-permute-start.11 = (bf16[2,8,64,128]{3,2,1,0:T(8,128)(2,1)S(1)}, bf16[2,8,64,128]{3,2,1,0:T(8,128)(2,1)S(1)}, u32[]{:S(2)}, u32[]{:S(2)}) collective-permute-start(bf16[2,8,64,128]{3,2,1,0:T(8,128)(2,1)S(1)} %get-tuple-element.29), channel_id=1, source_target_pairs={{0,20},{4,24},{8,28},{12,0},{16,4},{20,8},{24,12},{28,16},{1,21},{... | collective-permute-start | bytes 786440 | tf_op jit(solution)/shard_map/ppermute | solution.py:160
  180.8 1.6 copy-start
  197.2 17.8 %collective-permute-start.12 = (bf16[2,8,64,128]{3,2,1,0:T(8,128)(2,1)S(1)}, bf16[2,8,64,128]{3,2,1,0:T(8,128)(2,1)S(1)}, u32[]{:S(2)}, u32[]{:S(2)}) collective-permute-start(bf16[2,8,64,128]{3,2,1,0:T(8,128)(2,1)S(1)} %get-tuple-element.28), channel_id=1, source_target_pairs={{0,24},{4,28},{8,0},{12,4},{16,8},{20,12},{24,16},{28,20},{1,25},{... | collective-permute-start | bytes 786440 | tf_op jit(solution)/shard_map/ppermute | solution.py:160
  201.3 14.4 %collective-permute-start.13 = (bf16[2,8,64,128]{3,2,1,0:T(8,128)(2,1)S(1)}, bf16[2,8,64,128]{3,2,1,0:T(8,128)(2,1)S(1)}, u32[]{:S(2)}, u32[]{:S(2)}) collective-permute-start(bf16[2,8,64,128]{3,2,1,0:T(8,128)(2,1)S(1)} %get-tuple-element.27), channel_id=1, source_target_pairs={{0,28},{4,0},{8,4},{12,8},{16,12},{20,16},{24,20},{28,24},{1,29},{... | collective-permute-start | bytes 786440 | tf_op jit(solution)/shard_map/ppermute | solution.py:160

commit v15 on v14

--- a/solution.py
+++ b/solution.py
@@ -156,7 +156,12 @@
     result = lax.dynamic_update_index_in_dim(
         result, lax.dynamic_index_in_dim(blocks, me, keepdims=False), me, axis=0
     )
-    for shift in range(1, seq_count):
+    shifts = []
+    for low in range(1, seq_count // 2 + 1):
+        for shift in (low, seq_count - low):
+            if shift not in shifts and 0 < shift < seq_count:
+                shifts.append(shift)
+    for shift in shifts:
         sent = lax.ppermute(
             lax.dynamic_index_in_dim(blocks, (me + shift) % seq_count, keepdims=False),
             "seq",

time: 224 us -> 226 us (level); the launches traced: 220 us -> 225 us
  waiting for transfers between devices: 42.6 us -> 72.6 us
  starting transfers between devices: 59.7 us -> 35 us
    ppermute x14, waiting for transfers between devices: 35.3 us -> 65.2 us  [seq_exchange(): lax.ppermute(lax.dynamic_index_in_dim(blocks, (me + shift) % seq_count, k...]
    all_to_all x1, starting transfers between devices: 30.6 us -> 3.85 us  [per_device(): back = lax.all_to_all(part, 'seq', split_axis=0, concat_axis=0, tiled=True)]
  transfers between devices with their start and end apart: 16 -> 16, of which waited for: 4 -> 5; matrix products, arithmetic and copies ran while one was open for 19% -> 19% of each run, Pallas kernels for 8% -> 8%
where the time goes in v15:
time: 226 us; the launch traced here: 225 us
  waiting for transfers between devices  72.6 us (32%)
  local copies, waits for them, and re-layouts  54 us (24%)
  starting transfers between devices  35 us (15%)
  Pallas kernels  21.5 us (10%)
  matrix products  16.8 us (7%)
  blocking collectives  15.5 us (7%)
  other arithmetic  8.74 us (4%)
    ppermute x14, waiting for transfers between devices, seq_exchange(): lax.ppermute(lax.dynamic_index_in_dim(blocks, (me + shift) % seq_count, k...  65.2 us
    ppermute x14, starting transfers between devices, seq_exchange(): lax.ppermute(lax.dynamic_index_in_dim(blocks, (me + shift) % seq_count, k...  24.8 us
    dynamic_update_slice x14, local copies, waits for them, and re-layouts, seq_exchange(): lax.dynamic_update_index_in_dim(result, sent, (me - shift) % seq_count, a...  16 us
    pallas_call x1, Pallas kernels, kv_grads(): pl.pallas_call(kv_kernel, grid_spec=grid_spec, out_shape=[out_shape, out_...  14.7 us
    unnamed x20, local copies, waits for them, and re-layouts  10.3 us
    all_to_all x1, blocking collectives, per_device(): lax.all_to_all(span_stats[slot_span], 'seq', split_axis=0, concat_axis=0,...  9.29 us
    dot_general x1, matrix products, per_device(): jnp.einsum('bhid,bhjd->bhij', grad_heads, value_heads, preferred_element_...  9 us
    all_to_all x1, waiting for transfers between devices, per_device(): back = lax.all_to_all(part, 'seq', split_axis=0, concat_axis=0, tiled=True)  7.32 us
  transfers between devices with their start and end apart: 16, of which 5 were waited for; matrix products, arithmetic and copies ran while one was open for 19% of the time, Pallas kernels for 8%

profile of v15, /device:TPU:0, one launch (start us, length us, event | category | flops | bytes accessed | tf_op | source)
XLA Modules:
  0.0 225.0 jit_solution(9718014753227925619)
XLA Ops:
  0.6 6.3 %all-gather = s32[4,2,2]{2,1,0:T(2,128)S(1)} all-gather(s32[1,2,2]{2,1,0:T(2,128)} %bitcast.127), channel_id=1, replica_groups=mesh['seq'=8,'mp'=4] {'mp'}, dimensions={0}, use_global_device_ids=true | all-gather | bytes 80 | tf_op jit(solution)/shard_map/all_gather | solution.py:178
  8.8 6.3 %all-to-all-start = ((s32[8,2,1]{1,2,0:T(1,128)}), s32[8,2,1]{1,2,0:T(1,128)S(1)}, u32[]{:S(2)}, u32[]{:S(2)}) async-start(s32[8,2,1]{1,2,0:T(1,128)} %bitcast.22), calls=%async_computation | async-start | bytes 8192 | tf_op jit(solution)/shard_map/all_to_all | solution.py:211
  15.8 1.2 copy-done.1
  17.0 1.2 copy-done.2
  18.3 3.3 %shard_map.76 = bf16[16,2,8,64,128]{4,3,2,1,0:T(8,128)(2,1)} custom-call(s32[16]{0:T(128)S(1)} %broadcast_clamp_fusion.1.span_ref, bf16[8,64,1024]{2,1,0:T(8,128)(2,1)S(1)} %copy-done.1, bf16[8,64,1024]{2,1,0:T(8,128)(2,1)S(1)} %copy-done.2), custom_call_target="tpu_custom_call" | custom-call | tf_op jit(solution)/shard_map/pallas_call | solution.py:112
  21.5 3.0 %broadcast_in_dim.80 = bf16[8,2,2,8,64,128]{5,4,3,2,1,0:T(8,128)(2,1)} broadcast(bf16[]{:T(256)} %constant.228.clone.1), dimensions={} | broadcast | bytes 4194306 | tf_op jit(solution)/shard_map/broadcast_in_dim | solution.py:155
  24.6 2.4 %dynamic-slice_bitcast_fusion = (bf16[2,2,8,64,128]{4,3,2,1,0:T(8,128)(2,1)}, bf16[2,2,8,64,128]{4,3,2,1,0:T(8,128)(2,1)}, bf16[2,2,8,64,128]{4,3,2,1,0:T(8,128)...) fusion(bf16[8,2,2,8,64,128]{5,4,3,2,1,0:T(8,128)(2,1)S(1)} %bit, ...), kind=kLoop, calls=%fused_computation.26 | loop fusion | bytes 8388640 | tf_op jit(solution)/shard_map/jit(dynamic_index_in_dim)/squeeze | solution.py:166
  27.0 2.0 collective-permute-start
  29.0 2.7 %collective-permute-start.1 = (bf16[2,2,8,64,128]{4,3,2,1,0:T(8,128)(2,1)}, bf16[2,2,8,64,128]{4,3,2,1,0:T(8,128)(2,1)}, u32[]{:S(2)}, u32[]{:S(2)}) collective-permute-start(bf16[2,2,8,64,128]{4,3,2,1,0:T(8,128)(2,1)} %get-tuple-element.24), channel_id=1, source_target_pairs={{0,28},{4,0},{8,4},{12,8},{16,12},{20,16},{24,20},{28,24},{1,29},{... | collective-permute-start | bytes 1572872 | tf_op jit(solution)/shard_map/ppermute | solution.py:165
  31.9 3.7 %collective-permute-start.3 = (bf16[2,2,8,64,128]{4,3,2,1,0:T(8,128)(2,1)}, bf16[2,2,8,64,128]{4,3,2,1,0:T(8,128)(2,1)S(1)}, u32[]{:S(2)}, u32[]{:S(2)}) collective-permute-start(bf16[2,2,8,64,128]{4,3,2,1,0:T(8,128)(2,1)} %get-tuple-element.22), channel_id=1, source_target_pairs={{0,24},{4,28},{8,0},{12,4},{16,8},{20,12},{24,16},{28,20},{1,25},{... | collective-permute-start | bytes 1572872 | tf_op jit(solution)/shard_map/ppermute | solution.py:165
  35.8 2.4 %copy.26 = bf16[8,128,1024]{1,2,0:T(8,128)(2,1)} copy(bf16[8,128,1024]{2,1,0:T(8,128)(2,1)S(1)} %copy-done.6) | data formatting | bytes 4194304 | tf_op args[2]
  38.2 3.0 %copy.27 = bf16[8,128,8,128]{3,1,2,0:T(8,128)(2,1)S(1)} copy(bf16[8,128,8,128]{1,3,2,0:T(8,128)(2,1)} %bitcast.124) | data formatting | bytes 4194304 | tf_op jit(solution)/shard_map/reshape | solution.py:17
  41.2 3.9 %copy.29 = bf16[8,128,1024]{1,2,0:T(8,128)(2,1)} copy(bf16[8,128,1024]{2,1,0:T(8,128)(2,1)} %param.8) | data formatting | bytes 4194304 | tf_op args[3]
  45.1 3.9 %copy.30 = bf16[8,128,8,128]{3,1,2,0:T(8,128)(2,1)} copy(bf16[8,128,8,128]{1,3,2,0:T(8,128)(2,1)} %bitcast.125) | data formatting | bytes 4194304 | tf_op jit(solution)/shard_map/reshape | solution.py:17
  50.3 3.0 %gather_fusion.2 = bf16[16,8,128,128]{3,2,1,0:T(8,128)(2,1)} fusion(bf16[8,8,128,128]{3,2,1,0:T(8,128)(2,1)S(1)} %bitcast.120, s32[1024]{0:T(1024)S(1)} %pad_clamp_fusion.2), kind=kCustom, calls=%fused_computation.2 | custom fusion | bytes 8388672 | tf_op jit(solution)/shard_map/gather | solution.py:216
  53.3 4.7 %gather_fusion.3 = bf16[16,8,128,128]{3,2,1,0:T(8,128)(2,1)} fusion(bf16[8,8,128,128]{3,2,1,0:T(8,128)(2,1)} %bitcast.121, s32[1024]{0:T(1024)S(1)} %pad_clamp_fusion.2), kind=kCustom, calls=%fused_computation.3 | custom fusion | bytes 8388672 | tf_op jit(solution)/shard_map/gather | solution.py:217
  58.1 3.9 %collective-permute-start.5 = (bf16[2,2,8,64,128]{4,3,2,1,0:T(8,128)(2,1)S(1)}, bf16[2,2,8,64,128]{4,3,2,1,0:T(8,128)(2,1)S(1)}, u32[]{:S(2)}, u32[]{:S(2)}) collective-permute-start(bf16[2,2,8,64,128]{4,3,2,1,0:T(8,128)(2,1)S(1)} %copy-done.8), channel_id=1, source_target_pairs={{0,20},{4,24},{8,28},{12,0},{16,4},{20,8},{24,12},{28,16},{1,21},{... | collective-permute-start | bytes 1572872 | tf_op jit(solution)/shard_map/ppermute | solution.py:165
  62.0 1.9 bitcast_dynamic-update-slice_fusion.6
  63.8 1.9 bitcast_dynamic-update-slice_fusion.5
  65.8 1.9 bitcast_dynamic-update-slice_fusion.4
  67.6 0.8 bitcast_dynamic-update-slice_fusion.3
  68.5 21.0 %collective-permute-done.4 = bf16[2,2,8,64,128]{4,3,2,1,0:T(8,128)(2,1)S(1)} collective-permute-done((bf16[2,2,8,64,128]{4,3,2,1,0:T(8,128)(2,1)}, bf16[2,2,8,64,128]{4,3,2,1,0:T(8,128)(2,1)S(1)}, u32[]{:S(2)}, u32[]{:S(2)}) %collective-permute-start.4) | collective-permute-done | bytes 524320 | tf_op jit(solution)/shard_map/ppermute | solution.py:165
  89.5 0.8 bitcast_dynamic-update-slice_fusion.2
  90.3 0.8 bitcast_dynamic-update-slice_fusion.1
  91.1 31.9 %collective-permute-done.6 = bf16[2,2,8,64,128]{4,3,2,1,0:T(8,128)(2,1)S(1)} collective-permute-done((bf16[2,2,8,64,128]{4,3,2,1,0:T(8,128)(2,1)S(1)}, bf16[2,2,8,64,128]{4,3,2,1,0:T(8,128)(2,1)S(1)}, u32[]{:S(2)}, u32[]{:S(2)}) %collective-permute-start.6) | collective-permute-done | bytes 524320 | tf_op jit(solution)/shard_map/ppermute | solution.py:165
  123.0 0.9 bitcast_dynamic-update-slice_fusion
  123.8 6.6 %multiply_reduce_fusion.1 = (f32[16,8,64]{2,1,0:T(8,128)S(1)}, f32[16,8,64,128]{3,2,1,0:T(8,128)}) fusion(bf16[16,8,128,128]{3,2,1,0:T(8,128)(2,1)S(1)} %copy-done.3, bf16[16,2,8,64,128]{4,3,2,1,0:T(8,128)(2,1)} %bitcast.18.pair_ref), kind=kOutput, calls=%fused_computation.12 | convolution fusion | flops 270524416 | bytes 10518528 | tf_op jit(solution)/shard_map/bhid,bhjd->bhij/dot_general | solution.py:220
  130.5 9.0 %fusion = (f32[16,8,64]{2,1,0:T(8,128)S(1)}, f32[16,8,64]{2,1,0:T(8,128)S(1)}, f32[16,8,64,128]{3,2,1,0:T(8,128)}) fusion(f32[16,8,64,128]{3,2,1,0:T(8,128)} %get-tuple-element.44, f32[16,8,64]{2,1,0:T(8,128)S(1)} %get-tuple-element.43, bf16[16,8,128,128]{3,2,1,0:T(8,128)(2,1)} %gather_fusion.3, bf16[16,2,8,64,128]{4,3,2,1,0:T(8,128)(2,1)} %bitcast.18.pair_ref), kind=kOutput, calls=%fused_computation.10 | convolution fusion | flops 273661952 | bytes 14778368 | tf_op jit(solution)/shard_map/bhid,bhjd->bhij/dot_general | solution.py:223
  139.7 0.7 pad_maximum_fusion
  140.4 3.9 %all-to-all-start.1 = ((f32[16,3,512]{2,1,0:T(4,128)}), f32[16,3,512]{2,1,0:T(4,128)S(1)}, u32[]{:S(2)}, u32[]{:S(2)}) async-start(f32[16,3,512]{2,1,0:T(4,128)} %pad_maximum_fusion), calls=%async_computation.1 | async-start | bytes 262144 | tf_op jit(solution)/shard_map/all_to_all | solution.py:231
  144.3 7.3 %all-to-all-done.1 = f32[16,3,512]{2,1,0:T(4,128)S(1)} async-done(((f32[16,3,512]{2,1,0:T(4,128)}), f32[16,3,512]{2,1,0:T(4,128)S(1)}, u32[]{:S(2)}, u32[]{:S(2)}) %all-to-all-start.1) | async-done | bytes 98336 | tf_op jit(solution)/shard_map/all_to_all | solution.py:231
  153.2 9.3 %all_to_all.18 = f32[16,2,512]{2,1,0:T(2,128)S(1)} all-to-all(f32[16,2,512]{2,1,0:T(2,128)S(1)} %gather_fusion.5), channel_id=1, replica_groups=mesh['seq'=8,'mp'=4] {'seq'}, dimensions={0} | all-to-all | bytes 131072 | tf_op jit(solution)/shard_map/all_to_all | solution.py:243
  162.9 6.6 %fusion.1 = (bf16[16,8,64,128]{3,2,1,0:T(8,128)(2,1)}, bf16[16,8,64,128]{3,2,1,0:T(8,128)(2,1)S(1)}) fusion(f32[16,8,64,128]{3,2,1,0:T(8,128)} %get-tuple-element.44, f32[16,8,64]{2,1,0:T(8,128)S(1)} %sub.87, f32[16,8,64,128]{3,2,1,0:T(8,128)} %get-tuple-element.45, f32[16,8,64]{2,1,0:T(8,128)S(1)} %sub.90), kind=kLoop, calls=%fused_computation.11 | loop fusion | flops 7340032 | bytes 12648448 | tf_op jit(solution)/shard_map/convert_element_type | solution.py:251
  169.4 1.2 convolution_convert_fusion
  170.6 1.9 broadcast_in_dim.79
  172.5 1.0 dynamic-slice_bitcast_fusion.7
  173.9 4.3 %collective-permute-start.8 = (bf16[2,8,64,128]{3,2,1,0:T(8,128)(2,1)}, bf16[2,8,64,128]{3,2,1,0:T(8,128)(2,1)}, u32[]{:S(2)}, u32[]{:S(2)}) collective-permute-start(bf16[2,8,64,128]{3,2,1,0:T(8,128)(2,1)} %get-tuple-element.32), channel_id=1, source_target_pairs={{0,28},{4,0},{8,4},{12,8},{16,12},{20,16},{24,20},{28,24},{1,29},{... | collective-permute-start | bytes 786440 | tf_op jit(solution)/shard_map/ppermute | solution.py:165
  178.3 3.8 %collective-permute-start.10 = (bf16[2,8,64,128]{3,2,1,0:T(8,128)(2,1)S(1)}, bf16[2,8,64,128]{3,2,1,0:T(8,128)(2,1)S(1)}, u32[]{:S(2)}, u32[]{:S(2)}) collective-permute-start(bf16[2,8,64,128]{3,2,1,0:T(8,128)(2,1)S(1)} %get-tuple-element.30), channel_id=1, source_target_pairs={{0,24},{4,28},{8,0},{12,4},{16,8},{20,12},{24,16},{28,20},{1,25},{... | collective-permute-start | bytes 786440 | tf_op jit(solution)/shard_map/ppermute | solution.py:165
  182.1 1.6 copy-done
  183.7 14.7 %shard_map.78 = (bf16[8,128,1024]{2,1,0:T(8,128)(2,1)}, bf16[8,128,1024]{2,1,0:T(8,128)(2,1)}) custom-call(s32[16]{0:T(128)S(1)} %all_to_all.14.rows_ref, bf16[16,8,64,128]{3,2,1,0:T(8,128)(2,1)S(1)} %copy-done, bf16[16,8,64,128]{3,2,1,0:T(8,128)(2,1)S(1)} %get-tuple-element.18.grads_ref, bf16[16,2,8,64,128]{4,3,2,1,0:T(8,128)(2,1)} %bitcast.18.pair_ref), custom_call_target="tpu_custom_call" | custom-call | tf_op jit(solution)/shard_map/pallas_call | solution.py:74
  198.5 3.8 %collective-permute-start.12 = (bf16[2,8,64,128]{3,2,1,0:T(8,128)(2,1)S(1)}, bf16[2,8,64,128]{3,2,1,0:T(8,128)(2,1)S(1)}, u32[]{:S(2)}, u32[]{:S(2)}) collective-permute-start(bf16[2,8,64,128]{3,2,1,0:T(8,128)(2,1)S(1)} %get-tuple-element.28), channel_id=1, source_target_pairs={{0,20},{4,24},{8,28},{12,0},{16,4},{20,8},{24,12},{28,16},{1,21},{... | collective-permute-start | bytes 786440 | tf_op jit(solution)/shard_map/ppermute | solution.py:165
  202.3 1.7 bitcast_dynamic-update-slice_fusion.13
  204.0 1.7 bitcast_dynamic-update-slice_fusion.12
  207.1 0.7 bitcast_dynamic-update-slice_fusion.9
  208.5 0.7 bitcast_dynamic-update-slice_fusion.8
  209.2 11.7 %collective-permute-done.13 = bf16[2,8,64,128]{3,2,1,0:T(8,128)(2,1)S(1)} collective-permute-done((bf16[2,8,64,128]{3,2,1,0:T(8,128)(2,1)S(1)}, bf16[2,8,64,128]{3,2,1,0:T(8,128)(2,1)S(1)}, u32[]{:S(2)}, u32[]{:S(2)}) %collective-permute-start.13) | collective-permute-done | bytes 262176 | tf_op jit(solution)/shard_map/ppermute | solution.py:165
  220.9 0.7 bitcast_dynamic-update-slice_fusion.7
  221.6 3.4 %shard_map.77 = bf16[8,64,1024]{2,1,0:T(8,128)(2,1)} custom-call(s32[16]{0:T(128)S(1)} %get-tuple-element.15.target_ref, bf16[16,8,64,128]{3,2,1,0:T(8,128)(2,1)} %bitcast.50.back_ref), custom_call_target="tpu_custom_call" | custom-call | tf_op jit(solution)/shard_map/pallas_call | solution.py:145
  (74 shorter events, 8.9 us)
Async XLA Ops:
  8.8 40.3 %all-to-all-start = ((s32[8,2,1]{1,2,0:T(1,128)}), s32[8,2,1]{1,2,0:T(1,128)S(1)}, u32[]{:S(2)}, u32[]{:S(2)}) async-start(s32[8,2,1]{1,2,0:T(1,128)} %bitcast.22), calls=%async_computation | async-start | bytes 8192 | tf_op jit(solution)/shard_map/all_to_all | solution.py:211
  15.8 1.2 copy-start.1
  17.0 1.2 copy-start.2
  21.5 3.0 %copy-start.5 = (bf16[16,2,8,64,128]{4,3,2,1,0:T(8,128)(2,1)S(1)}, bf16[16,2,8,64,128]{4,3,2,1,0:T(8,128)(2,1)}, u32[]{:S(2)}) copy-start(bf16[16,2,8,64,128]{4,3,2,1,0:T(8,128)(2,1)} %shard_map.76) | copy-start | bytes 12582916
  24.6 11.2 %copy-start.6 = (bf16[8,128,1024]{2,1,0:T(8,128)(2,1)S(1)}, bf16[8,128,1024]{2,1,0:T(8,128)(2,1)}, u32[]{:S(2)}) copy-start(bf16[8,128,1024]{2,1,0:T(8,128)(2,1)} %param.7) | copy-start | bytes 6291460
  27.0 31.1 %collective-permute-start = (bf16[2,2,8,64,128]{4,3,2,1,0:T(8,128)(2,1)}, bf16[2,2,8,64,128]{4,3,2,1,0:T(8,128)(2,1)}, u32[]{:S(2)}, u32[]{:S(2)}) collective-permute-start(bf16[2,2,8,64,128]{4,3,2,1,0:T(8,128)(2,1)} %get-tuple-element.25), channel_id=1, source_target_pairs={{0,4},{4,8},{8,12},{12,16},{16,20},{20,24},{24,28},{28,0},{1,5},{5... | collective-permute-start | bytes 1572872 | tf_op jit(solution)/shard_map/ppermute | solution.py:165
  29.0 34.8 %collective-permute-start.1 = (bf16[2,2,8,64,128]{4,3,2,1,0:T(8,128)(2,1)}, bf16[2,2,8,64,128]{4,3,2,1,0:T(8,128)(2,1)}, u32[]{:S(2)}, u32[]{:S(2)}) collective-permute-start(bf16[2,2,8,64,128]{4,3,2,1,0:T(8,128)(2,1)} %get-tuple-element.24), channel_id=1, source_target_pairs={{0,28},{4,0},{8,4},{12,8},{16,12},{20,16},{24,20},{28,24},{1,29},{... | collective-permute-start | bytes 1572872 | tf_op jit(solution)/shard_map/ppermute | solution.py:165
  31.7 34.1 %collective-permute-start.2 = (bf16[2,2,8,64,128]{4,3,2,1,0:T(8,128)(2,1)}, bf16[2,2,8,64,128]{4,3,2,1,0:T(8,128)(2,1)}, u32[]{:S(2)}, u32[]{:S(2)}) collective-permute-start(bf16[2,2,8,64,128]{4,3,2,1,0:T(8,128)(2,1)} %get-tuple-element.23), channel_id=1, source_target_pairs={{0,8},{4,12},{8,16},{12,20},{16,24},{20,28},{24,0},{28,4},{1,9},{5... | collective-permute-start | bytes 1572872 | tf_op jit(solution)/shard_map/ppermute | solution.py:165
  31.9 35.8 %collective-permute-start.3 = (bf16[2,2,8,64,128]{4,3,2,1,0:T(8,128)(2,1)}, bf16[2,2,8,64,128]{4,3,2,1,0:T(8,128)(2,1)S(1)}, u32[]{:S(2)}, u32[]{:S(2)}) collective-permute-start(bf16[2,2,8,64,128]{4,3,2,1,0:T(8,128)(2,1)} %get-tuple-element.22), channel_id=1, source_target_pairs={{0,24},{4,28},{8,0},{12,4},{16,8},{20,12},{24,16},{28,20},{1,25},{... | collective-permute-start | bytes 1572872 | tf_op jit(solution)/shard_map/ppermute | solution.py:165
  35.5 53.9 %collective-permute-start.4 = (bf16[2,2,8,64,128]{4,3,2,1,0:T(8,128)(2,1)}, bf16[2,2,8,64,128]{4,3,2,1,0:T(8,128)(2,1)S(1)}, u32[]{:S(2)}, u32[]{:S(2)}) collective-permute-start(bf16[2,2,8,64,128]{4,3,2,1,0:T(8,128)(2,1)} %get-tuple-element.21), channel_id=1, source_target_pairs={{0,12},{4,16},{8,20},{12,24},{16,28},{20,0},{24,4},{28,8},{1,13},{... | collective-permute-start | bytes 1572872 | tf_op jit(solution)/shard_map/ppermute | solution.py:165
  53.3 4.7 %copy-start.8 = (bf16[2,2,8,64,128]{4,3,2,1,0:T(8,128)(2,1)S(1)}, bf16[2,2,8,64,128]{4,3,2,1,0:T(8,128)(2,1)}, u32[]{:S(2)}) copy-start(bf16[2,2,8,64,128]{4,3,2,1,0:T(8,128)(2,1)} %get-tuple-element.20) | copy-start | bytes 1572868
  53.3 10.5 %copy-start.7 = (bf16[2,2,8,64,128]{4,3,2,1,0:T(8,128)(2,1)S(1)}, bf16[2,2,8,64,128]{4,3,2,1,0:T(8,128)(2,1)}, u32[]{:S(2)}) copy-start(bf16[2,2,8,64,128]{4,3,2,1,0:T(8,128)(2,1)} %get-tuple-element.19) | copy-start | bytes 1572868
  58.1 65.8 %copy-start.3 = (bf16[16,8,128,128]{3,2,1,0:T(8,128)(2,1)S(1)}, bf16[16,8,128,128]{3,2,1,0:T(8,128)(2,1)}, u32[]{:S(2)}) copy-start(bf16[16,8,128,128]{3,2,1,0:T(8,128)(2,1)} %gather_fusion.2) | copy-start | bytes 12582916
  58.1 32.2 %collective-permute-start.5 = (bf16[2,2,8,64,128]{4,3,2,1,0:T(8,128)(2,1)S(1)}, bf16[2,2,8,64,128]{4,3,2,1,0:T(8,128)(2,1)S(1)}, u32[]{:S(2)}, u32[]{:S(2)}) collective-permute-start(bf16[2,2,8,64,128]{4,3,2,1,0:T(8,128)(2,1)S(1)} %copy-done.8), channel_id=1, source_target_pairs={{0,20},{4,24},{8,28},{12,0},{16,4},{20,8},{24,12},{28,16},{1,21},{... | collective-permute-start | bytes 1572872 | tf_op jit(solution)/shard_map/ppermute | solution.py:165
  63.8 59.1 %collective-permute-start.6 = (bf16[2,2,8,64,128]{4,3,2,1,0:T(8,128)(2,1)S(1)}, bf16[2,2,8,64,128]{4,3,2,1,0:T(8,128)(2,1)S(1)}, u32[]{:S(2)}, u32[]{:S(2)}) collective-permute-start(bf16[2,2,8,64,128]{4,3,2,1,0:T(8,128)(2,1)S(1)} %copy-done.7), channel_id=1, source_target_pairs={{0,16},{4,20},{8,24},{12,28},{16,0},{20,4},{24,8},{28,12},{1,17},{... | collective-permute-start | bytes 1572872 | tf_op jit(solution)/shard_map/ppermute | solution.py:165
  140.4 11.2 %all-to-all-start.1 = ((f32[16,3,512]{2,1,0:T(4,128)}), f32[16,3,512]{2,1,0:T(4,128)S(1)}, u32[]{:S(2)}, u32[]{:S(2)}) async-start(f32[16,3,512]{2,1,0:T(4,128)} %pad_maximum_fusion), calls=%async_computation.1 | async-start | bytes 262144 | tf_op jit(solution)/shard_map/all_to_all | solution.py:231
  162.9 6.6 %copy-start.4 = (bf16[16,8,128,128]{3,2,1,0:T(8,128)(2,1)S(1)}, bf16[16,8,128,128]{3,2,1,0:T(8,128)(2,1)}, u32[]{:S(2)}) copy-start(bf16[16,8,128,128]{3,2,1,0:T(8,128)(2,1)} %gather_fusion.2) | copy-start | bytes 12582916
  173.5 25.0 %collective-permute-start.7 = (bf16[2,8,64,128]{3,2,1,0:T(8,128)(2,1)}, bf16[2,8,64,128]{3,2,1,0:T(8,128)(2,1)}, u32[]{:S(2)}, u32[]{:S(2)}) collective-permute-start(bf16[2,8,64,128]{3,2,1,0:T(8,128)(2,1)} %get-tuple-element.33), channel_id=1, source_target_pairs={{0,4},{4,8},{8,12},{12,16},{16,20},{20,24},{24,28},{28,0},{1,5},{5... | collective-permute-start | bytes 786440 | tf_op jit(solution)/shard_map/ppermute | solution.py:165
  173.9 30.1 %collective-permute-start.8 = (bf16[2,8,64,128]{3,2,1,0:T(8,128)(2,1)}, bf16[2,8,64,128]{3,2,1,0:T(8,128)(2,1)}, u32[]{:S(2)}, u32[]{:S(2)}) collective-permute-start(bf16[2,8,64,128]{3,2,1,0:T(8,128)(2,1)} %get-tuple-element.32), channel_id=1, source_target_pairs={{0,28},{4,0},{8,4},{12,8},{16,12},{20,16},{24,20},{28,24},{1,29},{... | collective-permute-start | bytes 786440 | tf_op jit(solution)/shard_map/ppermute | solution.py:165
  178.3 27.3 %collective-permute-start.9 = (bf16[2,8,64,128]{3,2,1,0:T(8,128)(2,1)S(1)}, bf16[2,8,64,128]{3,2,1,0:T(8,128)(2,1)S(1)}, u32[]{:S(2)}, u32[]{:S(2)}) collective-permute-start(bf16[2,8,64,128]{3,2,1,0:T(8,128)(2,1)S(1)} %get-tuple-element.31), channel_id=1, source_target_pairs={{0,8},{4,12},{8,16},{12,20},{16,24},{20,28},{24,0},{28,4},{1,9},{5... | collective-permute-start | bytes 786440 | tf_op jit(solution)/shard_map/ppermute | solution.py:165
  178.3 28.0 %collective-permute-start.10 = (bf16[2,8,64,128]{3,2,1,0:T(8,128)(2,1)S(1)}, bf16[2,8,64,128]{3,2,1,0:T(8,128)(2,1)S(1)}, u32[]{:S(2)}, u32[]{:S(2)}) collective-permute-start(bf16[2,8,64,128]{3,2,1,0:T(8,128)(2,1)S(1)} %get-tuple-element.30), channel_id=1, source_target_pairs={{0,24},{4,28},{8,0},{12,4},{16,8},{20,12},{24,16},{28,20},{1,25},{... | collective-permute-start | bytes 786440 | tf_op jit(solution)/shard_map/ppermute | solution.py:165
  182.1 24.9 %collective-permute-start.11 = (bf16[2,8,64,128]{3,2,1,0:T(8,128)(2,1)S(1)}, bf16[2,8,64,128]{3,2,1,0:T(8,128)(2,1)S(1)}, u32[]{:S(2)}, u32[]{:S(2)}) collective-permute-start(bf16[2,8,64,128]{3,2,1,0:T(8,128)(2,1)S(1)} %get-tuple-element.29), channel_id=1, source_target_pairs={{0,12},{4,16},{8,20},{12,24},{16,28},{20,0},{24,4},{28,8},{1,13},{... | collective-permute-start | bytes 786440 | tf_op jit(solution)/shard_map/ppermute | solution.py:165
  182.1 1.6 copy-start
  198.5 10.0 %collective-permute-start.12 = (bf16[2,8,64,128]{3,2,1,0:T(8,128)(2,1)S(1)}, bf16[2,8,64,128]{3,2,1,0:T(8,128)(2,1)S(1)}, u32[]{:S(2)}, u32[]{:S(2)}) collective-permute-start(bf16[2,8,64,128]{3,2,1,0:T(8,128)(2,1)S(1)} %get-tuple-element.28), channel_id=1, source_target_pairs={{0,20},{4,24},{8,28},{12,0},{16,4},{20,8},{24,12},{28,16},{1,21},{... | collective-permute-start | bytes 786440 | tf_op jit(solution)/shard_map/ppermute | solution.py:165
  204.0 16.9 %collective-permute-start.13 = (bf16[2,8,64,128]{3,2,1,0:T(8,128)(2,1)S(1)}, bf16[2,8,64,128]{3,2,1,0:T(8,128)(2,1)S(1)}, u32[]{:S(2)}, u32[]{:S(2)}) collective-permute-start(bf16[2,8,64,128]{3,2,1,0:T(8,128)(2,1)S(1)} %get-tuple-element.27), channel_id=1, source_target_pairs={{0,16},{4,20},{8,24},{12,28},{16,0},{20,4},{24,8},{28,12},{1,17},{... | collective-permute-start | bytes 786440 | tf_op jit(solution)/shard_map/ppermute | solution.py:165

commit v16 on v13

--- a/solution.py
+++ b/solution.py
@@ -150,6 +150,18 @@
     )(jnp.clip(target, 0, slot_total - 1), query_back)
 
 
+def gather_over(block, axis_name, axis_count):
+    me = lax.axis_index(axis_name)
+    result = jnp.zeros((axis_count,) + block.shape, block.dtype)
+    result = lax.dynamic_update_index_in_dim(result, block, me, axis=0)
+    for shift in range(1, axis_count):
+        sent = lax.ppermute(
+            block, axis_name, perm=[(i, (i + shift) % axis_count) for i in range(axis_count)]
+        )
+        result = lax.dynamic_update_index_in_dim(result, sent, (me - shift) % axis_count, axis=0)
+    return result
+
+
 def seq_exchange(blocks, seq_count):
     me = lax.axis_index("seq")
     result = jnp.zeros_like(blocks)
@@ -170,7 +182,9 @@
 
 def per_device(queries, out_grad, row_keys, row_values, neighbours):
     seq_count = lax.axis_size("seq")
-    own_lists = lax.all_gather(neighbours, "mp", axis=0, tiled=True)
+    own_lists = gather_over(neighbours, "mp", lax.axis_size("mp")).reshape(
+        (-1,) + neighbours.shape[1:]
+    )
     span_count = queries.shape[0]
     rows_here = row_keys.shape[0]
     width_here = queries.shape[2]

time: 224 us -> 223 us (level)
  blocking collectives: 6.25 us -> 0 us
  starting transfers between devices: 29.8 us -> 33.8 us
    all_gather x1 -> x0, blocking collectives: 6.25 us -> none  [per_device(): own_lists = lax.all_gather(neighbours, 'mp', axis=0, tiled=True)]
    ppermute x0 -> x3, starting transfers between devices: none -> 4.46 us  [gather_over(): lax.ppermute(block, axis_name, perm=[(i, (i + shift) % axis_count) for i...]
  transfers between devices with their start and end apart: 11 -> 14, of which waited for: 5 -> 6; matrix products, arithmetic and copies ran while one was open for 13% -> 14% of each run, Pallas kernels for 8% -> 8%
where the time goes in v16:
time: 223 us; the launch traced here: 219 us
  waiting for transfers between devices  95.2 us (43%)
  local copies, waits for them, and re-layouts  40.9 us (18%)
  starting transfers between devices  33.8 us (15%)
  Pallas kernels  21.5 us (10%)
  matrix products  18 us (8%)
  other arithmetic  8.74 us (4%)
    all_to_all x1, waiting for transfers between devices, per_device(): lax.all_to_all(pair_send, 'seq', split_axis=0, concat_axis=0, tiled=True)  71.2 us
    pallas_call x1, Pallas kernels, kv_grads(): pl.pallas_call(kv_kernel, grid_spec=grid_spec, out_shape=[out_shape, out_...  14.7 us
    unnamed x12, local copies, waits for them, and re-layouts  10.3 us
    ppermute x7, starting transfers between devices, seq_exchange(): lax.ppermute(lax.dynamic_index_in_dim(blocks, (me + shift) % seq_count, k...  10.2 us
    ppermute x7, waiting for transfers between devices, seq_exchange(): lax.ppermute(lax.dynamic_index_in_dim(blocks, (me + shift) % seq_count, k...  9.38 us
    dot_general x1, matrix products, per_device(): jnp.einsum('bhid,bhjd->bhij', grad_heads, value_heads, preferred_element_...  8.99 us
    dot_general x1, matrix products, per_device(): jnp.einsum('bhid,bhjd->bhij', query_heads, key_heads, preferred_element_t...  7.78 us
    all_to_all x1, waiting for transfers between devices, per_device(): back = lax.all_to_all(part, 'seq', split_axis=0, concat_axis=0, tiled=True)  7.32 us
  transfers between devices with their start and end apart: 14, of which 6 were waited for; matrix products, arithmetic and copies ran while one was open for 14% of the time, Pallas kernels for 8%

profile of v16, /device:TPU:0, one launch (start us, length us, event | category | flops | bytes accessed | tf_op | source)
XLA Modules:
  0.0 219.0 jit_solution(15271644484260182229)
XLA Ops:
  1.1 2.6 %collective-permute-start.1 = (s32[2,2]{1,0:T(2,128)}, s32[2,2]{1,0:T(2,128)S(1)}, u32[]{:S(2)}, u32[]{:S(2)}) collective-permute-start(s32[2,2]{1,0:T(2,128)} %param.9), channel_id=1, source_target_pairs={{0,2},{1,3},{2,0},{3,1},{4,6},{5,7},{6,4},{7,5},{8,10},{9,11},{10,... | collective-permute-start | bytes 56 | tf_op jit(solution)/shard_map/ppermute | solution.py:158
  3.7 1.4 collective-permute-start.2
  5.1 0.7 constant_dynamic-update-slice_fusion.3
  5.8 0.8 collective-permute-done.2
  7.2 0.7 gather_fusion.1
  7.8 0.7 select_n.238
  8.5 5.8 %all-to-all-start.1 = ((s32[8,2,1]{1,2,0:T(1,128)}), s32[8,2,1]{1,2,0:T(1,128)S(1)}, u32[]{:S(2)}, u32[]{:S(2)}) async-start(s32[8,2,1]{1,2,0:T(1,128)} %bitcast.9), calls=%async_computation.1 | async-start | bytes 8192 | tf_op jit(solution)/shard_map/all_to_all | solution.py:215
  15.0 1.2 copy-done.1
  16.2 1.2 copy-done.2
  17.5 3.3 %shard_map.76 = bf16[16,2,8,64,128]{4,3,2,1,0:T(8,128)(2,1)} custom-call(s32[16]{0:T(128)S(1)} %broadcast_clamp_fusion.1.span_ref, bf16[8,64,1024]{2,1,0:T(8,128)(2,1)S(1)} %copy-done.1, bf16[8,64,1024]{2,1,0:T(8,128)(2,1)S(1)} %copy-done.2), custom_call_target="tpu_custom_call" | custom-call | tf_op jit(solution)/shard_map/pallas_call | solution.py:112
  20.8 6.1 %all-to-all-start = ((bf16[16,2,8,64,128]{4,3,2,1,0:T(8,128)(2,1)}), bf16[16,2,8,64,128]{4,3,2,1,0:T(8,128)(2,1)}, u32[]{:S(2)}, u32[]{:S(2)}) async-start(bf16[16,2,8,64,128]{4,3,2,1,0:T(8,128)(2,1)} %shard_map.76), calls=%async_computation | async-start | bytes 8388608 | tf_op jit(solution)/shard_map/all_to_all | solution.py:214
  26.9 2.4 %copy.26 = bf16[8,128,1024]{1,2,0:T(8,128)(2,1)} copy(bf16[8,128,1024]{2,1,0:T(8,128)(2,1)S(1)} %copy-done.4) | data formatting | bytes 4194304 | tf_op args[2]
  29.3 3.0 %copy.27 = bf16[8,128,8,128]{3,1,2,0:T(8,128)(2,1)S(1)} copy(bf16[8,128,8,128]{1,3,2,0:T(8,128)(2,1)} %bitcast.100) | data formatting | bytes 4194304 | tf_op jit(solution)/shard_map/reshape | solution.py:17
  32.4 3.9 %copy.29 = bf16[8,128,1024]{1,2,0:T(8,128)(2,1)} copy(bf16[8,128,1024]{2,1,0:T(8,128)(2,1)} %param.8) | data formatting | bytes 4194304 | tf_op args[3]
  36.3 3.9 %copy.30 = bf16[8,128,8,128]{3,1,2,0:T(8,128)(2,1)} copy(bf16[8,128,8,128]{1,3,2,0:T(8,128)(2,1)} %bitcast.101) | data formatting | bytes 4194304 | tf_op jit(solution)/shard_map/reshape | solution.py:17
  40.8 0.7 fusion.15
  41.6 3.1 %gather_fusion.2 = bf16[16,8,128,128]{3,2,1,0:T(8,128)(2,1)} fusion(bf16[8,8,128,128]{3,2,1,0:T(8,128)(2,1)S(1)} %bitcast.97, s32[1024]{0:T(1024)S(1)} %pad_clamp_fusion.2), kind=kCustom, calls=%fused_computation.2 | custom fusion | bytes 8388672 | tf_op jit(solution)/shard_map/gather | solution.py:220
  44.6 4.6 %gather_fusion.3 = bf16[16,8,128,128]{3,2,1,0:T(8,128)(2,1)} fusion(bf16[8,8,128,128]{3,2,1,0:T(8,128)(2,1)} %bitcast.98, s32[1024]{0:T(1024)S(1)} %pad_clamp_fusion.2), kind=kCustom, calls=%fused_computation.3 | custom fusion | bytes 8388672 | tf_op jit(solution)/shard_map/gather | solution.py:221
  49.3 71.2 %all-to-all-done.pair_ref = bf16[16,2,8,64,128]{4,3,2,1,0:T(8,128)(2,1)} async-done(((bf16[16,2,8,64,128]{4,3,2,1,0:T(8,128)(2,1)}), bf16[16,2,8,64,128]{4,3,2,1,0:T(8,128)(2,1)}, u32[]{:S(2)}, u32[]{:S(2)}) %all-to-all-start) | async-done | bytes 4194336 | tf_op jit(solution)/shard_map/all_to_all | solution.py:214
  120.4 7.8 %multiply_reduce_fusion.1 = (f32[16,8,64]{2,1,0:T(8,128)S(1)}, f32[16,8,64,128]{3,2,1,0:T(8,128)}) fusion(bf16[16,8,128,128]{3,2,1,0:T(8,128)(2,1)} %gather_fusion.2, bf16[16,2,8,64,128]{4,3,2,1,0:T(8,128)(2,1)} %all-to-all-done.pair_ref), kind=kOutput, calls=%fused_computation.12 | convolution fusion | flops 270524416 | bytes 10518528 | tf_op jit(solution)/shard_map/bhid,bhjd->bhij/dot_general | solution.py:224
  128.3 9.0 %fusion = (f32[16,8,64]{2,1,0:T(8,128)S(1)}, f32[16,8,64]{2,1,0:T(8,128)S(1)}, f32[16,8,64,128]{3,2,1,0:T(8,128)}) fusion(f32[16,8,64,128]{3,2,1,0:T(8,128)} %get-tuple-element.36, f32[16,8,64]{2,1,0:T(8,128)S(1)} %get-tuple-element.35, bf16[16,8,128,128]{3,2,1,0:T(8,128)(2,1)} %gather_fusion.3, bf16[16,2,8,64,128]{4,3,2,1,0:T(8,128)(2,1)} %all-to-all-done.pair_ref), kind=kOutput, calls=%fused_computation.10 | convolution fusion | flops 273661952 | bytes 14778368 | tf_op jit(solution)/shard_map/bhid,bhjd->bhij/dot_general | solution.py:227
  137.5 0.7 pad_maximum_fusion
  138.2 3.6 %all-to-all-start.2 = ((f32[16,3,512]{2,1,0:T(4,128)}), f32[16,3,512]{2,1,0:T(4,128)S(1)}, u32[]{:S(2)}, u32[]{:S(2)}) async-start(f32[16,3,512]{2,1,0:T(4,128)} %pad_maximum_fusion), calls=%async_computation.2 | async-start | bytes 262144 | tf_op jit(solution)/shard_map/all_to_all | solution.py:235
  141.9 7.3 %all-to-all-done.2 = f32[16,3,512]{2,1,0:T(4,128)S(1)} async-done(((f32[16,3,512]{2,1,0:T(4,128)}), f32[16,3,512]{2,1,0:T(4,128)S(1)}, u32[]{:S(2)}, u32[]{:S(2)}) %all-to-all-start.2) | async-done | bytes 98336 | tf_op jit(solution)/shard_map/all_to_all | solution.py:235
  150.2 1.2 gather_fusion.5
  151.4 3.5 %all-to-all-start.3 = ((f32[16,2,512]{2,1,0:T(2,128)}), f32[16,2,512]{2,1,0:T(2,128)S(1)}, u32[]{:S(2)}, u32[]{:S(2)}) async-start(f32[16,2,512]{2,1,0:T(2,128)} %gather_fusion.5), calls=%async_computation.3 | async-start | bytes 131072 | tf_op jit(solution)/shard_map/all_to_all | solution.py:247
  155.1 6.6 %all-to-all-done.3 = f32[16,2,512]{2,1,0:T(2,128)S(1)} async-done(((f32[16,2,512]{2,1,0:T(2,128)}), f32[16,2,512]{2,1,0:T(2,128)S(1)}, u32[]{:S(2)}, u32[]{:S(2)}) %all-to-all-start.3) | async-done | bytes 65568 | tf_op jit(solution)/shard_map/all_to_all | solution.py:247
  162.0 6.6 %fusion.1 = (bf16[16,8,64,128]{3,2,1,0:T(8,128)(2,1)}, bf16[16,8,64,128]{3,2,1,0:T(8,128)(2,1)S(1)}) fusion(f32[16,8,64,128]{3,2,1,0:T(8,128)} %get-tuple-element.36, f32[16,8,64]{2,1,0:T(8,128)S(1)} %sub.85, f32[16,8,64,128]{3,2,1,0:T(8,128)} %get-tuple-element.37, f32[16,8,64]{2,1,0:T(8,128)S(1)} %sub.88), kind=kLoop, calls=%fused_computation.11 | loop fusion | flops 7340032 | bytes 12648448 | tf_op jit(solution)/shard_map/convert_element_type | solution.py:255
  168.5 1.2 convolution_convert_fusion
  169.8 1.9 broadcast_in_dim.70
  171.6 1.0 dynamic-slice_bitcast_fusion
  173.0 0.9 collective-permute-start.4
  173.9 1.3 collective-permute-start.5
  175.3 2.9 %collective-permute-start.6 = (bf16[2,8,64,128]{3,2,1,0:T(8,128)(2,1)S(1)}, bf16[2,8,64,128]{3,2,1,0:T(8,128)(2,1)S(1)}, u32[]{:S(2)}, u32[]{:S(2)}) collective-permute-start(bf16[2,8,64,128]{3,2,1,0:T(8,128)(2,1)S(1)} %get-tuple-element.22), channel_id=1, source_target_pairs={{0,16},{4,20},{8,24},{12,28},{16,0},{20,4},{24,8},{28,12},{1,17},{... | collective-permute-start | bytes 786440 | tf_op jit(solution)/shard_map/ppermute | solution.py:172
  178.4 1.6 copy-done
  180.0 14.7 %shard_map.78 = (bf16[8,128,1024]{2,1,0:T(8,128)(2,1)}, bf16[8,128,1024]{2,1,0:T(8,128)(2,1)}) custom-call(s32[16]{0:T(128)S(1)} %all_to_all.18.rows_ref, bf16[16,8,64,128]{3,2,1,0:T(8,128)(2,1)S(1)} %copy-done, bf16[16,8,64,128]{3,2,1,0:T(8,128)(2,1)S(1)} %get-tuple-element.18.grads_ref, bf16[16,2,8,64,128]{4,3,2,1,0:T(8,128)(2,1)} %all-to-all-done.pair_ref), custom_call_target="tpu_custom_call" | custom-call | tf_op jit(solution)/shard_map/pallas_call | solution.py:74
  194.8 2.5 %collective-permute-start.8 = (bf16[2,8,64,128]{3,2,1,0:T(8,128)(2,1)S(1)}, bf16[2,8,64,128]{3,2,1,0:T(8,128)(2,1)S(1)}, u32[]{:S(2)}, u32[]{:S(2)}) collective-permute-start(bf16[2,8,64,128]{3,2,1,0:T(8,128)(2,1)S(1)} %get-tuple-element.20), channel_id=1, source_target_pairs={{0,24},{4,28},{8,0},{12,4},{16,8},{20,12},{24,16},{28,20},{1,25},{... | collective-permute-start | bytes 786440 | tf_op jit(solution)/shard_map/ppermute | solution.py:172
  197.2 1.7 bitcast_dynamic-update-slice_fusion.6
  198.9 1.9 collective-permute-start.9
  200.8 1.7 bitcast_dynamic-update-slice_fusion.5
  202.5 1.4 collective-permute-done.5
  203.9 0.7 bitcast_dynamic-update-slice_fusion.4
  204.6 0.7 bitcast_dynamic-update-slice_fusion.3
  205.4 0.7 bitcast_dynamic-update-slice_fusion.2
  206.1 8.0 %collective-permute-done.8 = bf16[2,8,64,128]{3,2,1,0:T(8,128)(2,1)S(1)} collective-permute-done((bf16[2,8,64,128]{3,2,1,0:T(8,128)(2,1)S(1)}, bf16[2,8,64,128]{3,2,1,0:T(8,128)(2,1)S(1)}, u32[]{:S(2)}, u32[]{:S(2)}) %collective-permute-start.8) | collective-permute-done | bytes 262176 | tf_op jit(solution)/shard_map/ppermute | solution.py:172
  214.1 0.7 bitcast_dynamic-update-slice_fusion.1
  214.8 0.7 bitcast_dynamic-update-slice_fusion
  215.5 3.4 %shard_map.77 = bf16[8,64,1024]{2,1,0:T(8,128)(2,1)} custom-call(s32[16]{0:T(128)S(1)} %get-tuple-element.15.target_ref, bf16[16,8,64,128]{3,2,1,0:T(8,128)(2,1)} %bitcast.37.back_ref), custom_call_target="tpu_custom_call" | custom-call | tf_op jit(solution)/shard_map/pallas_call | solution.py:145
  (56 shorter events, 4.7 us)
Async XLA Ops:
  0.6 5.2 %collective-permute-start = (s32[2,2]{1,0:T(2,128)}, s32[2,2]{1,0:T(2,128)S(1)}, u32[]{:S(2)}, u32[]{:S(2)}) collective-permute-start(s32[2,2]{1,0:T(2,128)} %param.9), channel_id=1, source_target_pairs={{0,1},{1,2},{2,3},{3,0},{4,5},{5,6},{6,7},{7,4},{8,9},{9,10},{10,1... | collective-permute-start | bytes 56 | tf_op jit(solution)/shard_map/ppermute | solution.py:158
  1.1 4.7 %collective-permute-start.1 = (s32[2,2]{1,0:T(2,128)}, s32[2,2]{1,0:T(2,128)S(1)}, u32[]{:S(2)}, u32[]{:S(2)}) collective-permute-start(s32[2,2]{1,0:T(2,128)} %param.9), channel_id=1, source_target_pairs={{0,2},{1,3},{2,0},{3,1},{4,6},{5,7},{6,4},{7,5},{8,10},{9,11},{10,... | collective-permute-start | bytes 56 | tf_op jit(solution)/shard_map/ppermute | solution.py:158
  3.7 2.9 %collective-permute-start.2 = (s32[2,2]{1,0:T(2,128)}, s32[2,2]{1,0:T(2,128)S(1)}, u32[]{:S(2)}, u32[]{:S(2)}) collective-permute-start(s32[2,2]{1,0:T(2,128)} %param.9), channel_id=1, source_target_pairs={{0,3},{1,0},{2,1},{3,2},{4,7},{5,4},{6,5},{7,6},{8,11},{9,8},{10,9... | collective-permute-start | bytes 56 | tf_op jit(solution)/shard_map/ppermute | solution.py:158
  8.5 12.3 %all-to-all-start.1 = ((s32[8,2,1]{1,2,0:T(1,128)}), s32[8,2,1]{1,2,0:T(1,128)S(1)}, u32[]{:S(2)}, u32[]{:S(2)}) async-start(s32[8,2,1]{1,2,0:T(1,128)} %bitcast.9), calls=%async_computation.1 | async-start | bytes 8192 | tf_op jit(solution)/shard_map/all_to_all | solution.py:215
  15.0 1.2 copy-start.1
  16.2 1.2 copy-start.2
  20.8 6.1 %copy-start.4 = (bf16[8,128,1024]{2,1,0:T(8,128)(2,1)S(1)}, bf16[8,128,1024]{2,1,0:T(8,128)(2,1)}, u32[]{:S(2)}) copy-start(bf16[8,128,1024]{2,1,0:T(8,128)(2,1)} %param.7) | copy-start | bytes 6291460
  20.8 99.6 %all-to-all-start = ((bf16[16,2,8,64,128]{4,3,2,1,0:T(8,128)(2,1)}), bf16[16,2,8,64,128]{4,3,2,1,0:T(8,128)(2,1)}, u32[]{:S(2)}, u32[]{:S(2)}) async-start(bf16[16,2,8,64,128]{4,3,2,1,0:T(8,128)(2,1)} %shard_map.76), calls=%async_computation | async-start | bytes 8388608 | tf_op jit(solution)/shard_map/all_to_all | solution.py:214
  138.2 11.0 %all-to-all-start.2 = ((f32[16,3,512]{2,1,0:T(4,128)}), f32[16,3,512]{2,1,0:T(4,128)S(1)}, u32[]{:S(2)}, u32[]{:S(2)}) async-start(f32[16,3,512]{2,1,0:T(4,128)} %pad_maximum_fusion), calls=%async_computation.2 | async-start | bytes 262144 | tf_op jit(solution)/shard_map/all_to_all | solution.py:235
  151.4 10.2 %all-to-all-start.3 = ((f32[16,2,512]{2,1,0:T(2,128)}), f32[16,2,512]{2,1,0:T(2,128)S(1)}, u32[]{:S(2)}, u32[]{:S(2)}) async-start(f32[16,2,512]{2,1,0:T(2,128)} %gather_fusion.5), calls=%async_computation.3 | async-start | bytes 131072 | tf_op jit(solution)/shard_map/all_to_all | solution.py:247
  162.0 6.6 %copy-start.3 = (bf16[16,8,128,128]{3,2,1,0:T(8,128)(2,1)S(1)}, bf16[16,8,128,128]{3,2,1,0:T(8,128)(2,1)}, u32[]{:S(2)}) copy-start(bf16[16,8,128,128]{3,2,1,0:T(8,128)(2,1)} %gather_fusion.2) | copy-start | bytes 12582916
  172.6 22.2 %collective-permute-start.3 = (bf16[2,8,64,128]{3,2,1,0:T(8,128)(2,1)}, bf16[2,8,64,128]{3,2,1,0:T(8,128)(2,1)}, u32[]{:S(2)}, u32[]{:S(2)}) collective-permute-start(bf16[2,8,64,128]{3,2,1,0:T(8,128)(2,1)} %get-tuple-element.25), channel_id=1, source_target_pairs={{0,4},{4,8},{8,12},{12,16},{16,20},{20,24},{24,28},{28,0},{1,5},{5... | collective-permute-start | bytes 786440 | tf_op jit(solution)/shard_map/ppermute | solution.py:172
  173.0 25.9 %collective-permute-start.4 = (bf16[2,8,64,128]{3,2,1,0:T(8,128)(2,1)}, bf16[2,8,64,128]{3,2,1,0:T(8,128)(2,1)}, u32[]{:S(2)}, u32[]{:S(2)}) collective-permute-start(bf16[2,8,64,128]{3,2,1,0:T(8,128)(2,1)} %get-tuple-element.24), channel_id=1, source_target_pairs={{0,8},{4,12},{8,16},{12,20},{16,24},{20,28},{24,0},{28,4},{1,9},{5... | collective-permute-start | bytes 786440 | tf_op jit(solution)/shard_map/ppermute | solution.py:172
  173.9 30.0 %collective-permute-start.5 = (bf16[2,8,64,128]{3,2,1,0:T(8,128)(2,1)S(1)}, bf16[2,8,64,128]{3,2,1,0:T(8,128)(2,1)S(1)}, u32[]{:S(2)}, u32[]{:S(2)}) collective-permute-start(bf16[2,8,64,128]{3,2,1,0:T(8,128)(2,1)S(1)} %get-tuple-element.23), channel_id=1, source_target_pairs={{0,12},{4,16},{8,20},{12,24},{16,28},{20,0},{24,4},{28,8},{1,13},{... | collective-permute-start | bytes 786440 | tf_op jit(solution)/shard_map/ppermute | solution.py:172
  175.3 29.3 %collective-permute-start.6 = (bf16[2,8,64,128]{3,2,1,0:T(8,128)(2,1)S(1)}, bf16[2,8,64,128]{3,2,1,0:T(8,128)(2,1)S(1)}, u32[]{:S(2)}, u32[]{:S(2)}) collective-permute-start(bf16[2,8,64,128]{3,2,1,0:T(8,128)(2,1)S(1)} %get-tuple-element.22), channel_id=1, source_target_pairs={{0,16},{4,20},{8,24},{12,28},{16,0},{20,4},{24,8},{28,12},{1,17},{... | collective-permute-start | bytes 786440 | tf_op jit(solution)/shard_map/ppermute | solution.py:172
  178.2 27.2 %collective-permute-start.7 = (bf16[2,8,64,128]{3,2,1,0:T(8,128)(2,1)S(1)}, bf16[2,8,64,128]{3,2,1,0:T(8,128)(2,1)S(1)}, u32[]{:S(2)}, u32[]{:S(2)}) collective-permute-start(bf16[2,8,64,128]{3,2,1,0:T(8,128)(2,1)S(1)} %get-tuple-element.21), channel_id=1, source_target_pairs={{0,20},{4,24},{8,28},{12,0},{16,4},{20,8},{24,12},{28,16},{1,21},{... | collective-permute-start | bytes 786440 | tf_op jit(solution)/shard_map/ppermute | solution.py:172
  178.4 1.6 copy-start
  194.8 19.3 %collective-permute-start.8 = (bf16[2,8,64,128]{3,2,1,0:T(8,128)(2,1)S(1)}, bf16[2,8,64,128]{3,2,1,0:T(8,128)(2,1)S(1)}, u32[]{:S(2)}, u32[]{:S(2)}) collective-permute-start(bf16[2,8,64,128]{3,2,1,0:T(8,128)(2,1)S(1)} %get-tuple-element.20), channel_id=1, source_target_pairs={{0,24},{4,28},{8,0},{12,4},{16,8},{20,12},{24,16},{28,20},{1,25},{... | collective-permute-start | bytes 786440 | tf_op jit(solution)/shard_map/ppermute | solution.py:172
  198.9 15.9 %collective-permute-start.9 = (bf16[2,8,64,128]{3,2,1,0:T(8,128)(2,1)S(1)}, bf16[2,8,64,128]{3,2,1,0:T(8,128)(2,1)S(1)}, u32[]{:S(2)}, u32[]{:S(2)}) collective-permute-start(bf16[2,8,64,128]{3,2,1,0:T(8,128)(2,1)S(1)} %get-tuple-element.19), channel_id=1, source_target_pairs={{0,28},{4,0},{8,4},{12,8},{16,12},{20,16},{24,20},{28,24},{1,29},{... | collective-permute-start | bytes 786440 | tf_op jit(solution)/shard_map/ppermute | solution.py:172

commit v17 on v16

--- a/solution.py
+++ b/solution.py
@@ -180,6 +180,13 @@
     return result
 
 
+def seq_move(tensor, seq_count, slot_depth):
+    if seq_count > 8:
+        return lax.all_to_all(tensor, "seq", split_axis=0, concat_axis=0, tiled=True)
+    blocks = tensor.reshape((seq_count, slot_depth) + tensor.shape[1:])
+    return seq_exchange(blocks, seq_count).reshape(tensor.shape)
+
+
 def per_device(queries, out_grad, row_keys, row_values, neighbours):
     seq_count = lax.axis_size("seq")
     own_lists = gather_over(neighbours, "mp", lax.axis_size("mp")).reshape(
@@ -232,7 +239,7 @@
     part = jnp.stack(
         [highest, jnp.sum(expons, axis=3), jnp.sum(expons * grad_p, axis=3)], axis=1
     ).reshape(slot_total, 3, heads_here * SPAN)
-    back = lax.all_to_all(part, "seq", split_axis=0, concat_axis=0, tiled=True)
+    back = seq_move(part, seq_count, slot_depth)
 
     item_part = back[target].reshape(span_count, NBR, 3, heads_here * SPAN)
     item_max = item_part[:, :, 0]
@@ -244,9 +251,7 @@
     log_total = span_max[:, 0] + jnp.log(span_sum)
     row_delta = jnp.sum(item_cross * factor, axis=1) / span_sum
     span_stats = jnp.stack([log_total, row_delta], axis=1)
-    stats_recv = lax.all_to_all(
-        span_stats[slot_span], "seq", split_axis=0, concat_axis=0, tiled=True
-    )
+    stats_recv = seq_move(span_stats[slot_span], seq_count, slot_depth)
 
     norm_here = stats_recv[:, 0].reshape(slot_total, heads_here, SPAN)
     delta_here = stats_recv[:, 1].reshape(slot_total, heads_here, SPAN)

time: 223 us -> 225 us (level)
  starting transfers between devices: 33.8 us -> 49.6 us
  waiting for transfers between devices: 95.2 us -> 83.2 us
    ppermute x7 -> x21, starting transfers between devices: 10.2 us -> 33.2 us  [seq_exchange(): lax.ppermute(lax.dynamic_index_in_dim(blocks, (me + shift) % seq_count, k...]
    all_to_all x2 -> x0, waiting for transfers between devices: 13.9 us -> none  [the longest x1 7.32 us: per_device(): back = lax.all_to_all(part, 'seq', split_axis=0, concat_axis=0, tiled=True)]
    all_to_all x2 -> x0, starting transfers between devices: 7.17 us -> none  [the longest x1 3.63 us: per_device(): back = lax.all_to_all(part, 'seq', split_axis=0, concat_axis=0, tiled=True)]
    ppermute x7 -> x21, waiting for transfers between devices: 9.38 us -> 11.3 us  [seq_exchange(): lax.ppermute(lax.dynamic_index_in_dim(blocks, (me + shift) % seq_count, k...]
    dynamic_update_slice x7 -> x21, local copies, waits for them, and re-layouts: 7 us -> 7.13 us  [seq_exchange(): lax.dynamic_update_index_in_dim(result, sent, (me - shift) % seq_count, a...]
  transfers between devices with their start and end apart: 14 -> 26, of which waited for: 6 -> 8; matrix products, arithmetic and copies ran while one was open for 14% -> 14% of each run, Pallas kernels for 8% -> 8%
where the time goes in v17:
time: 225 us; the launch traced here: 222 us
  waiting for transfers between devices  83.2 us (37%)
  starting transfers between devices  49.6 us (22%)
  local copies, waits for them, and re-layouts  40.5 us (18%)
  Pallas kernels  21.5 us (10%)
  matrix products  18 us (8%)
  other arithmetic  8.09 us (4%)
    all_to_all x1, waiting for transfers between devices, per_device(): lax.all_to_all(pair_send, 'seq', split_axis=0, concat_axis=0, tiled=True)  71.2 us
    ppermute x21, starting transfers between devices, seq_exchange(): lax.ppermute(lax.dynamic_index_in_dim(blocks, (me + shift) % seq_count, k...  33.2 us
    pallas_call x1, Pallas kernels, kv_grads(): pl.pallas_call(kv_kernel, grid_spec=grid_spec, out_shape=[out_shape, out_...  14.7 us
    ppermute x21, waiting for transfers between devices, seq_exchange(): lax.ppermute(lax.dynamic_index_in_dim(blocks, (me + shift) % seq_count, k...  11.3 us
    unnamed x12, local copies, waits for them, and re-layouts  10.3 us
    dot_general x1, matrix products, per_device(): jnp.einsum('bhid,bhjd->bhij', grad_heads, value_heads, preferred_element_...  9 us
    dot_general x1, matrix products, per_device(): jnp.einsum('bhid,bhjd->bhij', query_heads, key_heads, preferred_element_t...  7.76 us
    dynamic_update_slice x21, local copies, waits for them, and re-layouts, seq_exchange(): lax.dynamic_update_index_in_dim(result, sent, (me - shift) % seq_count, a...  7.13 us
  transfers between devices with their start and end apart: 26, of which 8 were waited for; matrix products, arithmetic and copies ran while one was open for 14% of the time, Pallas kernels for 8%

profile of v17, /device:TPU:0, one launch (start us, length us, event | category | flops | bytes accessed | tf_op | source)
XLA Modules:
  0.0 221.7 jit_solution(11375839221598377411)
XLA Ops:
  1.1 2.6 %collective-permute-start.1 = (s32[2,2]{1,0:T(2,128)}, s32[2,2]{1,0:T(2,128)S(1)}, u32[]{:S(2)}, u32[]{:S(2)}) collective-permute-start(s32[2,2]{1,0:T(2,128)} %param.9), channel_id=1, source_target_pairs={{0,2},{1,3},{2,0},{3,1},{4,6},{5,7},{6,4},{7,5},{8,10},{9,11},{10,... | collective-permute-start | bytes 56 | tf_op jit(solution)/shard_map/ppermute | solution.py:158
  3.7 1.4 collective-permute-start.2
  5.8 0.8 collective-permute-done.2
  8.5 5.8 %all-to-all-start.1 = ((s32[8,2,1]{1,2,0:T(1,128)}), s32[8,2,1]{1,2,0:T(1,128)S(1)}, u32[]{:S(2)}, u32[]{:S(2)}) async-start(s32[8,2,1]{1,2,0:T(1,128)} %bitcast.9), calls=%async_computation.1 | async-start | bytes 8192 | tf_op jit(solution)/shard_map/all_to_all | solution.py:222
  15.0 1.2 copy-done.1
  16.2 1.2 copy-done.2
  17.5 3.3 %shard_map.76 = bf16[16,2,8,64,128]{4,3,2,1,0:T(8,128)(2,1)} custom-call(s32[16]{0:T(128)S(1)} %broadcast_clamp_fusion.1.span_ref, bf16[8,64,1024]{2,1,0:T(8,128)(2,1)S(1)} %copy-done.1, bf16[8,64,1024]{2,1,0:T(8,128)(2,1)S(1)} %copy-done.2), custom_call_target="tpu_custom_call" | custom-call | tf_op jit(solution)/shard_map/pallas_call | solution.py:112
  20.8 6.1 %all-to-all-start = ((bf16[16,2,8,64,128]{4,3,2,1,0:T(8,128)(2,1)}), bf16[16,2,8,64,128]{4,3,2,1,0:T(8,128)(2,1)}, u32[]{:S(2)}, u32[]{:S(2)}) async-start(bf16[16,2,8,64,128]{4,3,2,1,0:T(8,128)(2,1)} %shard_map.76), calls=%async_computation | async-start | bytes 8388608 | tf_op jit(solution)/shard_map/all_to_all | solution.py:221
  26.9 2.4 %copy.45 = bf16[8,128,1024]{1,2,0:T(8,128)(2,1)} copy(bf16[8,128,1024]{2,1,0:T(8,128)(2,1)S(1)} %copy-done.4) | data formatting | bytes 4194304 | tf_op args[2]
  29.3 3.0 %copy.46 = bf16[8,128,8,128]{3,1,2,0:T(8,128)(2,1)S(1)} copy(bf16[8,128,8,128]{1,3,2,0:T(8,128)(2,1)} %bitcast.159) | data formatting | bytes 4194304 | tf_op jit(solution)/shard_map/reshape | solution.py:17
  32.3 3.9 %copy.48 = bf16[8,128,1024]{1,2,0:T(8,128)(2,1)} copy(bf16[8,128,1024]{2,1,0:T(8,128)(2,1)} %param.8) | data formatting | bytes 4194304 | tf_op args[3]
  36.3 3.9 %copy.49 = bf16[8,128,8,128]{3,1,2,0:T(8,128)(2,1)} copy(bf16[8,128,8,128]{1,3,2,0:T(8,128)(2,1)} %bitcast.160) | data formatting | bytes 4194304 | tf_op jit(solution)/shard_map/reshape | solution.py:17
  41.6 3.1 %gather_fusion.2 = bf16[16,8,128,128]{3,2,1,0:T(8,128)(2,1)} fusion(bf16[8,8,128,128]{3,2,1,0:T(8,128)(2,1)S(1)} %bitcast.156, s32[1024]{0:T(1024)S(1)} %pad_clamp_fusion.2), kind=kCustom, calls=%fused_computation.2 | custom fusion | bytes 8388672 | tf_op jit(solution)/shard_map/gather | solution.py:227
  44.7 4.6 %gather_fusion.3 = bf16[16,8,128,128]{3,2,1,0:T(8,128)(2,1)} fusion(bf16[8,8,128,128]{3,2,1,0:T(8,128)(2,1)} %bitcast.157, s32[1024]{0:T(1024)S(1)} %pad_clamp_fusion.2), kind=kCustom, calls=%fused_computation.3 | custom fusion | bytes 8388672 | tf_op jit(solution)/shard_map/gather | solution.py:228
  49.3 71.2 %all-to-all-done.pair_ref = bf16[16,2,8,64,128]{4,3,2,1,0:T(8,128)(2,1)} async-done(((bf16[16,2,8,64,128]{4,3,2,1,0:T(8,128)(2,1)}), bf16[16,2,8,64,128]{4,3,2,1,0:T(8,128)(2,1)}, u32[]{:S(2)}, u32[]{:S(2)}) %all-to-all-start) | async-done | bytes 4194336 | tf_op jit(solution)/shard_map/all_to_all | solution.py:221
  120.4 7.8 %multiply_reduce_fusion.1 = (f32[16,8,64]{2,1,0:T(8,128)S(1)}, f32[16,8,64,128]{3,2,1,0:T(8,128)}) fusion(bf16[16,8,128,128]{3,2,1,0:T(8,128)(2,1)} %gather_fusion.2, bf16[16,2,8,64,128]{4,3,2,1,0:T(8,128)(2,1)} %all-to-all-done.pair_ref), kind=kOutput, calls=%fused_computation.12 | convolution fusion | flops 270524416 | bytes 10518528 | tf_op jit(solution)/shard_map/bhid,bhjd->bhij/dot_general | solution.py:231
  128.3 9.0 %fusion = (f32[16,8,64]{2,1,0:T(8,128)S(1)}, f32[16,8,64]{2,1,0:T(8,128)S(1)}, f32[16,8,64,128]{3,2,1,0:T(8,128)}) fusion(f32[16,8,64,128]{3,2,1,0:T(8,128)} %get-tuple-element.52, f32[16,8,64]{2,1,0:T(8,128)S(1)} %get-tuple-element.51, bf16[16,8,128,128]{3,2,1,0:T(8,128)(2,1)} %gather_fusion.3, bf16[16,2,8,64,128]{4,3,2,1,0:T(8,128)(2,1)} %all-to-all-done.pair_ref), kind=kOutput, calls=%fused_computation.10 | convolution fusion | flops 273661952 | bytes 14778368 | tf_op jit(solution)/shard_map/bhid,bhjd->bhij/dot_general | solution.py:234
  137.7 1.5 collective-permute-start.3
  139.2 2.8 %collective-permute-start.5 = (f32[2,3,512]{2,1,0:T(4,128)S(1)}, f32[2,3,512]{2,1,0:T(4,128)S(1)}, u32[]{:S(2)}, u32[]{:S(2)}) collective-permute-start(f32[2,3,512]{2,1,0:T(4,128)S(1)} %get-tuple-element.35), channel_id=1, source_target_pairs={{0,12},{4,16},{8,20},{12,24},{16,28},{20,0},{24,4},{28,8},{1,13},{... | collective-permute-start | bytes 36872 | tf_op jit(solution)/shard_map/ppermute | solution.py:172
  142.0 1.1 collective-permute-start.6
  143.1 2.0 collective-permute-start.7
  145.0 1.8 collective-permute-start.8
  147.7 1.4 collective-permute-done.8
  149.1 1.5 collective-permute-done.9
  152.3 2.0 collective-permute-start.10
  154.3 1.5 collective-permute-start.11
  156.2 2.0 collective-permute-start.13
  158.2 2.4 %collective-permute-start.14 = (f32[2,2,512]{2,1,0:T(2,128)S(1)}, f32[2,2,512]{2,1,0:T(2,128)S(1)}, u32[]{:S(2)}, u32[]{:S(2)}) collective-permute-start(f32[2,2,512]{2,1,0:T(2,128)S(1)} %get-tuple-element.41), channel_id=1, source_target_pairs={{0,20},{4,24},{8,28},{12,0},{16,4},{20,8},{24,12},{28,16},{1,21},{... | collective-permute-start | bytes 24584 | tf_op jit(solution)/shard_map/ppermute | solution.py:172
  160.6 1.5 collective-permute-start.15
  162.1 2.0 collective-permute-start.16
  164.3 1.4 collective-permute-done.16
  166.0 6.6 %fusion.1 = (bf16[16,8,64,128]{3,2,1,0:T(8,128)(2,1)}, bf16[16,8,64,128]{3,2,1,0:T(8,128)(2,1)S(1)}) fusion(f32[16,8,64,128]{3,2,1,0:T(8,128)} %get-tuple-element.52, f32[16,8,64]{2,1,0:T(8,128)S(1)} %sub.106, f32[16,8,64,128]{3,2,1,0:T(8,128)} %get-tuple-element.53, f32[16,8,64]{2,1,0:T(8,128)S(1)} %sub.109), kind=kLoop, calls=%fused_computation.11 | loop fusion | flops 7340032 | bytes 12648448 | tf_op jit(solution)/shard_map/convert_element_type | solution.py:260
  172.6 1.2 convolution_convert_fusion
  173.8 1.9 broadcast_in_dim.122
  175.7 1.0 dynamic-slice_bitcast_fusion
  176.7 1.4 collective-permute-start.17
  178.1 1.5 collective-permute-start.18
  179.7 1.1 collective-permute-start.19
  180.8 2.0 collective-permute-start.20
  182.8 3.6 %collective-permute-start.21 = (bf16[2,8,64,128]{3,2,1,0:T(8,128)(2,1)S(1)}, bf16[2,8,64,128]{3,2,1,0:T(8,128)(2,1)S(1)}, u32[]{:S(2)}, u32[]{:S(2)}) collective-permute-start(bf16[2,8,64,128]{3,2,1,0:T(8,128)(2,1)S(1)} %get-tuple-element.21), channel_id=1, source_target_pairs={{0,20},{4,24},{8,28},{12,0},{16,4},{20,8},{24,12},{28,16},{1,21},{... | collective-permute-start | bytes 786440 | tf_op jit(solution)/shard_map/ppermute | solution.py:172
  186.4 1.6 copy-done
  188.0 14.7 %shard_map.78 = (bf16[8,128,1024]{2,1,0:T(8,128)(2,1)}, bf16[8,128,1024]{2,1,0:T(8,128)(2,1)}) custom-call(s32[16]{0:T(128)S(1)} %all_to_all.10.rows_ref, bf16[16,8,64,128]{3,2,1,0:T(8,128)(2,1)S(1)} %copy-done, bf16[16,8,64,128]{3,2,1,0:T(8,128)(2,1)S(1)} %get-tuple-element.18.grads_ref, bf16[16,2,8,64,128]{4,3,2,1,0:T(8,128)(2,1)} %all-to-all-done.pair_ref), custom_call_target="tpu_custom_call" | custom-call | tf_op jit(solution)/shard_map/pallas_call | solution.py:74
  202.8 1.7 bitcast_dynamic-update-slice_fusion.6
  204.4 2.0 collective-permute-start.23
  206.4 1.7 bitcast_dynamic-update-slice_fusion.5
  208.8 0.7 bitcast_dynamic-update-slice_fusion.3
  210.2 6.6 %collective-permute-done.22 = bf16[2,8,64,128]{3,2,1,0:T(8,128)(2,1)S(1)} collective-permute-done((bf16[2,8,64,128]{3,2,1,0:T(8,128)(2,1)S(1)}, bf16[2,8,64,128]{3,2,1,0:T(8,128)(2,1)S(1)}, u32[]{:S(2)}, u32[]{:S(2)}) %collective-permute-start.22) | collective-permute-done | bytes 262176 | tf_op jit(solution)/shard_map/ppermute | solution.py:172
  218.3 3.4 %shard_map.77 = bf16[8,64,1024]{2,1,0:T(8,128)(2,1)} custom-call(s32[16]{0:T(128)S(1)} %get-tuple-element.15.target_ref, bf16[16,8,64,128]{3,2,1,0:T(8,128)(2,1)} %bitcast.68.back_ref), custom_call_target="tpu_custom_call" | custom-call | tf_op jit(solution)/shard_map/pallas_call | solution.py:145
  (98 shorter events, 12.1 us)
Async XLA Ops:
  0.6 5.2 %collective-permute-start = (s32[2,2]{1,0:T(2,128)}, s32[2,2]{1,0:T(2,128)S(1)}, u32[]{:S(2)}, u32[]{:S(2)}) collective-permute-start(s32[2,2]{1,0:T(2,128)} %param.9), channel_id=1, source_target_pairs={{0,1},{1,2},{2,3},{3,0},{4,5},{5,6},{6,7},{7,4},{8,9},{9,10},{10,1... | collective-permute-start | bytes 56 | tf_op jit(solution)/shard_map/ppermute | solution.py:158
  1.1 4.7 %collective-permute-start.1 = (s32[2,2]{1,0:T(2,128)}, s32[2,2]{1,0:T(2,128)S(1)}, u32[]{:S(2)}, u32[]{:S(2)}) collective-permute-start(s32[2,2]{1,0:T(2,128)} %param.9), channel_id=1, source_target_pairs={{0,2},{1,3},{2,0},{3,1},{4,6},{5,7},{6,4},{7,5},{8,10},{9,11},{10,... | collective-permute-start | bytes 56 | tf_op jit(solution)/shard_map/ppermute | solution.py:158
  3.7 2.9 %collective-permute-start.2 = (s32[2,2]{1,0:T(2,128)}, s32[2,2]{1,0:T(2,128)S(1)}, u32[]{:S(2)}, u32[]{:S(2)}) collective-permute-start(s32[2,2]{1,0:T(2,128)} %param.9), channel_id=1, source_target_pairs={{0,3},{1,0},{2,1},{3,2},{4,7},{5,4},{6,5},{7,6},{8,11},{9,8},{10,9... | collective-permute-start | bytes 56 | tf_op jit(solution)/shard_map/ppermute | solution.py:158
  8.5 12.3 %all-to-all-start.1 = ((s32[8,2,1]{1,2,0:T(1,128)}), s32[8,2,1]{1,2,0:T(1,128)S(1)}, u32[]{:S(2)}, u32[]{:S(2)}) async-start(s32[8,2,1]{1,2,0:T(1,128)} %bitcast.9), calls=%async_computation.1 | async-start | bytes 8192 | tf_op jit(solution)/shard_map/all_to_all | solution.py:222
  15.0 1.2 copy-start.1
  16.2 1.2 copy-start.2
  20.8 6.1 %copy-start.4 = (bf16[8,128,1024]{2,1,0:T(8,128)(2,1)S(1)}, bf16[8,128,1024]{2,1,0:T(8,128)(2,1)}, u32[]{:S(2)}) copy-start(bf16[8,128,1024]{2,1,0:T(8,128)(2,1)} %param.7) | copy-start | bytes 6291460
  20.8 99.6 %all-to-all-start = ((bf16[16,2,8,64,128]{4,3,2,1,0:T(8,128)(2,1)}), bf16[16,2,8,64,128]{4,3,2,1,0:T(8,128)(2,1)}, u32[]{:S(2)}, u32[]{:S(2)}) async-start(bf16[16,2,8,64,128]{4,3,2,1,0:T(8,128)(2,1)} %shard_map.76), calls=%async_computation | async-start | bytes 8388608 | tf_op jit(solution)/shard_map/all_to_all | solution.py:221
  137.7 7.4 %collective-permute-start.3 = (f32[2,3,512]{2,1,0:T(4,128)S(1)}, f32[2,3,512]{2,1,0:T(4,128)S(1)}, u32[]{:S(2)}, u32[]{:S(2)}) collective-permute-start(f32[2,3,512]{2,1,0:T(4,128)S(1)} %get-tuple-element.37), channel_id=1, source_target_pairs={{0,4},{4,8},{8,12},{12,16},{16,20},{20,24},{24,28},{28,0},{1,5},{5... | collective-permute-start | bytes 36872 | tf_op jit(solution)/shard_map/ppermute | solution.py:172
  139.2 7.7 %collective-permute-start.4 = (f32[2,3,512]{2,1,0:T(4,128)S(1)}, f32[2,3,512]{2,1,0:T(4,128)S(1)}, u32[]{:S(2)}, u32[]{:S(2)}) collective-permute-start(f32[2,3,512]{2,1,0:T(4,128)S(1)} %get-tuple-element.36), channel_id=1, source_target_pairs={{0,8},{4,12},{8,16},{12,20},{16,24},{20,28},{24,0},{28,4},{1,9},{5... | collective-permute-start | bytes 36872 | tf_op jit(solution)/shard_map/ppermute | solution.py:172
  139.2 8.3 %collective-permute-start.5 = (f32[2,3,512]{2,1,0:T(4,128)S(1)}, f32[2,3,512]{2,1,0:T(4,128)S(1)}, u32[]{:S(2)}, u32[]{:S(2)}) collective-permute-start(f32[2,3,512]{2,1,0:T(4,128)S(1)} %get-tuple-element.35), channel_id=1, source_target_pairs={{0,12},{4,16},{8,20},{12,24},{16,28},{20,0},{24,4},{28,8},{1,13},{... | collective-permute-start | bytes 36872 | tf_op jit(solution)/shard_map/ppermute | solution.py:172
  142.0 5.5 %collective-permute-start.6 = (f32[2,3,512]{2,1,0:T(4,128)S(1)}, f32[2,3,512]{2,1,0:T(4,128)S(1)}, u32[]{:S(2)}, u32[]{:S(2)}) collective-permute-start(f32[2,3,512]{2,1,0:T(4,128)S(1)} %get-tuple-element.34), channel_id=1, source_target_pairs={{0,16},{4,20},{8,24},{12,28},{16,0},{20,4},{24,8},{28,12},{1,17},{... | collective-permute-start | bytes 36872 | tf_op jit(solution)/shard_map/ppermute | solution.py:172
  143.1 4.6 %collective-permute-start.7 = (f32[2,3,512]{2,1,0:T(4,128)S(1)}, f32[2,3,512]{2,1,0:T(4,128)S(1)}, u32[]{:S(2)}, u32[]{:S(2)}) collective-permute-start(f32[2,3,512]{2,1,0:T(4,128)S(1)} %get-tuple-element.33), channel_id=1, source_target_pairs={{0,20},{4,24},{8,28},{12,0},{16,4},{20,8},{24,12},{28,16},{1,21},{... | collective-permute-start | bytes 36872 | tf_op jit(solution)/shard_map/ppermute | solution.py:172
  145.0 4.1 %collective-permute-start.8 = (f32[2,3,512]{2,1,0:T(4,128)S(1)}, f32[2,3,512]{2,1,0:T(4,128)S(1)}, u32[]{:S(2)}, u32[]{:S(2)}) collective-permute-start(f32[2,3,512]{2,1,0:T(4,128)S(1)} %get-tuple-element.32), channel_id=1, source_target_pairs={{0,24},{4,28},{8,0},{12,4},{16,8},{20,12},{24,16},{28,20},{1,25},{... | collective-permute-start | bytes 36872 | tf_op jit(solution)/shard_map/ppermute | solution.py:172
  146.8 3.8 %collective-permute-start.9 = (f32[2,3,512]{2,1,0:T(4,128)S(1)}, f32[2,3,512]{2,1,0:T(4,128)S(1)}, u32[]{:S(2)}, u32[]{:S(2)}) collective-permute-start(f32[2,3,512]{2,1,0:T(4,128)S(1)} %get-tuple-element.31), channel_id=1, source_target_pairs={{0,28},{4,0},{8,4},{12,8},{16,12},{20,16},{24,20},{28,24},{1,29},{... | collective-permute-start | bytes 36872 | tf_op jit(solution)/shard_map/ppermute | solution.py:172
  152.3 8.3 %collective-permute-start.10 = (f32[2,2,512]{2,1,0:T(2,128)S(1)}, f32[2,2,512]{2,1,0:T(2,128)S(1)}, u32[]{:S(2)}, u32[]{:S(2)}) collective-permute-start(f32[2,2,512]{2,1,0:T(2,128)S(1)} %get-tuple-element.45), channel_id=1, source_target_pairs={{0,4},{4,8},{8,12},{12,16},{16,20},{20,24},{24,28},{28,0},{1,5},{5... | collective-permute-start | bytes 24584 | tf_op jit(solution)/shard_map/ppermute | solution.py:172
  154.3 7.8 %collective-permute-start.11 = (f32[2,2,512]{2,1,0:T(2,128)S(1)}, f32[2,2,512]{2,1,0:T(2,128)S(1)}, u32[]{:S(2)}, u32[]{:S(2)}) collective-permute-start(f32[2,2,512]{2,1,0:T(2,128)S(1)} %get-tuple-element.44), channel_id=1, source_target_pairs={{0,8},{4,12},{8,16},{12,20},{16,24},{20,28},{24,0},{28,4},{1,9},{5... | collective-permute-start | bytes 24584 | tf_op jit(solution)/shard_map/ppermute | solution.py:172
  155.8 8.2 %collective-permute-start.12 = (f32[2,2,512]{2,1,0:T(2,128)S(1)}, f32[2,2,512]{2,1,0:T(2,128)S(1)}, u32[]{:S(2)}, u32[]{:S(2)}) collective-permute-start(f32[2,2,512]{2,1,0:T(2,128)S(1)} %get-tuple-element.43), channel_id=1, source_target_pairs={{0,12},{4,16},{8,20},{12,24},{16,28},{20,0},{24,4},{28,8},{1,13},{... | collective-permute-start | bytes 24584 | tf_op jit(solution)/shard_map/ppermute | solution.py:172
  156.2 7.9 %collective-permute-start.13 = (f32[2,2,512]{2,1,0:T(2,128)S(1)}, f32[2,2,512]{2,1,0:T(2,128)S(1)}, u32[]{:S(2)}, u32[]{:S(2)}) collective-permute-start(f32[2,2,512]{2,1,0:T(2,128)S(1)} %get-tuple-element.42), channel_id=1, source_target_pairs={{0,16},{4,20},{8,24},{12,28},{16,0},{20,4},{24,8},{28,12},{1,17},{... | collective-permute-start | bytes 24584 | tf_op jit(solution)/shard_map/ppermute | solution.py:172
  158.2 5.9 %collective-permute-start.14 = (f32[2,2,512]{2,1,0:T(2,128)S(1)}, f32[2,2,512]{2,1,0:T(2,128)S(1)}, u32[]{:S(2)}, u32[]{:S(2)}) collective-permute-start(f32[2,2,512]{2,1,0:T(2,128)S(1)} %get-tuple-element.41), channel_id=1, source_target_pairs={{0,20},{4,24},{8,28},{12,0},{16,4},{20,8},{24,12},{28,16},{1,21},{... | collective-permute-start | bytes 24584 | tf_op jit(solution)/shard_map/ppermute | solution.py:172
  160.6 3.7 %collective-permute-start.15 = (f32[2,2,512]{2,1,0:T(2,128)S(1)}, f32[2,2,512]{2,1,0:T(2,128)S(1)}, u32[]{:S(2)}, u32[]{:S(2)}) collective-permute-start(f32[2,2,512]{2,1,0:T(2,128)S(1)} %get-tuple-element.40), channel_id=1, source_target_pairs={{0,24},{4,28},{8,0},{12,4},{16,8},{20,12},{24,16},{28,20},{1,25},{... | collective-permute-start | bytes 24584 | tf_op jit(solution)/shard_map/ppermute | solution.py:172
  162.1 3.7 %collective-permute-start.16 = (f32[2,2,512]{2,1,0:T(2,128)S(1)}, f32[2,2,512]{2,1,0:T(2,128)S(1)}, u32[]{:S(2)}, u32[]{:S(2)}) collective-permute-start(f32[2,2,512]{2,1,0:T(2,128)S(1)} %get-tuple-element.39), channel_id=1, source_target_pairs={{0,28},{4,0},{8,4},{12,8},{16,12},{20,16},{24,20},{28,24},{1,29},{... | collective-permute-start | bytes 24584 | tf_op jit(solution)/shard_map/ppermute | solution.py:172
  166.0 6.6 %copy-start.3 = (bf16[16,8,128,128]{3,2,1,0:T(8,128)(2,1)S(1)}, bf16[16,8,128,128]{3,2,1,0:T(8,128)(2,1)}, u32[]{:S(2)}) copy-start(bf16[16,8,128,128]{3,2,1,0:T(8,128)(2,1)} %gather_fusion.2) | copy-start | bytes 12582916
  176.7 26.1 %collective-permute-start.17 = (bf16[2,8,64,128]{3,2,1,0:T(8,128)(2,1)}, bf16[2,8,64,128]{3,2,1,0:T(8,128)(2,1)}, u32[]{:S(2)}, u32[]{:S(2)}) collective-permute-start(bf16[2,8,64,128]{3,2,1,0:T(8,128)(2,1)} %get-tuple-element.25), channel_id=1, source_target_pairs={{0,4},{4,8},{8,12},{12,16},{16,20},{20,24},{24,28},{28,0},{1,5},{5... | collective-permute-start | bytes 786440 | tf_op jit(solution)/shard_map/ppermute | solution.py:172
  178.1 26.4 %collective-permute-start.18 = (bf16[2,8,64,128]{3,2,1,0:T(8,128)(2,1)}, bf16[2,8,64,128]{3,2,1,0:T(8,128)(2,1)}, u32[]{:S(2)}, u32[]{:S(2)}) collective-permute-start(bf16[2,8,64,128]{3,2,1,0:T(8,128)(2,1)} %get-tuple-element.24), channel_id=1, source_target_pairs={{0,8},{4,12},{8,16},{12,20},{16,24},{20,28},{24,0},{28,4},{1,9},{5... | collective-permute-start | bytes 786440 | tf_op jit(solution)/shard_map/ppermute | solution.py:172
  179.7 28.4 %collective-permute-start.19 = (bf16[2,8,64,128]{3,2,1,0:T(8,128)(2,1)S(1)}, bf16[2,8,64,128]{3,2,1,0:T(8,128)(2,1)S(1)}, u32[]{:S(2)}, u32[]{:S(2)}) collective-permute-start(bf16[2,8,64,128]{3,2,1,0:T(8,128)(2,1)S(1)} %get-tuple-element.23), channel_id=1, source_target_pairs={{0,12},{4,16},{8,20},{12,24},{16,28},{20,0},{24,4},{28,8},{1,13},{... | collective-permute-start | bytes 786440 | tf_op jit(solution)/shard_map/ppermute | solution.py:172
  180.8 28.0 %collective-permute-start.20 = (bf16[2,8,64,128]{3,2,1,0:T(8,128)(2,1)S(1)}, bf16[2,8,64,128]{3,2,1,0:T(8,128)(2,1)S(1)}, u32[]{:S(2)}, u32[]{:S(2)}) collective-permute-start(bf16[2,8,64,128]{3,2,1,0:T(8,128)(2,1)S(1)} %get-tuple-element.22), channel_id=1, source_target_pairs={{0,16},{4,20},{8,24},{12,28},{16,0},{20,4},{24,8},{28,12},{1,17},{... | collective-permute-start | bytes 786440 | tf_op jit(solution)/shard_map/ppermute | solution.py:172
  182.8 26.7 %collective-permute-start.21 = (bf16[2,8,64,128]{3,2,1,0:T(8,128)(2,1)S(1)}, bf16[2,8,64,128]{3,2,1,0:T(8,128)(2,1)S(1)}, u32[]{:S(2)}, u32[]{:S(2)}) collective-permute-start(bf16[2,8,64,128]{3,2,1,0:T(8,128)(2,1)S(1)} %get-tuple-element.21), channel_id=1, source_target_pairs={{0,20},{4,24},{8,28},{12,0},{16,4},{20,8},{24,12},{28,16},{1,21},{... | collective-permute-start | bytes 786440 | tf_op jit(solution)/shard_map/ppermute | solution.py:172
  186.4 1.6 copy-start
  202.8 14.1 %collective-permute-start.22 = (bf16[2,8,64,128]{3,2,1,0:T(8,128)(2,1)S(1)}, bf16[2,8,64,128]{3,2,1,0:T(8,128)(2,1)S(1)}, u32[]{:S(2)}, u32[]{:S(2)}) collective-permute-start(bf16[2,8,64,128]{3,2,1,0:T(8,128)(2,1)S(1)} %get-tuple-element.20), channel_id=1, source_target_pairs={{0,24},{4,28},{8,0},{12,4},{16,8},{20,12},{24,16},{28,20},{1,25},{... | collective-permute-start | bytes 786440 | tf_op jit(solution)/shard_map/ppermute | solution.py:172
  204.4 13.1 %collective-permute-start.23 = (bf16[2,8,64,128]{3,2,1,0:T(8,128)(2,1)S(1)}, bf16[2,8,64,128]{3,2,1,0:T(8,128)(2,1)S(1)}, u32[]{:S(2)}, u32[]{:S(2)}) collective-permute-start(bf16[2,8,64,128]{3,2,1,0:T(8,128)(2,1)S(1)} %get-tuple-element.19), channel_id=1, source_target_pairs={{0,28},{4,0},{8,4},{12,8},{16,12},{20,16},{24,20},{28,24},{1,29},{... | collective-permute-start | bytes 786440 | tf_op jit(solution)/shard_map/ppermute | solution.py:172

commit v18 on v16

--- a/solution.py
+++ b/solution.py
@@ -81,18 +81,19 @@
     )(row_recv, probs_low, grad_s, pair_recv)
 
 
-def pair_kernel(span_ref, query_ref, grad_ref, pair_out):
-    heads = pair_out.shape[2]
+def pair_kernel(span_ref, query_hbm, grad_hbm, pair_hbm, done):
+    heads = pair_hbm.shape[2]
 
     def body(t, carry):
         source = span_ref[t]
         for h in range(heads):
             cols = pl.ds(h * HEAD, HEAD)
-            pair_out[t, 0, h] = query_ref[source, :, cols]
-            pair_out[t, 1, h] = grad_ref[source, :, cols]
+            pltpu.make_async_copy(query_hbm.at[source, :, cols], pair_hbm.at[t, 0, h], done).start()
+            pltpu.make_async_copy(grad_hbm.at[source, :, cols], pair_hbm.at[t, 1, h], done).start()
         return carry
 
-    lax.fori_loop(0, pair_out.shape[0], body, 0)
+    lax.fori_loop(0, pair_hbm.shape[0], body, 0)
+    pltpu.make_async_copy(pair_hbm, pair_hbm, done).wait()
 
 
 def gather_pairs(slot_span, queries, out_grad):
@@ -103,17 +104,14 @@
     grid_spec = pltpu.PrefetchScalarGridSpec(
         num_scalar_prefetch=1,
         grid=(1,),
-        in_specs=[
-            pl.BlockSpec((span_count, span_len, width), lambda i, spans: (0, 0, 0)),
-            pl.BlockSpec((span_count, span_len, width), lambda i, spans: (0, 0, 0)),
-        ],
-        out_specs=pl.BlockSpec(pair_shape, lambda i, spans: (0, 0, 0, 0, 0)),
+        in_specs=[pl.BlockSpec(memory_space=pl.ANY), pl.BlockSpec(memory_space=pl.ANY)],
+        out_specs=pl.BlockSpec(memory_space=pl.ANY),
+        scratch_shapes=[pltpu.SemaphoreType.DMA(())],
     )
     return pl.pallas_call(
         pair_kernel,
         grid_spec=grid_spec,
         out_shape=jax.ShapeDtypeStruct(pair_shape, queries.dtype),
-        compiler_params=pltpu.CompilerParams(vmem_limit_bytes=48 * 1024 * 1024),
     )(jnp.clip(slot_span, 0, span_count - 1), queries, out_grad)
 
 

time: 223 us -> 347 us (1.56)
  Pallas kernels: 21.5 us -> 147 us
    pallas_call x1, Pallas kernels: 3.33 us -> 129 us  [gather_pairs(): pl.pallas_call(pair_kernel, grid_spec=grid_spec, out_shape=jax.ShapeDtype...]
    unnamed x12 -> x8, local copies, waits for them, and re-layouts: 10.3 us -> 7.89 us
  transfers between devices with their start and end apart: 14 -> 14, of which waited for: 6 -> 6; matrix products, arithmetic and copies ran while one was open for 14% -> 9% of each run, Pallas kernels for 8% -> 42%
where the time goes in v18:
time: 347 us; the launch traced here: 343 us
  Pallas kernels  147 us (42%)
  waiting for transfers between devices  95.2 us (27%)
  local copies, waits for them, and re-layouts  38.5 us (11%)
  starting transfers between devices  33.8 us (10%)
  matrix products  18 us (5%)
  other arithmetic  9.26 us (3%)
    pallas_call x1, Pallas kernels, gather_pairs(): pl.pallas_call(pair_kernel, grid_spec=grid_spec, out_shape=jax.ShapeDtype...  129 us
    all_to_all x1, waiting for transfers between devices, per_device(): lax.all_to_all(pair_send, 'seq', split_axis=0, concat_axis=0, tiled=True)  71.2 us
    pallas_call x1, Pallas kernels, kv_grads(): pl.pallas_call(kv_kernel, grid_spec=grid_spec, out_shape=[out_shape, out_...  14.7 us
    ppermute x7, starting transfers between devices, seq_exchange(): lax.ppermute(lax.dynamic_index_in_dim(blocks, (me + shift) % seq_count, k...  10.2 us
    ppermute x7, waiting for transfers between devices, seq_exchange(): lax.ppermute(lax.dynamic_index_in_dim(blocks, (me + shift) % seq_count, k...  9.38 us
    dot_general x1, matrix products, per_device(): jnp.einsum('bhid,bhjd->bhij', grad_heads, value_heads, preferred_element_...  8.98 us
    unnamed x8, local copies, waits for them, and re-layouts  7.89 us
    dot_general x1, matrix products, per_device(): jnp.einsum('bhid,bhjd->bhij', query_heads, key_heads, preferred_element_t...  7.78 us
  transfers between devices with their start and end apart: 14, of which 6 were waited for; matrix products, arithmetic and copies ran while one was open for 9% of the time, Pallas kernels for 42%

profile of v18, /device:TPU:0, one launch (start us, length us, event | category | flops | bytes accessed | tf_op | source)
XLA Modules:
  0.0 342.6 jit_solution(15947349358971227905)
XLA Ops:
  1.1 2.6 collective-permute-start.1
  3.7 1.4 collective-permute-start.2
  5.1 0.7 constant_dynamic-update-slice_fusion.3
  5.8 0.8 collective-permute-done.2
  7.2 0.7 gather_fusion.1
  7.8 0.7 select_n.238
  8.5 5.8 %all-to-all-start.1 = ((s32[8,2,1]{1,2,0:T(1,128)}), s32[8,2,1]{1,2,0:T(1,128)S(1)}, u32[]{:S(2)}, u32[]{:S(2)}) async-start(s32[8,2,1]{1,2,0:T(1,128)} %bitcast.9), calls=%async_computation.1 | async-start | bytes 8192 | tf_op jit(solution)/shard_map/all_to_all | solution.py:213
  14.3 0.7 gather_fusion
  15.5 128.8 %shard_map.76 = bf16[16,2,8,64,128]{4,3,2,1,0:T(8,128)(2,1)} custom-call(s32[16]{0:T(128)} %broadcast_clamp_fusion.1.span_ref, bf16[8,64,1024]{2,1,0:T(8,128)(2,1)} %query_hbm.1, bf16[8,64,1024]{2,1,0:T(8,128)(2,1)} %grad_hbm.1), custom_call_target="tpu_custom_call" | custom-call | tf_op jit(solution)/shard_map/pallas_call | solution.py:111
  144.4 6.1 %all-to-all-start = ((bf16[16,2,8,64,128]{4,3,2,1,0:T(8,128)(2,1)}), bf16[16,2,8,64,128]{4,3,2,1,0:T(8,128)(2,1)}, u32[]{:S(2)}, u32[]{:S(2)}) async-start(bf16[16,2,8,64,128]{4,3,2,1,0:T(8,128)(2,1)} %shard_map.76), calls=%async_computation | async-start | bytes 8388608 | tf_op jit(solution)/shard_map/all_to_all | solution.py:212
  150.5 2.4 copy.26
  152.9 3.0 copy.27
  156.0 3.9 %copy.29 = bf16[8,128,1024]{1,2,0:T(8,128)(2,1)} copy(bf16[8,128,1024]{2,1,0:T(8,128)(2,1)} %param.8) | data formatting | bytes 4194304 | tf_op args[3]
  159.9 3.9 %copy.30 = bf16[8,128,8,128]{3,1,2,0:T(8,128)(2,1)} copy(bf16[8,128,8,128]{1,3,2,0:T(8,128)(2,1)} %bitcast.101) | data formatting | bytes 4194304 | tf_op jit(solution)/shard_map/reshape | solution.py:17
  164.4 0.7 fusion.15
  165.2 3.1 gather_fusion.2
  168.2 4.6 %gather_fusion.3 = bf16[16,8,128,128]{3,2,1,0:T(8,128)(2,1)} fusion(bf16[8,8,128,128]{3,2,1,0:T(8,128)(2,1)} %bitcast.98, s32[1024]{0:T(1024)S(1)} %pad_clamp_fusion.2), kind=kCustom, calls=%fused_computation.3 | custom fusion | bytes 8388672 | tf_op jit(solution)/shard_map/gather | solution.py:219
  172.9 71.2 %all-to-all-done.pair_ref = bf16[16,2,8,64,128]{4,3,2,1,0:T(8,128)(2,1)} async-done(((bf16[16,2,8,64,128]{4,3,2,1,0:T(8,128)(2,1)}), bf16[16,2,8,64,128]{4,3,2,1,0:T(8,128)(2,1)}, u32[]{:S(2)}, u32[]{:S(2)}) %all-to-all-start) | async-done | bytes 4194336 | tf_op jit(solution)/shard_map/all_to_all | solution.py:212
  244.0 7.8 %multiply_reduce_fusion.1 = (f32[16,8,64]{2,1,0:T(8,128)S(1)}, f32[16,8,64,128]{3,2,1,0:T(8,128)}) fusion(bf16[16,8,128,128]{3,2,1,0:T(8,128)(2,1)} %gather_fusion.2, bf16[16,2,8,64,128]{4,3,2,1,0:T(8,128)(2,1)} %all-to-all-done.pair_ref), kind=kOutput, calls=%fused_computation.12 | convolution fusion | flops 270524416 | bytes 10518528 | tf_op jit(solution)/shard_map/bhid,bhjd->bhij/dot_general | solution.py:222
  251.9 9.0 %fusion = (f32[16,8,64]{2,1,0:T(8,128)S(1)}, f32[16,8,64]{2,1,0:T(8,128)S(1)}, f32[16,8,64,128]{3,2,1,0:T(8,128)}) fusion(f32[16,8,64,128]{3,2,1,0:T(8,128)} %get-tuple-element.36, f32[16,8,64]{2,1,0:T(8,128)S(1)} %get-tuple-element.35, bf16[16,8,128,128]{3,2,1,0:T(8,128)(2,1)} %gather_fusion.3, bf16[16,2,8,64,128]{4,3,2,1,0:T(8,128)(2,1)} %all-to-all-done.pair_ref), kind=kOutput, calls=%fused_computation.10 | convolution fusion | flops 273661952 | bytes 14778368 | tf_op jit(solution)/shard_map/bhid,bhjd->bhij/dot_general | solution.py:225
  261.1 0.7 pad_maximum_fusion
  261.8 3.6 %all-to-all-start.2 = ((f32[16,3,512]{2,1,0:T(4,128)}), f32[16,3,512]{2,1,0:T(4,128)S(1)}, u32[]{:S(2)}, u32[]{:S(2)}) async-start(f32[16,3,512]{2,1,0:T(4,128)} %pad_maximum_fusion), calls=%async_computation.2 | async-start | bytes 262144 | tf_op jit(solution)/shard_map/all_to_all | solution.py:233
  265.5 7.3 %all-to-all-done.2 = f32[16,3,512]{2,1,0:T(4,128)S(1)} async-done(((f32[16,3,512]{2,1,0:T(4,128)}), f32[16,3,512]{2,1,0:T(4,128)S(1)}, u32[]{:S(2)}, u32[]{:S(2)}) %all-to-all-start.2) | async-done | bytes 98336 | tf_op jit(solution)/shard_map/all_to_all | solution.py:233
  272.8 0.6 gather_fusion.4
  273.8 1.2 gather_fusion.5
  275.0 3.5 %all-to-all-start.3 = ((f32[16,2,512]{2,1,0:T(2,128)}), f32[16,2,512]{2,1,0:T(2,128)S(1)}, u32[]{:S(2)}, u32[]{:S(2)}) async-start(f32[16,2,512]{2,1,0:T(2,128)} %gather_fusion.5), calls=%async_computation.3 | async-start | bytes 131072 | tf_op jit(solution)/shard_map/all_to_all | solution.py:245
  278.7 6.6 %all-to-all-done.3 = f32[16,2,512]{2,1,0:T(2,128)S(1)} async-done(((f32[16,2,512]{2,1,0:T(2,128)}), f32[16,2,512]{2,1,0:T(2,128)S(1)}, u32[]{:S(2)}, u32[]{:S(2)}) %all-to-all-start.3) | async-done | bytes 65568 | tf_op jit(solution)/shard_map/all_to_all | solution.py:245
  285.6 6.6 %fusion.1 = (bf16[16,8,64,128]{3,2,1,0:T(8,128)(2,1)}, bf16[16,8,64,128]{3,2,1,0:T(8,128)(2,1)S(1)}) fusion(f32[16,8,64,128]{3,2,1,0:T(8,128)} %get-tuple-element.36, f32[16,8,64]{2,1,0:T(8,128)S(1)} %sub.85, f32[16,8,64,128]{3,2,1,0:T(8,128)} %get-tuple-element.37, f32[16,8,64]{2,1,0:T(8,128)S(1)} %sub.88), kind=kLoop, calls=%fused_computation.11 | loop fusion | flops 7340032 | bytes 12648448 | tf_op jit(solution)/shard_map/convert_element_type | solution.py:253
  292.1 1.2 convolution_convert_fusion
  293.4 1.9 broadcast_in_dim.70
  295.2 1.0 dynamic-slice_bitcast_fusion
  296.6 0.9 collective-permute-start.4
  297.5 1.3 collective-permute-start.5
  298.9 2.9 collective-permute-start.6
  302.0 1.6 copy-done
  303.6 14.7 %shard_map.78 = (bf16[8,128,1024]{2,1,0:T(8,128)(2,1)}, bf16[8,128,1024]{2,1,0:T(8,128)(2,1)}) custom-call(s32[16]{0:T(128)S(1)} %all_to_all.18.rows_ref, bf16[16,8,64,128]{3,2,1,0:T(8,128)(2,1)S(1)} %copy-done, bf16[16,8,64,128]{3,2,1,0:T(8,128)(2,1)S(1)} %get-tuple-element.18.grads_ref, bf16[16,2,8,64,128]{4,3,2,1,0:T(8,128)(2,1)} %all-to-all-done.pair_ref), custom_call_target="tpu_custom_call" | custom-call | tf_op jit(solution)/shard_map/pallas_call | solution.py:74
  318.4 2.5 collective-permute-start.8
  320.8 1.7 bitcast_dynamic-update-slice_fusion.6
  322.5 1.9 collective-permute-start.9
  324.4 1.7 bitcast_dynamic-update-slice_fusion.5
  326.1 1.4 collective-permute-done.5
  327.5 0.7 bitcast_dynamic-update-slice_fusion.4
  328.2 0.7 bitcast_dynamic-update-slice_fusion.3
  329.0 0.7 bitcast_dynamic-update-slice_fusion.2
  329.7 8.0 %collective-permute-done.8 = bf16[2,8,64,128]{3,2,1,0:T(8,128)(2,1)S(1)} collective-permute-done((bf16[2,8,64,128]{3,2,1,0:T(8,128)(2,1)S(1)}, bf16[2,8,64,128]{3,2,1,0:T(8,128)(2,1)S(1)}, u32[]{:S(2)}, u32[]{:S(2)}) %collective-permute-start.8) | collective-permute-done | bytes 262176 | tf_op jit(solution)/shard_map/ppermute | solution.py:170
  337.7 0.7 bitcast_dynamic-update-slice_fusion.1
  338.4 0.7 bitcast_dynamic-update-slice_fusion
  339.1 3.4 %shard_map.77 = bf16[8,64,1024]{2,1,0:T(8,128)(2,1)} custom-call(s32[16]{0:T(128)S(1)} %get-tuple-element.15.target_ref, bf16[16,8,64,128]{3,2,1,0:T(8,128)(2,1)} %bitcast.37.back_ref), custom_call_target="tpu_custom_call" | custom-call | tf_op jit(solution)/shard_map/pallas_call | solution.py:143
  (52 shorter events, 4.0 us)
Async XLA Ops:
  0.6 5.2 %collective-permute-start = (s32[2,2]{1,0:T(2,128)}, s32[2,2]{1,0:T(2,128)S(1)}, u32[]{:S(2)}, u32[]{:S(2)}) collective-permute-start(s32[2,2]{1,0:T(2,128)} %param.9), channel_id=1, source_target_pairs={{0,1},{1,2},{2,3},{3,0},{4,5},{5,6},{6,7},{7,4},{8,9},{9,10},{10,1... | collective-permute-start | bytes 56 | tf_op jit(solution)/shard_map/ppermute | solution.py:156
  1.1 4.7 %collective-permute-start.1 = (s32[2,2]{1,0:T(2,128)}, s32[2,2]{1,0:T(2,128)S(1)}, u32[]{:S(2)}, u32[]{:S(2)}) collective-permute-start(s32[2,2]{1,0:T(2,128)} %param.9), channel_id=1, source_target_pairs={{0,2},{1,3},{2,0},{3,1},{4,6},{5,7},{6,4},{7,5},{8,10},{9,11},{10,... | collective-permute-start | bytes 56 | tf_op jit(solution)/shard_map/ppermute | solution.py:156
  3.7 2.9 collective-permute-start.2
  8.5 135.9 %all-to-all-start.1 = ((s32[8,2,1]{1,2,0:T(1,128)}), s32[8,2,1]{1,2,0:T(1,128)S(1)}, u32[]{:S(2)}, u32[]{:S(2)}) async-start(s32[8,2,1]{1,2,0:T(1,128)} %bitcast.9), calls=%async_computation.1 | async-start | bytes 8192 | tf_op jit(solution)/shard_map/all_to_all | solution.py:213
  144.4 6.2 %copy-start.2 = (bf16[8,128,1024]{2,1,0:T(8,128)(2,1)S(1)}, bf16[8,128,1024]{2,1,0:T(8,128)(2,1)}, u32[]{:S(2)}) copy-start(bf16[8,128,1024]{2,1,0:T(8,128)(2,1)} %param.7) | copy-start | bytes 6291460
  144.4 99.6 %all-to-all-start = ((bf16[16,2,8,64,128]{4,3,2,1,0:T(8,128)(2,1)}), bf16[16,2,8,64,128]{4,3,2,1,0:T(8,128)(2,1)}, u32[]{:S(2)}, u32[]{:S(2)}) async-start(bf16[16,2,8,64,128]{4,3,2,1,0:T(8,128)(2,1)} %shard_map.76), calls=%async_computation | async-start | bytes 8388608 | tf_op jit(solution)/shard_map/all_to_all | solution.py:212
  261.8 11.0 %all-to-all-start.2 = ((f32[16,3,512]{2,1,0:T(4,128)}), f32[16,3,512]{2,1,0:T(4,128)S(1)}, u32[]{:S(2)}, u32[]{:S(2)}) async-start(f32[16,3,512]{2,1,0:T(4,128)} %pad_maximum_fusion), calls=%async_computation.2 | async-start | bytes 262144 | tf_op jit(solution)/shard_map/all_to_all | solution.py:233
  275.0 10.2 %all-to-all-start.3 = ((f32[16,2,512]{2,1,0:T(2,128)}), f32[16,2,512]{2,1,0:T(2,128)S(1)}, u32[]{:S(2)}, u32[]{:S(2)}) async-start(f32[16,2,512]{2,1,0:T(2,128)} %gather_fusion.5), calls=%async_computation.3 | async-start | bytes 131072 | tf_op jit(solution)/shard_map/all_to_all | solution.py:245
  285.6 6.6 %copy-start.1 = (bf16[16,8,128,128]{3,2,1,0:T(8,128)(2,1)S(1)}, bf16[16,8,128,128]{3,2,1,0:T(8,128)(2,1)}, u32[]{:S(2)}) copy-start(bf16[16,8,128,128]{3,2,1,0:T(8,128)(2,1)} %gather_fusion.2) | copy-start | bytes 12582916
  296.2 22.2 %collective-permute-start.3 = (bf16[2,8,64,128]{3,2,1,0:T(8,128)(2,1)}, bf16[2,8,64,128]{3,2,1,0:T(8,128)(2,1)}, u32[]{:S(2)}, u32[]{:S(2)}) collective-permute-start(bf16[2,8,64,128]{3,2,1,0:T(8,128)(2,1)} %get-tuple-element.25), channel_id=1, source_target_pairs={{0,4},{4,8},{8,12},{12,16},{16,20},{20,24},{24,28},{28,0},{1,5},{5... | collective-permute-start | bytes 786440 | tf_op jit(solution)/shard_map/ppermute | solution.py:170
  296.6 25.9 %collective-permute-start.4 = (bf16[2,8,64,128]{3,2,1,0:T(8,128)(2,1)}, bf16[2,8,64,128]{3,2,1,0:T(8,128)(2,1)}, u32[]{:S(2)}, u32[]{:S(2)}) collective-permute-start(bf16[2,8,64,128]{3,2,1,0:T(8,128)(2,1)} %get-tuple-element.24), channel_id=1, source_target_pairs={{0,8},{4,12},{8,16},{12,20},{16,24},{20,28},{24,0},{28,4},{1,9},{5... | collective-permute-start | bytes 786440 | tf_op jit(solution)/shard_map/ppermute | solution.py:170
  297.5 30.0 %collective-permute-start.5 = (bf16[2,8,64,128]{3,2,1,0:T(8,128)(2,1)S(1)}, bf16[2,8,64,128]{3,2,1,0:T(8,128)(2,1)S(1)}, u32[]{:S(2)}, u32[]{:S(2)}) collective-permute-start(bf16[2,8,64,128]{3,2,1,0:T(8,128)(2,1)S(1)} %get-tuple-element.23), channel_id=1, source_target_pairs={{0,12},{4,16},{8,20},{12,24},{16,28},{20,0},{24,4},{28,8},{1,13},{... | collective-permute-start | bytes 786440 | tf_op jit(solution)/shard_map/ppermute | solution.py:170
  298.9 29.3 %collective-permute-start.6 = (bf16[2,8,64,128]{3,2,1,0:T(8,128)(2,1)S(1)}, bf16[2,8,64,128]{3,2,1,0:T(8,128)(2,1)S(1)}, u32[]{:S(2)}, u32[]{:S(2)}) collective-permute-start(bf16[2,8,64,128]{3,2,1,0:T(8,128)(2,1)S(1)} %get-tuple-element.22), channel_id=1, source_target_pairs={{0,16},{4,20},{8,24},{12,28},{16,0},{20,4},{24,8},{28,12},{1,17},{... | collective-permute-start | bytes 786440 | tf_op jit(solution)/shard_map/ppermute | solution.py:170
  301.8 27.2 %collective-permute-start.7 = (bf16[2,8,64,128]{3,2,1,0:T(8,128)(2,1)S(1)}, bf16[2,8,64,128]{3,2,1,0:T(8,128)(2,1)S(1)}, u32[]{:S(2)}, u32[]{:S(2)}) collective-permute-start(bf16[2,8,64,128]{3,2,1,0:T(8,128)(2,1)S(1)} %get-tuple-element.21), channel_id=1, source_target_pairs={{0,20},{4,24},{8,28},{12,0},{16,4},{20,8},{24,12},{28,16},{1,21},{... | collective-permute-start | bytes 786440 | tf_op jit(solution)/shard_map/ppermute | solution.py:170
  302.0 1.6 copy-start
  318.4 19.3 %collective-permute-start.8 = (bf16[2,8,64,128]{3,2,1,0:T(8,128)(2,1)S(1)}, bf16[2,8,64,128]{3,2,1,0:T(8,128)(2,1)S(1)}, u32[]{:S(2)}, u32[]{:S(2)}) collective-permute-start(bf16[2,8,64,128]{3,2,1,0:T(8,128)(2,1)S(1)} %get-tuple-element.20), channel_id=1, source_target_pairs={{0,24},{4,28},{8,0},{12,4},{16,8},{20,12},{24,16},{28,20},{1,25},{... | collective-permute-start | bytes 786440 | tf_op jit(solution)/shard_map/ppermute | solution.py:170
  322.5 15.9 %collective-permute-start.9 = (bf16[2,8,64,128]{3,2,1,0:T(8,128)(2,1)S(1)}, bf16[2,8,64,128]{3,2,1,0:T(8,128)(2,1)S(1)}, u32[]{:S(2)}, u32[]{:S(2)}) collective-permute-start(bf16[2,8,64,128]{3,2,1,0:T(8,128)(2,1)S(1)} %get-tuple-element.19), channel_id=1, source_target_pairs={{0,28},{4,0},{8,4},{12,8},{16,12},{20,16},{24,20},{28,24},{1,29},{... | collective-permute-start | bytes 786440 | tf_op jit(solution)/shard_map/ppermute | solution.py:170

commit v19 on v16

--- a/solution.py
+++ b/solution.py
@@ -252,7 +252,6 @@
     delta_here = stats_recv[:, 1].reshape(slot_total, heads_here, SPAN)
     softmax_p = jnp.exp(scores - norm_here[..., None])
     grad_s = (softmax_p * (grad_p - delta_here[..., None]) * score_scale).astype(jnp.bfloat16)
-    probs_low = softmax_p.astype(jnp.bfloat16)
     query_part = jnp.einsum(
         "bhij,bhjd->bhid", grad_s, key_heads, preferred_element_type=jnp.float32
     ).astype(jnp.bfloat16)
@@ -263,6 +262,8 @@
     else:
         query_back = lax.all_to_all(query_part, "seq", split_axis=0, concat_axis=0, tiled=True)
 
+    held_scores, _ = lax.optimization_barrier((scores, query_part))
+    probs_low = jnp.exp(held_scores - norm_here[..., None]).astype(jnp.bfloat16)
     key_grad, value_grad = kv_grads(row_recv, probs_low, grad_s, pair_recv, rows_here)
 
     query_grad = sum_parts(target, query_back)

time: 223 us -> 217 us (0.973)
  the two profiles are of different devices: /device:TPU:0 before, /device:TPU:15 now
where the time goes in v19:
time: 217 us; the launch traced here: 216 us
  waiting for transfers between devices  104 us (48%)
  starting transfers between devices  33.7 us (16%)
  local copies, waits for them, and re-layouts  30.5 us (14%)
  Pallas kernels  19.9 us (9%)
  matrix products  18 us (8%)
  other arithmetic  8.99 us (4%)
    all_to_all x1, waiting for transfers between devices, per_device(): lax.all_to_all(pair_send, 'seq', split_axis=0, concat_axis=0, tiled=True)  68.4 us
    ppermute x7, waiting for transfers between devices, seq_exchange(): lax.ppermute(lax.dynamic_index_in_dim(blocks, (me + shift) % seq_count, k...  25.1 us
    pallas_call x1, Pallas kernels, kv_grads(): pl.pallas_call(kv_kernel, grid_spec=grid_spec, out_shape=[out_shape, out_...  14.7 us
    dot_general x1, matrix products, per_device(): jnp.einsum('bhid,bhjd->bhij', grad_heads, value_heads, preferred_element_...  9 us
    ppermute x7, starting transfers between devices, seq_exchange(): lax.ppermute(lax.dynamic_index_in_dim(blocks, (me + shift) % seq_count, k...  8.81 us
    unnamed x12, local copies, waits for them, and re-layouts  8.74 us
    dot_general x1, matrix products, per_device(): jnp.einsum('bhid,bhjd->bhij', query_heads, key_heads, preferred_element_t...  7.78 us
    reshape x2, local copies, waits for them, and re-layouts, split_heads(): return tensor.reshape(tensor.shape[:-1] + (tensor.shape[-1] // HEAD, HEAD))  6.94 us
  transfers between devices with their start and end apart: 14, of which 8 were waited for; matrix products, arithmetic and copies ran while one was open for 12% of the time, Pallas kernels for 8%

profile of v19, /device:TPU:15, one launch (start us, length us, event | category | flops | bytes accessed | tf_op | source)
XLA Modules:
  0.0 216.1 jit_solution(6883099488669425616)
XLA Ops:
  0.6 0.9 collective-permute-start
  1.5 1.2 collective-permute-start.1
  2.7 0.7 constant_dynamic-update-slice_fusion.3
  3.4 0.7 collective-permute-done.1
  4.2 1.7 collective-permute-done.2
  6.0 0.2 convert_reduce_fusion
  6.5 0.7 gather_fusion.1
  7.1 0.7 select_n.238
  7.8 5.7 %all-to-all-start.1 = ((s32[8,2,1]{1,2,0:T(1,128)}), s32[8,2,1]{1,2,0:T(1,128)S(1)}, u32[]{:S(2)}, u32[]{:S(2)}) async-start(s32[8,2,1]{1,2,0:T(1,128)} %bitcast.9), calls=%async_computation.1 | async-start | bytes 8192 | tf_op jit(solution)/shard_map/all_to_all | solution.py:215
  13.5 0.7 gather_fusion
  14.2 1.2 copy-done
  15.4 1.2 copy-done.1
  16.6 3.3 %shard_map.76 = bf16[16,2,8,64,128]{4,3,2,1,0:T(8,128)(2,1)} custom-call(s32[16]{0:T(128)S(1)} %broadcast_clamp_fusion.1.span_ref, bf16[8,64,1024]{2,1,0:T(8,128)(2,1)S(1)} %copy-done, bf16[8,64,1024]{2,1,0:T(8,128)(2,1)S(1)} %copy-done.1), custom_call_target="tpu_custom_call" | custom-call | tf_op jit(solution)/shard_map/pallas_call | solution.py:112
  20.0 5.6 %all-to-all-start = ((bf16[16,2,8,64,128]{4,3,2,1,0:T(8,128)(2,1)}), bf16[16,2,8,64,128]{4,3,2,1,0:T(8,128)(2,1)}, u32[]{:S(2)}, u32[]{:S(2)}) async-start(bf16[16,2,8,64,128]{4,3,2,1,0:T(8,128)(2,1)} %shard_map.76), calls=%async_computation | async-start | bytes 8388608 | tf_op jit(solution)/shard_map/all_to_all | solution.py:214
  25.5 2.4 %copy.26 = bf16[8,128,1024]{1,2,0:T(8,128)(2,1)} copy(bf16[8,128,1024]{2,1,0:T(8,128)(2,1)S(1)} %copy-done.4) | data formatting | bytes 4194304 | tf_op args[2]
  27.9 3.0 %copy.27 = bf16[8,128,8,128]{3,1,2,0:T(8,128)(2,1)S(1)} copy(bf16[8,128,8,128]{1,3,2,0:T(8,128)(2,1)} %bitcast.101) | data formatting | bytes 4194304 | tf_op jit(solution)/shard_map/reshape | solution.py:17
  30.9 3.9 %copy.29 = bf16[8,128,1024]{1,2,0:T(8,128)(2,1)} copy(bf16[8,128,1024]{2,1,0:T(8,128)(2,1)} %param.8) | data formatting | bytes 4194304 | tf_op args[3]
  34.8 3.9 %copy.30 = bf16[8,128,8,128]{3,1,2,0:T(8,128)(2,1)} copy(bf16[8,128,8,128]{1,3,2,0:T(8,128)(2,1)} %bitcast.102) | data formatting | bytes 4194304 | tf_op jit(solution)/shard_map/reshape | solution.py:17
  38.9 0.5 broadcast.317
  39.4 0.7 fusion.13
  40.1 3.1 %gather_fusion.2 = bf16[16,8,128,128]{3,2,1,0:T(8,128)(2,1)} fusion(bf16[8,8,128,128]{3,2,1,0:T(8,128)(2,1)S(1)} %bitcast.98, s32[1024]{0:T(1024)S(1)} %pad_clamp_fusion.2), kind=kCustom, calls=%fused_computation.2 | custom fusion | bytes 8388672 | tf_op jit(solution)/shard_map/gather | solution.py:220
  43.2 4.6 %gather_fusion.3 = bf16[16,8,128,128]{3,2,1,0:T(8,128)(2,1)} fusion(bf16[8,8,128,128]{3,2,1,0:T(8,128)(2,1)} %bitcast.99, s32[1024]{0:T(1024)S(1)} %pad_clamp_fusion.2), kind=kCustom, calls=%fused_computation.3 | custom fusion | bytes 8388672 | tf_op jit(solution)/shard_map/gather | solution.py:221
  47.8 68.4 %all-to-all-done.pair_ref = bf16[16,2,8,64,128]{4,3,2,1,0:T(8,128)(2,1)} async-done(((bf16[16,2,8,64,128]{4,3,2,1,0:T(8,128)(2,1)}), bf16[16,2,8,64,128]{4,3,2,1,0:T(8,128)(2,1)}, u32[]{:S(2)}, u32[]{:S(2)}) %all-to-all-start) | async-done | bytes 4194336 | tf_op jit(solution)/shard_map/all_to_all | solution.py:214
  116.2 7.8 %fusion.15 = (f32[16,8,64]{2,1,0:T(8,128)S(1)}, f32[16,8,64,128]{3,2,1,0:T(8,128)}) fusion(bf16[16,8,128,128]{3,2,1,0:T(8,128)(2,1)} %gather_fusion.2, bf16[16,2,8,64,128]{4,3,2,1,0:T(8,128)(2,1)} %all-to-all-done.pair_ref), kind=kOutput, calls=%fused_computation.88 | convolution fusion | flops 270524416 | bytes 10518528 | tf_op jit(solution)/shard_map/bhid,bhjd->bhij/dot_general | solution.py:224
  124.1 9.0 %fusion = (f32[16,8,64]{2,1,0:T(8,128)S(1)}, f32[16,8,64]{2,1,0:T(8,128)S(1)}, f32[16,8,64,128]{3,2,1,0:T(8,128)}) fusion(f32[16,8,64,128]{3,2,1,0:T(8,128)} %get-tuple-element.6, f32[16,8,64]{2,1,0:T(8,128)S(1)} %get-tuple-element.35, bf16[16,8,128,128]{3,2,1,0:T(8,128)(2,1)} %gather_fusion.3, bf16[16,2,8,64,128]{4,3,2,1,0:T(8,128)(2,1)} %all-to-all-done.pair_ref), kind=kOutput, calls=%fused_computation.10 | convolution fusion | flops 272613376 | bytes 14778368 | tf_op jit(solution)/shard_map/bhid,bhjd->bhij/dot_general | solution.py:227
  133.3 0.7 pad_maximum_fusion
  134.0 6.5 %all-to-all-start.2 = ((f32[16,3,512]{2,1,0:T(4,128)}), f32[16,3,512]{2,1,0:T(4,128)S(1)}, u32[]{:S(2)}, u32[]{:S(2)}) async-start(f32[16,3,512]{2,1,0:T(4,128)} %pad_maximum_fusion), calls=%async_computation.2 | async-start | bytes 262144 | tf_op jit(solution)/shard_map/all_to_all | solution.py:235
  140.5 4.3 %all-to-all-done.2 = f32[16,3,512]{2,1,0:T(4,128)S(1)} async-done(((f32[16,3,512]{2,1,0:T(4,128)}), f32[16,3,512]{2,1,0:T(4,128)S(1)}, u32[]{:S(2)}, u32[]{:S(2)}) %all-to-all-start.2) | async-done | bytes 98336 | tf_op jit(solution)/shard_map/all_to_all | solution.py:235
  144.8 0.6 gather_fusion.4
  145.8 1.2 gather_fusion.5
  147.0 5.2 %all-to-all-start.3 = ((f32[16,2,512]{2,1,0:T(2,128)}), f32[16,2,512]{2,1,0:T(2,128)S(1)}, u32[]{:S(2)}, u32[]{:S(2)}) async-start(f32[16,2,512]{2,1,0:T(2,128)} %gather_fusion.5), calls=%async_computation.3 | async-start | bytes 131072 | tf_op jit(solution)/shard_map/all_to_all | solution.py:247
  152.3 3.8 %all-to-all-done.3 = f32[16,2,512]{2,1,0:T(2,128)S(1)} async-done(((f32[16,2,512]{2,1,0:T(2,128)}), f32[16,2,512]{2,1,0:T(2,128)S(1)}, u32[]{:S(2)}, u32[]{:S(2)}) %all-to-all-start.3) | async-done | bytes 65568 | tf_op jit(solution)/shard_map/all_to_all | solution.py:247
  156.1 0.2 slice_reduce_fusion.1
  156.4 5.5 %multiply_convert_fusion.grads_ref = bf16[16,8,64,128]{3,2,1,0:T(8,128)(2,1)S(1)} fusion(f32[16,8,64,128]{3,2,1,0:T(8,128)} %get-tuple-element.37, f32[16,8,64,128]{3,2,1,0:T(8,128)} %get-tuple-element.6, f32[16,8,64]{2,1,0:T(8,128)S(1)} %sub.94, f32[16,8,64]{2,1,0:T(8,128)S(1)} %sub.91), kind=kLoop, calls=%fused_computation.7 | loop fusion | flops 5242880 | bytes 10551296 | tf_op jit(solution)/shard_map/convert_element_type | solution.py:254
  161.9 1.2 convolution_convert_fusion
  163.1 0.5 broadcast_in_dim.70
  163.7 0.3 dynamic-slice_bitcast_fusion
  163.9 1.0 collective-permute-start.3
  164.9 0.4 collective-permute-start.4
  165.3 2.8 %collective-permute-start.5 = (bf16[2,8,64,128]{3,2,1,0:T(8,128)(2,1)S(1)}, bf16[2,8,64,128]{3,2,1,0:T(8,128)(2,1)S(1)}, u32[]{:S(2)}, u32[]{:S(2)}) collective-permute-start(bf16[2,8,64,128]{3,2,1,0:T(8,128)(2,1)S(1)} %get-tuple-element.23), channel_id=1, source_target_pairs={{0,12},{4,16},{8,20},{12,24},{16,28},{20,0},{24,4},{28,8},{1,13},{... | collective-permute-start | bytes 786440 | tf_op jit(solution)/shard_map/ppermute | solution.py:172
  168.1 2.3 %collective-permute-start.7 = (bf16[2,8,64,128]{3,2,1,0:T(8,128)(2,1)S(1)}, bf16[2,8,64,128]{3,2,1,0:T(8,128)(2,1)S(1)}, u32[]{:S(2)}, u32[]{:S(2)}) collective-permute-start(bf16[2,8,64,128]{3,2,1,0:T(8,128)(2,1)S(1)} %get-tuple-element.21), channel_id=1, source_target_pairs={{0,20},{4,24},{8,28},{12,0},{16,4},{20,8},{24,12},{28,16},{1,21},{... | collective-permute-start | bytes 786440 | tf_op jit(solution)/shard_map/ppermute | solution.py:172
  170.3 1.4 exponential_convert_fusion.probs_ref
  171.7 14.7 %shard_map.78 = (bf16[8,128,1024]{2,1,0:T(8,128)(2,1)}, bf16[8,128,1024]{2,1,0:T(8,128)(2,1)}) custom-call(s32[16]{0:T(128)S(1)} %all_to_all.18.rows_ref, bf16[16,8,64,128]{3,2,1,0:T(8,128)(2,1)S(1)} %exponential_convert_fusion.probs_ref, bf16[16,8,64,128]{3,2,1,0:T(8,128)(2,1)S(1)} %multiply_convert_fusion.grads_ref, ...), custom_call_target="tpu_custom_call" | custom-call | tf_op jit(solution)/shard_map/pallas_call | solution.py:74
  186.4 2.4 %collective-permute-start.8 = (bf16[2,8,64,128]{3,2,1,0:T(8,128)(2,1)S(1)}, bf16[2,8,64,128]{3,2,1,0:T(8,128)(2,1)S(1)}, u32[]{:S(2)}, u32[]{:S(2)}) collective-permute-start(bf16[2,8,64,128]{3,2,1,0:T(8,128)(2,1)S(1)} %get-tuple-element.20), channel_id=1, source_target_pairs={{0,24},{4,28},{8,0},{12,4},{16,8},{20,12},{24,16},{28,20},{1,25},{... | collective-permute-start | bytes 786440 | tf_op jit(solution)/shard_map/ppermute | solution.py:172
  189.0 12.2 %collective-permute-done.5 = bf16[2,8,64,128]{3,2,1,0:T(8,128)(2,1)S(1)} collective-permute-done((bf16[2,8,64,128]{3,2,1,0:T(8,128)(2,1)S(1)}, bf16[2,8,64,128]{3,2,1,0:T(8,128)(2,1)S(1)}, u32[]{:S(2)}, u32[]{:S(2)}) %collective-permute-start.5) | collective-permute-done | bytes 262176 | tf_op jit(solution)/shard_map/ppermute | solution.py:172
  201.2 5.6 %collective-permute-done.6 = bf16[2,8,64,128]{3,2,1,0:T(8,128)(2,1)S(1)} collective-permute-done((bf16[2,8,64,128]{3,2,1,0:T(8,128)(2,1)S(1)}, bf16[2,8,64,128]{3,2,1,0:T(8,128)(2,1)S(1)}, u32[]{:S(2)}, u32[]{:S(2)}) %collective-permute-start.6) | collective-permute-done | bytes 262176 | tf_op jit(solution)/shard_map/ppermute | solution.py:172
  206.9 7.3 %collective-permute-done.8 = bf16[2,8,64,128]{3,2,1,0:T(8,128)(2,1)S(1)} collective-permute-done((bf16[2,8,64,128]{3,2,1,0:T(8,128)(2,1)S(1)}, bf16[2,8,64,128]{3,2,1,0:T(8,128)(2,1)S(1)}, u32[]{:S(2)}, u32[]{:S(2)}) %collective-permute-start.8) | collective-permute-done | bytes 262176 | tf_op jit(solution)/shard_map/ppermute | solution.py:172
  214.3 1.8 shard_map.77
  (57 shorter events, 1.8 us)
Async XLA Ops:
  0.6 2.8 %collective-permute-start = (s32[2,2]{1,0:T(2,128)}, s32[2,2]{1,0:T(2,128)S(1)}, u32[]{:S(2)}, u32[]{:S(2)}) collective-permute-start(s32[2,2]{1,0:T(2,128)} %param.9), channel_id=1, source_target_pairs={{0,1},{1,2},{2,3},{3,0},{4,5},{5,6},{6,7},{7,4},{8,9},{9,10},{10,1... | collective-permute-start | bytes 56 | tf_op jit(solution)/shard_map/ppermute | solution.py:158
  1.5 2.7 %collective-permute-start.1 = (s32[2,2]{1,0:T(2,128)}, s32[2,2]{1,0:T(2,128)S(1)}, u32[]{:S(2)}, u32[]{:S(2)}) collective-permute-start(s32[2,2]{1,0:T(2,128)} %param.9), channel_id=1, source_target_pairs={{0,2},{1,3},{2,0},{3,1},{4,6},{5,7},{6,4},{7,5},{8,10},{9,11},{10,... | collective-permute-start | bytes 56 | tf_op jit(solution)/shard_map/ppermute | solution.py:158
  2.7 3.2 %collective-permute-start.2 = (s32[2,2]{1,0:T(2,128)}, s32[2,2]{1,0:T(2,128)S(1)}, u32[]{:S(2)}, u32[]{:S(2)}) collective-permute-start(s32[2,2]{1,0:T(2,128)} %param.9), channel_id=1, source_target_pairs={{0,3},{1,0},{2,1},{3,2},{4,7},{5,4},{6,5},{7,6},{8,11},{9,8},{10,9... | collective-permute-start | bytes 56 | tf_op jit(solution)/shard_map/ppermute | solution.py:158
  7.8 12.1 %all-to-all-start.1 = ((s32[8,2,1]{1,2,0:T(1,128)}), s32[8,2,1]{1,2,0:T(1,128)S(1)}, u32[]{:S(2)}, u32[]{:S(2)}) async-start(s32[8,2,1]{1,2,0:T(1,128)} %bitcast.9), calls=%async_computation.1 | async-start | bytes 8192 | tf_op jit(solution)/shard_map/all_to_all | solution.py:215
  14.2 1.2 copy-start
  15.4 1.2 copy-start.1
  19.9 5.6 %copy-start.4 = (bf16[8,128,1024]{2,1,0:T(8,128)(2,1)S(1)}, bf16[8,128,1024]{2,1,0:T(8,128)(2,1)}, u32[]{:S(2)}) copy-start(bf16[8,128,1024]{2,1,0:T(8,128)(2,1)} %param.7) | copy-start | bytes 6291460
  20.0 96.3 %all-to-all-start = ((bf16[16,2,8,64,128]{4,3,2,1,0:T(8,128)(2,1)}), bf16[16,2,8,64,128]{4,3,2,1,0:T(8,128)(2,1)}, u32[]{:S(2)}, u32[]{:S(2)}) async-start(bf16[16,2,8,64,128]{4,3,2,1,0:T(8,128)(2,1)} %shard_map.76), calls=%async_computation | async-start | bytes 8388608 | tf_op jit(solution)/shard_map/all_to_all | solution.py:214
  134.0 10.8 %all-to-all-start.2 = ((f32[16,3,512]{2,1,0:T(4,128)}), f32[16,3,512]{2,1,0:T(4,128)S(1)}, u32[]{:S(2)}, u32[]{:S(2)}) async-start(f32[16,3,512]{2,1,0:T(4,128)} %pad_maximum_fusion), calls=%async_computation.2 | async-start | bytes 262144 | tf_op jit(solution)/shard_map/all_to_all | solution.py:235
  147.0 9.0 %all-to-all-start.3 = ((f32[16,2,512]{2,1,0:T(2,128)}), f32[16,2,512]{2,1,0:T(2,128)S(1)}, u32[]{:S(2)}, u32[]{:S(2)}) async-start(f32[16,2,512]{2,1,0:T(2,128)} %gather_fusion.5), calls=%async_computation.3 | async-start | bytes 131072 | tf_op jit(solution)/shard_map/all_to_all | solution.py:247
  156.4 5.5 %copy-start.3 = (bf16[16,8,128,128]{3,2,1,0:T(8,128)(2,1)S(1)}, bf16[16,8,128,128]{3,2,1,0:T(8,128)(2,1)}, u32[]{:S(2)}) copy-start(bf16[16,8,128,128]{3,2,1,0:T(8,128)(2,1)} %gather_fusion.2) | copy-start | bytes 12582916
  163.1 7.2 %copy-start.2 = (f32[16,8,64,128]{3,2,1,0:T(8,128)S(1)}, f32[16,8,64,128]{3,2,1,0:T(8,128)}, u32[]{:S(2)}) copy-start(f32[16,8,64,128]{3,2,1,0:T(8,128)} %get-tuple-element.6) | copy-start | bytes 12582916
  163.9 22.5 %collective-permute-start.3 = (bf16[2,8,64,128]{3,2,1,0:T(8,128)(2,1)S(1)}, bf16[2,8,64,128]{3,2,1,0:T(8,128)(2,1)S(1)}, u32[]{:S(2)}, u32[]{:S(2)}) collective-permute-start(bf16[2,8,64,128]{3,2,1,0:T(8,128)(2,1)S(1)} %get-tuple-element.25), channel_id=1, source_target_pairs={{0,4},{4,8},{8,12},{12,16},{16,20},{20,24},{24,28},{28,0},{1,5},{5... | collective-permute-start | bytes 786440 | tf_op jit(solution)/shard_map/ppermute | solution.py:172
  164.9 23.9 %collective-permute-start.4 = (bf16[2,8,64,128]{3,2,1,0:T(8,128)(2,1)S(1)}, bf16[2,8,64,128]{3,2,1,0:T(8,128)(2,1)S(1)}, u32[]{:S(2)}, u32[]{:S(2)}) collective-permute-start(bf16[2,8,64,128]{3,2,1,0:T(8,128)(2,1)S(1)} %get-tuple-element.24), channel_id=1, source_target_pairs={{0,8},{4,12},{8,16},{12,20},{16,24},{20,28},{24,0},{28,4},{1,9},{5... | collective-permute-start | bytes 786440 | tf_op jit(solution)/shard_map/ppermute | solution.py:172
  165.3 35.9 %collective-permute-start.5 = (bf16[2,8,64,128]{3,2,1,0:T(8,128)(2,1)S(1)}, bf16[2,8,64,128]{3,2,1,0:T(8,128)(2,1)S(1)}, u32[]{:S(2)}, u32[]{:S(2)}) collective-permute-start(bf16[2,8,64,128]{3,2,1,0:T(8,128)(2,1)S(1)} %get-tuple-element.23), channel_id=1, source_target_pairs={{0,12},{4,16},{8,20},{12,24},{16,28},{20,0},{24,4},{28,8},{1,13},{... | collective-permute-start | bytes 786440 | tf_op jit(solution)/shard_map/ppermute | solution.py:172
  168.1 38.7 %collective-permute-start.6 = (bf16[2,8,64,128]{3,2,1,0:T(8,128)(2,1)S(1)}, bf16[2,8,64,128]{3,2,1,0:T(8,128)(2,1)S(1)}, u32[]{:S(2)}, u32[]{:S(2)}) collective-permute-start(bf16[2,8,64,128]{3,2,1,0:T(8,128)(2,1)S(1)} %get-tuple-element.22), channel_id=1, source_target_pairs={{0,16},{4,20},{8,24},{12,28},{16,0},{20,4},{24,8},{28,12},{1,17},{... | collective-permute-start | bytes 786440 | tf_op jit(solution)/shard_map/ppermute | solution.py:172
  168.1 38.8 %collective-permute-start.7 = (bf16[2,8,64,128]{3,2,1,0:T(8,128)(2,1)S(1)}, bf16[2,8,64,128]{3,2,1,0:T(8,128)(2,1)S(1)}, u32[]{:S(2)}, u32[]{:S(2)}) collective-permute-start(bf16[2,8,64,128]{3,2,1,0:T(8,128)(2,1)S(1)} %get-tuple-element.21), channel_id=1, source_target_pairs={{0,20},{4,24},{8,28},{12,0},{16,4},{20,8},{24,12},{28,16},{1,21},{... | collective-permute-start | bytes 786440 | tf_op jit(solution)/shard_map/ppermute | solution.py:172
  186.4 27.7 %collective-permute-start.8 = (bf16[2,8,64,128]{3,2,1,0:T(8,128)(2,1)S(1)}, bf16[2,8,64,128]{3,2,1,0:T(8,128)(2,1)S(1)}, u32[]{:S(2)}, u32[]{:S(2)}) collective-permute-start(bf16[2,8,64,128]{3,2,1,0:T(8,128)(2,1)S(1)} %get-tuple-element.20), channel_id=1, source_target_pairs={{0,24},{4,28},{8,0},{12,4},{16,8},{20,12},{24,16},{28,20},{1,25},{... | collective-permute-start | bytes 786440 | tf_op jit(solution)/shard_map/ppermute | solution.py:172
  188.8 25.4 %collective-permute-start.9 = (bf16[2,8,64,128]{3,2,1,0:T(8,128)(2,1)S(1)}, bf16[2,8,64,128]{3,2,1,0:T(8,128)(2,1)S(1)}, u32[]{:S(2)}, u32[]{:S(2)}) collective-permute-start(bf16[2,8,64,128]{3,2,1,0:T(8,128)(2,1)S(1)} %get-tuple-element.19), channel_id=1, source_target_pairs={{0,28},{4,0},{8,4},{12,8},{16,12},{20,16},{24,20},{28,24},{1,29},{... | collective-permute-start | bytes 786440 | tf_op jit(solution)/shard_map/ppermute | solution.py:172

commit v20 on v19

--- a/solution.py
+++ b/solution.py
@@ -233,6 +233,16 @@
         [highest, jnp.sum(expons, axis=3), jnp.sum(expons * grad_p, axis=3)], axis=1
     ).reshape(slot_total, 3, heads_here * SPAN)
     back = lax.all_to_all(part, "seq", split_axis=0, concat_axis=0, tiled=True)
+    query_heads, grad_heads, key_heads, value_heads, _ = lax.optimization_barrier(
+        (query_heads, grad_heads, key_heads, value_heads, part)
+    )
+    scores = (
+        jnp.einsum("bhid,bhjd->bhij", query_heads, key_heads, preferred_element_type=jnp.float32)
+        * score_scale
+    )
+    grad_p = jnp.einsum(
+        "bhid,bhjd->bhij", grad_heads, value_heads, preferred_element_type=jnp.float32
+    )
 
     item_part = back[target].reshape(span_count, NBR, 3, heads_here * SPAN)
     item_max = item_part[:, :, 0]

time: 217 us -> 223 us (1.028)
  the two profiles are of different devices: /device:TPU:15 before, /device:TPU:0 now
where the time goes in v20:
time: 223 us; the launch traced here: 219 us
  waiting for transfers between devices  90 us (40%)
  starting transfers between devices  36.1 us (16%)
  local copies, waits for them, and re-layouts  35.2 us (16%)
  matrix products  29.5 us (13%)
  Pallas kernels  19.9 us (9%)
  other arithmetic  7.48 us (3%)
    all_to_all x1, waiting for transfers between devices, per_device(): lax.all_to_all(pair_send, 'seq', split_axis=0, concat_axis=0, tiled=True)  71 us
    dot_general x2, matrix products, per_device(): jnp.einsum('bhid,bhjd->bhij', query_heads, key_heads, preferred_element_t...  15.5 us
    ppermute x7, waiting for transfers between devices, seq_exchange(): lax.ppermute(lax.dynamic_index_in_dim(blocks, (me + shift) % seq_count, k...  15.5 us
    pallas_call x1, Pallas kernels, kv_grads(): pl.pallas_call(kv_kernel, grid_spec=grid_spec, out_shape=[out_shape, out_...  14.7 us
    dot_general x2, matrix products, per_device(): jnp.einsum('bhid,bhjd->bhij', grad_heads, value_heads, preferred_element_...  12.8 us
    ppermute x7, starting transfers between devices, seq_exchange(): lax.ppermute(lax.dynamic_index_in_dim(blocks, (me + shift) % seq_count, k...  12.5 us
    unnamed x12, local copies, waits for them, and re-layouts  8.75 us
    reshape x2, local copies, waits for them, and re-layouts, split_heads(): return tensor.reshape(tensor.shape[:-1] + (tensor.shape[-1] // HEAD, HEAD))  6.94 us
  transfers between devices with their start and end apart: 14, of which 6 were waited for; matrix products, arithmetic and copies ran while one was open for 17% of the time, Pallas kernels for 8%

profile of v20, /device:TPU:0, one launch (start us, length us, event | category | flops | bytes accessed | tf_op | source)
XLA Modules:
  0.0 219.1 jit_solution(10803803105419905717)
XLA Ops:
  0.6 0.5 collective-permute-start
  1.1 2.6 %collective-permute-start.1 = (s32[2,2]{1,0:T(2,128)}, s32[2,2]{1,0:T(2,128)S(1)}, u32[]{:S(2)}, u32[]{:S(2)}) collective-permute-start(s32[2,2]{1,0:T(2,128)} %param.9), channel_id=1, source_target_pairs={{0,2},{1,3},{2,0},{3,1},{4,6},{5,7},{6,4},{7,5},{8,10},{9,11},{10,... | collective-permute-start | bytes 56 | tf_op jit(solution)/shard_map/ppermute | solution.py:158
  3.7 1.4 collective-permute-start.2
  5.1 0.7 constant_dynamic-update-slice_fusion.3
  5.8 0.8 collective-permute-done.2
  7.2 0.7 gather_fusion.1
  7.8 0.7 select_n.238
  8.5 5.8 %all-to-all-start.1 = ((s32[8,2,1]{1,2,0:T(1,128)}), s32[8,2,1]{1,2,0:T(1,128)S(1)}, u32[]{:S(2)}, u32[]{:S(2)}) async-start(s32[8,2,1]{1,2,0:T(1,128)} %bitcast.10), calls=%async_computation.1 | async-start | bytes 8192 | tf_op jit(solution)/shard_map/all_to_all | solution.py:215
  14.3 0.7 gather_fusion
  15.0 1.2 copy-done
  16.2 1.2 copy-done.1
  17.5 3.3 %shard_map.76 = bf16[16,2,8,64,128]{4,3,2,1,0:T(8,128)(2,1)} custom-call(s32[16]{0:T(128)S(1)} %broadcast_clamp_fusion.1.span_ref, bf16[8,64,1024]{2,1,0:T(8,128)(2,1)S(1)} %copy-done, bf16[8,64,1024]{2,1,0:T(8,128)(2,1)S(1)} %copy-done.1), custom_call_target="tpu_custom_call" | custom-call | tf_op jit(solution)/shard_map/pallas_call | solution.py:112
  20.8 6.1 %all-to-all-start = ((bf16[16,2,8,64,128]{4,3,2,1,0:T(8,128)(2,1)}), bf16[16,2,8,64,128]{4,3,2,1,0:T(8,128)(2,1)}, u32[]{:S(2)}, u32[]{:S(2)}) async-start(bf16[16,2,8,64,128]{4,3,2,1,0:T(8,128)(2,1)} %shard_map.76), calls=%async_computation | async-start | bytes 8388608 | tf_op jit(solution)/shard_map/all_to_all | solution.py:214
  26.9 2.4 %copy.26 = bf16[8,128,1024]{1,2,0:T(8,128)(2,1)} copy(bf16[8,128,1024]{2,1,0:T(8,128)(2,1)S(1)} %copy-done.4) | data formatting | bytes 4194304 | tf_op args[2]
  29.3 3.0 %copy.27 = bf16[8,128,8,128]{3,1,2,0:T(8,128)(2,1)S(1)} copy(bf16[8,128,8,128]{1,3,2,0:T(8,128)(2,1)} %bitcast.103) | data formatting | bytes 4194304 | tf_op jit(solution)/shard_map/reshape | solution.py:17
  32.3 3.9 %copy.29 = bf16[8,128,1024]{1,2,0:T(8,128)(2,1)} copy(bf16[8,128,1024]{2,1,0:T(8,128)(2,1)} %param.8) | data formatting | bytes 4194304 | tf_op args[3]
  36.3 3.9 %copy.30 = bf16[8,128,8,128]{3,1,2,0:T(8,128)(2,1)} copy(bf16[8,128,8,128]{1,3,2,0:T(8,128)(2,1)} %bitcast.104) | data formatting | bytes 4194304 | tf_op jit(solution)/shard_map/reshape | solution.py:17
  40.3 0.5 broadcast.320
  40.8 0.7 fusion.13
  41.6 3.1 %gather_fusion.2 = bf16[16,8,128,128]{3,2,1,0:T(8,128)(2,1)} fusion(bf16[8,8,128,128]{3,2,1,0:T(8,128)(2,1)S(1)} %bitcast.100, s32[1024]{0:T(1024)S(1)} %pad_clamp_fusion.2), kind=kCustom, calls=%fused_computation.2 | custom fusion | bytes 8388672 | tf_op jit(solution)/shard_map/gather | solution.py:220
  44.7 4.6 %gather_fusion.3 = bf16[16,8,128,128]{3,2,1,0:T(8,128)(2,1)} fusion(bf16[8,8,128,128]{3,2,1,0:T(8,128)(2,1)} %bitcast.101, s32[1024]{0:T(1024)S(1)} %pad_clamp_fusion.2), kind=kCustom, calls=%fused_computation.3 | custom fusion | bytes 8388672 | tf_op jit(solution)/shard_map/gather | solution.py:221
  49.4 71.0 %all-to-all-done.pair_ref = bf16[16,2,8,64,128]{4,3,2,1,0:T(8,128)(2,1)} async-done(((bf16[16,2,8,64,128]{4,3,2,1,0:T(8,128)(2,1)}), bf16[16,2,8,64,128]{4,3,2,1,0:T(8,128)(2,1)}, u32[]{:S(2)}, u32[]{:S(2)}) %all-to-all-start) | async-done | bytes 4194336 | tf_op jit(solution)/shard_map/all_to_all | solution.py:214
  120.4 7.8 %multiply_reduce_fusion.1 = (f32[16,8,64]{2,1,0:T(8,128)S(1)}, f32[16,8,64,128]{3,2,1,0:T(8,128)}) fusion(bf16[16,8,128,128]{3,2,1,0:T(8,128)(2,1)} %gather_fusion.2, bf16[16,2,8,64,128]{4,3,2,1,0:T(8,128)(2,1)} %all-to-all-done.pair_ref), kind=kOutput, calls=%fused_computation.10 | convolution fusion | flops 270524416 | bytes 10518528 | tf_op jit(solution)/shard_map/bhid,bhjd->bhij/dot_general | solution.py:224
  128.3 3.9 %fusion = f32[16,8,64]{2,1,0:T(8,128)S(1)} fusion(f32[16,8,64,128]{3,2,1,0:T(8,128)} %get-tuple-element.44, f32[16,8,64]{2,1,0:T(8,128)S(1)} %get-tuple-element.43), kind=kLoop, calls=%fused_computation.11 | loop fusion | flops 3137536 | bytes 4259840 | tf_op jit(solution)/shard_map/reduce_sum | solution.py:233
  132.3 7.2 %multiply_reduce_fusion = f32[16,8,64]{2,1,0:T(8,128)S(1)} fusion(f32[16,8,64,128]{3,2,1,0:T(8,128)} %get-tuple-element.44, bf16[16,8,128,128]{3,2,1,0:T(8,128)(2,1)} %gather_fusion.3, f32[16,8,64]{2,1,0:T(8,128)S(1)} %get-tuple-element.43, bf16[16,2,8,64,128]{4,3,2,1,0:T(8,128)(2,1)} %all-to-all-done.pair_ref), kind=kOutput, calls=%fused_computation.8 | convolution fusion | flops 272621568 | bytes 10551296 | tf_op jit(solution)/shard_map/bhid,bhjd->bhij/dot_general | solution.py:227
  139.6 0.7 pad_maximum_fusion
  140.3 3.6 %all-to-all-start.2 = ((f32[16,3,512]{2,1,0:T(4,128)}), f32[16,3,512]{2,1,0:T(4,128)S(1)}, u32[]{:S(2)}, u32[]{:S(2)}) async-start(f32[16,3,512]{2,1,0:T(4,128)} %pad_maximum_fusion), calls=%async_computation.2 | async-start | bytes 262144 | tf_op jit(solution)/shard_map/all_to_all | solution.py:235
  144.0 4.7 %slice_bitcast_fusion = (bf16[16,8,64,128]{3,2,1,0:T(8,128)(2,1)S(1)}, bf16[16,8,64,128]{3,2,1,0:T(8,128)(2,1)}) fusion(bf16[16,2,8,64,128]{4,3,2,1,0:T(8,128)(2,1)} %all-to-all-done.pair_ref), kind=kLoop, calls=%fused_computation.13 | loop fusion | bytes 8388608 | tf_op jit(solution)/shard_map/squeeze | solution.py:219
  148.7 2.7 %all-to-all-done.2 = f32[16,3,512]{2,1,0:T(4,128)S(1)} async-done(((f32[16,3,512]{2,1,0:T(4,128)}), f32[16,3,512]{2,1,0:T(4,128)S(1)}, u32[]{:S(2)}, u32[]{:S(2)}) %all-to-all-start.2) | async-done | bytes 98336 | tf_op jit(solution)/shard_map/all_to_all | solution.py:235
  151.3 0.6 gather_fusion.4
  152.3 1.2 gather_fusion.5
  153.5 3.5 %all-to-all-start.3 = ((f32[16,2,512]{2,1,0:T(2,128)}), f32[16,2,512]{2,1,0:T(2,128)S(1)}, u32[]{:S(2)}, u32[]{:S(2)}) async-start(f32[16,2,512]{2,1,0:T(2,128)} %gather_fusion.5), calls=%async_computation.3 | async-start | bytes 131072 | tf_op jit(solution)/shard_map/all_to_all | solution.py:257
  157.1 7.8 %convolution_multiply_fusion = f32[16,8,64,128]{3,2,1,0:T(8,128)} fusion(bf16[16,8,64,128]{3,2,1,0:T(8,128)(2,1)} %get-tuple-element.10, bf16[16,8,128,128]{3,2,1,0:T(8,128)(2,1)} %gather_fusion.2), kind=kOutput, calls=%fused_computation.12 | convolution fusion | flops 269484032 | bytes 10485760 | tf_op jit(solution)/shard_map/bhid,bhjd->bhij/dot_general | solution.py:240
  165.2 5.6 %multiply_convert_fusion.grads_ref = bf16[16,8,64,128]{3,2,1,0:T(8,128)(2,1)S(1)} fusion(f32[16,8,64,128]{3,2,1,0:T(8,128)} %convolution_multiply_fusion, bf16[16,8,64,128]{3,2,1,0:T(8,128)(2,1)S(1)} %get-tuple-element.12, bf16[16,8,128,128]{3,2,1,0:T(8,128)(2,1)} %gather_fusion.3, f32[16,8,64]{2,1,0:T(8,128)S(1)} %sub.94, f32[16,8,64]{2,1,0:T(8,128)S(1)} %sub.91), kind=kOutput, calls=%fused_computation.7 | convolution fusion | flops 273678336 | bytes 12648448 | tf_op jit(solution)/shard_map/bhid,bhjd->bhij/dot_general | solution.py:243
  170.8 1.2 convolution_convert_fusion
  172.0 0.5 broadcast_in_dim.70
  172.8 1.9 collective-permute-start.3
  174.7 1.5 collective-permute-start.4
  176.1 1.4 exponential_convert_fusion.probs_ref
  177.5 2.4 %collective-permute-start.5 = (bf16[2,8,64,128]{3,2,1,0:T(8,128)(2,1)S(1)}, bf16[2,8,64,128]{3,2,1,0:T(8,128)(2,1)S(1)}, u32[]{:S(2)}, u32[]{:S(2)}) collective-permute-start(bf16[2,8,64,128]{3,2,1,0:T(8,128)(2,1)S(1)} %get-tuple-element.31), channel_id=1, source_target_pairs={{0,12},{4,16},{8,20},{12,24},{16,28},{20,0},{24,4},{28,8},{1,13},{... | collective-permute-start | bytes 786440 | tf_op jit(solution)/shard_map/ppermute | solution.py:172
  179.9 1.5 collective-permute-start.6
  181.4 2.4 %collective-permute-start.7 = (bf16[2,8,64,128]{3,2,1,0:T(8,128)(2,1)S(1)}, bf16[2,8,64,128]{3,2,1,0:T(8,128)(2,1)S(1)}, u32[]{:S(2)}, u32[]{:S(2)}) collective-permute-start(bf16[2,8,64,128]{3,2,1,0:T(8,128)(2,1)S(1)} %get-tuple-element.29), channel_id=1, source_target_pairs={{0,20},{4,24},{8,28},{12,0},{16,4},{20,8},{24,12},{28,16},{1,21},{... | collective-permute-start | bytes 786440 | tf_op jit(solution)/shard_map/ppermute | solution.py:172
  183.7 14.7 %shard_map.78 = (bf16[8,128,1024]{2,1,0:T(8,128)(2,1)}, bf16[8,128,1024]{2,1,0:T(8,128)(2,1)}) custom-call(s32[16]{0:T(128)S(1)} %all_to_all.18.rows_ref, bf16[16,8,64,128]{3,2,1,0:T(8,128)(2,1)S(1)} %exponential_convert_fusion.probs_ref, bf16[16,8,64,128]{3,2,1,0:T(8,128)(2,1)S(1)} %multiply_convert_fusion.grads_ref, ...), custom_call_target="tpu_custom_call" | custom-call | tf_op jit(solution)/shard_map/pallas_call | solution.py:74
  198.5 1.5 collective-permute-start.8
  200.0 1.5 collective-permute-start.9
  201.5 3.9 %collective-permute-done.5 = bf16[2,8,64,128]{3,2,1,0:T(8,128)(2,1)S(1)} collective-permute-done((bf16[2,8,64,128]{3,2,1,0:T(8,128)(2,1)S(1)}, bf16[2,8,64,128]{3,2,1,0:T(8,128)(2,1)S(1)}, u32[]{:S(2)}, u32[]{:S(2)}) %collective-permute-start.5) | collective-permute-done | bytes 262176 | tf_op jit(solution)/shard_map/ppermute | solution.py:172
  206.1 11.1 %collective-permute-done.8 = bf16[2,8,64,128]{3,2,1,0:T(8,128)(2,1)S(1)} collective-permute-done((bf16[2,8,64,128]{3,2,1,0:T(8,128)(2,1)S(1)}, bf16[2,8,64,128]{3,2,1,0:T(8,128)(2,1)S(1)}, u32[]{:S(2)}, u32[]{:S(2)}) %collective-permute-start.8) | collective-permute-done | bytes 262176 | tf_op jit(solution)/shard_map/ppermute | solution.py:172
  217.3 1.8 shard_map.77
  (60 shorter events, 2.8 us)
Async XLA Ops:
  0.6 5.2 %collective-permute-start = (s32[2,2]{1,0:T(2,128)}, s32[2,2]{1,0:T(2,128)S(1)}, u32[]{:S(2)}, u32[]{:S(2)}) collective-permute-start(s32[2,2]{1,0:T(2,128)} %param.9), channel_id=1, source_target_pairs={{0,1},{1,2},{2,3},{3,0},{4,5},{5,6},{6,7},{7,4},{8,9},{9,10},{10,1... | collective-permute-start | bytes 56 | tf_op jit(solution)/shard_map/ppermute | solution.py:158
  1.1 4.7 %collective-permute-start.1 = (s32[2,2]{1,0:T(2,128)}, s32[2,2]{1,0:T(2,128)S(1)}, u32[]{:S(2)}, u32[]{:S(2)}) collective-permute-start(s32[2,2]{1,0:T(2,128)} %param.9), channel_id=1, source_target_pairs={{0,2},{1,3},{2,0},{3,1},{4,6},{5,7},{6,4},{7,5},{8,10},{9,11},{10,... | collective-permute-start | bytes 56 | tf_op jit(solution)/shard_map/ppermute | solution.py:158
  3.7 2.9 %collective-permute-start.2 = (s32[2,2]{1,0:T(2,128)}, s32[2,2]{1,0:T(2,128)S(1)}, u32[]{:S(2)}, u32[]{:S(2)}) collective-permute-start(s32[2,2]{1,0:T(2,128)} %param.9), channel_id=1, source_target_pairs={{0,3},{1,0},{2,1},{3,2},{4,7},{5,4},{6,5},{7,6},{8,11},{9,8},{10,9... | collective-permute-start | bytes 56 | tf_op jit(solution)/shard_map/ppermute | solution.py:158
  8.5 12.3 %all-to-all-start.1 = ((s32[8,2,1]{1,2,0:T(1,128)}), s32[8,2,1]{1,2,0:T(1,128)S(1)}, u32[]{:S(2)}, u32[]{:S(2)}) async-start(s32[8,2,1]{1,2,0:T(1,128)} %bitcast.10), calls=%async_computation.1 | async-start | bytes 8192 | tf_op jit(solution)/shard_map/all_to_all | solution.py:215
  15.0 1.2 copy-start
  16.2 1.2 copy-start.1
  20.8 6.1 %copy-start.4 = (bf16[8,128,1024]{2,1,0:T(8,128)(2,1)S(1)}, bf16[8,128,1024]{2,1,0:T(8,128)(2,1)}, u32[]{:S(2)}) copy-start(bf16[8,128,1024]{2,1,0:T(8,128)(2,1)} %param.7) | copy-start | bytes 6291460
  20.8 99.6 %all-to-all-start = ((bf16[16,2,8,64,128]{4,3,2,1,0:T(8,128)(2,1)}), bf16[16,2,8,64,128]{4,3,2,1,0:T(8,128)(2,1)}, u32[]{:S(2)}, u32[]{:S(2)}) async-start(bf16[16,2,8,64,128]{4,3,2,1,0:T(8,128)(2,1)} %shard_map.76), calls=%async_computation | async-start | bytes 8388608 | tf_op jit(solution)/shard_map/all_to_all | solution.py:214
  140.3 11.0 %all-to-all-start.2 = ((f32[16,3,512]{2,1,0:T(4,128)}), f32[16,3,512]{2,1,0:T(4,128)S(1)}, u32[]{:S(2)}, u32[]{:S(2)}) async-start(f32[16,3,512]{2,1,0:T(4,128)} %pad_maximum_fusion), calls=%async_computation.2 | async-start | bytes 262144 | tf_op jit(solution)/shard_map/all_to_all | solution.py:235
  153.5 11.3 %all-to-all-start.3 = ((f32[16,2,512]{2,1,0:T(2,128)}), f32[16,2,512]{2,1,0:T(2,128)S(1)}, u32[]{:S(2)}, u32[]{:S(2)}) async-start(f32[16,2,512]{2,1,0:T(2,128)} %gather_fusion.5), calls=%async_computation.3 | async-start | bytes 131072 | tf_op jit(solution)/shard_map/all_to_all | solution.py:257
  165.2 5.6 %copy-start.2 = (bf16[16,8,128,128]{3,2,1,0:T(8,128)(2,1)S(1)}, bf16[16,8,128,128]{3,2,1,0:T(8,128)(2,1)}, u32[]{:S(2)}) copy-start(bf16[16,8,128,128]{3,2,1,0:T(8,128)(2,1)} %gather_fusion.2) | copy-start | bytes 12582916
  172.0 4.1 %copy-start.3 = (f32[16,8,64,128]{3,2,1,0:T(8,128)S(1)}, f32[16,8,64,128]{3,2,1,0:T(8,128)}, u32[]{:S(2)}) copy-start(f32[16,8,64,128]{3,2,1,0:T(8,128)} %convolution_multiply_fusion) | copy-start | bytes 12582916
  172.8 25.7 %collective-permute-start.3 = (bf16[2,8,64,128]{3,2,1,0:T(8,128)(2,1)S(1)}, bf16[2,8,64,128]{3,2,1,0:T(8,128)(2,1)S(1)}, u32[]{:S(2)}, u32[]{:S(2)}) collective-permute-start(bf16[2,8,64,128]{3,2,1,0:T(8,128)(2,1)S(1)} %get-tuple-element.33), channel_id=1, source_target_pairs={{0,4},{4,8},{8,12},{12,16},{16,20},{20,24},{24,28},{28,0},{1,5},{5... | collective-permute-start | bytes 786440 | tf_op jit(solution)/shard_map/ppermute | solution.py:172
  174.7 25.3 %collective-permute-start.4 = (bf16[2,8,64,128]{3,2,1,0:T(8,128)(2,1)S(1)}, bf16[2,8,64,128]{3,2,1,0:T(8,128)(2,1)S(1)}, u32[]{:S(2)}, u32[]{:S(2)}) collective-permute-start(bf16[2,8,64,128]{3,2,1,0:T(8,128)(2,1)S(1)} %get-tuple-element.32), channel_id=1, source_target_pairs={{0,8},{4,12},{8,16},{12,20},{16,24},{20,28},{24,0},{28,4},{1,9},{5... | collective-permute-start | bytes 786440 | tf_op jit(solution)/shard_map/ppermute | solution.py:172
  177.5 28.0 %collective-permute-start.5 = (bf16[2,8,64,128]{3,2,1,0:T(8,128)(2,1)S(1)}, bf16[2,8,64,128]{3,2,1,0:T(8,128)(2,1)S(1)}, u32[]{:S(2)}, u32[]{:S(2)}) collective-permute-start(bf16[2,8,64,128]{3,2,1,0:T(8,128)(2,1)S(1)} %get-tuple-element.31), channel_id=1, source_target_pairs={{0,12},{4,16},{8,20},{12,24},{16,28},{20,0},{24,4},{28,8},{1,13},{... | collective-permute-start | bytes 786440 | tf_op jit(solution)/shard_map/ppermute | solution.py:172
  179.9 26.1 %collective-permute-start.6 = (bf16[2,8,64,128]{3,2,1,0:T(8,128)(2,1)S(1)}, bf16[2,8,64,128]{3,2,1,0:T(8,128)(2,1)S(1)}, u32[]{:S(2)}, u32[]{:S(2)}) collective-permute-start(bf16[2,8,64,128]{3,2,1,0:T(8,128)(2,1)S(1)} %get-tuple-element.30), channel_id=1, source_target_pairs={{0,16},{4,20},{8,24},{12,28},{16,0},{20,4},{24,8},{28,12},{1,17},{... | collective-permute-start | bytes 786440 | tf_op jit(solution)/shard_map/ppermute | solution.py:172
  181.4 24.6 %collective-permute-start.7 = (bf16[2,8,64,128]{3,2,1,0:T(8,128)(2,1)S(1)}, bf16[2,8,64,128]{3,2,1,0:T(8,128)(2,1)S(1)}, u32[]{:S(2)}, u32[]{:S(2)}) collective-permute-start(bf16[2,8,64,128]{3,2,1,0:T(8,128)(2,1)S(1)} %get-tuple-element.29), channel_id=1, source_target_pairs={{0,20},{4,24},{8,28},{12,0},{16,4},{20,8},{24,12},{28,16},{1,21},{... | collective-permute-start | bytes 786440 | tf_op jit(solution)/shard_map/ppermute | solution.py:172
  198.5 18.7 %collective-permute-start.8 = (bf16[2,8,64,128]{3,2,1,0:T(8,128)(2,1)S(1)}, bf16[2,8,64,128]{3,2,1,0:T(8,128)(2,1)S(1)}, u32[]{:S(2)}, u32[]{:S(2)}) collective-permute-start(bf16[2,8,64,128]{3,2,1,0:T(8,128)(2,1)S(1)} %get-tuple-element.28), channel_id=1, source_target_pairs={{0,24},{4,28},{8,0},{12,4},{16,8},{20,12},{24,16},{28,20},{1,25},{... | collective-permute-start | bytes 786440 | tf_op jit(solution)/shard_map/ppermute | solution.py:172
  200.0 17.2 %collective-permute-start.9 = (bf16[2,8,64,128]{3,2,1,0:T(8,128)(2,1)S(1)}, bf16[2,8,64,128]{3,2,1,0:T(8,128)(2,1)S(1)}, u32[]{:S(2)}, u32[]{:S(2)}) collective-permute-start(bf16[2,8,64,128]{3,2,1,0:T(8,128)(2,1)S(1)} %get-tuple-element.27), channel_id=1, source_target_pairs={{0,28},{4,0},{8,4},{12,8},{16,12},{20,16},{24,20},{28,24},{1,29},{... | collective-permute-start | bytes 786440 | tf_op jit(solution)/shard_map/ppermute | solution.py:172

commit v21 on v19

--- a/solution.py
+++ b/solution.py
@@ -211,7 +211,12 @@
 
     pair_send = gather_pairs(slot_span, queries, out_grad)
     row_send = jnp.where(slot_valid, local_row[slot_item], -1)
-    pair_recv = lax.all_to_all(pair_send, "seq", split_axis=0, concat_axis=0, tiled=True)
+    if seq_count <= 8:
+        pair_recv = seq_exchange(
+            pair_send.reshape((seq_count, slot_depth) + pair_send.shape[1:]), seq_count
+        ).reshape(pair_send.shape)
+    else:
+        pair_recv = lax.all_to_all(pair_send, "seq", split_axis=0, concat_axis=0, tiled=True)
     row_recv = lax.all_to_all(row_send, "seq", split_axis=0, concat_axis=0, tiled=True)
 
     row_index = jnp.clip(row_recv, 0, rows_here - 1)

time: 217 us -> 226 us (1.041)
  local copies, waits for them, and re-layouts: 30.5 us -> 42.3 us
    all_to_all x1 -> x0, waiting for transfers between devices: 68.4 us -> none  [per_device(): lax.all_to_all(pair_send, 'seq', split_axis=0, concat_axis=0, tiled=True)]
    ppermute x7 -> x14, waiting for transfers between devices: 25.1 us -> 91.1 us  [seq_exchange(): lax.ppermute(lax.dynamic_index_in_dim(blocks, (me + shift) % seq_count, k...]
    dynamic_update_slice x7 -> x14, local copies, waits for them, and re-layouts: 0.26 us -> 9.31 us  [seq_exchange(): lax.dynamic_update_index_in_dim(result, sent, (me - shift) % seq_count, a...]
    ppermute x7 -> x14, starting transfers between devices: 8.81 us -> 17.6 us  [seq_exchange(): lax.ppermute(lax.dynamic_index_in_dim(blocks, (me + shift) % seq_count, k...]
    all_to_all x1 -> x0, starting transfers between devices: 5.57 us -> none  [per_device(): lax.all_to_all(pair_send, 'seq', split_axis=0, concat_axis=0, tiled=True)]
    broadcast_in_dim x1 -> x2, local copies, waits for them, and re-layouts: 0.51 us -> 3.54 us  [seq_exchange(): result = jnp.zeros_like(blocks)]
    all_to_all x1, waiting for transfers between devices: 0.01 us -> 2.64 us  [per_device(): lax.all_to_all(row_send, 'seq', split_axis=0, concat_axis=0, tiled=True)]
    ppermute x3, waiting for transfers between devices: 2.47 us -> 0.01 us  [gather_over(): lax.ppermute(block, axis_name, perm=[(i, (i + shift) % axis_count) for i...]
  transfers between devices with their start and end apart: 14 -> 20, of which waited for: 8 -> 9; matrix products, arithmetic and copies ran while one was open for 12% -> 15% of each run, Pallas kernels for 8% -> 7%
where the time goes in v21:
time: 226 us; the launch traced here: 225 us
  waiting for transfers between devices  102 us (45%)
  local copies, waits for them, and re-layouts  42.3 us (19%)
  starting transfers between devices  33.8 us (15%)
  Pallas kernels  19.9 us (9%)
  matrix products  16.8 us (7%)
  other arithmetic  9.03 us (4%)
    ppermute x14, waiting for transfers between devices, seq_exchange(): lax.ppermute(lax.dynamic_index_in_dim(blocks, (me + shift) % seq_count, k...  91.1 us
    ppermute x14, starting transfers between devices, seq_exchange(): lax.ppermute(lax.dynamic_index_in_dim(blocks, (me + shift) % seq_count, k...  17.6 us
    pallas_call x1, Pallas kernels, kv_grads(): pl.pallas_call(kv_kernel, grid_spec=grid_spec, out_shape=[out_shape, out_...  14.7 us
    dynamic_update_slice x14, local copies, waits for them, and re-layouts, seq_exchange(): lax.dynamic_update_index_in_dim(result, sent, (me - shift) % seq_count, a...  9.31 us
    dot_general x1, matrix products, per_device(): jnp.einsum('bhid,bhjd->bhij', grad_heads, value_heads, preferred_element_...  8.99 us
    unnamed x22, local copies, waits for them, and re-layouts  7.12 us
    dot_general x1, matrix products, per_device(): jnp.einsum('bhid,bhjd->bhij', query_heads, key_heads, preferred_element_t...  6.56 us
    reshape x2, local copies, waits for them, and re-layouts, split_heads(): return tensor.reshape(tensor.shape[:-1] + (tensor.shape[-1] // HEAD, HEAD))  6.49 us
  transfers between devices with their start and end apart: 20, of which 9 were waited for; matrix products, arithmetic and copies ran while one was open for 15% of the time, Pallas kernels for 7%

profile of v21, /device:TPU:15, one launch (start us, length us, event | category | flops | bytes accessed | tf_op | source)
XLA Modules:
  0.0 224.9 jit_solution(16988757855321148630)
XLA Ops:
  0.6 0.9 collective-permute-start
  1.5 1.2 collective-permute-start.1
  2.7 3.0 %copy.26 = bf16[8,128,1024]{1,2,0:T(8,128)(2,1)S(1)} copy(bf16[8,128,1024]{2,1,0:T(8,128)(2,1)} %param.7) | data formatting | bytes 4194304 | tf_op args[2]
  5.7 2.6 %copy.27 = bf16[8,128,8,128]{3,1,2,0:T(8,128)(2,1)} copy(bf16[8,128,8,128]{1,3,2,0:T(8,128)(2,1)S(1)} %bitcast.132) | data formatting | bytes 4194304 | tf_op jit(solution)/shard_map/reshape | solution.py:17
  8.4 4.1 %copy.29 = bf16[8,128,1024]{1,2,0:T(8,128)(2,1)} copy(bf16[8,128,1024]{2,1,0:T(8,128)(2,1)} %param.8) | data formatting | bytes 4194304 | tf_op args[3]
  12.4 3.9 %copy.30 = bf16[8,128,8,128]{3,1,2,0:T(8,128)(2,1)} copy(bf16[8,128,8,128]{1,3,2,0:T(8,128)(2,1)} %bitcast.133) | data formatting | bytes 4194304 | tf_op jit(solution)/shard_map/reshape | solution.py:17
  18.5 3.3 %shard_map.76 = bf16[16,2,8,64,128]{4,3,2,1,0:T(8,128)(2,1)} custom-call(s32[16]{0:T(128)S(1)} %broadcast_clamp_fusion.1.span_ref, bf16[8,64,1024]{2,1,0:T(8,128)(2,1)S(1)} %copy-done, bf16[8,64,1024]{2,1,0:T(8,128)(2,1)S(1)} %copy-done.1), custom_call_target="tpu_custom_call" | custom-call | tf_op jit(solution)/shard_map/pallas_call | solution.py:112
  21.8 3.0 %broadcast_in_dim.97 = bf16[8,2,2,8,64,128]{5,4,3,2,1,0:T(8,128)(2,1)} broadcast(bf16[]{:T(256)} %constant.263.clone.1), dimensions={} | broadcast | bytes 4194306 | tf_op jit(solution)/shard_map/broadcast_in_dim | solution.py:167
  24.8 2.3 %dynamic-slice_bitcast_fusion = (bf16[2,2,8,64,128]{4,3,2,1,0:T(8,128)(2,1)}, bf16[2,2,8,64,128]{4,3,2,1,0:T(8,128)(2,1)}, bf16[2,2,8,64,128]{4,3,2,1,0:T(8,128)...) fusion(bf16[8,2,2,8,64,128]{5,4,3,2,1,0:T(8,128)(2,1)S(1)} %bit, ...), kind=kLoop, calls=%fused_computation.24 | loop fusion | bytes 8388640 | tf_op jit(solution)/shard_map/jit(dynamic_index_in_dim)/squeeze | solution.py:173
  27.2 1.3 collective-permute-start.3
  29.2 4.7 %all-to-all-start = ((s32[8,2,1]{1,2,0:T(1,128)}), s32[8,2,1]{1,2,0:T(1,128)S(1)}, u32[]{:S(2)}, u32[]{:S(2)}) async-start(s32[8,2,1]{1,2,0:T(1,128)} %bitcast.25), calls=%async_computation | async-start | bytes 8192 | tf_op jit(solution)/shard_map/all_to_all | solution.py:220
  33.9 1.2 collective-permute-start.4
  35.0 0.9 collective-permute-start.5
  36.0 1.4 collective-permute-start.6
  37.4 1.2 collective-permute-start.7
  38.6 2.6 %all-to-all-done = s32[8,2,1]{1,2,0:T(1,128)S(1)} async-done(((s32[8,2,1]{1,2,0:T(1,128)}), s32[8,2,1]{1,2,0:T(1,128)S(1)}, u32[]{:S(2)}, u32[]{:S(2)}) %all-to-all-start) | async-done | bytes 96 | tf_op jit(solution)/shard_map/all_to_all | solution.py:220
  42.7 3.0 %gather_fusion.2 = bf16[16,8,128,128]{3,2,1,0:T(8,128)(2,1)} fusion(bf16[8,8,128,128]{3,2,1,0:T(8,128)(2,1)S(1)} %bitcast.128, s32[1024]{0:T(1024)S(1)} %pad_clamp_fusion.2), kind=kCustom, calls=%fused_computation.2 | custom fusion | bytes 8388672 | tf_op jit(solution)/shard_map/gather | solution.py:225
  45.7 4.7 %gather_fusion.3 = bf16[16,8,128,128]{3,2,1,0:T(8,128)(2,1)} fusion(bf16[8,8,128,128]{3,2,1,0:T(8,128)(2,1)} %bitcast.129, s32[1024]{0:T(1024)S(1)} %pad_clamp_fusion.2), kind=kCustom, calls=%fused_computation.3 | custom fusion | bytes 8388672 | tf_op jit(solution)/shard_map/gather | solution.py:226
  50.4 1.3 collective-permute-start.8
  51.7 0.8 bitcast_dynamic-update-slice_fusion.6
  52.5 1.4 collective-permute-start.9
  54.0 1.9 bitcast_dynamic-update-slice_fusion.5
  55.9 51.0 %collective-permute-done.5 = bf16[2,2,8,64,128]{4,3,2,1,0:T(8,128)(2,1)} collective-permute-done((bf16[2,2,8,64,128]{4,3,2,1,0:T(8,128)(2,1)}, bf16[2,2,8,64,128]{4,3,2,1,0:T(8,128)(2,1)}, u32[]{:S(2)}, u32[]{:S(2)}) %collective-permute-start.5) | collective-permute-done | bytes 524320 | tf_op jit(solution)/shard_map/ppermute | solution.py:172
  106.9 1.9 bitcast_dynamic-update-slice_fusion.4
  108.8 9.3 %collective-permute-done.6 = bf16[2,2,8,64,128]{4,3,2,1,0:T(8,128)(2,1)} collective-permute-done((bf16[2,2,8,64,128]{4,3,2,1,0:T(8,128)(2,1)}, bf16[2,2,8,64,128]{4,3,2,1,0:T(8,128)(2,1)}, u32[]{:S(2)}, u32[]{:S(2)}) %collective-permute-start.6) | collective-permute-done | bytes 524320 | tf_op jit(solution)/shard_map/ppermute | solution.py:172
  118.1 1.9 bitcast_dynamic-update-slice_fusion.3
  120.0 0.8 bitcast_dynamic-update-slice_fusion.2
  120.9 0.8 bitcast_dynamic-update-slice_fusion.1
  121.8 5.6 %collective-permute-done.9 = bf16[2,2,8,64,128]{4,3,2,1,0:T(8,128)(2,1)S(1)} collective-permute-done((bf16[2,2,8,64,128]{4,3,2,1,0:T(8,128)(2,1)S(1)}, bf16[2,2,8,64,128]{4,3,2,1,0:T(8,128)(2,1)S(1)}, u32[]{:S(2)}, u32[]{:S(2)}) %collective-permute-start.9) | collective-permute-done | bytes 524320 | tf_op jit(solution)/shard_map/ppermute | solution.py:172
  127.3 0.9 bitcast_dynamic-update-slice_fusion
  128.2 6.6 %fusion.15 = (f32[16,8,64]{2,1,0:T(8,128)S(1)}, f32[16,8,64,128]{3,2,1,0:T(8,128)}) fusion(bf16[16,8,128,128]{3,2,1,0:T(8,128)(2,1)S(1)} %copy-done.3, bf16[16,2,8,64,128]{4,3,2,1,0:T(8,128)(2,1)} %bitcast.21.pair_ref), kind=kOutput, calls=%fused_computation.103 | convolution fusion | flops 270524416 | bytes 10518528 | tf_op jit(solution)/shard_map/bhid,bhjd->bhij/dot_general | solution.py:229
  134.9 9.0 %fusion = (f32[16,8,64]{2,1,0:T(8,128)S(1)}, f32[16,8,64]{2,1,0:T(8,128)S(1)}, f32[16,8,64,128]{3,2,1,0:T(8,128)}) fusion(f32[16,8,64,128]{3,2,1,0:T(8,128)} %get-tuple-element.6, f32[16,8,64]{2,1,0:T(8,128)S(1)} %get-tuple-element.43, bf16[16,8,128,128]{3,2,1,0:T(8,128)(2,1)} %gather_fusion.3, bf16[16,2,8,64,128]{4,3,2,1,0:T(8,128)(2,1)} %bitcast.21.pair_ref), kind=kOutput, calls=%fused_computation.10 | convolution fusion | flops 272613376 | bytes 14778368 | tf_op jit(solution)/shard_map/bhid,bhjd->bhij/dot_general | solution.py:232
  144.8 4.5 %all-to-all-start.1 = ((f32[16,3,512]{2,1,0:T(4,128)}), f32[16,3,512]{2,1,0:T(4,128)S(1)}, u32[]{:S(2)}, u32[]{:S(2)}) async-start(f32[16,3,512]{2,1,0:T(4,128)} %pad_maximum_fusion), calls=%async_computation.1 | async-start | bytes 262144 | tf_op jit(solution)/shard_map/all_to_all | solution.py:240
  149.3 4.6 %all-to-all-done.1 = f32[16,3,512]{2,1,0:T(4,128)S(1)} async-done(((f32[16,3,512]{2,1,0:T(4,128)}), f32[16,3,512]{2,1,0:T(4,128)S(1)}, u32[]{:S(2)}, u32[]{:S(2)}) %all-to-all-start.1) | async-done | bytes 98336 | tf_op jit(solution)/shard_map/all_to_all | solution.py:240
  154.9 1.2 gather_fusion.5
  156.1 4.9 %all-to-all-start.2 = ((f32[16,2,512]{2,1,0:T(2,128)}), f32[16,2,512]{2,1,0:T(2,128)S(1)}, u32[]{:S(2)}, u32[]{:S(2)}) async-start(f32[16,2,512]{2,1,0:T(2,128)} %gather_fusion.5), calls=%async_computation.2 | async-start | bytes 131072 | tf_op jit(solution)/shard_map/all_to_all | solution.py:252
  161.1 3.7 %all-to-all-done.2 = f32[16,2,512]{2,1,0:T(2,128)S(1)} async-done(((f32[16,2,512]{2,1,0:T(2,128)}), f32[16,2,512]{2,1,0:T(2,128)S(1)}, u32[]{:S(2)}, u32[]{:S(2)}) %all-to-all-start.2) | async-done | bytes 65568 | tf_op jit(solution)/shard_map/all_to_all | solution.py:252
  165.1 5.5 %multiply_convert_fusion.grads_ref = bf16[16,8,64,128]{3,2,1,0:T(8,128)(2,1)S(1)} fusion(f32[16,8,64,128]{3,2,1,0:T(8,128)} %get-tuple-element.45, f32[16,8,64,128]{3,2,1,0:T(8,128)} %get-tuple-element.6, f32[16,8,64]{2,1,0:T(8,128)S(1)} %sub.108, f32[16,8,64]{2,1,0:T(8,128)S(1)} %sub.105), kind=kLoop, calls=%fused_computation.7 | loop fusion | flops 5242880 | bytes 10551296 | tf_op jit(solution)/shard_map/convert_element_type | solution.py:259
  170.6 1.2 convolution_convert_fusion
  172.6 1.1 collective-permute-start.10
  174.0 2.8 %collective-permute-start.12 = (bf16[2,8,64,128]{3,2,1,0:T(8,128)(2,1)S(1)}, bf16[2,8,64,128]{3,2,1,0:T(8,128)(2,1)S(1)}, u32[]{:S(2)}, u32[]{:S(2)}) collective-permute-start(bf16[2,8,64,128]{3,2,1,0:T(8,128)(2,1)S(1)} %get-tuple-element.31), channel_id=1, source_target_pairs={{0,12},{4,16},{8,20},{12,24},{16,28},{20,0},{24,4},{28,8},{1,13},{... | collective-permute-start | bytes 786440 | tf_op jit(solution)/shard_map/ppermute | solution.py:172
  176.9 2.3 %collective-permute-start.14 = (bf16[2,8,64,128]{3,2,1,0:T(8,128)(2,1)S(1)}, bf16[2,8,64,128]{3,2,1,0:T(8,128)(2,1)S(1)}, u32[]{:S(2)}, u32[]{:S(2)}) collective-permute-start(bf16[2,8,64,128]{3,2,1,0:T(8,128)(2,1)S(1)} %get-tuple-element.29), channel_id=1, source_target_pairs={{0,20},{4,24},{8,28},{12,0},{16,4},{20,8},{24,12},{28,16},{1,21},{... | collective-permute-start | bytes 786440 | tf_op jit(solution)/shard_map/ppermute | solution.py:172
  179.1 1.4 exponential_convert_fusion.probs_ref
  180.5 14.7 %shard_map.78 = (bf16[8,128,1024]{2,1,0:T(8,128)(2,1)}, bf16[8,128,1024]{2,1,0:T(8,128)(2,1)}) custom-call(s32[16]{0:T(128)S(1)} %all_to_all.14.rows_ref, bf16[16,8,64,128]{3,2,1,0:T(8,128)(2,1)S(1)} %exponential_convert_fusion.probs_ref, bf16[16,8,64,128]{3,2,1,0:T(8,128)(2,1)S(1)} %multiply_convert_fusion.grads_ref, ...), custom_call_target="tpu_custom_call" | custom-call | tf_op jit(solution)/shard_map/pallas_call | solution.py:74
  195.2 2.4 %collective-permute-start.15 = (bf16[2,8,64,128]{3,2,1,0:T(8,128)(2,1)S(1)}, bf16[2,8,64,128]{3,2,1,0:T(8,128)(2,1)S(1)}, u32[]{:S(2)}, u32[]{:S(2)}) collective-permute-start(bf16[2,8,64,128]{3,2,1,0:T(8,128)(2,1)S(1)} %get-tuple-element.28), channel_id=1, source_target_pairs={{0,24},{4,28},{8,0},{12,4},{16,8},{20,12},{24,16},{28,20},{1,25},{... | collective-permute-start | bytes 786440 | tf_op jit(solution)/shard_map/ppermute | solution.py:172
  197.8 15.8 %collective-permute-done.13 = bf16[2,8,64,128]{3,2,1,0:T(8,128)(2,1)S(1)} collective-permute-done((bf16[2,8,64,128]{3,2,1,0:T(8,128)(2,1)S(1)}, bf16[2,8,64,128]{3,2,1,0:T(8,128)(2,1)S(1)}, u32[]{:S(2)}, u32[]{:S(2)}) %collective-permute-start.13) | collective-permute-done | bytes 262176 | tf_op jit(solution)/shard_map/ppermute | solution.py:172
  213.7 9.2 %collective-permute-done.15 = bf16[2,8,64,128]{3,2,1,0:T(8,128)(2,1)S(1)} collective-permute-done((bf16[2,8,64,128]{3,2,1,0:T(8,128)(2,1)S(1)}, bf16[2,8,64,128]{3,2,1,0:T(8,128)(2,1)S(1)}, u32[]{:S(2)}, u32[]{:S(2)}) %collective-permute-start.15) | collective-permute-done | bytes 262176 | tf_op jit(solution)/shard_map/ppermute | solution.py:172
  223.0 1.8 shard_map.77
  (88 shorter events, 8.1 us)
Async XLA Ops:
  0.6 15.8 %collective-permute-start = (s32[2,2]{1,0:T(2,128)}, s32[2,2]{1,0:T(2,128)S(1)}, u32[]{:S(2)}, u32[]{:S(2)}) collective-permute-start(s32[2,2]{1,0:T(2,128)} %param.9), channel_id=1, source_target_pairs={{0,1},{1,2},{2,3},{3,0},{4,5},{5,6},{6,7},{7,4},{8,9},{9,10},{10,1... | collective-permute-start | bytes 56 | tf_op jit(solution)/shard_map/ppermute | solution.py:158
  1.5 14.9 %collective-permute-start.1 = (s32[2,2]{1,0:T(2,128)}, s32[2,2]{1,0:T(2,128)S(1)}, u32[]{:S(2)}, u32[]{:S(2)}) collective-permute-start(s32[2,2]{1,0:T(2,128)} %param.9), channel_id=1, source_target_pairs={{0,2},{1,3},{2,0},{3,1},{4,6},{5,7},{6,4},{7,5},{8,10},{9,11},{10,... | collective-permute-start | bytes 56 | tf_op jit(solution)/shard_map/ppermute | solution.py:158
  2.7 13.8 %collective-permute-start.2 = (s32[2,2]{1,0:T(2,128)}, s32[2,2]{1,0:T(2,128)S(1)}, u32[]{:S(2)}, u32[]{:S(2)}) collective-permute-start(s32[2,2]{1,0:T(2,128)} %param.9), channel_id=1, source_target_pairs={{0,3},{1,0},{2,1},{3,2},{4,7},{5,4},{6,5},{7,6},{8,11},{9,8},{10,9... | collective-permute-start | bytes 56 | tf_op jit(solution)/shard_map/ppermute | solution.py:158
  8.3 8.0 %copy-start.9 = (s32[2,2]{1,0:T(2,128)S(1)}, s32[2,2]{1,0:T(2,128)}, u32[]{:S(2)}) copy-start(s32[2,2]{1,0:T(2,128)} %param.9) | copy-start | bytes 52
  8.3 10.1 %copy-start = (bf16[8,64,1024]{2,1,0:T(8,128)(2,1)S(1)}, bf16[8,64,1024]{2,1,0:T(8,128)(2,1)}, u32[]{:S(2)}) copy-start(bf16[8,64,1024]{2,1,0:T(8,128)(2,1)} %query_ref.1) | copy-start | bytes 3145732
  8.4 10.1 %copy-start.1 = (bf16[8,64,1024]{2,1,0:T(8,128)(2,1)S(1)}, bf16[8,64,1024]{2,1,0:T(8,128)(2,1)}, u32[]{:S(2)}) copy-start(bf16[8,64,1024]{2,1,0:T(8,128)(2,1)} %grad_ref.1) | copy-start | bytes 3145732
  21.8 3.0 %copy-start.6 = (bf16[16,2,8,64,128]{4,3,2,1,0:T(8,128)(2,1)S(1)}, bf16[16,2,8,64,128]{4,3,2,1,0:T(8,128)(2,1)}, u32[]{:S(2)}) copy-start(bf16[16,2,8,64,128]{4,3,2,1,0:T(8,128)(2,1)} %shard_map.76) | copy-start | bytes 12582916
  24.8 17.8 %copy-start.5 = (bf16[8,128,8,128]{3,1,2,0:T(8,128)(2,1)S(1)}, bf16[8,128,8,128]{3,1,2,0:T(8,128)(2,1)}, u32[]{:S(2)}) copy-start(bf16[8,128,8,128]{3,1,2,0:T(8,128)(2,1)} %copy.27) | copy-start | bytes 6291460
  27.2 23.3 %collective-permute-start.3 = (bf16[2,2,8,64,128]{4,3,2,1,0:T(8,128)(2,1)}, bf16[2,2,8,64,128]{4,3,2,1,0:T(8,128)(2,1)S(1)}, u32[]{:S(2)}, u32[]{:S(2)}) collective-permute-start(bf16[2,2,8,64,128]{4,3,2,1,0:T(8,128)(2,1)} %get-tuple-element.25), channel_id=1, source_target_pairs={{0,4},{4,8},{8,12},{12,16},{16,20},{20,24},{24,28},{28,0},{1,5},{5... | collective-permute-start | bytes 1572872 | tf_op jit(solution)/shard_map/ppermute | solution.py:172
  29.2 12.1 %all-to-all-start = ((s32[8,2,1]{1,2,0:T(1,128)}), s32[8,2,1]{1,2,0:T(1,128)S(1)}, u32[]{:S(2)}, u32[]{:S(2)}) async-start(s32[8,2,1]{1,2,0:T(1,128)} %bitcast.25), calls=%async_computation | async-start | bytes 8192 | tf_op jit(solution)/shard_map/all_to_all | solution.py:220
  33.9 18.7 %collective-permute-start.4 = (bf16[2,2,8,64,128]{4,3,2,1,0:T(8,128)(2,1)}, bf16[2,2,8,64,128]{4,3,2,1,0:T(8,128)(2,1)}, u32[]{:S(2)}, u32[]{:S(2)}) collective-permute-start(bf16[2,2,8,64,128]{4,3,2,1,0:T(8,128)(2,1)} %get-tuple-element.24), channel_id=1, source_target_pairs={{0,8},{4,12},{8,16},{12,20},{16,24},{20,28},{24,0},{28,4},{1,9},{5... | collective-permute-start | bytes 1572872 | tf_op jit(solution)/shard_map/ppermute | solution.py:172
  35.0 71.9 %collective-permute-start.5 = (bf16[2,2,8,64,128]{4,3,2,1,0:T(8,128)(2,1)}, bf16[2,2,8,64,128]{4,3,2,1,0:T(8,128)(2,1)}, u32[]{:S(2)}, u32[]{:S(2)}) collective-permute-start(bf16[2,2,8,64,128]{4,3,2,1,0:T(8,128)(2,1)} %get-tuple-element.23), channel_id=1, source_target_pairs={{0,12},{4,16},{8,20},{12,24},{16,28},{20,0},{24,4},{28,8},{1,13},{... | collective-permute-start | bytes 1572872 | tf_op jit(solution)/shard_map/ppermute | solution.py:172
  36.0 82.2 %collective-permute-start.6 = (bf16[2,2,8,64,128]{4,3,2,1,0:T(8,128)(2,1)}, bf16[2,2,8,64,128]{4,3,2,1,0:T(8,128)(2,1)}, u32[]{:S(2)}, u32[]{:S(2)}) collective-permute-start(bf16[2,2,8,64,128]{4,3,2,1,0:T(8,128)(2,1)} %get-tuple-element.22), channel_id=1, source_target_pairs={{0,16},{4,20},{8,24},{12,28},{16,0},{20,4},{24,8},{28,12},{1,17},{... | collective-permute-start | bytes 1572872 | tf_op jit(solution)/shard_map/ppermute | solution.py:172
  37.4 82.6 %collective-permute-start.7 = (bf16[2,2,8,64,128]{4,3,2,1,0:T(8,128)(2,1)}, bf16[2,2,8,64,128]{4,3,2,1,0:T(8,128)(2,1)S(1)}, u32[]{:S(2)}, u32[]{:S(2)}) collective-permute-start(bf16[2,2,8,64,128]{4,3,2,1,0:T(8,128)(2,1)} %get-tuple-element.21), channel_id=1, source_target_pairs={{0,20},{4,24},{8,28},{12,0},{16,4},{20,8},{24,12},{28,16},{1,21},{... | collective-permute-start | bytes 1572872 | tf_op jit(solution)/shard_map/ppermute | solution.py:172
  45.7 4.7 %copy-start.8 = (bf16[2,2,8,64,128]{4,3,2,1,0:T(8,128)(2,1)S(1)}, bf16[2,2,8,64,128]{4,3,2,1,0:T(8,128)(2,1)}, u32[]{:S(2)}) copy-start(bf16[2,2,8,64,128]{4,3,2,1,0:T(8,128)(2,1)} %get-tuple-element.20) | copy-start | bytes 1572868
  45.7 6.9 %copy-start.7 = (bf16[2,2,8,64,128]{4,3,2,1,0:T(8,128)(2,1)S(1)}, bf16[2,2,8,64,128]{4,3,2,1,0:T(8,128)(2,1)}, u32[]{:S(2)}) copy-start(bf16[2,2,8,64,128]{4,3,2,1,0:T(8,128)(2,1)} %get-tuple-element.19) | copy-start | bytes 1572868
  50.4 77.8 %copy-start.3 = (bf16[16,8,128,128]{3,2,1,0:T(8,128)(2,1)S(1)}, bf16[16,8,128,128]{3,2,1,0:T(8,128)(2,1)}, u32[]{:S(2)}) copy-start(bf16[16,8,128,128]{3,2,1,0:T(8,128)(2,1)} %gather_fusion.2) | copy-start | bytes 12582916
  50.4 70.5 %collective-permute-start.8 = (bf16[2,2,8,64,128]{4,3,2,1,0:T(8,128)(2,1)S(1)}, bf16[2,2,8,64,128]{4,3,2,1,0:T(8,128)(2,1)S(1)}, u32[]{:S(2)}, u32[]{:S(2)}) collective-permute-start(bf16[2,2,8,64,128]{4,3,2,1,0:T(8,128)(2,1)S(1)} %copy-done.8), channel_id=1, source_target_pairs={{0,24},{4,28},{8,0},{12,4},{16,8},{20,12},{24,16},{28,20},{1,25},{... | collective-permute-start | bytes 1572872 | tf_op jit(solution)/shard_map/ppermute | solution.py:172
  52.5 74.8 %collective-permute-start.9 = (bf16[2,2,8,64,128]{4,3,2,1,0:T(8,128)(2,1)S(1)}, bf16[2,2,8,64,128]{4,3,2,1,0:T(8,128)(2,1)S(1)}, u32[]{:S(2)}, u32[]{:S(2)}) collective-permute-start(bf16[2,2,8,64,128]{4,3,2,1,0:T(8,128)(2,1)S(1)} %copy-done.7), channel_id=1, source_target_pairs={{0,28},{4,0},{8,4},{12,8},{16,12},{20,16},{24,20},{28,24},{1,29},{... | collective-permute-start | bytes 1572872 | tf_op jit(solution)/shard_map/ppermute | solution.py:172
  144.8 9.1 %all-to-all-start.1 = ((f32[16,3,512]{2,1,0:T(4,128)}), f32[16,3,512]{2,1,0:T(4,128)S(1)}, u32[]{:S(2)}, u32[]{:S(2)}) async-start(f32[16,3,512]{2,1,0:T(4,128)} %pad_maximum_fusion), calls=%async_computation.1 | async-start | bytes 262144 | tf_op jit(solution)/shard_map/all_to_all | solution.py:240
  156.1 8.7 %all-to-all-start.2 = ((f32[16,2,512]{2,1,0:T(2,128)}), f32[16,2,512]{2,1,0:T(2,128)S(1)}, u32[]{:S(2)}, u32[]{:S(2)}) async-start(f32[16,2,512]{2,1,0:T(2,128)} %gather_fusion.5), calls=%async_computation.2 | async-start | bytes 131072 | tf_op jit(solution)/shard_map/all_to_all | solution.py:252
  165.1 5.5 %copy-start.4 = (bf16[16,8,128,128]{3,2,1,0:T(8,128)(2,1)S(1)}, bf16[16,8,128,128]{3,2,1,0:T(8,128)(2,1)}, u32[]{:S(2)}) copy-start(bf16[16,8,128,128]{3,2,1,0:T(8,128)(2,1)} %gather_fusion.2) | copy-start | bytes 12582916
  171.8 7.3 %copy-start.2 = (f32[16,8,64,128]{3,2,1,0:T(8,128)S(1)}, f32[16,8,64,128]{3,2,1,0:T(8,128)}, u32[]{:S(2)}) copy-start(f32[16,8,64,128]{3,2,1,0:T(8,128)} %get-tuple-element.6) | copy-start | bytes 12582916
  172.6 22.6 %collective-permute-start.10 = (bf16[2,8,64,128]{3,2,1,0:T(8,128)(2,1)S(1)}, bf16[2,8,64,128]{3,2,1,0:T(8,128)(2,1)S(1)}, u32[]{:S(2)}, u32[]{:S(2)}) collective-permute-start(bf16[2,8,64,128]{3,2,1,0:T(8,128)(2,1)S(1)} %get-tuple-element.33), channel_id=1, source_target_pairs={{0,4},{4,8},{8,12},{12,16},{16,20},{20,24},{24,28},{28,0},{1,5},{5... | collective-permute-start | bytes 786440 | tf_op jit(solution)/shard_map/ppermute | solution.py:172
  173.7 23.9 %collective-permute-start.11 = (bf16[2,8,64,128]{3,2,1,0:T(8,128)(2,1)S(1)}, bf16[2,8,64,128]{3,2,1,0:T(8,128)(2,1)S(1)}, u32[]{:S(2)}, u32[]{:S(2)}) collective-permute-start(bf16[2,8,64,128]{3,2,1,0:T(8,128)(2,1)S(1)} %get-tuple-element.32), channel_id=1, source_target_pairs={{0,8},{4,12},{8,16},{12,20},{16,24},{20,28},{24,0},{28,4},{1,9},{5... | collective-permute-start | bytes 786440 | tf_op jit(solution)/shard_map/ppermute | solution.py:172
  174.0 23.7 %collective-permute-start.12 = (bf16[2,8,64,128]{3,2,1,0:T(8,128)(2,1)S(1)}, bf16[2,8,64,128]{3,2,1,0:T(8,128)(2,1)S(1)}, u32[]{:S(2)}, u32[]{:S(2)}) collective-permute-start(bf16[2,8,64,128]{3,2,1,0:T(8,128)(2,1)S(1)} %get-tuple-element.31), channel_id=1, source_target_pairs={{0,12},{4,16},{8,20},{12,24},{16,28},{20,0},{24,4},{28,8},{1,13},{... | collective-permute-start | bytes 786440 | tf_op jit(solution)/shard_map/ppermute | solution.py:172
  176.8 36.8 %collective-permute-start.13 = (bf16[2,8,64,128]{3,2,1,0:T(8,128)(2,1)S(1)}, bf16[2,8,64,128]{3,2,1,0:T(8,128)(2,1)S(1)}, u32[]{:S(2)}, u32[]{:S(2)}) collective-permute-start(bf16[2,8,64,128]{3,2,1,0:T(8,128)(2,1)S(1)} %get-tuple-element.30), channel_id=1, source_target_pairs={{0,16},{4,20},{8,24},{12,28},{16,0},{20,4},{24,8},{28,12},{1,17},{... | collective-permute-start | bytes 786440 | tf_op jit(solution)/shard_map/ppermute | solution.py:172
  176.9 36.8 %collective-permute-start.14 = (bf16[2,8,64,128]{3,2,1,0:T(8,128)(2,1)S(1)}, bf16[2,8,64,128]{3,2,1,0:T(8,128)(2,1)S(1)}, u32[]{:S(2)}, u32[]{:S(2)}) collective-permute-start(bf16[2,8,64,128]{3,2,1,0:T(8,128)(2,1)S(1)} %get-tuple-element.29), channel_id=1, source_target_pairs={{0,20},{4,24},{8,28},{12,0},{16,4},{20,8},{24,12},{28,16},{1,21},{... | collective-permute-start | bytes 786440 | tf_op jit(solution)/shard_map/ppermute | solution.py:172
  195.2 27.8 %collective-permute-start.15 = (bf16[2,8,64,128]{3,2,1,0:T(8,128)(2,1)S(1)}, bf16[2,8,64,128]{3,2,1,0:T(8,128)(2,1)S(1)}, u32[]{:S(2)}, u32[]{:S(2)}) collective-permute-start(bf16[2,8,64,128]{3,2,1,0:T(8,128)(2,1)S(1)} %get-tuple-element.28), channel_id=1, source_target_pairs={{0,24},{4,28},{8,0},{12,4},{16,8},{20,12},{24,16},{28,20},{1,25},{... | collective-permute-start | bytes 786440 | tf_op jit(solution)/shard_map/ppermute | solution.py:172
  197.6 25.4 %collective-permute-start.16 = (bf16[2,8,64,128]{3,2,1,0:T(8,128)(2,1)S(1)}, bf16[2,8,64,128]{3,2,1,0:T(8,128)(2,1)S(1)}, u32[]{:S(2)}, u32[]{:S(2)}) collective-permute-start(bf16[2,8,64,128]{3,2,1,0:T(8,128)(2,1)S(1)} %get-tuple-element.27), channel_id=1, source_target_pairs={{0,28},{4,0},{8,4},{12,8},{16,12},{20,16},{24,20},{28,24},{1,29},{... | collective-permute-start | bytes 786440 | tf_op jit(solution)/shard_map/ppermute | solution.py:172
